TPU v7x, 512 devices: a whole 4x8x8 slice. The times are simulated.
512 devices in a mesh: seq: 64 (over x, z, y_lo), head: 8 (over y_hi, core).
Axes of the slice: x: 4, y: 8 (y_hi: 4, y_lo: 2; y = y_hi * 2 + y_lo), z: 8, core: 2. Of those that a mesh axis runs over, the one named last changes fastest.
Arguments:
- queries: bfloat16 [8192, 8192], P('seq', 'head'), may hold values from -14 to 14, as said below
- key_tokens: bfloat16 [8192, 1024], P(('seq', 'head')), may hold values from -6 to 6, as said below
- value_tokens: bfloat16 [8192, 1024], P(('seq', 'head')), may hold values from -6 to 6
- key_scales: bfloat16 [128, 8], P('seq', 'head'), may hold values from 0.25 to 2.5
- value_scales: bfloat16 [128, 8], P('seq', 'head'), may hold values from 0.25 to 2.5
- value_means: float32 [1024], P('head'), may hold values from -4 to 4
- doc_lengths: int32 [64], replicated, may hold values from 1 to 5120, 8192 in all
Outputs:
- attended: bfloat16 [8192, 8192], P('seq', 'head')
Inputs may be any that keep to these rules, and one draw needn't show every extreme that they name: `doc_lengths`: positive lengths of the documents in order; they sum to 8192, and the longest has exactly 5120 tokens. `queries`: finite values. `key_tokens`: finite values.
All inputs are finite; a program needn't handle non-finite values.
Results may differ from a plain program's by a relative error of at most 0.002.
Values may be sent and summed in bfloat16 or wider, within the bound.
No kernel may reach another device: no remote copies, remote signals or barrier semaphores. Data moves between devices by JAX's collectives and lax.ppermute only.
A program may use at most 64 MiB of HBM per device.

v0:
```python
import math

import jax
import jax.numpy as jnp
from jax import lax
from jax.sharding import PartitionSpec as P

QH = 64
KVH = 8
HD = 128
BLK = 64


NEG = -1e30


def doc_index(positions, starts):
    return jnp.sum((starts[None, :] <= positions[:, None]).astype(jnp.int32), axis=1) - 1


def block_update(
    totals,
    query_tile,
    query_pos,
    query_doc,
    key_tile,
    value_tile,
    key_scale,
    value_scale,
    key_pos,
    starts,
):
    inv_scale = 1.0 / math.sqrt(HD)
    key_doc = doc_index(key_pos, starts)
    allowed = (key_doc[None, :] == query_doc[:, None]) & (key_pos[None, :] <= query_pos[:, None])

    def update(current):
        run_max, run_sum, accumulate = current
        scores = jnp.einsum(
            "kgrd,nkd->kgrn", query_tile, key_tile, preferred_element_type=jnp.float32
        )
        scores = scores * (key_scale.T * inv_scale)[:, None, None, :]
        scores = jnp.where(allowed[None, None], scores, NEG)
        new_max = jnp.maximum(run_max, jnp.max(scores, axis=-1))
        weights = jnp.where(allowed[None, None], jnp.exp(scores - new_max[..., None]), 0.0)
        factor = jnp.exp(run_max - new_max)
        run_sum = run_sum * factor + jnp.sum(weights, axis=-1)
        scaled = (weights * value_scale.T[:, None, None, :]).astype(jnp.bfloat16)
        accumulate = accumulate * factor[..., None] + jnp.einsum(
            "kgrn,nkd->kgrd", scaled, value_tile, preferred_element_type=jnp.float32
        )
        return (new_max, run_sum, accumulate)

    def keep_state(current):
        return current

    return lax.cond(jnp.any(allowed), update, keep_state, totals)


def fold_packet(totals, packet, query_tile, query_pos, query_doc, starts, heads_kv):
    block_count = packet.shape[0]
    sub_blocks = math.gcd(block_count, max(1, 256 // BLK))
    step_count = block_count // sub_blocks
    key_count = sub_blocks * BLK
    key_part = packet[:, 0, :BLK, :].reshape(step_count, key_count, heads_kv, HD)
    value_part = packet[:, 1, :BLK, :].reshape(step_count, key_count, heads_kv, HD)
    key_scale = packet[:, 0, BLK, :].reshape(block_count, heads_kv, HD)[:, :, 0].astype(jnp.float32)
    value_scale = (
        packet[:, 1, BLK, :].reshape(block_count, heads_kv, HD)[:, :, 0].astype(jnp.float32)
    )
    key_scale = jnp.repeat(key_scale, BLK, axis=0).reshape(step_count, key_count, heads_kv)
    value_scale = jnp.repeat(value_scale, BLK, axis=0).reshape(step_count, key_count, heads_kv)
    offsets = jnp.arange(step_count, dtype=jnp.int32) * key_count

    def one_step(current, scan_item):
        key_tile, value_tile, key_sc, value_sc, offset = scan_item
        key_pos = offset + jnp.arange(key_count, dtype=jnp.int32)
        return (
            block_update(
                current,
                query_tile,
                query_pos,
                query_doc,
                key_tile,
                value_tile,
                key_sc,
                value_sc,
                key_pos,
                starts,
            ),
            None,
        )

    totals, _ = lax.scan(one_step, totals, (key_part, value_part, key_scale, value_scale, offsets))
    return totals


def finish(totals, value_means, heads_kv, group_size, row_count):
    run_max, run_sum, accumulate = totals
    result = accumulate / run_sum[..., None] + value_means.reshape(heads_kv, 1, 1, HD)
    return (
        result.transpose(2, 0, 1, 3)
        .reshape(row_count, heads_kv * group_size * HD)
        .astype(jnp.bfloat16)
    )


def shards(queries, key_tokens, value_tokens, key_scales, value_scales, value_means, doc_lengths):
    local_keys, local_values = (
        lax.all_to_all(key_tokens, "head", split_axis=1, concat_axis=0, tiled=True),
        lax.all_to_all(value_tokens, "head", split_axis=1, concat_axis=0, tiled=True),
    )
    row_count = local_keys.shape[0]
    heads_kv = local_keys.shape[1] // HD
    group_size = QH // KVH
    blocks = row_count // BLK
    seq_index = lax.axis_index("seq")
    starts = jnp.cumsum(doc_lengths) - doc_lengths
    key_rows = jnp.concatenate(
        [
            local_keys.reshape(blocks, BLK, heads_kv * HD),
            jnp.repeat(key_scales, HD, axis=1)[:, None, :],
        ],
        axis=1,
    )
    value_rows = jnp.concatenate(
        [
            local_values.reshape(blocks, BLK, heads_kv * HD),
            jnp.repeat(value_scales, HD, axis=1)[:, None, :],
        ],
        axis=1,
    )
    bundle = jnp.stack([key_rows, value_rows], axis=1)

    def prepare(query_rows, query_pos):
        query_tile = query_rows.reshape(query_rows.shape[0], heads_kv, group_size, HD).transpose(
            1, 2, 0, 3
        )
        query_doc = doc_index(query_pos, starts)
        count_rows = query_rows.shape[0]
        initial = (
            jnp.full((heads_kv, group_size, count_rows), NEG, jnp.float32),
            jnp.zeros((heads_kv, group_size, count_rows), jnp.float32),
            jnp.zeros((heads_kv, group_size, count_rows, HD), jnp.float32),
        )

        def folder(totals, packet, first_block):
            return fold_packet(totals, packet, query_tile, query_pos, query_doc, starts, heads_kv)

        return (folder, initial)

    own_pos = seq_index * row_count + jnp.arange(row_count, dtype=jnp.int32)
    folder, initial = prepare(queries, own_pos)
    totals = folder(initial, lax.all_gather(bundle, "seq", axis=0, tiled=True), jnp.int32(0))
    attended = finish(totals, value_means, heads_kv, group_size, row_count)
    return attended


def solution(mesh):
    in_specs = (
        P("seq", "head"),
        P(("seq", "head"), None),
        P(("seq", "head"), None),
        P("seq", "head"),
        P("seq", "head"),
        P("head"),
        P(),
    )
    out_specs = P("seq", "head")
    return jax.shard_map(shards, mesh=mesh, in_specs=in_specs, out_specs=out_specs, check_vma=False)
```

profile of v0, /device:TPU:278, one launch (start us, length us, event | category | flops | bytes accessed | tf_op | source)
XLA Modules:
  0.0 488.1 jit_solution(16897507009504821495)
XLA Ops:
  7.9 7.4 %all-to-all-start = ((bf16[16,8,128]{2,0,1:T(8,128)(2,1)}), bf16[16,8,128]{2,0,1:T(8,128)(2,1)S(1)}, u32[]{:S(2)}, u32[]{:S(2)}) async-start(bf16[16,8,128]{2,0,1:T(8,128)(2,1)} %copy_bitcast_fusion.2), calls=%async_computation | async-start | bytes 65536 | tf_op jit(solution)/shard_map/all_to_all | solution.py:110
  15.3 1.4 copy_bitcast_fusion.1
  16.7 0.8 reduce.9
  17.5 0.8 reduce.10
  18.3 2.6 all-to-all-done
  20.8 5.7 %all-to-all-start.1 = ((bf16[16,8,128]{2,0,1:T(8,128)(2,1)}), bf16[16,8,128]{2,0,1:T(8,128)(2,1)S(1)}, u32[]{:S(2)}, u32[]{:S(2)}) async-start(bf16[16,8,128]{2,0,1:T(8,128)(2,1)} %copy_bitcast_fusion.1), calls=%async_computation.1 | async-start | bytes 65536 | tf_op jit(solution)/shard_map/all_to_all | solution.py:111
  26.6 5.4 %all-to-all-done.1 = bf16[16,8,128]{2,0,1:T(8,128)(2,1)S(1)} async-done(((bf16[16,8,128]{2,0,1:T(8,128)(2,1)}), bf16[16,8,128]{2,0,1:T(8,128)(2,1)S(1)}, u32[]{:S(2)}, u32[]{:S(2)}) %all-to-all-start.1) | async-done | bytes 32800 | tf_op jit(solution)/shard_map/all_to_all | solution.py:111
  34.4 1.1 copy.42
  35.9 297.4 %all-gather.2.cloned.1.call-done = bf16[128,2,65,128]{3,2,0,1:T(8,128)(2,1)} async-done(((bf16[2,2,65,128]{3,2,0,1:T(8,128)(2,1)}), bf16[128,2,65,128]{3,2,0,1:T(8,128)(2,1)}) %all-gather.2.cloned.1.call-update) | async-done | bytes 4259856 | tf_op jit(solution)/shard_map/all_gather | solution.py:154
  333.2 1.1 fusion.27
  334.8 4.6 fusion.28
  339.4 140.6 %while.17 = (s32[]{:T(128)}, f32[1,8,128]{2,1,0:T(8,128)S(1)}, f32[1,8,128]{2,1,0:T(8,128)S(1)}, f32[1,8,128,128]{3,2,1,0:T(8,128)S(1)}, s32[64]{0:T(128)S(1)}, ...) while((s32[]{:T(128)}, f32[1,8,128]{2,1,0:T(8,128)S(1)}, ...), condition=%wide.region_9.10_spmd.clone, body=%wide.region_2.9_spmd.clone.sunk | while | flops 137285248 | bytes 4997679 | solution.py:94
  340.8 0.8 fusion.32
  343.6 0.8 fusion.32
  346.4 0.8 fusion.32
  349.3 0.8 fusion.32
  352.1 0.8 fusion.32
  354.9 0.8 fusion.32
  357.7 0.8 fusion.32
  360.5 0.8 fusion.32
  363.3 0.8 fusion.32
  364.8 2.4 conditional.3
  365.2 1.2 fusion.26
  370.0 2.4 conditional.3
  370.4 1.1 fusion.26
  375.2 2.4 conditional.3
  375.7 1.1 fusion.26
  380.4 2.4 conditional.3
  380.9 1.1 fusion.26
  385.6 2.4 conditional.3
  386.1 1.1 fusion.26
  390.9 2.4 conditional.3
  391.3 1.1 fusion.26
  396.1 2.4 conditional.3
  396.5 1.1 fusion.26
  401.3 2.4 conditional.3
  401.8 1.1 fusion.26
  406.5 2.4 conditional.3
  407.0 1.1 fusion.26
  411.7 2.4 conditional.3
  412.2 1.1 fusion.26
  417.0 2.4 conditional.3
  417.4 1.1 fusion.26
  422.2 2.4 conditional.3
  422.7 1.1 fusion.26
  427.4 2.4 conditional.3
  427.9 1.1 fusion.26
  432.6 2.4 conditional.3
  433.1 1.1 fusion.26
  437.9 2.4 conditional.3
  438.3 1.1 fusion.26
  443.1 2.4 conditional.3
  443.5 1.1 fusion.26
  448.3 2.4 conditional.3
  448.8 1.1 fusion.26
  452.1 0.8 fusion.32
  453.5 2.4 conditional.3
  454.0 1.1 fusion.26
  458.7 2.4 conditional.3
  459.2 1.1 fusion.26
  464.0 2.4 conditional.3
  464.4 1.1 fusion.26
  469.2 2.4 conditional.3
  469.6 1.1 fusion.26
  (435 shorter events, 90.3 us)
Async XLA Ops:
  6.5 0.8 copy-start
  7.9 12.9 %all-to-all-start = ((bf16[16,8,128]{2,0,1:T(8,128)(2,1)}), bf16[16,8,128]{2,0,1:T(8,128)(2,1)S(1)}, u32[]{:S(2)}, u32[]{:S(2)}) async-start(bf16[16,8,128]{2,0,1:T(8,128)(2,1)} %copy_bitcast_fusion.2), calls=%async_computation | async-start | bytes 65536 | tf_op jit(solution)/shard_map/all_to_all | solution.py:110
  20.8 11.2 %all-to-all-start.1 = ((bf16[16,8,128]{2,0,1:T(8,128)(2,1)}), bf16[16,8,128]{2,0,1:T(8,128)(2,1)S(1)}, u32[]{:S(2)}, u32[]{:S(2)}) async-start(bf16[16,8,128]{2,0,1:T(8,128)(2,1)} %copy_bitcast_fusion.1), calls=%async_computation.1 | async-start | bytes 65536 | tf_op jit(solution)/shard_map/all_to_all | solution.py:111
  26.5 306.7 %all-gather.2.cloned.1.call-start = ((), (), s32[]{:S(2)}) async-start(), calls=%async_computation.2 | async-start | bytes 4792320 | tf_op jit(solution)/shard_map/all_gather | solution.py:154
  339.4 140.6 %copy-start.1 = (f32[128]{0:T(128)S(1)}, f32[128]{0:T(128)}, u32[]{:S(2)}) copy-start(f32[128]{0:T(128)} %param.16) | copy-start | bytes 1540
Sparse Core Ops, SparseCore 0:
  32.9 300.2 all-gather.1
where the time goes:
time: 490 us; the launch traced here: 488 us
  waiting for transfers between devices  305 us (62%)
  other arithmetic  57 us (12%)
  local copies, waits for them, and re-layouts  38.9 us (8%)
  matrix products  35.7 us (7%)
  loops' own time  24.4 us (5%)
  between operations  13.5 us (3%)
  starting transfers between devices  13.1 us (3%)
    all_gather x1, waiting for transfers between devices, shards(): lax.all_gather(bundle, 'seq', axis=0, tiled=True)  297 us
    reduce_or x32, other arithmetic, block_update(): return lax.cond(jnp.any(allowed), update, keep_state, totals)  24.6 us
    dot_general x21, matrix products, update(): jnp.einsum('kgrd,nkd->kgrn', query_tile, key_tile, preferred_element_type...  24.1 us
    another operation x1, loops' own time, fold_packet(): lax.scan(one_step, totals, (key_part, value_part, key_scale, value_scale,...  22.2 us
    add x32, other arithmetic, one_step(): key_pos = offset + jnp.arange(key_count, dtype=jnp.int32)  20.7 us
    dynamic_slice x32, local copies, waits for them, and re-layouts, fold_packet(): lax.scan(one_step, totals, (key_part, value_part, key_scale, value_scale,...  18.8 us
    dot_general x21, matrix products, update(): jnp.einsum('kgrn,nkd->kgrd', scaled, value_tile, preferred_element_type=j...  11.6 us
  transfers between devices with their start and end apart: 3, of which 3 were waited for; matrix products, arithmetic and copies ran while one was open for 1% of the time, Pallas kernels for 0%

commit v1 on v0

--- a/solution.py
+++ b/solution.py
@@ -9,6 +9,7 @@
 KVH = 8
 HD = 128
 BLK = 64
+MOST = 5120
 
 
 NEG = -1e30
@@ -105,6 +106,23 @@
     )
 
 
+def shift_from(x, offset, count):
+    pairs = [(i, (i + offset) % count) for i in range(count)]
+    return lax.ppermute(x, "seq", pairs)
+
+
+def gather_window(packet, count, depth):
+    held = packet[None]
+    for width, shifts in ((1, (1, 2, 3)), (4, (4, 8, 12)), (16, (16, 32))):
+        parts = [held]
+        for offset in shifts:
+            need = min(width, depth - offset)
+            if need > 0:
+                parts.append(shift_from(held[:need], offset, count))
+        held = jnp.concatenate(parts, axis=0)
+    return held
+
+
 def shards(queries, key_tokens, value_tokens, key_scales, value_scales, value_means, doc_lengths):
     local_keys, local_values = (
         lax.all_to_all(key_tokens, "head", split_axis=1, concat_axis=0, tiled=True),
@@ -114,46 +132,55 @@
     heads_kv = local_keys.shape[1] // HD
     group_size = QH // KVH
     blocks = row_count // BLK
+    seq_count = lax.axis_size("seq")
     seq_index = lax.axis_index("seq")
     starts = jnp.cumsum(doc_lengths) - doc_lengths
-    key_rows = jnp.concatenate(
-        [
-            local_keys.reshape(blocks, BLK, heads_kv * HD),
-            jnp.repeat(key_scales, HD, axis=1)[:, None, :],
-        ],
-        axis=1,
+    depth = min(seq_count, -(-(MOST - 1) // row_count) + 1)
+    pad_rows = 8
+    scale_rows = jnp.zeros((2, pad_rows, heads_kv * HD), jnp.bfloat16)
+    scale_rows = scale_rows.at[0, :blocks].set(jnp.repeat(key_scales, HD, axis=1))
+    scale_rows = scale_rows.at[1, :blocks].set(jnp.repeat(value_scales, HD, axis=1))
+    packet = jnp.concatenate([jnp.stack([local_keys, local_values]), scale_rows], axis=1)
+    window = gather_window(packet, seq_count, depth)
+    slots = window.shape[0]
+    pair = 2
+    padded = -(-slots // pair) * pair
+    window = jnp.concatenate(
+        [window, jnp.zeros((padded - slots,) + window.shape[1:], window.dtype)], axis=0
     )
-    value_rows = jnp.concatenate(
-        [
-            local_values.reshape(blocks, BLK, heads_kv * HD),
-            jnp.repeat(value_scales, HD, axis=1)[:, None, :],
-        ],
-        axis=1,
+    shard_of = (seq_index - jnp.arange(padded, dtype=jnp.int32)) % seq_count
+    key_pos = shard_of[:, None] * row_count + jnp.arange(row_count, dtype=jnp.int32)[None, :]
+    key_pos = jnp.where(jnp.arange(padded)[:, None] < slots, key_pos, jnp.int32(2**30))
+    steps = padded // pair
+    key_count = pair * row_count
+    key_part = window[:, 0, :row_count].reshape(steps, key_count, heads_kv, HD)
+    value_part = window[:, 1, :row_count].reshape(steps, key_count, heads_kv, HD)
+    key_sc = jnp.repeat(window[:, 0, row_count:row_count + blocks, ::HD], BLK, axis=1)
+    value_sc = jnp.repeat(window[:, 1, row_count:row_count + blocks, ::HD], BLK, axis=1)
+    key_sc = key_sc.astype(jnp.float32).reshape(steps, key_count, heads_kv)
+    value_sc = value_sc.astype(jnp.float32).reshape(steps, key_count, heads_kv)
+    key_pos = key_pos.reshape(steps, key_count)
+
+    own_pos = seq_index * row_count + jnp.arange(row_count, dtype=jnp.int32)
+    query_tile = queries.reshape(row_count, heads_kv, group_size, HD).transpose(1, 2, 0, 3)
+    query_doc = doc_index(own_pos, starts)
+    initial = (
+        jnp.full((heads_kv, group_size, row_count), NEG, jnp.float32),
+        jnp.zeros((heads_kv, group_size, row_count), jnp.float32),
+        jnp.zeros((heads_kv, group_size, row_count, HD), jnp.float32),
     )
-    bundle = jnp.stack([key_rows, value_rows], axis=1)
 
-    def prepare(query_rows, query_pos):
-        query_tile = query_rows.reshape(query_rows.shape[0], heads_kv, group_size, HD).transpose(
-            1, 2, 0, 3
-        )
-        query_doc = doc_index(query_pos, starts)
-        count_rows = query_rows.shape[0]
-        initial = (
-            jnp.full((heads_kv, group_size, count_rows), NEG, jnp.float32),
-            jnp.zeros((heads_kv, group_size, count_rows), jnp.float32),
-            jnp.zeros((heads_kv, group_size, count_rows, HD), jnp.float32),
+    def one_step(current, scan_item):
+        k_tile, v_tile, k_sc, v_sc, pos = scan_item
+        return (
+            block_update(
+                current, query_tile, own_pos, query_doc, k_tile, v_tile, k_sc, v_sc, pos, starts
+            ),
+            None,
         )
 
-        def folder(totals, packet, first_block):
-            return fold_packet(totals, packet, query_tile, query_pos, query_doc, starts, heads_kv)
-
-        return (folder, initial)
-
-    own_pos = seq_index * row_count + jnp.arange(row_count, dtype=jnp.int32)
-    folder, initial = prepare(queries, own_pos)
-    totals = folder(initial, lax.all_gather(bundle, "seq", axis=0, tiled=True), jnp.int32(0))
-    attended = finish(totals, value_means, heads_kv, group_size, row_count)
-    return attended
+    totals, _ = lax.scan(one_step, initial, (key_part, value_part, key_sc, value_sc, key_pos))
+    return finish(totals, value_means, heads_kv, group_size, row_count)
 
 
 def solution(mesh):

time: 490 us -> 215 us (0.44)
  the two profiles are of different devices: /device:TPU:278 before, /device:TPU:262 now
where the time goes in v1:
time: 215 us; the launch traced here: 213 us
  waiting for transfers between devices  69 us (32%)
  starting transfers between devices  39.6 us (18%)
  matrix products  34.1 us (16%)
  other arithmetic  27.4 us (13%)
  local copies, waits for them, and re-layouts  24.9 us (12%)
  loops' own time  17.4 us (8%)
    ppermute x8, waiting for transfers between devices, shift_from(): return lax.ppermute(x, 'seq', pairs)  56.3 us
    ppermute x8, starting transfers between devices, shift_from(): return lax.ppermute(x, 'seq', pairs)  29.2 us
    dot_general x20, matrix products, update(): jnp.einsum('kgrd,nkd->kgrn', query_tile, key_tile, preferred_element_type...  23.1 us
    reduce_or x21, other arithmetic, block_update(): return lax.cond(jnp.any(allowed), update, keep_state, totals)  17.8 us
    another operation x1, loops' own time, shards(): lax.scan(one_step, initial, (key_part, value_part, key_sc, value_sc, key_...  15.5 us
    dot_general x20, matrix products, update(): jnp.einsum('kgrn,nkd->kgrd', scaled, value_tile, preferred_element_type=j...  11 us
    all_to_all x1, waiting for transfers between devices, shards(): lax.all_to_all(value_tokens, 'head', split_axis=1, concat_axis=0, tiled=T...  7.71 us
    unnamed x25, local copies, waits for them, and re-layouts  7.38 us
  transfers between devices with their start and end apart: 10, of which 6 were waited for; matrix products, arithmetic and copies ran while one was open for 5% of the time, Pallas kernels for 0%

profile of v1, /device:TPU:262, one launch (start us, length us, event | category | flops | bytes accessed | tf_op | source)
XLA Modules:
  0.0 212.7 jit_solution(3362630339141129495)
XLA Ops:
  1.4 7.1 %all-to-all-start = ((bf16[16,8,128]{2,0,1:T(8,128)(2,1)}), bf16[16,8,128]{2,0,1:T(8,128)(2,1)S(1)}, u32[]{:S(2)}, u32[]{:S(2)}) async-start(bf16[16,8,128]{2,0,1:T(8,128)(2,1)} %copy_bitcast_fusion.2), calls=%async_computation | async-start | bytes 65536 | tf_op jit(solution)/shard_map/all_to_all | solution.py:128
  8.5 1.4 copy_bitcast_fusion.1
  11.4 5.0 %all-to-all-done = bf16[16,8,128]{2,0,1:T(8,128)(2,1)S(1)} async-done(((bf16[16,8,128]{2,0,1:T(8,128)(2,1)}), bf16[16,8,128]{2,0,1:T(8,128)(2,1)S(1)}, u32[]{:S(2)}, u32[]{:S(2)}) %all-to-all-start) | async-done | bytes 32800 | tf_op jit(solution)/shard_map/all_to_all | solution.py:128
  16.4 3.3 %all-to-all-start.1 = ((bf16[16,8,128]{2,0,1:T(8,128)(2,1)}), bf16[16,8,128]{2,0,1:T(8,128)(2,1)S(1)}, u32[]{:S(2)}, u32[]{:S(2)}) async-start(bf16[16,8,128]{2,0,1:T(8,128)(2,1)} %copy_bitcast_fusion.1), calls=%async_computation.1 | async-start | bytes 65536 | tf_op jit(solution)/shard_map/all_to_all | solution.py:129
  19.9 7.7 %all-to-all-done.1 = bf16[16,8,128]{2,0,1:T(8,128)(2,1)S(1)} async-done(((bf16[16,8,128]{2,0,1:T(8,128)(2,1)}), bf16[16,8,128]{2,0,1:T(8,128)(2,1)S(1)}, u32[]{:S(2)}, u32[]{:S(2)}) %all-to-all-start.1) | async-done | bytes 32800 | tf_op jit(solution)/shard_map/all_to_all | solution.py:129
  27.6 2.6 %collective-permute-start = (bf16[1,2,136,128]{3,2,1,0:T(8,128)(2,1)S(1)}, bf16[1,2,136,128]{3,2,1,0:T(8,128)(2,1)S(1)}, u32[]{:S(2)}, u32[]{:S(2)}) collective-permute-start(bf16[1,2,136,128]{3,2,1,0:T(8,128)(2,1)S(1)} %maximum_bitcast_fusion), channel_id=1, source_target_pairs={{0,8},{8,16},{16,24},{24,32},{32,40},{40,48},{48,56},{56,64},{64,7... | collective-permute-start | bytes 208904 | tf_op jit(solution)/shard_map/ppermute | solution.py:111
  30.2 3.4 %collective-permute-start.1 = (bf16[1,2,136,128]{3,2,1,0:T(8,128)(2,1)S(1)}, bf16[1,2,136,128]{3,2,1,0:T(8,128)(2,1)S(1)}, u32[]{:S(2)}, u32[]{:S(2)}) collective-permute-start(bf16[1,2,136,128]{3,2,1,0:T(8,128)(2,1)S(1)} %maximum_bitcast_fusion), channel_id=1, source_target_pairs={{0,16},{8,24},{16,32},{24,40},{32,48},{40,56},{48,64},{56,72},{64,... | collective-permute-start | bytes 208904 | tf_op jit(solution)/shard_map/ppermute | solution.py:111
  33.6 5.1 %collective-permute-start.2 = (bf16[1,2,136,128]{3,2,1,0:T(8,128)(2,1)S(1)}, bf16[1,2,136,128]{3,2,1,0:T(8,128)(2,1)S(1)}, u32[]{:S(2)}, u32[]{:S(2)}) collective-permute-start(bf16[1,2,136,128]{3,2,1,0:T(8,128)(2,1)S(1)} %maximum_bitcast_fusion), channel_id=1, source_target_pairs={{0,24},{8,32},{16,40},{24,48},{32,56},{40,64},{48,72},{56,80},{64,... | collective-permute-start | bytes 208904 | tf_op jit(solution)/shard_map/ppermute | solution.py:111
  39.4 4.2 %collective-permute-done.2 = bf16[1,2,136,128]{3,2,1,0:T(8,128)(2,1)S(1)} collective-permute-done((bf16[1,2,136,128]{3,2,1,0:T(8,128)(2,1)S(1)}, bf16[1,2,136,128]{3,2,1,0:T(8,128)(2,1)S(1)}, u32[]{:S(2)}, u32[]{:S(2)}) %collective-permute-start.2) | collective-permute-done | bytes 69664 | tf_op jit(solution)/shard_map/ppermute | solution.py:111
  43.6 2.8 %collective-permute-start.3 = (bf16[4,2,136,128]{3,2,1,0:T(8,128)(2,1)S(1)}, bf16[4,2,136,128]{3,2,1,0:T(8,128)(2,1)S(1)}, u32[]{:S(2)}, u32[]{:S(2)}) collective-permute-start(bf16[4,2,136,128]{3,2,1,0:T(8,128)(2,1)S(1)} %pad_maximum_fusion), channel_id=1, source_target_pairs={{0,32},{8,40},{16,48},{24,56},{32,64},{40,72},{48,80},{56,88},{64,... | collective-permute-start | bytes 835592 | tf_op jit(solution)/shard_map/ppermute | solution.py:111
  46.4 4.2 %collective-permute-start.4 = (bf16[4,2,136,128]{3,2,1,0:T(8,128)(2,1)S(1)}, bf16[4,2,136,128]{3,2,1,0:T(8,128)(2,1)S(1)}, u32[]{:S(2)}, u32[]{:S(2)}) collective-permute-start(bf16[4,2,136,128]{3,2,1,0:T(8,128)(2,1)S(1)} %pad_maximum_fusion), channel_id=1, source_target_pairs={{0,64},{8,72},{16,80},{24,88},{32,96},{40,104},{48,112},{56,120},{... | collective-permute-start | bytes 835592 | tf_op jit(solution)/shard_map/ppermute | solution.py:111
  50.6 4.7 %collective-permute-start.5 = (bf16[4,2,136,128]{3,2,1,0:T(8,128)(2,1)S(1)}, bf16[4,2,136,128]{3,2,1,0:T(8,128)(2,1)S(1)}, u32[]{:S(2)}, u32[]{:S(2)}) collective-permute-start(bf16[4,2,136,128]{3,2,1,0:T(8,128)(2,1)S(1)} %pad_maximum_fusion), channel_id=1, source_target_pairs={{0,96},{8,104},{16,112},{24,120},{32,128},{40,136},{48,144},{56,15... | collective-permute-start | bytes 835592 | tf_op jit(solution)/shard_map/ppermute | solution.py:111
  57.5 10.0 %collective-permute-done.3 = bf16[4,2,136,128]{3,2,1,0:T(8,128)(2,1)S(1)} collective-permute-done((bf16[4,2,136,128]{3,2,1,0:T(8,128)(2,1)S(1)}, bf16[4,2,136,128]{3,2,1,0:T(8,128)(2,1)S(1)}, u32[]{:S(2)}, u32[]{:S(2)}) %collective-permute-start.3) | collective-permute-done | bytes 278560 | tf_op jit(solution)/shard_map/ppermute | solution.py:111
  67.5 0.9 constant_dynamic-update-slice_fusion.8
  68.4 0.9 constant_dynamic-update-slice_fusion.7
  69.4 8.1 %collective-permute-done.5 = bf16[4,2,136,128]{3,2,1,0:T(8,128)(2,1)S(1)} collective-permute-done((bf16[4,2,136,128]{3,2,1,0:T(8,128)(2,1)S(1)}, bf16[4,2,136,128]{3,2,1,0:T(8,128)(2,1)S(1)}, u32[]{:S(2)}, u32[]{:S(2)}) %collective-permute-start.5) | collective-permute-done | bytes 278560 | tf_op jit(solution)/shard_map/ppermute | solution.py:111
  78.3 3.9 %collective-permute-start.6 = (bf16[16,2,136,128]{3,2,1,0:T(8,128)(2,1)}, bf16[16,2,136,128]{3,2,1,0:T(8,128)(2,1)S(1)}, u32[]{:S(2)}, u32[]{:S(2)}) collective-permute-start(bf16[16,2,136,128]{3,2,1,0:T(8,128)(2,1)} %get-tuple-element.489), channel_id=1, source_target_pairs={{0,128},{8,136},{16,144},{24,152},{32,160},{40,168},{48,176},{56,1... | collective-permute-start | bytes 3342344 | tf_op jit(solution)/shard_map/ppermute | solution.py:111
  82.7 2.5 %collective-permute-start.7 = (bf16[9,2,136,128]{3,2,1,0:T(8,128)(2,1)S(1)}, bf16[9,2,136,128]{3,2,1,0:T(8,128)(2,1)S(1)}, u32[]{:S(2)}, u32[]{:S(2)}) collective-permute-start(bf16[9,2,136,128]{3,2,1,0:T(8,128)(2,1)S(1)} %slice.72), channel_id=1, source_target_pairs={{0,256},{8,264},{16,272},{24,280},{32,288},{40,296},{48,304},{56,3... | collective-permute-start | bytes 1880072 | tf_op jit(solution)/shard_map/ppermute | solution.py:111
  85.9 34.0 %collective-permute-done.6 = bf16[16,2,136,128]{3,2,1,0:T(8,128)(2,1)S(1)} collective-permute-done((bf16[16,2,136,128]{3,2,1,0:T(8,128)(2,1)}, bf16[16,2,136,128]{3,2,1,0:T(8,128)(2,1)S(1)}, u32[]{:S(2)}, u32[]{:S(2)}) %collective-permute-start.6) | collective-permute-done | bytes 1114144 | tf_op jit(solution)/shard_map/ppermute | solution.py:111
  119.9 1.1 constant_dynamic-update-slice_fusion.15
  121.1 0.9 constant_dynamic-update-slice_fusion.14
  122.6 3.1 %fusion.31 = (bf16[42,1,128,128]{3,2,1,0:T(8,128)(2,1)S(1)}, bf16[42,1,128,128]{3,2,1,0:T(8,128)(2,1)}) fusion(bf16[42,2,136,128]{3,2,1,0:T(8,128)(2,1)} %constant_dynamic-update-slice_fusion.13), kind=kLoop, calls=%fused_computation.83 | loop fusion | bytes 5505024 | tf_op jit(solution)/shard_map/slice | solution.py:157
  125.7 1.0 fusion.30
  127.2 84.3 %while.19 = (s32[]{:T(128)}, f32[1,8,128]{2,1,0:T(8,128)S(1)}, f32[1,8,128]{2,1,0:T(8,128)S(1)}, f32[1,8,128,128]{3,2,1,0:T(8,128)S(1)}, s32[64]{0:T(128)S(1)}, ...) while((s32[]{:T(128)}, f32[1,8,128]{2,1,0:T(8,128)S(1)}, ...), condition=%wide.region_9.10_spmd.clone, body=%wide.region_2.9_spmd.clone.sunk | while | flops 137284992 | bytes 4930755 | solution.py:182
  128.9 2.4 %conditional.3 = ((f32[1,8,128]{2,1,0:T(8,128)S(1)}, f32[1,8,128]{2,1,0:T(8,128)S(1)}, f32[1,8,128,128]{3,2,1,0:T(8,128)S(1)})) conditional(s32[]{:T(128)} %convert_element_type.102, (f32[1,8,128]{2,1,0:T(8,128)S(1)}, f32[1,8,128]{2,1,0:T(8,128)S(1)}, f32[1,8,128,128]{3,2,1,0:T(8,128)S(1)}) %tuple.83, (pred[128,256]{0,1:T(8,128)(4,1)S(1)}, ...), branch_computations={%region_5.5_spmd, %region_6.8_spmd} | conditional | flops 137104640 | bytes 4887752 | solution.py:58
  129.3 1.2 fusion.29
  133.0 2.4 %conditional.3 = ((f32[1,8,128]{2,1,0:T(8,128)S(1)}, f32[1,8,128]{2,1,0:T(8,128)S(1)}, f32[1,8,128,128]{3,2,1,0:T(8,128)S(1)})) conditional(s32[]{:T(128)} %convert_element_type.102, (f32[1,8,128]{2,1,0:T(8,128)S(1)}, f32[1,8,128]{2,1,0:T(8,128)S(1)}, f32[1,8,128,128]{3,2,1,0:T(8,128)S(1)}) %tuple.83, (pred[128,256]{0,1:T(8,128)(4,1)S(1)}, ...), branch_computations={%region_5.5_spmd, %region_6.8_spmd} | conditional | flops 137104640 | bytes 4887752 | solution.py:58
  133.5 1.2 fusion.29
  137.1 2.4 %conditional.3 = ((f32[1,8,128]{2,1,0:T(8,128)S(1)}, f32[1,8,128]{2,1,0:T(8,128)S(1)}, f32[1,8,128,128]{3,2,1,0:T(8,128)S(1)})) conditional(s32[]{:T(128)} %convert_element_type.102, (f32[1,8,128]{2,1,0:T(8,128)S(1)}, f32[1,8,128]{2,1,0:T(8,128)S(1)}, f32[1,8,128,128]{3,2,1,0:T(8,128)S(1)}) %tuple.83, (pred[128,256]{0,1:T(8,128)(4,1)S(1)}, ...), branch_computations={%region_5.5_spmd, %region_6.8_spmd} | conditional | flops 137104640 | bytes 4887752 | solution.py:58
  137.6 1.2 fusion.29
  141.3 2.4 %conditional.3 = ((f32[1,8,128]{2,1,0:T(8,128)S(1)}, f32[1,8,128]{2,1,0:T(8,128)S(1)}, f32[1,8,128,128]{3,2,1,0:T(8,128)S(1)})) conditional(s32[]{:T(128)} %convert_element_type.102, (f32[1,8,128]{2,1,0:T(8,128)S(1)}, f32[1,8,128]{2,1,0:T(8,128)S(1)}, f32[1,8,128,128]{3,2,1,0:T(8,128)S(1)}) %tuple.83, (pred[128,256]{0,1:T(8,128)(4,1)S(1)}, ...), branch_computations={%region_5.5_spmd, %region_6.8_spmd} | conditional | flops 137104640 | bytes 4887752 | solution.py:58
  141.7 1.2 fusion.29
  145.4 2.4 %conditional.3 = ((f32[1,8,128]{2,1,0:T(8,128)S(1)}, f32[1,8,128]{2,1,0:T(8,128)S(1)}, f32[1,8,128,128]{3,2,1,0:T(8,128)S(1)})) conditional(s32[]{:T(128)} %convert_element_type.102, (f32[1,8,128]{2,1,0:T(8,128)S(1)}, f32[1,8,128]{2,1,0:T(8,128)S(1)}, f32[1,8,128,128]{3,2,1,0:T(8,128)S(1)}) %tuple.83, (pred[128,256]{0,1:T(8,128)(4,1)S(1)}, ...), branch_computations={%region_5.5_spmd, %region_6.8_spmd} | conditional | flops 137104640 | bytes 4887752 | solution.py:58
  145.9 1.2 fusion.29
  149.5 2.4 %conditional.3 = ((f32[1,8,128]{2,1,0:T(8,128)S(1)}, f32[1,8,128]{2,1,0:T(8,128)S(1)}, f32[1,8,128,128]{3,2,1,0:T(8,128)S(1)})) conditional(s32[]{:T(128)} %convert_element_type.102, (f32[1,8,128]{2,1,0:T(8,128)S(1)}, f32[1,8,128]{2,1,0:T(8,128)S(1)}, f32[1,8,128,128]{3,2,1,0:T(8,128)S(1)}) %tuple.83, (pred[128,256]{0,1:T(8,128)(4,1)S(1)}, ...), branch_computations={%region_5.5_spmd, %region_6.8_spmd} | conditional | flops 137104640 | bytes 4887752 | solution.py:58
  150.0 1.2 fusion.29
  153.7 2.4 %conditional.3 = ((f32[1,8,128]{2,1,0:T(8,128)S(1)}, f32[1,8,128]{2,1,0:T(8,128)S(1)}, f32[1,8,128,128]{3,2,1,0:T(8,128)S(1)})) conditional(s32[]{:T(128)} %convert_element_type.102, (f32[1,8,128]{2,1,0:T(8,128)S(1)}, f32[1,8,128]{2,1,0:T(8,128)S(1)}, f32[1,8,128,128]{3,2,1,0:T(8,128)S(1)}) %tuple.83, (pred[128,256]{0,1:T(8,128)(4,1)S(1)}, ...), branch_computations={%region_5.5_spmd, %region_6.8_spmd} | conditional | flops 137104640 | bytes 4887752 | solution.py:58
  154.1 1.2 fusion.29
  157.8 2.4 %conditional.3 = ((f32[1,8,128]{2,1,0:T(8,128)S(1)}, f32[1,8,128]{2,1,0:T(8,128)S(1)}, f32[1,8,128,128]{3,2,1,0:T(8,128)S(1)})) conditional(s32[]{:T(128)} %convert_element_type.102, (f32[1,8,128]{2,1,0:T(8,128)S(1)}, f32[1,8,128]{2,1,0:T(8,128)S(1)}, f32[1,8,128,128]{3,2,1,0:T(8,128)S(1)}) %tuple.83, (pred[128,256]{0,1:T(8,128)(4,1)S(1)}, ...), branch_computations={%region_5.5_spmd, %region_6.8_spmd} | conditional | flops 137104640 | bytes 4887752 | solution.py:58
  158.3 1.2 fusion.29
  161.9 2.4 %conditional.3 = ((f32[1,8,128]{2,1,0:T(8,128)S(1)}, f32[1,8,128]{2,1,0:T(8,128)S(1)}, f32[1,8,128,128]{3,2,1,0:T(8,128)S(1)})) conditional(s32[]{:T(128)} %convert_element_type.102, (f32[1,8,128]{2,1,0:T(8,128)S(1)}, f32[1,8,128]{2,1,0:T(8,128)S(1)}, f32[1,8,128,128]{3,2,1,0:T(8,128)S(1)}) %tuple.83, (pred[128,256]{0,1:T(8,128)(4,1)S(1)}, ...), branch_computations={%region_5.5_spmd, %region_6.8_spmd} | conditional | flops 137104640 | bytes 4887752 | solution.py:58
  162.4 1.2 fusion.29
  166.1 2.4 %conditional.3 = ((f32[1,8,128]{2,1,0:T(8,128)S(1)}, f32[1,8,128]{2,1,0:T(8,128)S(1)}, f32[1,8,128,128]{3,2,1,0:T(8,128)S(1)})) conditional(s32[]{:T(128)} %convert_element_type.102, (f32[1,8,128]{2,1,0:T(8,128)S(1)}, f32[1,8,128]{2,1,0:T(8,128)S(1)}, f32[1,8,128,128]{3,2,1,0:T(8,128)S(1)}) %tuple.83, (pred[128,256]{0,1:T(8,128)(4,1)S(1)}, ...), branch_computations={%region_5.5_spmd, %region_6.8_spmd} | conditional | flops 137104640 | bytes 4887752 | solution.py:58
  166.5 1.2 fusion.29
  170.2 2.4 %conditional.3 = ((f32[1,8,128]{2,1,0:T(8,128)S(1)}, f32[1,8,128]{2,1,0:T(8,128)S(1)}, f32[1,8,128,128]{3,2,1,0:T(8,128)S(1)})) conditional(s32[]{:T(128)} %convert_element_type.102, (f32[1,8,128]{2,1,0:T(8,128)S(1)}, f32[1,8,128]{2,1,0:T(8,128)S(1)}, f32[1,8,128,128]{3,2,1,0:T(8,128)S(1)}) %tuple.83, (pred[128,256]{0,1:T(8,128)(4,1)S(1)}, ...), branch_computations={%region_5.5_spmd, %region_6.8_spmd} | conditional | flops 137104640 | bytes 4887752 | solution.py:58
  170.7 1.2 fusion.29
  174.3 2.4 %conditional.3 = ((f32[1,8,128]{2,1,0:T(8,128)S(1)}, f32[1,8,128]{2,1,0:T(8,128)S(1)}, f32[1,8,128,128]{3,2,1,0:T(8,128)S(1)})) conditional(s32[]{:T(128)} %convert_element_type.102, (f32[1,8,128]{2,1,0:T(8,128)S(1)}, f32[1,8,128]{2,1,0:T(8,128)S(1)}, f32[1,8,128,128]{3,2,1,0:T(8,128)S(1)}) %tuple.83, (pred[128,256]{0,1:T(8,128)(4,1)S(1)}, ...), branch_computations={%region_5.5_spmd, %region_6.8_spmd} | conditional | flops 137104640 | bytes 4887752 | solution.py:58
  174.8 1.2 fusion.29
  178.4 2.4 %conditional.3 = ((f32[1,8,128]{2,1,0:T(8,128)S(1)}, f32[1,8,128]{2,1,0:T(8,128)S(1)}, f32[1,8,128,128]{3,2,1,0:T(8,128)S(1)})) conditional(s32[]{:T(128)} %convert_element_type.102, (f32[1,8,128]{2,1,0:T(8,128)S(1)}, f32[1,8,128]{2,1,0:T(8,128)S(1)}, f32[1,8,128,128]{3,2,1,0:T(8,128)S(1)}) %tuple.83, (pred[128,256]{0,1:T(8,128)(4,1)S(1)}, ...), branch_computations={%region_5.5_spmd, %region_6.8_spmd} | conditional | flops 137104640 | bytes 4887752 | solution.py:58
  178.9 1.2 fusion.29
  182.6 2.4 %conditional.3 = ((f32[1,8,128]{2,1,0:T(8,128)S(1)}, f32[1,8,128]{2,1,0:T(8,128)S(1)}, f32[1,8,128,128]{3,2,1,0:T(8,128)S(1)})) conditional(s32[]{:T(128)} %convert_element_type.102, (f32[1,8,128]{2,1,0:T(8,128)S(1)}, f32[1,8,128]{2,1,0:T(8,128)S(1)}, f32[1,8,128,128]{3,2,1,0:T(8,128)S(1)}) %tuple.83, (pred[128,256]{0,1:T(8,128)(4,1)S(1)}, ...), branch_computations={%region_5.5_spmd, %region_6.8_spmd} | conditional | flops 137104640 | bytes 4887752 | solution.py:58
  183.0 1.2 fusion.29
  186.7 2.4 %conditional.3 = ((f32[1,8,128]{2,1,0:T(8,128)S(1)}, f32[1,8,128]{2,1,0:T(8,128)S(1)}, f32[1,8,128,128]{3,2,1,0:T(8,128)S(1)})) conditional(s32[]{:T(128)} %convert_element_type.102, (f32[1,8,128]{2,1,0:T(8,128)S(1)}, f32[1,8,128]{2,1,0:T(8,128)S(1)}, f32[1,8,128,128]{3,2,1,0:T(8,128)S(1)}) %tuple.83, (pred[128,256]{0,1:T(8,128)(4,1)S(1)}, ...), branch_computations={%region_5.5_spmd, %region_6.8_spmd} | conditional | flops 137104640 | bytes 4887752 | solution.py:58
  187.2 1.2 fusion.29
  190.8 2.4 %conditional.3 = ((f32[1,8,128]{2,1,0:T(8,128)S(1)}, f32[1,8,128]{2,1,0:T(8,128)S(1)}, f32[1,8,128,128]{3,2,1,0:T(8,128)S(1)})) conditional(s32[]{:T(128)} %convert_element_type.102, (f32[1,8,128]{2,1,0:T(8,128)S(1)}, f32[1,8,128]{2,1,0:T(8,128)S(1)}, f32[1,8,128,128]{3,2,1,0:T(8,128)S(1)}) %tuple.83, (pred[128,256]{0,1:T(8,128)(4,1)S(1)}, ...), branch_computations={%region_5.5_spmd, %region_6.8_spmd} | conditional | flops 137104640 | bytes 4887752 | solution.py:58
  191.3 1.2 fusion.29
  195.0 2.4 %conditional.3 = ((f32[1,8,128]{2,1,0:T(8,128)S(1)}, f32[1,8,128]{2,1,0:T(8,128)S(1)}, f32[1,8,128,128]{3,2,1,0:T(8,128)S(1)})) conditional(s32[]{:T(128)} %convert_element_type.102, (f32[1,8,128]{2,1,0:T(8,128)S(1)}, f32[1,8,128]{2,1,0:T(8,128)S(1)}, f32[1,8,128,128]{3,2,1,0:T(8,128)S(1)}) %tuple.83, (pred[128,256]{0,1:T(8,128)(4,1)S(1)}, ...), branch_computations={%region_5.5_spmd, %region_6.8_spmd} | conditional | flops 137104640 | bytes 4887752 | solution.py:58
  195.4 1.2 fusion.29
  199.1 2.4 %conditional.3 = ((f32[1,8,128]{2,1,0:T(8,128)S(1)}, f32[1,8,128]{2,1,0:T(8,128)S(1)}, f32[1,8,128,128]{3,2,1,0:T(8,128)S(1)})) conditional(s32[]{:T(128)} %convert_element_type.102, (f32[1,8,128]{2,1,0:T(8,128)S(1)}, f32[1,8,128]{2,1,0:T(8,128)S(1)}, f32[1,8,128,128]{3,2,1,0:T(8,128)S(1)}) %tuple.83, (pred[128,256]{0,1:T(8,128)(4,1)S(1)}, ...), branch_computations={%region_5.5_spmd, %region_6.8_spmd} | conditional | flops 137104640 | bytes 4887752 | solution.py:58
  199.6 1.2 fusion.29
  203.2 2.4 %conditional.3 = ((f32[1,8,128]{2,1,0:T(8,128)S(1)}, f32[1,8,128]{2,1,0:T(8,128)S(1)}, f32[1,8,128,128]{3,2,1,0:T(8,128)S(1)})) conditional(s32[]{:T(128)} %convert_element_type.102, (f32[1,8,128]{2,1,0:T(8,128)S(1)}, f32[1,8,128]{2,1,0:T(8,128)S(1)}, f32[1,8,128,128]{3,2,1,0:T(8,128)S(1)}) %tuple.83, (pred[128,256]{0,1:T(8,128)(4,1)S(1)}, ...), branch_computations={%region_5.5_spmd, %region_6.8_spmd} | conditional | flops 137104640 | bytes 4887752 | solution.py:58
  203.7 1.2 fusion.29
  207.4 2.4 %conditional.3 = ((f32[1,8,128]{2,1,0:T(8,128)S(1)}, f32[1,8,128]{2,1,0:T(8,128)S(1)}, f32[1,8,128,128]{3,2,1,0:T(8,128)S(1)})) conditional(s32[]{:T(128)} %convert_element_type.102, (f32[1,8,128]{2,1,0:T(8,128)S(1)}, f32[1,8,128]{2,1,0:T(8,128)S(1)}, f32[1,8,128,128]{3,2,1,0:T(8,128)S(1)}) %tuple.83, (pred[128,256]{0,1:T(8,128)(4,1)S(1)}, ...), branch_computations={%region_5.5_spmd, %region_6.8_spmd} | conditional | flops 137104640 | bytes 4887752 | solution.py:58
  207.8 1.2 fusion.29
  (364 shorter events, 54.0 us)
Async XLA Ops:
  0.0 0.8 copy-start
  0.0 82.2 %copy-start.2 = (s32[64]{0:T(128)S(1)}, s32[64]{0:T(128)}, u32[]{:S(2)}) copy-start(s32[64]{0:T(128)} %param.21) | copy-start | bytes 772
  1.4 15.0 %all-to-all-start = ((bf16[16,8,128]{2,0,1:T(8,128)(2,1)}), bf16[16,8,128]{2,0,1:T(8,128)(2,1)S(1)}, u32[]{:S(2)}, u32[]{:S(2)}) async-start(bf16[16,8,128]{2,0,1:T(8,128)(2,1)} %copy_bitcast_fusion.2), calls=%async_computation | async-start | bytes 65536 | tf_op jit(solution)/shard_map/all_to_all | solution.py:128
  16.4 11.2 %all-to-all-start.1 = ((bf16[16,8,128]{2,0,1:T(8,128)(2,1)}), bf16[16,8,128]{2,0,1:T(8,128)(2,1)S(1)}, u32[]{:S(2)}, u32[]{:S(2)}) async-start(bf16[16,8,128]{2,0,1:T(8,128)(2,1)} %copy_bitcast_fusion.1), calls=%async_computation.1 | async-start | bytes 65536 | tf_op jit(solution)/shard_map/all_to_all | solution.py:129
  27.6 11.8 %collective-permute-start = (bf16[1,2,136,128]{3,2,1,0:T(8,128)(2,1)S(1)}, bf16[1,2,136,128]{3,2,1,0:T(8,128)(2,1)S(1)}, u32[]{:S(2)}, u32[]{:S(2)}) collective-permute-start(bf16[1,2,136,128]{3,2,1,0:T(8,128)(2,1)S(1)} %maximum_bitcast_fusion), channel_id=1, source_target_pairs={{0,8},{8,16},{16,24},{24,32},{32,40},{40,48},{48,56},{56,64},{64,7... | collective-permute-start | bytes 208904 | tf_op jit(solution)/shard_map/ppermute | solution.py:111
  30.2 9.2 %collective-permute-start.1 = (bf16[1,2,136,128]{3,2,1,0:T(8,128)(2,1)S(1)}, bf16[1,2,136,128]{3,2,1,0:T(8,128)(2,1)S(1)}, u32[]{:S(2)}, u32[]{:S(2)}) collective-permute-start(bf16[1,2,136,128]{3,2,1,0:T(8,128)(2,1)S(1)} %maximum_bitcast_fusion), channel_id=1, source_target_pairs={{0,16},{8,24},{16,32},{24,40},{32,48},{40,56},{48,64},{56,72},{64,... | collective-permute-start | bytes 208904 | tf_op jit(solution)/shard_map/ppermute | solution.py:111
  33.6 10.0 %collective-permute-start.2 = (bf16[1,2,136,128]{3,2,1,0:T(8,128)(2,1)S(1)}, bf16[1,2,136,128]{3,2,1,0:T(8,128)(2,1)S(1)}, u32[]{:S(2)}, u32[]{:S(2)}) collective-permute-start(bf16[1,2,136,128]{3,2,1,0:T(8,128)(2,1)S(1)} %maximum_bitcast_fusion), channel_id=1, source_target_pairs={{0,24},{8,32},{16,40},{24,48},{32,56},{40,64},{48,72},{56,80},{64,... | collective-permute-start | bytes 208904 | tf_op jit(solution)/shard_map/ppermute | solution.py:111
  39.4 46.1 %copy-start.1 = (bf16[128,1024]{1,0:T(8,128)(2,1)S(1)}, bf16[128,1024]{1,0:T(8,128)(2,1)}, u32[]{:S(2)}) copy-start(bf16[128,1024]{1,0:T(8,128)(2,1)} %param.15) | copy-start | bytes 786436
  43.6 23.9 %collective-permute-start.3 = (bf16[4,2,136,128]{3,2,1,0:T(8,128)(2,1)S(1)}, bf16[4,2,136,128]{3,2,1,0:T(8,128)(2,1)S(1)}, u32[]{:S(2)}, u32[]{:S(2)}) collective-permute-start(bf16[4,2,136,128]{3,2,1,0:T(8,128)(2,1)S(1)} %pad_maximum_fusion), channel_id=1, source_target_pairs={{0,32},{8,40},{16,48},{24,56},{32,64},{40,72},{48,80},{56,88},{64,... | collective-permute-start | bytes 835592 | tf_op jit(solution)/shard_map/ppermute | solution.py:111
  46.4 22.1 %collective-permute-start.4 = (bf16[4,2,136,128]{3,2,1,0:T(8,128)(2,1)S(1)}, bf16[4,2,136,128]{3,2,1,0:T(8,128)(2,1)S(1)}, u32[]{:S(2)}, u32[]{:S(2)}) collective-permute-start(bf16[4,2,136,128]{3,2,1,0:T(8,128)(2,1)S(1)} %pad_maximum_fusion), channel_id=1, source_target_pairs={{0,64},{8,72},{16,80},{24,88},{32,96},{40,104},{48,112},{56,120},{... | collective-permute-start | bytes 835592 | tf_op jit(solution)/shard_map/ppermute | solution.py:111
  50.6 26.8 %collective-permute-start.5 = (bf16[4,2,136,128]{3,2,1,0:T(8,128)(2,1)S(1)}, bf16[4,2,136,128]{3,2,1,0:T(8,128)(2,1)S(1)}, u32[]{:S(2)}, u32[]{:S(2)}) collective-permute-start(bf16[4,2,136,128]{3,2,1,0:T(8,128)(2,1)S(1)} %pad_maximum_fusion), channel_id=1, source_target_pairs={{0,96},{8,104},{16,112},{24,120},{32,128},{40,136},{48,144},{56,15... | collective-permute-start | bytes 835592 | tf_op jit(solution)/shard_map/ppermute | solution.py:111
  78.3 41.6 %collective-permute-start.6 = (bf16[16,2,136,128]{3,2,1,0:T(8,128)(2,1)}, bf16[16,2,136,128]{3,2,1,0:T(8,128)(2,1)S(1)}, u32[]{:S(2)}, u32[]{:S(2)}) collective-permute-start(bf16[16,2,136,128]{3,2,1,0:T(8,128)(2,1)} %get-tuple-element.489), channel_id=1, source_target_pairs={{0,128},{8,136},{16,144},{24,152},{32,160},{40,168},{48,176},{56,1... | collective-permute-start | bytes 3342344 | tf_op jit(solution)/shard_map/ppermute | solution.py:111
  82.7 38.4 %collective-permute-start.7 = (bf16[9,2,136,128]{3,2,1,0:T(8,128)(2,1)S(1)}, bf16[9,2,136,128]{3,2,1,0:T(8,128)(2,1)S(1)}, u32[]{:S(2)}, u32[]{:S(2)}) collective-permute-start(bf16[9,2,136,128]{3,2,1,0:T(8,128)(2,1)S(1)} %slice.72), channel_id=1, source_target_pairs={{0,256},{8,264},{16,272},{24,280},{32,288},{40,296},{48,304},{56,3... | collective-permute-start | bytes 1880072 | tf_op jit(solution)/shard_map/ppermute | solution.py:111
  127.2 84.4 %copy-start.3 = (f32[128]{0:T(128)S(1)}, f32[128]{0:T(128)}, u32[]{:S(2)}) copy-start(f32[128]{0:T(128)} %param.20) | copy-start | bytes 1540

commit v2 on v1

--- a/solution.py
+++ b/solution.py
@@ -3,6 +3,8 @@
 import jax
 import jax.numpy as jnp
 from jax import lax
+from jax.experimental import pallas as pl
+from jax.experimental.pallas import tpu as pltpu
 from jax.sharding import PartitionSpec as P
 
 QH = 64
@@ -123,6 +125,73 @@
     return held
 
 
+def attention_kernel(
+    info_ref, query_ref, window_ref, low_ref, mean_ref, out_ref, max_ref, sum_ref, acc_ref
+):
+    rows = query_ref.shape[0]
+    group_size = query_ref.shape[1] // HD
+    inv_scale = 1.0 / math.sqrt(HD)
+    seq_index = info_ref[0]
+    used = info_ref[1]
+    max_ref[...] = jnp.full(max_ref.shape, NEG, jnp.float32)
+    sum_ref[...] = jnp.zeros(sum_ref.shape, jnp.float32)
+    acc_ref[...] = jnp.zeros(acc_ref.shape, jnp.float32)
+    query_pos = seq_index * rows + lax.broadcasted_iota(jnp.int32, (rows, rows), 0)
+    low = low_ref[...]
+    lane = lax.broadcasted_iota(jnp.int32, (rows, rows), 1)
+    lane_row = lax.broadcasted_iota(jnp.int32, (1, rows), 1)
+
+    def one_slot(slot, carry):
+        key_pos = (seq_index - slot) * rows + lane
+        allowed = (key_pos <= query_pos) & (key_pos >= low)
+        key_tile = window_ref[slot, 0, :rows, :]
+        value_tile = window_ref[slot, 1, :rows, :]
+        key_rows = window_ref[slot, 0, rows:rows + 8, :].astype(jnp.float32)
+        value_rows = window_ref[slot, 1, rows:rows + 8, :].astype(jnp.float32)
+        key_scale = jnp.where(lane_row < BLK, key_rows[0:1], key_rows[1:2]) * inv_scale
+        value_scale = jnp.where(lane_row < BLK, value_rows[0:1], value_rows[1:2])
+        for g in range(group_size):
+            query_tile = query_ref[:, g * HD:(g + 1) * HD]
+            scores = lax.dot_general(
+                query_tile, key_tile, (((1,), (1,)), ((), ())), preferred_element_type=jnp.float32
+            )
+            scores = jnp.where(allowed, scores * key_scale, NEG)
+            run_max = max_ref[g][:, :1]
+            new_max = jnp.maximum(run_max, jnp.max(scores, axis=1, keepdims=True))
+            weights = jnp.where(allowed, jnp.exp(scores - new_max), 0.0)
+            factor = jnp.exp(run_max - new_max)
+            run_sum = sum_ref[g][:, :1] * factor + jnp.sum(weights, axis=1, keepdims=True)
+            scaled = (weights * value_scale).astype(jnp.bfloat16)
+            acc_ref[g] = acc_ref[g] * factor + jnp.dot(
+                scaled, value_tile, preferred_element_type=jnp.float32
+            )
+            max_ref[g] = jnp.broadcast_to(new_max, (rows, HD))
+            sum_ref[g] = jnp.broadcast_to(run_sum, (rows, HD))
+        return carry
+
+    lax.fori_loop(0, used, one_slot, 0)
+    mean = mean_ref[...]
+    for g in range(group_size):
+        out_ref[:, g * HD:(g + 1) * HD] = (acc_ref[g] / sum_ref[g] + mean).astype(jnp.bfloat16)
+
+
+def attend(info, queries, window, low, mean):
+    rows, width = queries.shape
+    group_size = width // HD
+    full = lambda shape: pl.BlockSpec(shape, lambda i, info: (0,) * len(shape))
+    return pl.pallas_call(
+        attention_kernel,
+        out_shape=jax.ShapeDtypeStruct((rows, width), jnp.bfloat16),
+        grid_spec=pltpu.PrefetchScalarGridSpec(
+            num_scalar_prefetch=1,
+            grid=(1,),
+            in_specs=[full(queries.shape), full(window.shape), full(low.shape), full(mean.shape)],
+            out_specs=full((rows, width)),
+            scratch_shapes=[pltpu.VMEM((group_size, rows, HD), jnp.float32)] * 3,
+        ),
+    )(info, queries, window, low, mean)
+
+
 def shards(queries, key_tokens, value_tokens, key_scales, value_scales, value_means, doc_lengths):
     local_keys, local_values = (
         lax.all_to_all(key_tokens, "head", split_axis=1, concat_axis=0, tiled=True),
@@ -143,44 +212,13 @@
     packet = jnp.concatenate([jnp.stack([local_keys, local_values]), scale_rows], axis=1)
     window = gather_window(packet, seq_count, depth)
     slots = window.shape[0]
-    pair = 2
-    padded = -(-slots // pair) * pair
-    window = jnp.concatenate(
-        [window, jnp.zeros((padded - slots,) + window.shape[1:], window.dtype)], axis=0
-    )
-    shard_of = (seq_index - jnp.arange(padded, dtype=jnp.int32)) % seq_count
-    key_pos = shard_of[:, None] * row_count + jnp.arange(row_count, dtype=jnp.int32)[None, :]
-    key_pos = jnp.where(jnp.arange(padded)[:, None] < slots, key_pos, jnp.int32(2**30))
-    steps = padded // pair
-    key_count = pair * row_count
-    key_part = window[:, 0, :row_count].reshape(steps, key_count, heads_kv, HD)
-    value_part = window[:, 1, :row_count].reshape(steps, key_count, heads_kv, HD)
-    key_sc = jnp.repeat(window[:, 0, row_count:row_count + blocks, ::HD], BLK, axis=1)
-    value_sc = jnp.repeat(window[:, 1, row_count:row_count + blocks, ::HD], BLK, axis=1)
-    key_sc = key_sc.astype(jnp.float32).reshape(steps, key_count, heads_kv)
-    value_sc = value_sc.astype(jnp.float32).reshape(steps, key_count, heads_kv)
-    key_pos = key_pos.reshape(steps, key_count)
-
     own_pos = seq_index * row_count + jnp.arange(row_count, dtype=jnp.int32)
-    query_tile = queries.reshape(row_count, heads_kv, group_size, HD).transpose(1, 2, 0, 3)
-    query_doc = doc_index(own_pos, starts)
-    initial = (
-        jnp.full((heads_kv, group_size, row_count), NEG, jnp.float32),
-        jnp.zeros((heads_kv, group_size, row_count), jnp.float32),
-        jnp.zeros((heads_kv, group_size, row_count, HD), jnp.float32),
-    )
-
-    def one_step(current, scan_item):
-        k_tile, v_tile, k_sc, v_sc, pos = scan_item
-        return (
-            block_update(
-                current, query_tile, own_pos, query_doc, k_tile, v_tile, k_sc, v_sc, pos, starts
-            ),
-            None,
-        )
-
-    totals, _ = lax.scan(one_step, initial, (key_part, value_part, key_sc, value_sc, key_pos))
-    return finish(totals, value_means, heads_kv, group_size, row_count)
+    low = starts[doc_index(own_pos, starts)]
+    used = jnp.clip(seq_index - low[0] // row_count + 1, 1, slots).astype(jnp.int32)
+    info = jnp.stack([seq_index.astype(jnp.int32), used])
+    low_tile = jnp.broadcast_to(low[:, None], (row_count, row_count)).astype(jnp.int32)
+    mean = value_means.reshape(1, HD)
+    return attend(info, queries, window, low_tile, mean)
 
 
 def solution(mesh):

time: 215 us -> 234 us (1.088)
  the two profiles are of different devices: /device:TPU:262 before, /device:TPU:6 now
where the time goes in v2:
time: 234 us; the launch traced here: 233 us
  Pallas kernels  105 us (45%)
  waiting for transfers between devices  65.3 us (28%)
  starting transfers between devices  45.9 us (20%)
  local copies, waits for them, and re-layouts  14 us (6%)
  other arithmetic  3.17 us (1%)
    pallas_call x1, Pallas kernels, attend(): pl.pallas_call(attention_kernel, out_shape=jax.ShapeDtypeStruct((rows, wi...  105 us
    ppermute x8, waiting for transfers between devices, shift_from(): return lax.ppermute(x, 'seq', pairs)  52.6 us
    ppermute x8, starting transfers between devices, shift_from(): return lax.ppermute(x, 'seq', pairs)  35.4 us
    all_to_all x1, waiting for transfers between devices, shards(): lax.all_to_all(key_tokens, 'head', split_axis=1, concat_axis=0, tiled=True)  7.71 us
    all_to_all x1, starting transfers between devices, shards(): lax.all_to_all(value_tokens, 'head', split_axis=1, concat_axis=0, tiled=T...  7.1 us
    unnamed x13, local copies, waits for them, and re-layouts  5.71 us
    all_to_all x1, waiting for transfers between devices, shards(): lax.all_to_all(value_tokens, 'head', split_axis=1, concat_axis=0, tiled=T...  5.01 us
  transfers between devices with their start and end apart: 10, of which 7 were waited for; matrix products, arithmetic and copies ran while one was open for 5% of the time, Pallas kernels for 0%

profile of v2, /device:TPU:6, one launch (start us, length us, event | category | flops | bytes accessed | tf_op | source)
XLA Modules:
  0.0 233.4 jit_solution(2245624028762129280)
XLA Ops:
  0.0 0.0 copy-start
  0.0 0.0 copy-start.3
  0.0 0.8 copy-done
  0.8 0.6 copy_bitcast_fusion
  1.4 7.1 %all-to-all-start.1 = ((bf16[16,8,128]{2,0,1:T(8,128)(2,1)}), bf16[16,8,128]{2,0,1:T(8,128)(2,1)S(1)}, u32[]{:S(2)}, u32[]{:S(2)}) async-start(bf16[16,8,128]{2,0,1:T(8,128)(2,1)} %copy_bitcast_fusion), calls=%async_computation.1 | async-start | bytes 65536 | tf_op jit(solution)/shard_map/all_to_all | solution.py:198
  8.5 1.4 copy_bitcast_fusion.1
  9.8 0.8 reduce.5
  10.6 0.8 reduce.6
  11.4 5.0 %all-to-all-done.1 = bf16[16,8,128]{2,0,1:T(8,128)(2,1)S(1)} async-done(((bf16[16,8,128]{2,0,1:T(8,128)(2,1)}), bf16[16,8,128]{2,0,1:T(8,128)(2,1)S(1)}, u32[]{:S(2)}, u32[]{:S(2)}) %all-to-all-start.1) | async-done | bytes 32800 | tf_op jit(solution)/shard_map/all_to_all | solution.py:198
  16.4 3.3 %all-to-all-start = ((bf16[16,8,128]{2,0,1:T(8,128)(2,1)}), bf16[16,8,128]{2,0,1:T(8,128)(2,1)S(1)}, u32[]{:S(2)}, u32[]{:S(2)}) async-start(bf16[16,8,128]{2,0,1:T(8,128)(2,1)} %copy_bitcast_fusion.1), calls=%async_computation | async-start | bytes 65536 | tf_op jit(solution)/shard_map/all_to_all | solution.py:197
  19.8 0.1 scatter.13
  19.8 0.1 broadcast_dynamic-update-slice_fusion
  19.9 7.7 %all-to-all-done = bf16[16,8,128]{2,0,1:T(8,128)(2,1)S(1)} async-done(((bf16[16,8,128]{2,0,1:T(8,128)(2,1)}), bf16[16,8,128]{2,0,1:T(8,128)(2,1)S(1)}, u32[]{:S(2)}, u32[]{:S(2)}) %all-to-all-start) | async-done | bytes 32800 | tf_op jit(solution)/shard_map/all_to_all | solution.py:197
  27.6 2.6 %collective-permute-start = (bf16[1,2,136,128]{3,2,1,0:T(8,128)(2,1)S(1)}, bf16[1,2,136,128]{3,2,1,0:T(8,128)(2,1)S(1)}, u32[]{:S(2)}, u32[]{:S(2)}) collective-permute-start(bf16[1,2,136,128]{3,2,1,0:T(8,128)(2,1)S(1)} %maximum_bitcast_fusion), channel_id=1, source_target_pairs={{0,8},{8,16},{16,24},{24,32},{32,40},{40,48},{48,56},{56,64},{64,7... | collective-permute-start | bytes 208904 | tf_op jit(solution)/shard_map/ppermute | solution.py:113
  30.2 4.3 %collective-permute-start.1 = (bf16[1,2,136,128]{3,2,1,0:T(8,128)(2,1)S(1)}, bf16[1,2,136,128]{3,2,1,0:T(8,128)(2,1)S(1)}, u32[]{:S(2)}, u32[]{:S(2)}) collective-permute-start(bf16[1,2,136,128]{3,2,1,0:T(8,128)(2,1)S(1)} %maximum_bitcast_fusion), channel_id=1, source_target_pairs={{0,16},{8,24},{16,32},{24,40},{32,48},{40,56},{48,64},{56,72},{64,... | collective-permute-start | bytes 208904 | tf_op jit(solution)/shard_map/ppermute | solution.py:113
  34.5 6.9 %collective-permute-start.2 = (bf16[1,2,136,128]{3,2,1,0:T(8,128)(2,1)S(1)}, bf16[1,2,136,128]{3,2,1,0:T(8,128)(2,1)S(1)}, u32[]{:S(2)}, u32[]{:S(2)}) collective-permute-start(bf16[1,2,136,128]{3,2,1,0:T(8,128)(2,1)S(1)} %maximum_bitcast_fusion), channel_id=1, source_target_pairs={{0,24},{8,32},{16,40},{24,48},{32,56},{40,64},{48,72},{56,80},{64,... | collective-permute-start | bytes 208904 | tf_op jit(solution)/shard_map/ppermute | solution.py:113
  41.4 0.7 constant_dynamic-update-slice_fusion.12
  42.0 0.0 collective-permute-done
  42.0 2.4 %collective-permute-done.1 = bf16[1,2,136,128]{3,2,1,0:T(8,128)(2,1)S(1)} collective-permute-done((bf16[1,2,136,128]{3,2,1,0:T(8,128)(2,1)S(1)}, bf16[1,2,136,128]{3,2,1,0:T(8,128)(2,1)S(1)}, u32[]{:S(2)}, u32[]{:S(2)}) %collective-permute-start.1) | collective-permute-done | bytes 69664 | tf_op jit(solution)/shard_map/ppermute | solution.py:113
  44.5 3.5 %collective-permute-done.2 = bf16[1,2,136,128]{3,2,1,0:T(8,128)(2,1)S(1)} collective-permute-done((bf16[1,2,136,128]{3,2,1,0:T(8,128)(2,1)S(1)}, bf16[1,2,136,128]{3,2,1,0:T(8,128)(2,1)S(1)}, u32[]{:S(2)}, u32[]{:S(2)}) %collective-permute-start.2) | collective-permute-done | bytes 69664 | tf_op jit(solution)/shard_map/ppermute | solution.py:113
  48.0 1.9 collective-permute-start.3
  49.9 7.3 %collective-permute-start.4 = (bf16[4,2,136,128]{3,2,1,0:T(8,128)(2,1)S(1)}, bf16[4,2,136,128]{3,2,1,0:T(8,128)(2,1)S(1)}, u32[]{:S(2)}, u32[]{:S(2)}) collective-permute-start(bf16[4,2,136,128]{3,2,1,0:T(8,128)(2,1)S(1)} %pad_maximum_fusion), channel_id=1, source_target_pairs={{0,64},{8,72},{16,80},{24,88},{32,96},{40,104},{48,112},{56,120},{... | collective-permute-start | bytes 835592 | tf_op jit(solution)/shard_map/ppermute | solution.py:113
  57.3 5.1 %collective-permute-start.5 = (bf16[4,2,136,128]{3,2,1,0:T(8,128)(2,1)S(1)}, bf16[4,2,136,128]{3,2,1,0:T(8,128)(2,1)S(1)}, u32[]{:S(2)}, u32[]{:S(2)}) collective-permute-start(bf16[4,2,136,128]{3,2,1,0:T(8,128)(2,1)S(1)} %pad_maximum_fusion), channel_id=1, source_target_pairs={{0,96},{8,104},{16,112},{24,120},{32,128},{40,136},{48,144},{56,15... | collective-permute-start | bytes 835592 | tf_op jit(solution)/shard_map/ppermute | solution.py:113
  62.4 0.7 constant_dynamic-update-slice_fusion.11
  63.1 0.7 constant_dynamic-update-slice_fusion.10
  63.7 0.7 constant_dynamic-update-slice_fusion.9
  64.4 9.4 %collective-permute-done.3 = bf16[4,2,136,128]{3,2,1,0:T(8,128)(2,1)S(1)} collective-permute-done((bf16[4,2,136,128]{3,2,1,0:T(8,128)(2,1)S(1)}, bf16[4,2,136,128]{3,2,1,0:T(8,128)(2,1)S(1)}, u32[]{:S(2)}, u32[]{:S(2)}) %collective-permute-start.3) | collective-permute-done | bytes 278560 | tf_op jit(solution)/shard_map/ppermute | solution.py:113
  73.8 0.8 constant_dynamic-update-slice_fusion.8
  74.6 0.0 collective-permute-done.4
  74.6 0.8 constant_dynamic-update-slice_fusion.7
  75.5 0.0 copy-start.2
  75.5 5.5 %collective-permute-done.5 = bf16[4,2,136,128]{3,2,1,0:T(8,128)(2,1)S(1)} collective-permute-done((bf16[4,2,136,128]{3,2,1,0:T(8,128)(2,1)S(1)}, bf16[4,2,136,128]{3,2,1,0:T(8,128)(2,1)S(1)}, u32[]{:S(2)}, u32[]{:S(2)}) %collective-permute-start.5) | collective-permute-done | bytes 278560 | tf_op jit(solution)/shard_map/ppermute | solution.py:113
  81.0 0.8 constant_dynamic-update-slice_fusion
  81.8 0.0 copy-done.2
  81.8 5.4 %collective-permute-start.6 = (bf16[16,2,136,128]{3,2,1,0:T(8,128)(2,1)}, bf16[16,2,136,128]{3,2,1,0:T(8,128)(2,1)}, u32[]{:S(2)}, u32[]{:S(2)}) collective-permute-start(bf16[16,2,136,128]{3,2,1,0:T(8,128)(2,1)} %get-tuple-element.35), channel_id=1, source_target_pairs={{0,128},{8,136},{16,144},{24,152},{32,160},{40,168},{48,176},{56,1... | collective-permute-start | bytes 3342344 | tf_op jit(solution)/shard_map/ppermute | solution.py:113
  87.2 0.0 copy-done.3
  87.2 0.1 copy.14
  87.3 0.1 reduce-window.9
  87.4 0.1 reduce.4
  87.6 1.1 slice.60
  88.7 1.9 collective-permute-start.7
  90.6 0.1 convert_reduce_fusion
  90.7 1.2 gather_fusion
  92.1 0.6 pad_add_fusion.info_ref
  92.7 31.7 %collective-permute-done.6 = bf16[16,2,136,128]{3,2,1,0:T(8,128)(2,1)} collective-permute-done((bf16[16,2,136,128]{3,2,1,0:T(8,128)(2,1)}, bf16[16,2,136,128]{3,2,1,0:T(8,128)(2,1)}, u32[]{:S(2)}, u32[]{:S(2)}) %collective-permute-start.6) | collective-permute-done | bytes 1114144 | tf_op jit(solution)/shard_map/ppermute | solution.py:113
  124.5 1.4 constant_dynamic-update-slice_fusion.14
  125.9 0.0 collective-permute-done.7
  125.9 1.2 constant_dynamic-update-slice_fusion.13.window_ref
  127.0 0.0 copy-start.1
  127.1 0.8 broadcast_in_dim.5.low_ref
  127.9 0.7 copy-done.1
  128.6 104.7 %shard_map.76 = bf16[128,1024]{1,0:T(8,128)(2,1)} custom-call(s32[2]{0:T(128)} %pad_add_fusion.info_ref, bf16[128,1024]{1,0:T(8,128)(2,1)} %query_ref.1, bf16[41,2,136,128]{3,2,1,0:T(8,128)(2,1)} %copy-done.1, s32[128,128]{1,0:T(8,128)} %broadcast_in_dim.5.low_ref, f32[1,128]{1,0:T(1,128)} %bitcast.46), custom_call_target="tpu_custom_call" | custom-call | tf_op jit(solution)/shard_map/pallas_call | solution.py:182
  (7 shorter events, 0.1 us)
Async XLA Ops:
  0.0 0.8 copy-start
  0.0 87.2 %copy-start.3 = (s32[64]{0:T(128)S(1)}, s32[64]{0:T(128)}, u32[]{:S(2)}) copy-start(s32[64]{0:T(128)} %param.17) | copy-start | bytes 772
  1.4 15.0 %all-to-all-start.1 = ((bf16[16,8,128]{2,0,1:T(8,128)(2,1)}), bf16[16,8,128]{2,0,1:T(8,128)(2,1)S(1)}, u32[]{:S(2)}, u32[]{:S(2)}) async-start(bf16[16,8,128]{2,0,1:T(8,128)(2,1)} %copy_bitcast_fusion), calls=%async_computation.1 | async-start | bytes 65536 | tf_op jit(solution)/shard_map/all_to_all | solution.py:198
  16.4 11.2 %all-to-all-start = ((bf16[16,8,128]{2,0,1:T(8,128)(2,1)}), bf16[16,8,128]{2,0,1:T(8,128)(2,1)S(1)}, u32[]{:S(2)}, u32[]{:S(2)}) async-start(bf16[16,8,128]{2,0,1:T(8,128)(2,1)} %copy_bitcast_fusion.1), calls=%async_computation | async-start | bytes 65536 | tf_op jit(solution)/shard_map/all_to_all | solution.py:197
  27.6 14.4 %collective-permute-start = (bf16[1,2,136,128]{3,2,1,0:T(8,128)(2,1)S(1)}, bf16[1,2,136,128]{3,2,1,0:T(8,128)(2,1)S(1)}, u32[]{:S(2)}, u32[]{:S(2)}) collective-permute-start(bf16[1,2,136,128]{3,2,1,0:T(8,128)(2,1)S(1)} %maximum_bitcast_fusion), channel_id=1, source_target_pairs={{0,8},{8,16},{16,24},{24,32},{32,40},{40,48},{48,56},{56,64},{64,7... | collective-permute-start | bytes 208904 | tf_op jit(solution)/shard_map/ppermute | solution.py:113
  30.2 14.2 %collective-permute-start.1 = (bf16[1,2,136,128]{3,2,1,0:T(8,128)(2,1)S(1)}, bf16[1,2,136,128]{3,2,1,0:T(8,128)(2,1)S(1)}, u32[]{:S(2)}, u32[]{:S(2)}) collective-permute-start(bf16[1,2,136,128]{3,2,1,0:T(8,128)(2,1)S(1)} %maximum_bitcast_fusion), channel_id=1, source_target_pairs={{0,16},{8,24},{16,32},{24,40},{32,48},{40,56},{48,64},{56,72},{64,... | collective-permute-start | bytes 208904 | tf_op jit(solution)/shard_map/ppermute | solution.py:113
  34.5 13.5 %collective-permute-start.2 = (bf16[1,2,136,128]{3,2,1,0:T(8,128)(2,1)S(1)}, bf16[1,2,136,128]{3,2,1,0:T(8,128)(2,1)S(1)}, u32[]{:S(2)}, u32[]{:S(2)}) collective-permute-start(bf16[1,2,136,128]{3,2,1,0:T(8,128)(2,1)S(1)} %maximum_bitcast_fusion), channel_id=1, source_target_pairs={{0,24},{8,32},{16,40},{24,48},{32,56},{40,64},{48,72},{56,80},{64,... | collective-permute-start | bytes 208904 | tf_op jit(solution)/shard_map/ppermute | solution.py:113
  48.0 25.8 %collective-permute-start.3 = (bf16[4,2,136,128]{3,2,1,0:T(8,128)(2,1)S(1)}, bf16[4,2,136,128]{3,2,1,0:T(8,128)(2,1)S(1)}, u32[]{:S(2)}, u32[]{:S(2)}) collective-permute-start(bf16[4,2,136,128]{3,2,1,0:T(8,128)(2,1)S(1)} %pad_maximum_fusion), channel_id=1, source_target_pairs={{0,32},{8,40},{16,48},{24,56},{32,64},{40,72},{48,80},{56,88},{64,... | collective-permute-start | bytes 835592 | tf_op jit(solution)/shard_map/ppermute | solution.py:113
  49.9 24.7 %collective-permute-start.4 = (bf16[4,2,136,128]{3,2,1,0:T(8,128)(2,1)S(1)}, bf16[4,2,136,128]{3,2,1,0:T(8,128)(2,1)S(1)}, u32[]{:S(2)}, u32[]{:S(2)}) collective-permute-start(bf16[4,2,136,128]{3,2,1,0:T(8,128)(2,1)S(1)} %pad_maximum_fusion), channel_id=1, source_target_pairs={{0,64},{8,72},{16,80},{24,88},{32,96},{40,104},{48,112},{56,120},{... | collective-permute-start | bytes 835592 | tf_op jit(solution)/shard_map/ppermute | solution.py:113
  57.3 23.7 %collective-permute-start.5 = (bf16[4,2,136,128]{3,2,1,0:T(8,128)(2,1)S(1)}, bf16[4,2,136,128]{3,2,1,0:T(8,128)(2,1)S(1)}, u32[]{:S(2)}, u32[]{:S(2)}) collective-permute-start(bf16[4,2,136,128]{3,2,1,0:T(8,128)(2,1)S(1)} %pad_maximum_fusion), channel_id=1, source_target_pairs={{0,96},{8,104},{16,112},{24,120},{32,128},{40,136},{48,144},{56,15... | collective-permute-start | bytes 835592 | tf_op jit(solution)/shard_map/ppermute | solution.py:113
  75.5 6.4 %copy-start.2 = (bf16[12,2,136,128]{3,2,1,0:T(8,128)(2,1)}, bf16[12,2,136,128]{3,2,1,0:T(8,128)(2,1)S(1)}, u32[]{:S(2)}) copy-start(bf16[12,2,136,128]{3,2,1,0:T(8,128)(2,1)S(1)} %get-tuple-element.29) | copy-start | bytes 2506756
  81.8 42.6 %collective-permute-start.6 = (bf16[16,2,136,128]{3,2,1,0:T(8,128)(2,1)}, bf16[16,2,136,128]{3,2,1,0:T(8,128)(2,1)}, u32[]{:S(2)}, u32[]{:S(2)}) collective-permute-start(bf16[16,2,136,128]{3,2,1,0:T(8,128)(2,1)} %get-tuple-element.35), channel_id=1, source_target_pairs={{0,128},{8,136},{16,144},{24,152},{32,160},{40,168},{48,176},{56,1... | collective-permute-start | bytes 3342344 | tf_op jit(solution)/shard_map/ppermute | solution.py:113
  88.7 37.2 %collective-permute-start.7 = (bf16[9,2,136,128]{3,2,1,0:T(8,128)(2,1)S(1)}, bf16[9,2,136,128]{3,2,1,0:T(8,128)(2,1)}, u32[]{:S(2)}, u32[]{:S(2)}) collective-permute-start(bf16[9,2,136,128]{3,2,1,0:T(8,128)(2,1)S(1)} %slice.60), channel_id=1, source_target_pairs={{0,256},{8,264},{16,272},{24,280},{32,288},{40,296},{48,304},{56,3... | collective-permute-start | bytes 1880072 | tf_op jit(solution)/shard_map/ppermute | solution.py:113
  127.0 1.6 copy-start.1

commit v3 on v2

--- a/solution.py
+++ b/solution.py
@@ -128,56 +128,60 @@
 def attention_kernel(
     info_ref, query_ref, window_ref, low_ref, mean_ref, out_ref, max_ref, sum_ref, acc_ref
 ):
-    rows = query_ref.shape[0]
-    group_size = query_ref.shape[1] // HD
+    group_size, rows, _ = acc_ref.shape
     inv_scale = 1.0 / math.sqrt(HD)
     seq_index = info_ref[0]
-    used = info_ref[1]
+    pairs = info_ref[1]
     max_ref[...] = jnp.full(max_ref.shape, NEG, jnp.float32)
     sum_ref[...] = jnp.zeros(sum_ref.shape, jnp.float32)
     acc_ref[...] = jnp.zeros(acc_ref.shape, jnp.float32)
     query_pos = seq_index * rows + lax.broadcasted_iota(jnp.int32, (rows, rows), 0)
     low = low_ref[...]
     lane = lax.broadcasted_iota(jnp.int32, (rows, rows), 1)
-    lane_row = lax.broadcasted_iota(jnp.int32, (1, rows), 1)
-
-    def one_slot(slot, carry):
-        key_pos = (seq_index - slot) * rows + lane
-        allowed = (key_pos <= query_pos) & (key_pos >= low)
-        key_tile = window_ref[slot, 0, :rows, :]
-        value_tile = window_ref[slot, 1, :rows, :]
-        key_rows = window_ref[slot, 0, rows:rows + 8, :].astype(jnp.float32)
-        value_rows = window_ref[slot, 1, rows:rows + 8, :].astype(jnp.float32)
-        key_scale = jnp.where(lane_row < BLK, key_rows[0:1], key_rows[1:2]) * inv_scale
-        value_scale = jnp.where(lane_row < BLK, value_rows[0:1], value_rows[1:2])
-        for g in range(group_size):
-            query_tile = query_ref[:, g * HD:(g + 1) * HD]
-            scores = lax.dot_general(
-                query_tile, key_tile, (((1,), (1,)), ((), ())), preferred_element_type=jnp.float32
-            )
-            scores = jnp.where(allowed, scores * key_scale, NEG)
-            run_max = max_ref[g][:, :1]
-            new_max = jnp.maximum(run_max, jnp.max(scores, axis=1, keepdims=True))
+    query_all = query_ref[...]
+
+    def one_pair(pair, carry):
+        parts = []
+        for half in range(2):
+            slot = 2 * pair + half
+            key_pos = (seq_index - slot) * rows + lane
+            allowed = ((key_pos <= query_pos) & (key_pos >= low))[None]
+            key_t = window_ref[slot, 0, :HD, :]
+            key_scale = window_ref[slot, 0, HD:HD + 1, :].astype(jnp.float32) * inv_scale
+            value_scale = window_ref[slot, 1, rows:rows + 1, :].astype(jnp.float32)
+            scores = jnp.dot(query_all, key_t, preferred_element_type=jnp.float32)
+            scores = scores.reshape(group_size, rows, rows) * key_scale[None]
+            scores = jnp.where(allowed, scores, NEG)
+            parts.append((scores, allowed, value_scale[None], slot))
+        run_max = max_ref[...][:, :, :1]
+        new_max = run_max
+        for scores, _, _, _ in parts:
+            new_max = jnp.maximum(new_max, jnp.max(scores, axis=2, keepdims=True))
+        factor = jnp.exp(run_max - new_max)
+        run_sum = sum_ref[...][:, :, :1] * factor
+        acc = acc_ref[...] * factor
+        for scores, allowed, value_scale, slot in parts:
             weights = jnp.where(allowed, jnp.exp(scores - new_max), 0.0)
-            factor = jnp.exp(run_max - new_max)
-            run_sum = sum_ref[g][:, :1] * factor + jnp.sum(weights, axis=1, keepdims=True)
-            scaled = (weights * value_scale).astype(jnp.bfloat16)
-            acc_ref[g] = acc_ref[g] * factor + jnp.dot(
-                scaled, value_tile, preferred_element_type=jnp.float32
-            )
-            max_ref[g] = jnp.broadcast_to(new_max, (rows, HD))
-            sum_ref[g] = jnp.broadcast_to(run_sum, (rows, HD))
+            run_sum = run_sum + jnp.sum(weights, axis=2, keepdims=True)
+            scaled = (weights * value_scale).astype(jnp.bfloat16).reshape(group_size * rows, rows)
+            value_tile = window_ref[slot, 1, :rows, :]
+            mixed = jnp.dot(scaled, value_tile, preferred_element_type=jnp.float32)
+            acc = acc + mixed.reshape(group_size, rows, HD)
+        acc_ref[...] = acc
+        max_ref[...] = jnp.broadcast_to(new_max, max_ref.shape)
+        sum_ref[...] = jnp.broadcast_to(run_sum, sum_ref.shape)
         return carry
 
-    lax.fori_loop(0, used, one_slot, 0)
-    mean = mean_ref[...]
+    lax.fori_loop(0, pairs, one_pair, 0)
+    result = acc_ref[...] / sum_ref[...] + mean_ref[...][None]
     for g in range(group_size):
-        out_ref[:, g * HD:(g + 1) * HD] = (acc_ref[g] / sum_ref[g] + mean).astype(jnp.bfloat16)
+        out_ref[:, g * HD:(g + 1) * HD] = result[g].astype(jnp.bfloat16)
 
 
 def attend(info, queries, window, low, mean):
     rows, width = queries.shape
     group_size = width // HD
+    query_all = queries.reshape(rows, group_size, HD).transpose(1, 0, 2).reshape(-1, HD)
     full = lambda shape: pl.BlockSpec(shape, lambda i, info: (0,) * len(shape))
     return pl.pallas_call(
         attention_kernel,
@@ -185,11 +189,11 @@
         grid_spec=pltpu.PrefetchScalarGridSpec(
             num_scalar_prefetch=1,
             grid=(1,),
-            in_specs=[full(queries.shape), full(window.shape), full(low.shape), full(mean.shape)],
+            in_specs=[full(query_all.shape), full(window.shape), full(low.shape), full(mean.shape)],
             out_specs=full((rows, width)),
             scratch_shapes=[pltpu.VMEM((group_size, rows, HD), jnp.float32)] * 3,
         ),
-    )(info, queries, window, low, mean)
+    )(info, query_all, window, low, mean)
 
 
 def shards(queries, key_tokens, value_tokens, key_scales, value_scales, value_means, doc_lengths):
@@ -206,16 +210,20 @@
     starts = jnp.cumsum(doc_lengths) - doc_lengths
     depth = min(seq_count, -(-(MOST - 1) // row_count) + 1)
     pad_rows = 8
-    scale_rows = jnp.zeros((2, pad_rows, heads_kv * HD), jnp.bfloat16)
-    scale_rows = scale_rows.at[0, :blocks].set(jnp.repeat(key_scales, HD, axis=1))
-    scale_rows = scale_rows.at[1, :blocks].set(jnp.repeat(value_scales, HD, axis=1))
-    packet = jnp.concatenate([jnp.stack([local_keys, local_values]), scale_rows], axis=1)
+    key_scale_row = jnp.repeat(key_scales.reshape(-1), BLK)
+    value_scale_row = jnp.repeat(value_scales.reshape(-1), BLK)
+    scale_rows = jnp.zeros((2, pad_rows, row_count), jnp.bfloat16)
+    scale_rows = scale_rows.at[0, 0].set(key_scale_row).at[1, 0].set(value_scale_row)
+    packet = jnp.concatenate([jnp.stack([local_keys.T, local_values]), scale_rows], axis=1)
     window = gather_window(packet, seq_count, depth)
     slots = window.shape[0]
+    window = jnp.concatenate(
+        [window, jnp.zeros((slots % 2,) + window.shape[1:], window.dtype)], axis=0
+    )
     own_pos = seq_index * row_count + jnp.arange(row_count, dtype=jnp.int32)
     low = starts[doc_index(own_pos, starts)]
     used = jnp.clip(seq_index - low[0] // row_count + 1, 1, slots).astype(jnp.int32)
-    info = jnp.stack([seq_index.astype(jnp.int32), used])
+    info = jnp.stack([seq_index.astype(jnp.int32), (used + 1) // 2])
     low_tile = jnp.broadcast_to(low[:, None], (row_count, row_count)).astype(jnp.int32)
     mean = value_means.reshape(1, HD)
     return attend(info, queries, window, low_tile, mean)

time: 234 us -> 163 us (0.70)
  Pallas kernels: 105 us -> 33.4 us
    pallas_call x1, Pallas kernels: 105 us -> 33.4 us  [attend(): pl.pallas_call(attention_kernel, out_shape=jax.ShapeDtypeStruct((rows, wi...]
    all_to_all x1, starting transfers between devices: 3.34 us -> 7.1 us  [shards(): lax.all_to_all(key_tokens, 'head', split_axis=1, concat_axis=0, tiled=True)]
    all_to_all x1, starting transfers between devices: 7.1 us -> 3.34 us  [shards(): lax.all_to_all(value_tokens, 'head', split_axis=1, concat_axis=0, tiled=T...]
    unnamed x13 -> x14, local copies, waits for them, and re-layouts: 5.71 us -> 6.14 us
  transfers between devices with their start and end apart: 10 -> 10, of which waited for: 7 -> 7; matrix products, arithmetic and copies ran while one was open for 5% -> 9% of each run, Pallas kernels for 0% -> 0%
where the time goes in v3:
time: 163 us; the launch traced here: 162 us
  waiting for transfers between devices  63.5 us (39%)
  starting transfers between devices  45.8 us (28%)
  Pallas kernels  33.4 us (20%)
  local copies, waits for them, and re-layouts  15.9 us (10%)
  other arithmetic  3.12 us (2%)
    ppermute x8, waiting for transfers between devices, shift_from(): return lax.ppermute(x, 'seq', pairs)  51.1 us
    ppermute x8, starting transfers between devices, shift_from(): return lax.ppermute(x, 'seq', pairs)  35.4 us
    pallas_call x1, Pallas kernels, attend(): pl.pallas_call(attention_kernel, out_shape=jax.ShapeDtypeStruct((rows, wi...  33.4 us
    all_to_all x1, starting transfers between devices, shards(): lax.all_to_all(key_tokens, 'head', split_axis=1, concat_axis=0, tiled=True)  7.1 us
    all_to_all x1, waiting for transfers between devices, shards(): lax.all_to_all(key_tokens, 'head', split_axis=1, concat_axis=0, tiled=True)  6.56 us
    unnamed x14, local copies, waits for them, and re-layouts  6.14 us
    all_to_all x1, waiting for transfers between devices, shards(): lax.all_to_all(value_tokens, 'head', split_axis=1, concat_axis=0, tiled=T...  5.83 us
    all_to_all x1, starting transfers between devices, shards(): lax.all_to_all(value_tokens, 'head', split_axis=1, concat_axis=0, tiled=T...  3.34 us
  transfers between devices with their start and end apart: 10, of which 7 were waited for; matrix products, arithmetic and copies ran while one was open for 9% of the time, Pallas kernels for 0%

profile of v3, /device:TPU:6, one launch (start us, length us, event | category | flops | bytes accessed | tf_op | source)
XLA Modules:
  0.0 162.1 jit_solution(2641910447684589229)
XLA Ops:
  0.0 0.0 copy-start
  0.0 0.0 copy-start.3
  0.0 1.4 copy_bitcast_fusion.2
  1.4 7.1 %all-to-all-start = ((bf16[16,8,128]{2,0,1:T(8,128)(2,1)}), bf16[16,8,128]{2,0,1:T(8,128)(2,1)S(1)}, u32[]{:S(2)}, u32[]{:S(2)}) async-start(bf16[16,8,128]{2,0,1:T(8,128)(2,1)} %copy_bitcast_fusion.2), calls=%async_computation | async-start | bytes 65536 | tf_op jit(solution)/shard_map/all_to_all | solution.py:201
  8.5 1.4 copy_bitcast_fusion.1
  9.9 6.6 %all-to-all-done = bf16[16,8,128]{2,0,1:T(8,128)(2,1)S(1)} async-done(((bf16[16,8,128]{2,0,1:T(8,128)(2,1)}), bf16[16,8,128]{2,0,1:T(8,128)(2,1)S(1)}, u32[]{:S(2)}, u32[]{:S(2)}) %all-to-all-start) | async-done | bytes 32800 | tf_op jit(solution)/shard_map/all_to_all | solution.py:201
  16.5 3.3 %all-to-all-start.1 = ((bf16[16,8,128]{2,0,1:T(8,128)(2,1)}), bf16[16,8,128]{2,0,1:T(8,128)(2,1)S(1)}, u32[]{:S(2)}, u32[]{:S(2)}) async-start(bf16[16,8,128]{2,0,1:T(8,128)(2,1)} %copy_bitcast_fusion.1), calls=%async_computation.1 | async-start | bytes 65536 | tf_op jit(solution)/shard_map/all_to_all | solution.py:202
  19.8 0.8 reduce.5
  20.6 0.1 broadcast_in_dim.10
  20.7 0.1 reshape.148
  20.8 0.8 reduce.6
  21.5 0.1 broadcast_in_dim.11
  21.6 0.1 reshape.150
  21.7 0.1 copy.29
  21.8 5.8 %all-to-all-done.1 = bf16[16,8,128]{2,0,1:T(8,128)(2,1)S(1)} async-done(((bf16[16,8,128]{2,0,1:T(8,128)(2,1)}), bf16[16,8,128]{2,0,1:T(8,128)(2,1)S(1)}, u32[]{:S(2)}, u32[]{:S(2)}) %all-to-all-start.1) | async-done | bytes 32800 | tf_op jit(solution)/shard_map/all_to_all | solution.py:202
  27.7 2.6 %collective-permute-start = (bf16[1,2,136,128]{3,2,1,0:T(8,128)(2,1)S(1)}, bf16[1,2,136,128]{3,2,1,0:T(8,128)(2,1)S(1)}, u32[]{:S(2)}, u32[]{:S(2)}) collective-permute-start(bf16[1,2,136,128]{3,2,1,0:T(8,128)(2,1)S(1)} %maximum_bitcast_fusion), channel_id=1, source_target_pairs={{0,8},{8,16},{16,24},{24,32},{32,40},{40,48},{48,56},{56,64},{64,7... | collective-permute-start | bytes 208904 | tf_op jit(solution)/shard_map/ppermute | solution.py:113
  30.3 4.3 %collective-permute-start.1 = (bf16[1,2,136,128]{3,2,1,0:T(8,128)(2,1)S(1)}, bf16[1,2,136,128]{3,2,1,0:T(8,128)(2,1)S(1)}, u32[]{:S(2)}, u32[]{:S(2)}) collective-permute-start(bf16[1,2,136,128]{3,2,1,0:T(8,128)(2,1)S(1)} %maximum_bitcast_fusion), channel_id=1, source_target_pairs={{0,16},{8,24},{16,32},{24,40},{32,48},{40,56},{48,64},{56,72},{64,... | collective-permute-start | bytes 208904 | tf_op jit(solution)/shard_map/ppermute | solution.py:113
  34.6 6.9 %collective-permute-start.2 = (bf16[1,2,136,128]{3,2,1,0:T(8,128)(2,1)S(1)}, bf16[1,2,136,128]{3,2,1,0:T(8,128)(2,1)S(1)}, u32[]{:S(2)}, u32[]{:S(2)}) collective-permute-start(bf16[1,2,136,128]{3,2,1,0:T(8,128)(2,1)S(1)} %maximum_bitcast_fusion), channel_id=1, source_target_pairs={{0,24},{8,32},{16,40},{24,48},{32,56},{40,64},{48,72},{56,80},{64,... | collective-permute-start | bytes 208904 | tf_op jit(solution)/shard_map/ppermute | solution.py:113
  41.4 0.7 constant_dynamic-update-slice_fusion.12
  42.1 0.0 collective-permute-done
  42.1 2.4 %collective-permute-done.1 = bf16[1,2,136,128]{3,2,1,0:T(8,128)(2,1)S(1)} collective-permute-done((bf16[1,2,136,128]{3,2,1,0:T(8,128)(2,1)S(1)}, bf16[1,2,136,128]{3,2,1,0:T(8,128)(2,1)S(1)}, u32[]{:S(2)}, u32[]{:S(2)}) %collective-permute-start.1) | collective-permute-done | bytes 69664 | tf_op jit(solution)/shard_map/ppermute | solution.py:113
  44.5 3.5 %collective-permute-done.2 = bf16[1,2,136,128]{3,2,1,0:T(8,128)(2,1)S(1)} collective-permute-done((bf16[1,2,136,128]{3,2,1,0:T(8,128)(2,1)S(1)}, bf16[1,2,136,128]{3,2,1,0:T(8,128)(2,1)S(1)}, u32[]{:S(2)}, u32[]{:S(2)}) %collective-permute-start.2) | collective-permute-done | bytes 69664 | tf_op jit(solution)/shard_map/ppermute | solution.py:113
  48.1 1.9 %collective-permute-start.3 = (bf16[4,2,136,128]{3,2,1,0:T(8,128)(2,1)S(1)}, bf16[4,2,136,128]{3,2,1,0:T(8,128)(2,1)S(1)}, u32[]{:S(2)}, u32[]{:S(2)}) collective-permute-start(bf16[4,2,136,128]{3,2,1,0:T(8,128)(2,1)S(1)} %pad_maximum_fusion), channel_id=1, source_target_pairs={{0,32},{8,40},{16,48},{24,56},{32,64},{40,72},{48,80},{56,88},{64,... | collective-permute-start | bytes 835592 | tf_op jit(solution)/shard_map/ppermute | solution.py:113
  50.0 7.3 %collective-permute-start.4 = (bf16[4,2,136,128]{3,2,1,0:T(8,128)(2,1)S(1)}, bf16[4,2,136,128]{3,2,1,0:T(8,128)(2,1)S(1)}, u32[]{:S(2)}, u32[]{:S(2)}) collective-permute-start(bf16[4,2,136,128]{3,2,1,0:T(8,128)(2,1)S(1)} %pad_maximum_fusion), channel_id=1, source_target_pairs={{0,64},{8,72},{16,80},{24,88},{32,96},{40,104},{48,112},{56,120},{... | collective-permute-start | bytes 835592 | tf_op jit(solution)/shard_map/ppermute | solution.py:113
  57.3 5.1 %collective-permute-start.5 = (bf16[4,2,136,128]{3,2,1,0:T(8,128)(2,1)S(1)}, bf16[4,2,136,128]{3,2,1,0:T(8,128)(2,1)S(1)}, u32[]{:S(2)}, u32[]{:S(2)}) collective-permute-start(bf16[4,2,136,128]{3,2,1,0:T(8,128)(2,1)S(1)} %pad_maximum_fusion), channel_id=1, source_target_pairs={{0,96},{8,104},{16,112},{24,120},{32,128},{40,136},{48,144},{56,15... | collective-permute-start | bytes 835592 | tf_op jit(solution)/shard_map/ppermute | solution.py:113
  62.5 0.7 constant_dynamic-update-slice_fusion.11
  63.1 0.7 constant_dynamic-update-slice_fusion.10
  63.8 0.7 constant_dynamic-update-slice_fusion.9
  64.4 9.4 %collective-permute-done.3 = bf16[4,2,136,128]{3,2,1,0:T(8,128)(2,1)S(1)} collective-permute-done((bf16[4,2,136,128]{3,2,1,0:T(8,128)(2,1)S(1)}, bf16[4,2,136,128]{3,2,1,0:T(8,128)(2,1)S(1)}, u32[]{:S(2)}, u32[]{:S(2)}) %collective-permute-start.3) | collective-permute-done | bytes 278560 | tf_op jit(solution)/shard_map/ppermute | solution.py:113
  73.8 0.8 constant_dynamic-update-slice_fusion.8
  74.7 0.0 collective-permute-done.4
  74.7 0.8 constant_dynamic-update-slice_fusion.7
  75.5 0.0 copy-start.2
  75.5 5.5 %collective-permute-done.5 = bf16[4,2,136,128]{3,2,1,0:T(8,128)(2,1)S(1)} collective-permute-done((bf16[4,2,136,128]{3,2,1,0:T(8,128)(2,1)S(1)}, bf16[4,2,136,128]{3,2,1,0:T(8,128)(2,1)S(1)}, u32[]{:S(2)}, u32[]{:S(2)}) %collective-permute-start.5) | collective-permute-done | bytes 278560 | tf_op jit(solution)/shard_map/ppermute | solution.py:113
  81.1 0.8 constant_dynamic-update-slice_fusion
  81.9 0.0 copy-done.2
  81.9 5.4 %collective-permute-start.6 = (bf16[16,2,136,128]{3,2,1,0:T(8,128)(2,1)}, bf16[16,2,136,128]{3,2,1,0:T(8,128)(2,1)}, u32[]{:S(2)}, u32[]{:S(2)}) collective-permute-start(bf16[16,2,136,128]{3,2,1,0:T(8,128)(2,1)} %get-tuple-element.35), channel_id=1, source_target_pairs={{0,128},{8,136},{16,144},{24,152},{32,160},{40,168},{48,176},{56,1... | collective-permute-start | bytes 3342344 | tf_op jit(solution)/shard_map/ppermute | solution.py:113
  87.3 0.0 copy-done.3
  87.3 0.1 copy.26
  87.4 0.1 reduce-window.9
  87.5 0.1 reduce.4
  87.6 0.1 convert_reduce_fusion
  87.7 1.9 %slice.52 = bf16[9,2,136,128]{3,2,1,0:T(8,128)(2,1)} slice(bf16[12,2,136,128]{3,2,1,0:T(8,128)(2,1)} %copy-done.2), slice={[0:9], [0:2], [0:136], [0:128]} | slice | bytes 1253376 | tf_op jit(solution)/shard_map/slice | solution.py:123
  89.7 1.9 %collective-permute-start.7 = (bf16[9,2,136,128]{3,2,1,0:T(8,128)(2,1)}, bf16[9,2,136,128]{3,2,1,0:T(8,128)(2,1)}, u32[]{:S(2)}, u32[]{:S(2)}) collective-permute-start(bf16[9,2,136,128]{3,2,1,0:T(8,128)(2,1)} %slice.52), channel_id=1, source_target_pairs={{0,256},{8,264},{16,272},{24,280},{32,288},{40,296},{48,304},{56,3... | collective-permute-start | bytes 1880072 | tf_op jit(solution)/shard_map/ppermute | solution.py:113
  91.6 1.2 gather_fusion
  93.0 0.6 pad_add_fusion.info_ref
  93.6 0.0 copy-done
  93.6 0.8 copy_bitcast_fusion
  94.3 30.2 %collective-permute-done.6 = bf16[16,2,136,128]{3,2,1,0:T(8,128)(2,1)} collective-permute-done((bf16[16,2,136,128]{3,2,1,0:T(8,128)(2,1)}, bf16[16,2,136,128]{3,2,1,0:T(8,128)(2,1)}, u32[]{:S(2)}, u32[]{:S(2)}) %collective-permute-start.6) | collective-permute-done | bytes 1114144 | tf_op jit(solution)/shard_map/ppermute | solution.py:113
  124.5 1.4 constant_dynamic-update-slice_fusion.15
  125.9 0.0 collective-permute-done.7
  125.9 1.2 constant_dynamic-update-slice_fusion.14
  127.1 0.0 copy-start.1
  127.1 0.8 broadcast_in_dim.26.low_ref
  128.0 0.8 copy-done.1
  128.7 33.4 %shard_map.73 = bf16[128,1024]{1,0:T(8,128)(2,1)} custom-call(s32[2]{0:T(128)} %pad_add_fusion.info_ref, bf16[1024,128]{1,0:T(8,128)(2,1)} %bitcast.47, bf16[42,2,136,128]{3,2,1,0:T(8,128)(2,1)} %copy-done.1, s32[128,128]{1,0:T(8,128)} %broadcast_in_dim.26.low_ref, f32[1,128]{1,0:T(1,128)} %bitcast.58), custom_call_target="tpu_custom_call" | custom-call | tf_op jit(solution)/shard_map/pallas_call | solution.py:186
  (9 shorter events, 0.1 us)
Async XLA Ops:
  0.0 93.6 %copy-start = (bf16[128,1024]{1,0:T(8,128)(2,1)S(1)}, bf16[128,1024]{1,0:T(8,128)(2,1)}, u32[]{:S(2)}) copy-start(bf16[128,1024]{1,0:T(8,128)(2,1)} %param.11) | copy-start | bytes 786436
  0.0 87.3 %copy-start.3 = (s32[64]{0:T(128)S(1)}, s32[64]{0:T(128)}, u32[]{:S(2)}) copy-start(s32[64]{0:T(128)} %param.17) | copy-start | bytes 772
  1.4 15.0 %all-to-all-start = ((bf16[16,8,128]{2,0,1:T(8,128)(2,1)}), bf16[16,8,128]{2,0,1:T(8,128)(2,1)S(1)}, u32[]{:S(2)}, u32[]{:S(2)}) async-start(bf16[16,8,128]{2,0,1:T(8,128)(2,1)} %copy_bitcast_fusion.2), calls=%async_computation | async-start | bytes 65536 | tf_op jit(solution)/shard_map/all_to_all | solution.py:201
  16.5 11.2 %all-to-all-start.1 = ((bf16[16,8,128]{2,0,1:T(8,128)(2,1)}), bf16[16,8,128]{2,0,1:T(8,128)(2,1)S(1)}, u32[]{:S(2)}, u32[]{:S(2)}) async-start(bf16[16,8,128]{2,0,1:T(8,128)(2,1)} %copy_bitcast_fusion.1), calls=%async_computation.1 | async-start | bytes 65536 | tf_op jit(solution)/shard_map/all_to_all | solution.py:202
  27.7 14.4 %collective-permute-start = (bf16[1,2,136,128]{3,2,1,0:T(8,128)(2,1)S(1)}, bf16[1,2,136,128]{3,2,1,0:T(8,128)(2,1)S(1)}, u32[]{:S(2)}, u32[]{:S(2)}) collective-permute-start(bf16[1,2,136,128]{3,2,1,0:T(8,128)(2,1)S(1)} %maximum_bitcast_fusion), channel_id=1, source_target_pairs={{0,8},{8,16},{16,24},{24,32},{32,40},{40,48},{48,56},{56,64},{64,7... | collective-permute-start | bytes 208904 | tf_op jit(solution)/shard_map/ppermute | solution.py:113
  30.3 14.2 %collective-permute-start.1 = (bf16[1,2,136,128]{3,2,1,0:T(8,128)(2,1)S(1)}, bf16[1,2,136,128]{3,2,1,0:T(8,128)(2,1)S(1)}, u32[]{:S(2)}, u32[]{:S(2)}) collective-permute-start(bf16[1,2,136,128]{3,2,1,0:T(8,128)(2,1)S(1)} %maximum_bitcast_fusion), channel_id=1, source_target_pairs={{0,16},{8,24},{16,32},{24,40},{32,48},{40,56},{48,64},{56,72},{64,... | collective-permute-start | bytes 208904 | tf_op jit(solution)/shard_map/ppermute | solution.py:113
  34.6 13.5 %collective-permute-start.2 = (bf16[1,2,136,128]{3,2,1,0:T(8,128)(2,1)S(1)}, bf16[1,2,136,128]{3,2,1,0:T(8,128)(2,1)S(1)}, u32[]{:S(2)}, u32[]{:S(2)}) collective-permute-start(bf16[1,2,136,128]{3,2,1,0:T(8,128)(2,1)S(1)} %maximum_bitcast_fusion), channel_id=1, source_target_pairs={{0,24},{8,32},{16,40},{24,48},{32,56},{40,64},{48,72},{56,80},{64,... | collective-permute-start | bytes 208904 | tf_op jit(solution)/shard_map/ppermute | solution.py:113
  48.1 25.8 %collective-permute-start.3 = (bf16[4,2,136,128]{3,2,1,0:T(8,128)(2,1)S(1)}, bf16[4,2,136,128]{3,2,1,0:T(8,128)(2,1)S(1)}, u32[]{:S(2)}, u32[]{:S(2)}) collective-permute-start(bf16[4,2,136,128]{3,2,1,0:T(8,128)(2,1)S(1)} %pad_maximum_fusion), channel_id=1, source_target_pairs={{0,32},{8,40},{16,48},{24,56},{32,64},{40,72},{48,80},{56,88},{64,... | collective-permute-start | bytes 835592 | tf_op jit(solution)/shard_map/ppermute | solution.py:113
  50.0 24.7 %collective-permute-start.4 = (bf16[4,2,136,128]{3,2,1,0:T(8,128)(2,1)S(1)}, bf16[4,2,136,128]{3,2,1,0:T(8,128)(2,1)S(1)}, u32[]{:S(2)}, u32[]{:S(2)}) collective-permute-start(bf16[4,2,136,128]{3,2,1,0:T(8,128)(2,1)S(1)} %pad_maximum_fusion), channel_id=1, source_target_pairs={{0,64},{8,72},{16,80},{24,88},{32,96},{40,104},{48,112},{56,120},{... | collective-permute-start | bytes 835592 | tf_op jit(solution)/shard_map/ppermute | solution.py:113
  57.3 23.7 %collective-permute-start.5 = (bf16[4,2,136,128]{3,2,1,0:T(8,128)(2,1)S(1)}, bf16[4,2,136,128]{3,2,1,0:T(8,128)(2,1)S(1)}, u32[]{:S(2)}, u32[]{:S(2)}) collective-permute-start(bf16[4,2,136,128]{3,2,1,0:T(8,128)(2,1)S(1)} %pad_maximum_fusion), channel_id=1, source_target_pairs={{0,96},{8,104},{16,112},{24,120},{32,128},{40,136},{48,144},{56,15... | collective-permute-start | bytes 835592 | tf_op jit(solution)/shard_map/ppermute | solution.py:113
  75.5 6.4 %copy-start.2 = (bf16[12,2,136,128]{3,2,1,0:T(8,128)(2,1)}, bf16[12,2,136,128]{3,2,1,0:T(8,128)(2,1)S(1)}, u32[]{:S(2)}) copy-start(bf16[12,2,136,128]{3,2,1,0:T(8,128)(2,1)S(1)} %get-tuple-element.29) | copy-start | bytes 2506756
  81.9 42.6 %collective-permute-start.6 = (bf16[16,2,136,128]{3,2,1,0:T(8,128)(2,1)}, bf16[16,2,136,128]{3,2,1,0:T(8,128)(2,1)}, u32[]{:S(2)}, u32[]{:S(2)}) collective-permute-start(bf16[16,2,136,128]{3,2,1,0:T(8,128)(2,1)} %get-tuple-element.35), channel_id=1, source_target_pairs={{0,128},{8,136},{16,144},{24,152},{32,160},{40,168},{48,176},{56,1... | collective-permute-start | bytes 3342344 | tf_op jit(solution)/shard_map/ppermute | solution.py:113
  89.7 36.3 %collective-permute-start.7 = (bf16[9,2,136,128]{3,2,1,0:T(8,128)(2,1)}, bf16[9,2,136,128]{3,2,1,0:T(8,128)(2,1)}, u32[]{:S(2)}, u32[]{:S(2)}) collective-permute-start(bf16[9,2,136,128]{3,2,1,0:T(8,128)(2,1)} %slice.52), channel_id=1, source_target_pairs={{0,256},{8,264},{16,272},{24,280},{32,288},{40,296},{48,304},{56,3... | collective-permute-start | bytes 1880072 | tf_op jit(solution)/shard_map/ppermute | solution.py:113
  127.1 1.6 copy-start.1

commit v4 on v3

v4 whole, which is shorter than its diff:
```python
import functools
import math

import jax
import jax.numpy as jnp
from jax import lax
from jax.experimental import pallas as pl
from jax.experimental.pallas import tpu as pltpu
from jax.sharding import PartitionSpec as P

QH = 64
KVH = 8
HD = 128
BLK = 64
MOST = 5120

NEG = -1e30


def doc_index(positions, starts):
    return jnp.sum((starts[None, :] <= positions[:, None]).astype(jnp.int32), axis=1) - 1


def shift_from(x, offset, count):
    pairs = [(i, (i + offset) % count) for i in range(count)]
    return lax.ppermute(x, "seq", pairs)


def gather_stages(packet, count, depth):
    held = packet[None]
    stages = [held]
    for width, shifts in ((1, (1, 2, 3)), (4, (4, 8, 12)), (16, (16, 32))):
        parts = []
        for offset in shifts:
            need = min(width, depth - offset)
            if need > 0:
                parts.append(shift_from(held[:need], offset, count))
        stages.append(parts)
        held = jnp.concatenate([held] + parts, axis=0)
    return stages


def attention_kernel(first, last, offset, *refs):
    info_ref, query_ref, window_ref, low_ref, mean_ref = refs[:5]
    rest = refs[5:]
    if not first:
        max_in, sum_in, acc_in = rest[:3]
        rest = rest[3:]
    if last:
        out_ref = rest[0]
        rest = rest[1:]
    else:
        max_out, sum_out, acc_out = rest[:3]
        rest = rest[3:]
    max_ref, sum_ref, acc_ref = rest
    group_size, rows, _ = acc_ref.shape
    inv_scale = 1.0 / math.sqrt(HD)
    seq_index = info_ref[0]
    pairs = info_ref[1]
    if first:
        max_ref[...] = jnp.full(max_ref.shape, NEG, jnp.float32)
        sum_ref[...] = jnp.zeros(sum_ref.shape, jnp.float32)
        acc_ref[...] = jnp.zeros(acc_ref.shape, jnp.float32)
    else:
        max_ref[...] = max_in[...]
        sum_ref[...] = sum_in[...]
        acc_ref[...] = acc_in[...]
    query_pos = seq_index * rows + lax.broadcasted_iota(jnp.int32, (rows, rows), 0)
    low = low_ref[...]
    lane = lax.broadcasted_iota(jnp.int32, (rows, rows), 1)
    query_all = query_ref[...]

    def one_pair(pair, carry):
        parts = []
        for half in range(2):
            slot = 2 * pair + half
            key_pos = (seq_index - offset - slot) * rows + lane
            allowed = ((key_pos <= query_pos) & (key_pos >= low))[None]
            key_t = window_ref[slot, 0, :HD, :]
            key_scale = window_ref[slot, 0, HD:HD + 1, :].astype(jnp.float32) * inv_scale
            value_scale = window_ref[slot, 1, rows:rows + 1, :].astype(jnp.float32)
            scores = jnp.dot(query_all, key_t, preferred_element_type=jnp.float32)
            scores = scores.reshape(group_size, rows, rows) * key_scale[None]
            scores = jnp.where(allowed, scores, NEG)
            parts.append((scores, allowed, value_scale[None], slot))
        run_max = max_ref[...][:, :, :1]
        new_max = run_max
        for scores, _, _, _ in parts:
            new_max = jnp.maximum(new_max, jnp.max(scores, axis=2, keepdims=True))
        factor = jnp.exp(run_max - new_max)
        run_sum = sum_ref[...][:, :, :1] * factor
        acc = acc_ref[...] * factor
        for scores, allowed, value_scale, slot in parts:
            weights = jnp.where(allowed, jnp.exp(scores - new_max), 0.0)
            run_sum = run_sum + jnp.sum(weights, axis=2, keepdims=True)
            scaled = (weights * value_scale).astype(jnp.bfloat16).reshape(group_size * rows, rows)
            value_tile = window_ref[slot, 1, :rows, :]
            mixed = jnp.dot(scaled, value_tile, preferred_element_type=jnp.float32)
            acc = acc + mixed.reshape(group_size, rows, HD)
        acc_ref[...] = acc
        max_ref[...] = jnp.broadcast_to(new_max, max_ref.shape)
        sum_ref[...] = jnp.broadcast_to(run_sum, sum_ref.shape)
        return carry

    lax.fori_loop(0, pairs, one_pair, 0)
    if last:
        result = acc_ref[...] / sum_ref[...] + mean_ref[...][None]
        for g in range(group_size):
            out_ref[:, g * HD:(g + 1) * HD] = result[g].astype(jnp.bfloat16)
    else:
        max_out[...] = max_ref[...]
        sum_out[...] = sum_ref[...]
        acc_out[...] = acc_ref[...]


def attend_part(info, query_all, window, low, mean, state, offset, last, width):
    group_size = query_all.shape[0] // HD
    rows = low.shape[0]
    full = lambda shape: pl.BlockSpec(shape, lambda i, info: (0,) * len(shape))
    state_shape = jax.ShapeDtypeStruct((group_size, rows, HD), jnp.float32)
    operands = [query_all, window, low, mean] + ([] if state is None else list(state))
    if last:
        out_shape = jax.ShapeDtypeStruct((rows, width), jnp.bfloat16)
        out_specs = full((rows, width))
    else:
        out_shape = (state_shape,) * 3
        out_specs = (full(state_shape.shape),) * 3
    kernel = functools.partial(attention_kernel, state is None, last, offset)
    return pl.pallas_call(
        kernel,
        out_shape=out_shape,
        grid_spec=pltpu.PrefetchScalarGridSpec(
            num_scalar_prefetch=1,
            grid=(1,),
            in_specs=[full(x.shape) for x in operands],
            out_specs=out_specs,
            scratch_shapes=[pltpu.VMEM((group_size, rows, HD), jnp.float32)] * 3,
        ),
    )(info, *operands)


def shards(queries, key_tokens, value_tokens, key_scales, value_scales, value_means, doc_lengths):
    heads = lax.axis_size("head")
    both = jnp.stack([key_tokens, value_tokens], axis=1)
    both = both.reshape(both.shape[0], 2, heads, -1)
    both = lax.all_to_all(both, "head", split_axis=2, concat_axis=0, tiled=True)
    local_keys = both[:, 0, 0]
    local_values = both[:, 1, 0]
    row_count = local_keys.shape[0]
    group_size = QH // KVH
    seq_count = lax.axis_size("seq")
    seq_index = lax.axis_index("seq")
    starts = jnp.cumsum(doc_lengths) - doc_lengths
    depth = min(seq_count, -(-(MOST - 1) // row_count) + 1)
    pad_rows = 8
    key_scale_row = jnp.repeat(key_scales.reshape(-1), BLK)
    value_scale_row = jnp.repeat(value_scales.reshape(-1), BLK)
    scale_rows = jnp.zeros((2, pad_rows, row_count), jnp.bfloat16)
    scale_rows = scale_rows.at[0, 0].set(key_scale_row).at[1, 0].set(value_scale_row)
    packet = jnp.concatenate([jnp.stack([local_keys.T, local_values]), scale_rows], axis=1)
    stages = gather_stages(packet, seq_count, depth)
    own_pos = seq_index * row_count + jnp.arange(row_count, dtype=jnp.int32)
    low = starts[doc_index(own_pos, starts)]
    used = jnp.clip(seq_index - low[0] // row_count + 1, 1, depth).astype(jnp.int32)
    low_tile = jnp.broadcast_to(low[:, None], (row_count, row_count)).astype(jnp.int32)
    mean = value_means.reshape(1, HD)
    query_all = queries.reshape(row_count, group_size, HD).transpose(1, 0, 2).reshape(-1, HD)
    chunks = [
        jnp.concatenate([stages[0]] + stages[1], axis=0),
        jnp.concatenate(stages[2], axis=0),
        jnp.concatenate(stages[3], axis=0),
    ]
    state = None
    offset = 0
    for index, chunk in enumerate(chunks):
        slots = chunk.shape[0]
        if slots % 2:
            chunk = jnp.concatenate([chunk, jnp.zeros((1,) + chunk.shape[1:], chunk.dtype)])
        pairs = jnp.clip((used - offset + 1) // 2, 0, chunk.shape[0] // 2).astype(jnp.int32)
        info = jnp.stack([seq_index.astype(jnp.int32), pairs])
        last = index == len(chunks) - 1
        state = attend_part(
            info, query_all, chunk, low_tile, mean, state, offset, last, queries.shape[1]
        )
        offset += slots
    return state


def solution(mesh):
    in_specs = (
        P("seq", "head"),
        P(("seq", "head"), None),
        P(("seq", "head"), None),
        P("seq", "head"),
        P("seq", "head"),
        P("head"),
        P(),
    )
    out_specs = P("seq", "head")
    return jax.shard_map(shards, mesh=mesh, in_specs=in_specs, out_specs=out_specs, check_vma=False)
```

time: 163 us -> 138 us (0.85)
  waiting for transfers between devices: 63.5 us -> 34.2 us
  Pallas kernels: 33.4 us -> 40.3 us
  other arithmetic: 3.12 us -> 7.62 us
  local copies, waits for them, and re-layouts: 15.9 us -> 11.5 us
  starting transfers between devices: 45.8 us -> 43 us
    ppermute x8, waiting for transfers between devices: 51.1 us -> 29.5 us  [shift_from(): return lax.ppermute(x, 'seq', pairs)]
    all_to_all x2 -> x1, waiting for transfers between devices: 12.4 us -> 4.7 us  [shards(): both = lax.all_to_all(both, 'head', split_axis=2, concat_axis=0, tiled=True)]
    pallas_call x1 -> x3, Pallas kernels: 33.4 us -> 40.3 us  [attend_part(): pl.pallas_call(kernel, out_shape=out_shape, grid_spec=pltpu.PrefetchScala...]
    all_to_all x2 -> x1, starting transfers between devices: 10.4 us -> 7.1 us  [shards(): both = lax.all_to_all(both, 'head', split_axis=2, concat_axis=0, tiled=True)]
    all_to_all x3 -> x1, local copies, waits for them, and re-layouts: 2.91 us -> 0.01 us  [shards(): both = lax.all_to_all(both, 'head', split_axis=2, concat_axis=0, tiled=True)]
    concatenate x1 -> x3, other arithmetic: 0.04 us -> 2.55 us  [the longest x1 1.46 us: shards(): jnp.concatenate([chunk, jnp.zeros((1,) + chunk.shape[1:], chunk.dtype)])]
    unnamed x14 -> x13, local copies, waits for them, and re-layouts: 6.14 us -> 5.07 us
  transfers between devices with their start and end apart: 10 -> 9, of which waited for: 7 -> 6; matrix products, arithmetic and copies ran while one was open for 9% -> 11% of each run, Pallas kernels for 0% -> 14%
where the time goes in v4:
time: 138 us; the launch traced here: 137 us
  starting transfers between devices  43 us (31%)
  Pallas kernels  40.3 us (29%)
  waiting for transfers between devices  34.2 us (25%)
  local copies, waits for them, and re-layouts  11.5 us (8%)
  other arithmetic  7.62 us (6%)
    pallas_call x3, Pallas kernels, attend_part(): pl.pallas_call(kernel, out_shape=out_shape, grid_spec=pltpu.PrefetchScala...  40.3 us
    ppermute x8, starting transfers between devices, shift_from(): return lax.ppermute(x, 'seq', pairs)  35.9 us
    ppermute x8, waiting for transfers between devices, shift_from(): return lax.ppermute(x, 'seq', pairs)  29.5 us
    all_to_all x1, starting transfers between devices, shards(): both = lax.all_to_all(both, 'head', split_axis=2, concat_axis=0, tiled=True)  7.1 us
    unnamed x13, local copies, waits for them, and re-layouts  5.07 us
    all_to_all x1, waiting for transfers between devices, shards(): both = lax.all_to_all(both, 'head', split_axis=2, concat_axis=0, tiled=True)  4.7 us
  transfers between devices with their start and end apart: 9, of which 6 were waited for; matrix products, arithmetic and copies ran while one was open for 11% of the time, Pallas kernels for 14%

profile of v4, /device:TPU:6, one launch (start us, length us, event | category | flops | bytes accessed | tf_op | source)
XLA Modules:
  0.0 137.0 jit_solution(9474590096928180341)
XLA Ops:
  0.0 0.0 copy-start
  0.0 0.8 copy.34
  0.8 0.8 copy.33
  1.6 0.6 copy.29
  2.2 7.1 %all-to-all-start = ((bf16[16,2,8,128]{3,0,1,2:T(8,128)(2,1)}), bf16[16,2,8,128]{3,0,1,2:T(8,128)(2,1)S(1)}, u32[]{:S(2)}, u32[]{:S(2)}) async-start(bf16[16,2,8,128]{3,0,1,2:T(8,128)(2,1)} %copy.29), calls=%async_computation | async-start | bytes 131072 | tf_op jit(solution)/shard_map/all_to_all | solution.py:146
  9.3 0.7 copy.27
  10.1 0.1 reduce-window.9
  10.2 0.1 reduce.4
  10.3 0.7 sub.27
  10.9 0.8 reduce.5
  11.7 0.1 broadcast_in_dim.10
  11.8 0.1 reshape.146
  11.9 0.8 reduce.6
  12.7 0.1 broadcast_in_dim.11
  12.7 0.1 reshape.148
  12.9 4.7 %all-to-all-done = bf16[16,2,8,128]{3,0,1,2:T(8,128)(2,1)S(1)} async-done(((bf16[16,2,8,128]{3,0,1,2:T(8,128)(2,1)}), bf16[16,2,8,128]{3,0,1,2:T(8,128)(2,1)S(1)}, u32[]{:S(2)}, u32[]{:S(2)}) %all-to-all-start) | async-done | bytes 65568 | tf_op jit(solution)/shard_map/all_to_all | solution.py:146
  17.6 0.1 copy.31
  17.7 2.8 %collective-permute-start = (bf16[1,2,136,128]{3,2,1,0:T(8,128)(2,1)S(1)}, bf16[1,2,136,128]{3,2,1,0:T(8,128)(2,1)S(1)}, u32[]{:S(2)}, u32[]{:S(2)}) collective-permute-start(bf16[1,2,136,128]{3,2,1,0:T(8,128)(2,1)S(1)} %maximum_bitcast_fusion), channel_id=1, source_target_pairs={{0,8},{8,16},{16,24},{24,32},{32,40},{40,48},{48,56},{56,64},{64,7... | collective-permute-start | bytes 208904 | tf_op jit(solution)/shard_map/ppermute | solution.py:26
  20.6 4.3 %collective-permute-start.1 = (bf16[1,2,136,128]{3,2,1,0:T(8,128)(2,1)S(1)}, bf16[1,2,136,128]{3,2,1,0:T(8,128)(2,1)S(1)}, u32[]{:S(2)}, u32[]{:S(2)}) collective-permute-start(bf16[1,2,136,128]{3,2,1,0:T(8,128)(2,1)S(1)} %maximum_bitcast_fusion), channel_id=1, source_target_pairs={{0,16},{8,24},{16,32},{24,40},{32,48},{40,56},{48,64},{56,72},{64,... | collective-permute-start | bytes 208904 | tf_op jit(solution)/shard_map/ppermute | solution.py:26
  24.8 6.6 %collective-permute-start.2 = (bf16[1,2,136,128]{3,2,1,0:T(8,128)(2,1)S(1)}, bf16[1,2,136,128]{3,2,1,0:T(8,128)(2,1)S(1)}, u32[]{:S(2)}, u32[]{:S(2)}) collective-permute-start(bf16[1,2,136,128]{3,2,1,0:T(8,128)(2,1)S(1)} %maximum_bitcast_fusion), channel_id=1, source_target_pairs={{0,24},{8,32},{16,40},{24,48},{32,56},{40,64},{48,72},{56,80},{64,... | collective-permute-start | bytes 208904 | tf_op jit(solution)/shard_map/ppermute | solution.py:26
  31.5 0.6 constant_dynamic-update-slice_fusion.6
  32.1 0.0 collective-permute-done
  32.1 2.7 %collective-permute-done.1 = bf16[1,2,136,128]{3,2,1,0:T(8,128)(2,1)S(1)} collective-permute-done((bf16[1,2,136,128]{3,2,1,0:T(8,128)(2,1)S(1)}, bf16[1,2,136,128]{3,2,1,0:T(8,128)(2,1)S(1)}, u32[]{:S(2)}, u32[]{:S(2)}) %collective-permute-start.1) | collective-permute-done | bytes 69664 | tf_op jit(solution)/shard_map/ppermute | solution.py:26
  34.8 3.3 %collective-permute-done.2 = bf16[1,2,136,128]{3,2,1,0:T(8,128)(2,1)S(1)} collective-permute-done((bf16[1,2,136,128]{3,2,1,0:T(8,128)(2,1)S(1)}, bf16[1,2,136,128]{3,2,1,0:T(8,128)(2,1)S(1)}, u32[]{:S(2)}, u32[]{:S(2)}) %collective-permute-start.2) | collective-permute-done | bytes 69664 | tf_op jit(solution)/shard_map/ppermute | solution.py:26
  38.2 0.0 copy-start.1
  38.2 1.9 %collective-permute-start.3 = (bf16[4,2,136,128]{3,2,1,0:T(8,128)(2,1)S(1)}, bf16[4,2,136,128]{3,2,1,0:T(8,128)(2,1)S(1)}, u32[]{:S(2)}, u32[]{:S(2)}) collective-permute-start(bf16[4,2,136,128]{3,2,1,0:T(8,128)(2,1)S(1)} %pad_maximum_fusion.1.refs_2_), channel_id=1, source_target_pairs={{0,32},{8,40},{16,48},{24,56},{32,64},{40,72},{48,80},{56,88},{64,... | collective-permute-start | bytes 835592 | tf_op jit(solution)/shard_map/ppermute | solution.py:26
  40.1 7.3 %collective-permute-start.4 = (bf16[4,2,136,128]{3,2,1,0:T(8,128)(2,1)S(1)}, bf16[4,2,136,128]{3,2,1,0:T(8,128)(2,1)S(1)}, u32[]{:S(2)}, u32[]{:S(2)}) collective-permute-start(bf16[4,2,136,128]{3,2,1,0:T(8,128)(2,1)S(1)} %pad_maximum_fusion.1.refs_2_), channel_id=1, source_target_pairs={{0,64},{8,72},{16,80},{24,88},{32,96},{40,104},{48,112},{56,120},{... | collective-permute-start | bytes 835592 | tf_op jit(solution)/shard_map/ppermute | solution.py:26
  47.5 5.3 %collective-permute-start.5 = (bf16[4,2,136,128]{3,2,1,0:T(8,128)(2,1)S(1)}, bf16[4,2,136,128]{3,2,1,0:T(8,128)(2,1)S(1)}, u32[]{:S(2)}, u32[]{:S(2)}) collective-permute-start(bf16[4,2,136,128]{3,2,1,0:T(8,128)(2,1)S(1)} %pad_maximum_fusion.1.refs_2_), channel_id=1, source_target_pairs={{0,96},{8,104},{16,112},{24,120},{32,128},{40,136},{48,144},{56,15... | collective-permute-start | bytes 835592 | tf_op jit(solution)/shard_map/ppermute | solution.py:26
  52.8 0.6 constant_dynamic-update-slice_fusion.5
  53.4 0.6 constant_dynamic-update-slice_fusion.4
  54.1 0.6 constant_dynamic-update-slice_fusion.3
  54.7 9.5 %collective-permute-done.3 = bf16[4,2,136,128]{3,2,1,0:T(8,128)(2,1)S(1)} collective-permute-done((bf16[4,2,136,128]{3,2,1,0:T(8,128)(2,1)S(1)}, bf16[4,2,136,128]{3,2,1,0:T(8,128)(2,1)S(1)}, u32[]{:S(2)}, u32[]{:S(2)}) %collective-permute-start.3) | collective-permute-done | bytes 278560 | tf_op jit(solution)/shard_map/ppermute | solution.py:26
  64.2 0.8 constant_dynamic-update-slice_fusion.2
  65.0 0.0 collective-permute-done.4
  65.0 0.8 constant_dynamic-update-slice_fusion.1
  65.7 0.0 copy-done.1
  65.7 0.0 copy-start.2
  65.7 4.8 %collective-permute-done.5 = bf16[4,2,136,128]{3,2,1,0:T(8,128)(2,1)S(1)} collective-permute-done((bf16[4,2,136,128]{3,2,1,0:T(8,128)(2,1)S(1)}, bf16[4,2,136,128]{3,2,1,0:T(8,128)(2,1)S(1)}, u32[]{:S(2)}, u32[]{:S(2)}) %collective-permute-start.5) | collective-permute-done | bytes 278560 | tf_op jit(solution)/shard_map/ppermute | solution.py:26
  70.6 0.0 copy-done.2
  70.6 0.7 constant_dynamic-update-slice_fusion
  71.3 5.7 %collective-permute-start.6 = (bf16[16,2,136,128]{3,2,1,0:T(8,128)(2,1)}, bf16[16,2,136,128]{3,2,1,0:T(8,128)(2,1)S(1)}, u32[]{:S(2)}, u32[]{:S(2)}) collective-permute-start(bf16[16,2,136,128]{3,2,1,0:T(8,128)(2,1)} %constant_dynamic-update-slice_fusion), channel_id=1, source_target_pairs={{0,128},{8,136},{16,144},{24,152},{32,160},{40,168},{48,176},{56,1... | collective-permute-start | bytes 3342344 | tf_op jit(solution)/shard_map/ppermute | solution.py:26
  77.0 0.1 convert_reduce_fusion
  77.2 1.2 gather_fusion
  78.6 1.1 slice.62
  79.7 1.9 %collective-permute-start.7 = (bf16[9,2,136,128]{3,2,1,0:T(8,128)(2,1)S(1)}, bf16[9,2,136,128]{3,2,1,0:T(8,128)(2,1)S(1)}, u32[]{:S(2)}, u32[]{:S(2)}) collective-permute-start(bf16[9,2,136,128]{3,2,1,0:T(8,128)(2,1)S(1)} %slice.62), channel_id=1, source_target_pairs={{0,256},{8,264},{16,272},{24,280},{32,288},{40,296},{48,304},{56,3... | collective-permute-start | bytes 1880072 | tf_op jit(solution)/shard_map/ppermute | solution.py:26
  81.6 0.6 pad_add_fusion.refs_0_
  82.3 0.1 pad.16.clone
  82.3 0.7 pad_add_fusion.1.refs_0_
  83.0 0.6 pad_add_fusion.2.refs_0_
  83.6 0.0 copy-done
  83.6 0.8 copy_bitcast_fusion
  84.4 0.7 broadcast_in_dim.26.refs_3_
  85.1 6.2 %shard_map.73 = (f32[8,128,128]{2,1,0:T(8,128)}, f32[8,128,128]{2,1,0:T(8,128)}, f32[8,128,128]{2,1,0:T(8,128)}) custom-call(s32[2]{0:T(128)} %pad_add_fusion.2.refs_0_, bf16[1024,128]{1,0:T(8,128)(2,1)} %bitcast.49, bf16[4,2,136,128]{3,2,1,0:T(8,128)(2,1)} %copy-done.1, s32[128,128]{1,0:T(8,128)} %broadcast_in_dim.26.refs_3_, f32[1,128]{1,0:T(1,128)} %bitcast.58), custom_call_target="tpu_custom_call" | custom-call | tf_op jit(solution)/shard_map/pallas_call | solution.py:129
  91.3 1.1 pad_maximum_fusion.refs_2_
  92.3 13.2 %shard_map.74 = (f32[8,128,128]{2,1,0:T(8,128)}, f32[8,128,128]{2,1,0:T(8,128)}, f32[8,128,128]{2,1,0:T(8,128)}) custom-call(s32[2]{0:T(128)} %pad_add_fusion.1.refs_0_, bf16[1024,128]{1,0:T(8,128)(2,1)} %bitcast.50, bf16[12,2,136,128]{3,2,1,0:T(8,128)(2,1)} %pad_maximum_fusion.refs_2_, s32[128,128]{1,0:T(8,128)} %broadcast_in_dim.26.refs_3_, ...), custom_call_target="tpu_custom_call" | custom-call | tf_op jit(solution)/shard_map/pallas_call | solution.py:129
  105.5 0.0 collective-permute-done.7
  105.5 9.1 %collective-permute-done.6 = bf16[16,2,136,128]{3,2,1,0:T(8,128)(2,1)S(1)} collective-permute-done((bf16[16,2,136,128]{3,2,1,0:T(8,128)(2,1)}, bf16[16,2,136,128]{3,2,1,0:T(8,128)(2,1)S(1)}, u32[]{:S(2)}, u32[]{:S(2)}) %collective-permute-start.6) | collective-permute-done | bytes 1114144 | tf_op jit(solution)/shard_map/ppermute | solution.py:26
  114.6 1.5 %maximum_maximum_fusion.refs_2_ = bf16[26,2,136,128]{3,2,1,0:T(8,128)(2,1)} fusion(bf16[9,2,136,128]{3,2,1,0:T(8,128)(2,1)S(1)} %collective-permute-done.7, bf16[16,2,136,128]{3,2,1,0:T(8,128)(2,1)S(1)} %collective-permute-done.6, bf16[26]{0:T(256)(128)(2,1)S(1)} %pad.16.clone), kind=kLoop, calls=%fused_computation.1 | loop fusion | flops 1810432 | bytes 3551284 | tf_op jit(solution)/shard_map/concatenate | solution.py:178
  116.1 20.9 %shard_map.75 = bf16[128,1024]{1,0:T(8,128)(2,1)} custom-call(s32[2]{0:T(128)} %pad_add_fusion.refs_0_, bf16[1024,128]{1,0:T(8,128)(2,1)} %bitcast.51, bf16[26,2,136,128]{3,2,1,0:T(8,128)(2,1)} %maximum_maximum_fusion.refs_2_, s32[128,128]{1,0:T(8,128)} %broadcast_in_dim.26.refs_3_, f32[1,128]{1,0:T(1,128)} %bitcast.60, ...), custom_call_target="tpu_custom_call" | custom-call | tf_op jit(solution)/shard_map/pallas_call | solution.py:129
  (10 shorter events, 0.1 us)
Async XLA Ops:
  0.0 83.6 %copy-start = (bf16[128,1024]{1,0:T(8,128)(2,1)S(1)}, bf16[128,1024]{1,0:T(8,128)(2,1)}, u32[]{:S(2)}) copy-start(bf16[128,1024]{1,0:T(8,128)(2,1)} %param.11) | copy-start | bytes 786436
  2.2 15.3 %all-to-all-start = ((bf16[16,2,8,128]{3,0,1,2:T(8,128)(2,1)}), bf16[16,2,8,128]{3,0,1,2:T(8,128)(2,1)S(1)}, u32[]{:S(2)}, u32[]{:S(2)}) async-start(bf16[16,2,8,128]{3,0,1,2:T(8,128)(2,1)} %copy.29), calls=%async_computation | async-start | bytes 131072 | tf_op jit(solution)/shard_map/all_to_all | solution.py:146
  17.7 14.4 %collective-permute-start = (bf16[1,2,136,128]{3,2,1,0:T(8,128)(2,1)S(1)}, bf16[1,2,136,128]{3,2,1,0:T(8,128)(2,1)S(1)}, u32[]{:S(2)}, u32[]{:S(2)}) collective-permute-start(bf16[1,2,136,128]{3,2,1,0:T(8,128)(2,1)S(1)} %maximum_bitcast_fusion), channel_id=1, source_target_pairs={{0,8},{8,16},{16,24},{24,32},{32,40},{40,48},{48,56},{56,64},{64,7... | collective-permute-start | bytes 208904 | tf_op jit(solution)/shard_map/ppermute | solution.py:26
  20.6 14.2 %collective-permute-start.1 = (bf16[1,2,136,128]{3,2,1,0:T(8,128)(2,1)S(1)}, bf16[1,2,136,128]{3,2,1,0:T(8,128)(2,1)S(1)}, u32[]{:S(2)}, u32[]{:S(2)}) collective-permute-start(bf16[1,2,136,128]{3,2,1,0:T(8,128)(2,1)S(1)} %maximum_bitcast_fusion), channel_id=1, source_target_pairs={{0,16},{8,24},{16,32},{24,40},{32,48},{40,56},{48,64},{56,72},{64,... | collective-permute-start | bytes 208904 | tf_op jit(solution)/shard_map/ppermute | solution.py:26
  24.8 13.3 %collective-permute-start.2 = (bf16[1,2,136,128]{3,2,1,0:T(8,128)(2,1)S(1)}, bf16[1,2,136,128]{3,2,1,0:T(8,128)(2,1)S(1)}, u32[]{:S(2)}, u32[]{:S(2)}) collective-permute-start(bf16[1,2,136,128]{3,2,1,0:T(8,128)(2,1)S(1)} %maximum_bitcast_fusion), channel_id=1, source_target_pairs={{0,24},{8,32},{16,40},{24,48},{32,56},{40,64},{48,72},{56,80},{64,... | collective-permute-start | bytes 208904 | tf_op jit(solution)/shard_map/ppermute | solution.py:26
  38.2 27.6 %copy-start.1 = (bf16[4,2,136,128]{3,2,1,0:T(8,128)(2,1)}, bf16[4,2,136,128]{3,2,1,0:T(8,128)(2,1)S(1)}, u32[]{:S(2)}) copy-start(bf16[4,2,136,128]{3,2,1,0:T(8,128)(2,1)S(1)} %pad_maximum_fusion.1.refs_2_) | copy-start | bytes 835588
  38.2 26.0 %collective-permute-start.3 = (bf16[4,2,136,128]{3,2,1,0:T(8,128)(2,1)S(1)}, bf16[4,2,136,128]{3,2,1,0:T(8,128)(2,1)S(1)}, u32[]{:S(2)}, u32[]{:S(2)}) collective-permute-start(bf16[4,2,136,128]{3,2,1,0:T(8,128)(2,1)S(1)} %pad_maximum_fusion.1.refs_2_), channel_id=1, source_target_pairs={{0,32},{8,40},{16,48},{24,56},{32,64},{40,72},{48,80},{56,88},{64,... | collective-permute-start | bytes 835592 | tf_op jit(solution)/shard_map/ppermute | solution.py:26
  40.1 24.8 %collective-permute-start.4 = (bf16[4,2,136,128]{3,2,1,0:T(8,128)(2,1)S(1)}, bf16[4,2,136,128]{3,2,1,0:T(8,128)(2,1)S(1)}, u32[]{:S(2)}, u32[]{:S(2)}) collective-permute-start(bf16[4,2,136,128]{3,2,1,0:T(8,128)(2,1)S(1)} %pad_maximum_fusion.1.refs_2_), channel_id=1, source_target_pairs={{0,64},{8,72},{16,80},{24,88},{32,96},{40,104},{48,112},{56,120},{... | collective-permute-start | bytes 835592 | tf_op jit(solution)/shard_map/ppermute | solution.py:26
  47.5 23.1 %collective-permute-start.5 = (bf16[4,2,136,128]{3,2,1,0:T(8,128)(2,1)S(1)}, bf16[4,2,136,128]{3,2,1,0:T(8,128)(2,1)S(1)}, u32[]{:S(2)}, u32[]{:S(2)}) collective-permute-start(bf16[4,2,136,128]{3,2,1,0:T(8,128)(2,1)S(1)} %pad_maximum_fusion.1.refs_2_), channel_id=1, source_target_pairs={{0,96},{8,104},{16,112},{24,120},{32,128},{40,136},{48,144},{56,15... | collective-permute-start | bytes 835592 | tf_op jit(solution)/shard_map/ppermute | solution.py:26
  65.7 4.8 %copy-start.2 = (bf16[12,2,136,128]{3,2,1,0:T(8,128)(2,1)}, bf16[12,2,136,128]{3,2,1,0:T(8,128)(2,1)S(1)}, u32[]{:S(2)}) copy-start(bf16[12,2,136,128]{3,2,1,0:T(8,128)(2,1)S(1)} %get-tuple-element.42) | copy-start | bytes 2506756
  71.3 43.3 %collective-permute-start.6 = (bf16[16,2,136,128]{3,2,1,0:T(8,128)(2,1)}, bf16[16,2,136,128]{3,2,1,0:T(8,128)(2,1)S(1)}, u32[]{:S(2)}, u32[]{:S(2)}) collective-permute-start(bf16[16,2,136,128]{3,2,1,0:T(8,128)(2,1)} %constant_dynamic-update-slice_fusion), channel_id=1, source_target_pairs={{0,128},{8,136},{16,144},{24,152},{32,160},{40,168},{48,176},{56,1... | collective-permute-start | bytes 3342344 | tf_op jit(solution)/shard_map/ppermute | solution.py:26
  79.7 25.8 %collective-permute-start.7 = (bf16[9,2,136,128]{3,2,1,0:T(8,128)(2,1)S(1)}, bf16[9,2,136,128]{3,2,1,0:T(8,128)(2,1)S(1)}, u32[]{:S(2)}, u32[]{:S(2)}) collective-permute-start(bf16[9,2,136,128]{3,2,1,0:T(8,128)(2,1)S(1)} %slice.62), channel_id=1, source_target_pairs={{0,256},{8,264},{16,272},{24,280},{32,288},{40,296},{48,304},{56,3... | collective-permute-start | bytes 1880072 | tf_op jit(solution)/shard_map/ppermute | solution.py:26

commit v5 on v4

--- a/solution.py
+++ b/solution.py
@@ -70,18 +70,22 @@
     lane = lax.broadcasted_iota(jnp.int32, (rows, rows), 1)
     query_all = query_ref[...]
 
-    def one_pair(pair, carry):
+    low_top = info_ref[2]
+
+    def fold_pair(pair, masked):
         parts = []
         for half in range(2):
             slot = 2 * pair + half
-            key_pos = (seq_index - offset - slot) * rows + lane
-            allowed = ((key_pos <= query_pos) & (key_pos >= low))[None]
             key_t = window_ref[slot, 0, :HD, :]
             key_scale = window_ref[slot, 0, HD:HD + 1, :].astype(jnp.float32) * inv_scale
             value_scale = window_ref[slot, 1, rows:rows + 1, :].astype(jnp.float32)
             scores = jnp.dot(query_all, key_t, preferred_element_type=jnp.float32)
             scores = scores.reshape(group_size, rows, rows) * key_scale[None]
-            scores = jnp.where(allowed, scores, NEG)
+            allowed = None
+            if masked:
+                key_pos = (seq_index - offset - slot) * rows + lane
+                allowed = ((key_pos <= query_pos) & (key_pos >= low))[None]
+                scores = jnp.where(allowed, scores, NEG)
             parts.append((scores, allowed, value_scale[None], slot))
         run_max = max_ref[...][:, :, :1]
         new_max = run_max
@@ -91,7 +95,9 @@
         run_sum = sum_ref[...][:, :, :1] * factor
         acc = acc_ref[...] * factor
         for scores, allowed, value_scale, slot in parts:
-            weights = jnp.where(allowed, jnp.exp(scores - new_max), 0.0)
+            weights = jnp.exp(scores - new_max)
+            if masked:
+                weights = jnp.where(allowed, weights, 0.0)
             run_sum = run_sum + jnp.sum(weights, axis=2, keepdims=True)
             scaled = (weights * value_scale).astype(jnp.bfloat16).reshape(group_size * rows, rows)
             value_tile = window_ref[slot, 1, :rows, :]
@@ -100,6 +106,11 @@
         acc_ref[...] = acc
         max_ref[...] = jnp.broadcast_to(new_max, max_ref.shape)
         sum_ref[...] = jnp.broadcast_to(run_sum, sum_ref.shape)
+
+    def one_pair(pair, carry):
+        nearest = offset + 2 * pair
+        inside = (nearest >= 1) & ((seq_index - nearest - 1) * rows >= low_top)
+        lax.cond(inside, lambda: fold_pair(pair, False), lambda: fold_pair(pair, True))
         return carry
 
     lax.fori_loop(0, pairs, one_pair, 0)
@@ -177,7 +188,7 @@
         if slots % 2:
             chunk = jnp.concatenate([chunk, jnp.zeros((1,) + chunk.shape[1:], chunk.dtype)])
         pairs = jnp.clip((used - offset + 1) // 2, 0, chunk.shape[0] // 2).astype(jnp.int32)
-        info = jnp.stack([seq_index.astype(jnp.int32), pairs])
+        info = jnp.stack([seq_index.astype(jnp.int32), pairs, low[-1].astype(jnp.int32)])
         last = index == len(chunks) - 1
         state = attend_part(
             info, query_all, chunk, low_tile, mean, state, offset, last, queries.shape[1]

time: 138 us -> 141 us (1.022)
  the two profiles are of different devices: /device:TPU:6 before, /device:TPU:134 now
where the time goes in v5:
time: 141 us; the launch traced here: 140 us
  Pallas kernels  43.4 us (31%)
  starting transfers between devices  42.5 us (30%)
  waiting for transfers between devices  29.7 us (21%)
  local copies, waits for them, and re-layouts  12.2 us (9%)
  other arithmetic  9.59 us (7%)
  between operations  2.95 us (2%)
    pallas_call x3, Pallas kernels, attend_part(): pl.pallas_call(kernel, out_shape=out_shape, grid_spec=pltpu.PrefetchScala...  43.4 us
    ppermute x8, starting transfers between devices, shift_from(): return lax.ppermute(x, 'seq', pairs)  35.3 us
    ppermute x8, waiting for transfers between devices, shift_from(): return lax.ppermute(x, 'seq', pairs)  25.1 us
    all_to_all x1, starting transfers between devices, shards(): both = lax.all_to_all(both, 'head', split_axis=2, concat_axis=0, tiled=True)  7.1 us
    unnamed x13, local copies, waits for them, and re-layouts  5.08 us
    all_to_all x1, waiting for transfers between devices, shards(): both = lax.all_to_all(both, 'head', split_axis=2, concat_axis=0, tiled=True)  4.6 us
    another operation x3, other arithmetic, shards(): jnp.stack([seq_index.astype(jnp.int32), pairs, low[-1].astype(jnp.int32)])  3.85 us
  transfers between devices with their start and end apart: 9, of which 6 were waited for; matrix products, arithmetic and copies ran while one was open for 12% of the time, Pallas kernels for 14%

profile of v5, /device:TPU:134, one launch (start us, length us, event | category | flops | bytes accessed | tf_op | source)
XLA Modules:
  0.0 140.3 jit_solution(1877241590583081690)
XLA Ops:
  0.0 0.0 copy-start
  0.0 0.8 copy.34
  0.8 0.8 copy.33
  1.6 0.6 copy.29
  2.2 7.1 %all-to-all-start = ((bf16[16,2,8,128]{3,0,1,2:T(8,128)(2,1)}), bf16[16,2,8,128]{3,0,1,2:T(8,128)(2,1)S(1)}, u32[]{:S(2)}, u32[]{:S(2)}) async-start(bf16[16,2,8,128]{3,0,1,2:T(8,128)(2,1)} %copy.29), calls=%async_computation | async-start | bytes 131072 | tf_op jit(solution)/shard_map/all_to_all | solution.py:157
  9.3 0.7 copy.27
  10.1 0.1 reduce-window.9
  10.2 0.1 reduce.4
  10.3 0.7 sub.27
  11.0 0.8 reduce.5
  11.7 0.1 broadcast_in_dim.10
  11.8 0.1 reshape.146
  11.9 0.8 reduce.6
  12.7 0.1 broadcast_in_dim.11
  12.7 0.1 reshape.148
  12.9 0.1 convert_reduce_fusion
  13.0 4.6 %all-to-all-done = bf16[16,2,8,128]{3,0,1,2:T(8,128)(2,1)S(1)} async-done(((bf16[16,2,8,128]{3,0,1,2:T(8,128)(2,1)}), bf16[16,2,8,128]{3,0,1,2:T(8,128)(2,1)S(1)}, u32[]{:S(2)}, u32[]{:S(2)}) %all-to-all-start) | async-done | bytes 65568 | tf_op jit(solution)/shard_map/all_to_all | solution.py:157
  17.6 0.1 copy.31
  17.7 2.8 %collective-permute-start = (bf16[1,2,136,128]{3,2,1,0:T(8,128)(2,1)S(1)}, bf16[1,2,136,128]{3,2,1,0:T(8,128)(2,1)S(1)}, u32[]{:S(2)}, u32[]{:S(2)}) collective-permute-start(bf16[1,2,136,128]{3,2,1,0:T(8,128)(2,1)S(1)} %maximum_bitcast_fusion), channel_id=1, source_target_pairs={{0,8},{8,16},{16,24},{24,32},{32,40},{40,48},{48,56},{56,64},{64,7... | collective-permute-start | bytes 208904 | tf_op jit(solution)/shard_map/ppermute | solution.py:26
  20.6 4.3 %collective-permute-start.1 = (bf16[1,2,136,128]{3,2,1,0:T(8,128)(2,1)S(1)}, bf16[1,2,136,128]{3,2,1,0:T(8,128)(2,1)S(1)}, u32[]{:S(2)}, u32[]{:S(2)}) collective-permute-start(bf16[1,2,136,128]{3,2,1,0:T(8,128)(2,1)S(1)} %maximum_bitcast_fusion), channel_id=1, source_target_pairs={{0,16},{8,24},{16,32},{24,40},{32,48},{40,56},{48,64},{56,72},{64,... | collective-permute-start | bytes 208904 | tf_op jit(solution)/shard_map/ppermute | solution.py:26
  24.8 6.9 %collective-permute-start.2 = (bf16[1,2,136,128]{3,2,1,0:T(8,128)(2,1)S(1)}, bf16[1,2,136,128]{3,2,1,0:T(8,128)(2,1)S(1)}, u32[]{:S(2)}, u32[]{:S(2)}) collective-permute-start(bf16[1,2,136,128]{3,2,1,0:T(8,128)(2,1)S(1)} %maximum_bitcast_fusion), channel_id=1, source_target_pairs={{0,24},{8,32},{16,40},{24,48},{32,56},{40,64},{48,72},{56,80},{64,... | collective-permute-start | bytes 208904 | tf_op jit(solution)/shard_map/ppermute | solution.py:26
  31.8 0.7 constant_dynamic-update-slice_fusion.6
  32.4 0.0 collective-permute-done
  32.4 0.0 collective-permute-done.1
  32.4 1.3 collective-permute-done.2
  33.7 0.0 copy-start.1
  33.8 7.5 %collective-permute-start.3 = (bf16[4,2,136,128]{3,2,1,0:T(8,128)(2,1)S(1)}, bf16[4,2,136,128]{3,2,1,0:T(8,128)(2,1)S(1)}, u32[]{:S(2)}, u32[]{:S(2)}) collective-permute-start(bf16[4,2,136,128]{3,2,1,0:T(8,128)(2,1)S(1)} %pad_maximum_fusion.1.refs_2_), channel_id=1, source_target_pairs={{0,32},{8,40},{16,48},{24,56},{32,64},{40,72},{48,80},{56,88},{64,... | collective-permute-start | bytes 835592 | tf_op jit(solution)/shard_map/ppermute | solution.py:26
  41.3 4.9 %collective-permute-start.4 = (bf16[4,2,136,128]{3,2,1,0:T(8,128)(2,1)S(1)}, bf16[4,2,136,128]{3,2,1,0:T(8,128)(2,1)S(1)}, u32[]{:S(2)}, u32[]{:S(2)}) collective-permute-start(bf16[4,2,136,128]{3,2,1,0:T(8,128)(2,1)S(1)} %pad_maximum_fusion.1.refs_2_), channel_id=1, source_target_pairs={{0,64},{8,72},{16,80},{24,88},{32,96},{40,104},{48,112},{56,120},{... | collective-permute-start | bytes 835592 | tf_op jit(solution)/shard_map/ppermute | solution.py:26
  46.2 1.9 %collective-permute-start.5 = (bf16[4,2,136,128]{3,2,1,0:T(8,128)(2,1)S(1)}, bf16[4,2,136,128]{3,2,1,0:T(8,128)(2,1)S(1)}, u32[]{:S(2)}, u32[]{:S(2)}) collective-permute-start(bf16[4,2,136,128]{3,2,1,0:T(8,128)(2,1)S(1)} %pad_maximum_fusion.1.refs_2_), channel_id=1, source_target_pairs={{0,96},{8,104},{16,112},{24,120},{32,128},{40,136},{48,144},{56,15... | collective-permute-start | bytes 835592 | tf_op jit(solution)/shard_map/ppermute | solution.py:26
  48.1 0.7 constant_dynamic-update-slice_fusion.5
  48.8 0.7 constant_dynamic-update-slice_fusion.4
  49.4 0.6 constant_dynamic-update-slice_fusion.3
  50.1 8.1 %collective-permute-done.3 = bf16[4,2,136,128]{3,2,1,0:T(8,128)(2,1)S(1)} collective-permute-done((bf16[4,2,136,128]{3,2,1,0:T(8,128)(2,1)S(1)}, bf16[4,2,136,128]{3,2,1,0:T(8,128)(2,1)S(1)}, u32[]{:S(2)}, u32[]{:S(2)}) %collective-permute-start.3) | collective-permute-done | bytes 278560 | tf_op jit(solution)/shard_map/ppermute | solution.py:26
  58.2 0.8 constant_dynamic-update-slice_fusion.2
  59.0 8.4 %collective-permute-done.4 = bf16[4,2,136,128]{3,2,1,0:T(8,128)(2,1)S(1)} collective-permute-done((bf16[4,2,136,128]{3,2,1,0:T(8,128)(2,1)S(1)}, bf16[4,2,136,128]{3,2,1,0:T(8,128)(2,1)S(1)}, u32[]{:S(2)}, u32[]{:S(2)}) %collective-permute-start.4) | collective-permute-done | bytes 278560 | tf_op jit(solution)/shard_map/ppermute | solution.py:26
  67.4 0.8 constant_dynamic-update-slice_fusion.1
  68.2 0.0 copy-done.1
  68.2 0.0 copy-start.2
  68.2 3.4 %collective-permute-done.5 = bf16[4,2,136,128]{3,2,1,0:T(8,128)(2,1)S(1)} collective-permute-done((bf16[4,2,136,128]{3,2,1,0:T(8,128)(2,1)S(1)}, bf16[4,2,136,128]{3,2,1,0:T(8,128)(2,1)S(1)}, u32[]{:S(2)}, u32[]{:S(2)}) %collective-permute-start.5) | collective-permute-done | bytes 278560 | tf_op jit(solution)/shard_map/ppermute | solution.py:26
  71.6 0.0 copy-done.2
  71.6 0.7 constant_dynamic-update-slice_fusion
  72.3 5.0 %collective-permute-start.6 = (bf16[16,2,136,128]{3,2,1,0:T(8,128)(2,1)}, bf16[16,2,136,128]{3,2,1,0:T(8,128)(2,1)S(1)}, u32[]{:S(2)}, u32[]{:S(2)}) collective-permute-start(bf16[16,2,136,128]{3,2,1,0:T(8,128)(2,1)} %constant_dynamic-update-slice_fusion), channel_id=1, source_target_pairs={{0,128},{8,136},{16,144},{24,152},{32,160},{40,168},{48,176},{56,1... | collective-permute-start | bytes 3342344 | tf_op jit(solution)/shard_map/ppermute | solution.py:26
  77.4 1.2 gather_fusion
  78.6 0.6 fusion.1
  82.0 1.1 slice.68
  83.1 1.9 %collective-permute-start.7 = (bf16[9,2,136,128]{3,2,1,0:T(8,128)(2,1)S(1)}, bf16[9,2,136,128]{3,2,1,0:T(8,128)(2,1)S(1)}, u32[]{:S(2)}, u32[]{:S(2)}) collective-permute-start(bf16[9,2,136,128]{3,2,1,0:T(8,128)(2,1)S(1)} %slice.68), channel_id=1, source_target_pairs={{0,256},{8,264},{16,272},{24,280},{32,288},{40,296},{48,304},{56,3... | collective-permute-start | bytes 1880072 | tf_op jit(solution)/shard_map/ppermute | solution.py:26
  85.0 1.3 add_add_fusion.refs_0_
  86.4 0.1 pad.18.clone
  86.4 1.2 add_add_fusion.1.refs_0_
  87.7 1.3 add_add_fusion.2.refs_0_
  89.0 0.0 copy-done
  89.0 0.8 copy_bitcast_fusion
  89.7 0.7 broadcast_in_dim.26.refs_3_
  90.4 6.2 %shard_map.73 = (f32[8,128,128]{2,1,0:T(8,128)}, f32[8,128,128]{2,1,0:T(8,128)}, f32[8,128,128]{2,1,0:T(8,128)}) custom-call(s32[3]{0:T(128)} %add_add_fusion.2.refs_0_, bf16[1024,128]{1,0:T(8,128)(2,1)} %bitcast.48, bf16[4,2,136,128]{3,2,1,0:T(8,128)(2,1)} %copy-done.1, s32[128,128]{1,0:T(8,128)} %broadcast_in_dim.26.refs_3_, f32[1,128]{1,0:T(1,128)} %bitcast.57), custom_call_target="tpu_custom_call" | custom-call | tf_op jit(solution)/shard_map/pallas_call | solution.py:140
  96.6 1.1 pad_maximum_fusion.refs_2_
  97.7 13.2 %shard_map.74 = (f32[8,128,128]{2,1,0:T(8,128)}, f32[8,128,128]{2,1,0:T(8,128)}, f32[8,128,128]{2,1,0:T(8,128)}) custom-call(s32[3]{0:T(128)} %add_add_fusion.1.refs_0_, bf16[1024,128]{1,0:T(8,128)(2,1)} %bitcast.49, bf16[12,2,136,128]{3,2,1,0:T(8,128)(2,1)} %pad_maximum_fusion.refs_2_, s32[128,128]{1,0:T(8,128)} %broadcast_in_dim.26.refs_3_, ...), custom_call_target="tpu_custom_call" | custom-call | tf_op jit(solution)/shard_map/pallas_call | solution.py:140
  110.9 0.0 collective-permute-done.7
  110.9 3.9 %collective-permute-done.6 = bf16[16,2,136,128]{3,2,1,0:T(8,128)(2,1)S(1)} collective-permute-done((bf16[16,2,136,128]{3,2,1,0:T(8,128)(2,1)}, bf16[16,2,136,128]{3,2,1,0:T(8,128)(2,1)S(1)}, u32[]{:S(2)}, u32[]{:S(2)}) %collective-permute-start.6) | collective-permute-done | bytes 1114144 | tf_op jit(solution)/shard_map/ppermute | solution.py:26
  114.8 1.5 %maximum_maximum_fusion.refs_2_ = bf16[26,2,136,128]{3,2,1,0:T(8,128)(2,1)} fusion(bf16[9,2,136,128]{3,2,1,0:T(8,128)(2,1)S(1)} %collective-permute-done.7, bf16[16,2,136,128]{3,2,1,0:T(8,128)(2,1)S(1)} %collective-permute-done.6, bf16[26]{0:T(256)(128)(2,1)S(1)} %pad.18.clone), kind=kLoop, calls=%fused_computation.1 | loop fusion | flops 1810432 | bytes 3551284 | tf_op jit(solution)/shard_map/concatenate | solution.py:189
  116.2 24.1 %shard_map.75 = bf16[128,1024]{1,0:T(8,128)(2,1)} custom-call(s32[3]{0:T(128)} %add_add_fusion.refs_0_, bf16[1024,128]{1,0:T(8,128)(2,1)} %bitcast.50, bf16[26,2,136,128]{3,2,1,0:T(8,128)(2,1)} %maximum_maximum_fusion.refs_2_, s32[128,128]{1,0:T(8,128)} %broadcast_in_dim.26.refs_3_, f32[1,128]{1,0:T(1,128)} %bitcast.59, ...), custom_call_target="tpu_custom_call" | custom-call | tf_op jit(solution)/shard_map/pallas_call | solution.py:140
  (10 shorter events, 0.1 us)
Async XLA Ops:
  0.0 89.0 %copy-start = (bf16[128,1024]{1,0:T(8,128)(2,1)S(1)}, bf16[128,1024]{1,0:T(8,128)(2,1)}, u32[]{:S(2)}) copy-start(bf16[128,1024]{1,0:T(8,128)(2,1)} %param.11) | copy-start | bytes 786436
  2.2 15.3 %all-to-all-start = ((bf16[16,2,8,128]{3,0,1,2:T(8,128)(2,1)}), bf16[16,2,8,128]{3,0,1,2:T(8,128)(2,1)S(1)}, u32[]{:S(2)}, u32[]{:S(2)}) async-start(bf16[16,2,8,128]{3,0,1,2:T(8,128)(2,1)} %copy.29), calls=%async_computation | async-start | bytes 131072 | tf_op jit(solution)/shard_map/all_to_all | solution.py:157
  17.7 14.7 %collective-permute-start = (bf16[1,2,136,128]{3,2,1,0:T(8,128)(2,1)S(1)}, bf16[1,2,136,128]{3,2,1,0:T(8,128)(2,1)S(1)}, u32[]{:S(2)}, u32[]{:S(2)}) collective-permute-start(bf16[1,2,136,128]{3,2,1,0:T(8,128)(2,1)S(1)} %maximum_bitcast_fusion), channel_id=1, source_target_pairs={{0,8},{8,16},{16,24},{24,32},{32,40},{40,48},{48,56},{56,64},{64,7... | collective-permute-start | bytes 208904 | tf_op jit(solution)/shard_map/ppermute | solution.py:26
  20.6 11.9 %collective-permute-start.1 = (bf16[1,2,136,128]{3,2,1,0:T(8,128)(2,1)S(1)}, bf16[1,2,136,128]{3,2,1,0:T(8,128)(2,1)S(1)}, u32[]{:S(2)}, u32[]{:S(2)}) collective-permute-start(bf16[1,2,136,128]{3,2,1,0:T(8,128)(2,1)S(1)} %maximum_bitcast_fusion), channel_id=1, source_target_pairs={{0,16},{8,24},{16,32},{24,40},{32,48},{40,56},{48,64},{56,72},{64,... | collective-permute-start | bytes 208904 | tf_op jit(solution)/shard_map/ppermute | solution.py:26
  24.8 8.9 %collective-permute-start.2 = (bf16[1,2,136,128]{3,2,1,0:T(8,128)(2,1)S(1)}, bf16[1,2,136,128]{3,2,1,0:T(8,128)(2,1)S(1)}, u32[]{:S(2)}, u32[]{:S(2)}) collective-permute-start(bf16[1,2,136,128]{3,2,1,0:T(8,128)(2,1)S(1)} %maximum_bitcast_fusion), channel_id=1, source_target_pairs={{0,24},{8,32},{16,40},{24,48},{32,56},{40,64},{48,72},{56,80},{64,... | collective-permute-start | bytes 208904 | tf_op jit(solution)/shard_map/ppermute | solution.py:26
  33.7 34.4 %copy-start.1 = (bf16[4,2,136,128]{3,2,1,0:T(8,128)(2,1)}, bf16[4,2,136,128]{3,2,1,0:T(8,128)(2,1)S(1)}, u32[]{:S(2)}) copy-start(bf16[4,2,136,128]{3,2,1,0:T(8,128)(2,1)S(1)} %pad_maximum_fusion.1.refs_2_) | copy-start | bytes 835588
  33.8 24.4 %collective-permute-start.3 = (bf16[4,2,136,128]{3,2,1,0:T(8,128)(2,1)S(1)}, bf16[4,2,136,128]{3,2,1,0:T(8,128)(2,1)S(1)}, u32[]{:S(2)}, u32[]{:S(2)}) collective-permute-start(bf16[4,2,136,128]{3,2,1,0:T(8,128)(2,1)S(1)} %pad_maximum_fusion.1.refs_2_), channel_id=1, source_target_pairs={{0,32},{8,40},{16,48},{24,56},{32,64},{40,72},{48,80},{56,88},{64,... | collective-permute-start | bytes 835592 | tf_op jit(solution)/shard_map/ppermute | solution.py:26
  41.3 26.1 %collective-permute-start.4 = (bf16[4,2,136,128]{3,2,1,0:T(8,128)(2,1)S(1)}, bf16[4,2,136,128]{3,2,1,0:T(8,128)(2,1)S(1)}, u32[]{:S(2)}, u32[]{:S(2)}) collective-permute-start(bf16[4,2,136,128]{3,2,1,0:T(8,128)(2,1)S(1)} %pad_maximum_fusion.1.refs_2_), channel_id=1, source_target_pairs={{0,64},{8,72},{16,80},{24,88},{32,96},{40,104},{48,112},{56,120},{... | collective-permute-start | bytes 835592 | tf_op jit(solution)/shard_map/ppermute | solution.py:26
  46.2 25.4 %collective-permute-start.5 = (bf16[4,2,136,128]{3,2,1,0:T(8,128)(2,1)S(1)}, bf16[4,2,136,128]{3,2,1,0:T(8,128)(2,1)S(1)}, u32[]{:S(2)}, u32[]{:S(2)}) collective-permute-start(bf16[4,2,136,128]{3,2,1,0:T(8,128)(2,1)S(1)} %pad_maximum_fusion.1.refs_2_), channel_id=1, source_target_pairs={{0,96},{8,104},{16,112},{24,120},{32,128},{40,136},{48,144},{56,15... | collective-permute-start | bytes 835592 | tf_op jit(solution)/shard_map/ppermute | solution.py:26
  68.2 3.4 %copy-start.2 = (bf16[12,2,136,128]{3,2,1,0:T(8,128)(2,1)}, bf16[12,2,136,128]{3,2,1,0:T(8,128)(2,1)S(1)}, u32[]{:S(2)}) copy-start(bf16[12,2,136,128]{3,2,1,0:T(8,128)(2,1)S(1)} %get-tuple-element.42) | copy-start | bytes 2506756
  72.3 42.5 %collective-permute-start.6 = (bf16[16,2,136,128]{3,2,1,0:T(8,128)(2,1)}, bf16[16,2,136,128]{3,2,1,0:T(8,128)(2,1)S(1)}, u32[]{:S(2)}, u32[]{:S(2)}) collective-permute-start(bf16[16,2,136,128]{3,2,1,0:T(8,128)(2,1)} %constant_dynamic-update-slice_fusion), channel_id=1, source_target_pairs={{0,128},{8,136},{16,144},{24,152},{32,160},{40,168},{48,176},{56,1... | collective-permute-start | bytes 3342344 | tf_op jit(solution)/shard_map/ppermute | solution.py:26
  83.1 27.7 %collective-permute-start.7 = (bf16[9,2,136,128]{3,2,1,0:T(8,128)(2,1)S(1)}, bf16[9,2,136,128]{3,2,1,0:T(8,128)(2,1)S(1)}, u32[]{:S(2)}, u32[]{:S(2)}) collective-permute-start(bf16[9,2,136,128]{3,2,1,0:T(8,128)(2,1)S(1)} %slice.68), channel_id=1, source_target_pairs={{0,256},{8,264},{16,272},{24,280},{32,288},{40,296},{48,304},{56,3... | collective-permute-start | bytes 1880072 | tf_op jit(solution)/shard_map/ppermute | solution.py:26

commit v6 on v5

--- a/solution.py
+++ b/solution.py
@@ -88,21 +88,21 @@
                 scores = jnp.where(allowed, scores, NEG)
             parts.append((scores, allowed, value_scale[None], slot))
         run_max = max_ref[...][:, :, :1]
-        new_max = run_max
-        for scores, _, _, _ in parts:
-            new_max = jnp.maximum(new_max, jnp.max(scores, axis=2, keepdims=True))
+        both_max = jnp.maximum(parts[0][0], parts[1][0])
+        new_max = jnp.maximum(run_max, jnp.max(both_max, axis=2, keepdims=True))
         factor = jnp.exp(run_max - new_max)
-        run_sum = sum_ref[...][:, :, :1] * factor
         acc = acc_ref[...] * factor
+        weight_sum = None
         for scores, allowed, value_scale, slot in parts:
             weights = jnp.exp(scores - new_max)
             if masked:
                 weights = jnp.where(allowed, weights, 0.0)
-            run_sum = run_sum + jnp.sum(weights, axis=2, keepdims=True)
+            weight_sum = weights if weight_sum is None else weight_sum + weights
             scaled = (weights * value_scale).astype(jnp.bfloat16).reshape(group_size * rows, rows)
             value_tile = window_ref[slot, 1, :rows, :]
             mixed = jnp.dot(scaled, value_tile, preferred_element_type=jnp.float32)
             acc = acc + mixed.reshape(group_size, rows, HD)
+        run_sum = sum_ref[...][:, :, :1] * factor + jnp.sum(weight_sum, axis=2, keepdims=True)
         acc_ref[...] = acc
         max_ref[...] = jnp.broadcast_to(new_max, max_ref.shape)
         sum_ref[...] = jnp.broadcast_to(run_sum, sum_ref.shape)

time: 141 us -> 136 us (0.965)
  the two profiles are of different devices: /device:TPU:134 before, /device:TPU:388 now
where the time goes in v6:
time: 136 us; the launch traced here: 135 us
  Pallas kernels  48.7 us (36%)
  starting transfers between devices  33.1 us (24%)
  waiting for transfers between devices  28.9 us (21%)
  local copies, waits for them, and re-layouts  12.2 us (9%)
  other arithmetic  9.59 us (7%)
  between operations  2.95 us (2%)
    pallas_call x3, Pallas kernels, attend_part(): pl.pallas_call(kernel, out_shape=out_shape, grid_spec=pltpu.PrefetchScala...  48.7 us
    ppermute x8, starting transfers between devices, shift_from(): return lax.ppermute(x, 'seq', pairs)  26 us
    ppermute x8, waiting for transfers between devices, shift_from(): return lax.ppermute(x, 'seq', pairs)  24.3 us
    all_to_all x1, starting transfers between devices, shards(): both = lax.all_to_all(both, 'head', split_axis=2, concat_axis=0, tiled=True)  7.1 us
    unnamed x13, local copies, waits for them, and re-layouts  5.08 us
    all_to_all x1, waiting for transfers between devices, shards(): both = lax.all_to_all(both, 'head', split_axis=2, concat_axis=0, tiled=True)  4.6 us
    another operation x3, other arithmetic, shards(): jnp.stack([seq_index.astype(jnp.int32), pairs, low[-1].astype(jnp.int32)])  3.85 us
  transfers between devices with their start and end apart: 9, of which 7 were waited for; matrix products, arithmetic and copies ran while one was open for 13% of the time, Pallas kernels for 17%

profile of v6, /device:TPU:388, one launch (start us, length us, event | category | flops | bytes accessed | tf_op | source)
XLA Modules:
  0.0 135.4 jit_solution(4461426093987496146)
XLA Ops:
  0.0 0.0 copy-start
  0.0 0.8 copy.34
  0.8 0.8 copy.33
  1.6 0.6 copy.29
  2.2 7.1 %all-to-all-start = ((bf16[16,2,8,128]{3,0,1,2:T(8,128)(2,1)}), bf16[16,2,8,128]{3,0,1,2:T(8,128)(2,1)S(1)}, u32[]{:S(2)}, u32[]{:S(2)}) async-start(bf16[16,2,8,128]{3,0,1,2:T(8,128)(2,1)} %copy.29), calls=%async_computation | async-start | bytes 131072 | tf_op jit(solution)/shard_map/all_to_all | solution.py:157
  9.3 0.7 copy.27
  10.1 0.1 reduce-window.9
  10.2 0.1 reduce.4
  10.3 0.7 sub.27
  11.0 0.8 reduce.5
  11.7 0.1 broadcast_in_dim.10
  11.8 0.1 reshape.146
  11.9 0.8 reduce.6
  12.7 0.1 broadcast_in_dim.11
  12.7 0.1 reshape.148
  12.9 0.1 convert_reduce_fusion
  13.0 4.6 %all-to-all-done = bf16[16,2,8,128]{3,0,1,2:T(8,128)(2,1)S(1)} async-done(((bf16[16,2,8,128]{3,0,1,2:T(8,128)(2,1)}), bf16[16,2,8,128]{3,0,1,2:T(8,128)(2,1)S(1)}, u32[]{:S(2)}, u32[]{:S(2)}) %all-to-all-start) | async-done | bytes 65568 | tf_op jit(solution)/shard_map/all_to_all | solution.py:157
  17.6 0.1 copy.31
  17.7 2.8 %collective-permute-start = (bf16[1,2,136,128]{3,2,1,0:T(8,128)(2,1)S(1)}, bf16[1,2,136,128]{3,2,1,0:T(8,128)(2,1)S(1)}, u32[]{:S(2)}, u32[]{:S(2)}) collective-permute-start(bf16[1,2,136,128]{3,2,1,0:T(8,128)(2,1)S(1)} %maximum_bitcast_fusion), channel_id=1, source_target_pairs={{0,8},{8,16},{16,24},{24,32},{32,40},{40,48},{48,56},{56,64},{64,7... | collective-permute-start | bytes 208904 | tf_op jit(solution)/shard_map/ppermute | solution.py:26
  20.6 3.4 %collective-permute-start.1 = (bf16[1,2,136,128]{3,2,1,0:T(8,128)(2,1)S(1)}, bf16[1,2,136,128]{3,2,1,0:T(8,128)(2,1)S(1)}, u32[]{:S(2)}, u32[]{:S(2)}) collective-permute-start(bf16[1,2,136,128]{3,2,1,0:T(8,128)(2,1)S(1)} %maximum_bitcast_fusion), channel_id=1, source_target_pairs={{0,16},{8,24},{16,32},{24,40},{32,48},{40,56},{48,64},{56,72},{64,... | collective-permute-start | bytes 208904 | tf_op jit(solution)/shard_map/ppermute | solution.py:26
  23.9 1.9 %collective-permute-start.2 = (bf16[1,2,136,128]{3,2,1,0:T(8,128)(2,1)S(1)}, bf16[1,2,136,128]{3,2,1,0:T(8,128)(2,1)S(1)}, u32[]{:S(2)}, u32[]{:S(2)}) collective-permute-start(bf16[1,2,136,128]{3,2,1,0:T(8,128)(2,1)S(1)} %maximum_bitcast_fusion), channel_id=1, source_target_pairs={{0,24},{8,32},{16,40},{24,48},{32,56},{40,64},{48,72},{56,80},{64,... | collective-permute-start | bytes 208904 | tf_op jit(solution)/shard_map/ppermute | solution.py:26
  25.9 0.7 constant_dynamic-update-slice_fusion.6
  26.5 0.0 collective-permute-done
  26.5 0.2 collective-permute-done.1
  26.8 5.4 %collective-permute-done.2 = bf16[1,2,136,128]{3,2,1,0:T(8,128)(2,1)S(1)} collective-permute-done((bf16[1,2,136,128]{3,2,1,0:T(8,128)(2,1)S(1)}, bf16[1,2,136,128]{3,2,1,0:T(8,128)(2,1)S(1)}, u32[]{:S(2)}, u32[]{:S(2)}) %collective-permute-start.2) | collective-permute-done | bytes 69664 | tf_op jit(solution)/shard_map/ppermute | solution.py:26
  32.2 0.0 copy-start.1
  32.2 3.6 %collective-permute-start.3 = (bf16[4,2,136,128]{3,2,1,0:T(8,128)(2,1)S(1)}, bf16[4,2,136,128]{3,2,1,0:T(8,128)(2,1)S(1)}, u32[]{:S(2)}, u32[]{:S(2)}) collective-permute-start(bf16[4,2,136,128]{3,2,1,0:T(8,128)(2,1)S(1)} %pad_maximum_fusion.1.refs_2_), channel_id=1, source_target_pairs={{0,32},{8,40},{16,48},{24,56},{32,64},{40,72},{48,80},{56,88},{64,... | collective-permute-start | bytes 835592 | tf_op jit(solution)/shard_map/ppermute | solution.py:26
  35.9 6.7 %collective-permute-start.4 = (bf16[4,2,136,128]{3,2,1,0:T(8,128)(2,1)S(1)}, bf16[4,2,136,128]{3,2,1,0:T(8,128)(2,1)S(1)}, u32[]{:S(2)}, u32[]{:S(2)}) collective-permute-start(bf16[4,2,136,128]{3,2,1,0:T(8,128)(2,1)S(1)} %pad_maximum_fusion.1.refs_2_), channel_id=1, source_target_pairs={{0,64},{8,72},{16,80},{24,88},{32,96},{40,104},{48,112},{56,120},{... | collective-permute-start | bytes 835592 | tf_op jit(solution)/shard_map/ppermute | solution.py:26
  42.5 1.9 %collective-permute-start.5 = (bf16[4,2,136,128]{3,2,1,0:T(8,128)(2,1)S(1)}, bf16[4,2,136,128]{3,2,1,0:T(8,128)(2,1)S(1)}, u32[]{:S(2)}, u32[]{:S(2)}) collective-permute-start(bf16[4,2,136,128]{3,2,1,0:T(8,128)(2,1)S(1)} %pad_maximum_fusion.1.refs_2_), channel_id=1, source_target_pairs={{0,96},{8,104},{16,112},{24,120},{32,128},{40,136},{48,144},{56,15... | collective-permute-start | bytes 835592 | tf_op jit(solution)/shard_map/ppermute | solution.py:26
  44.5 0.7 constant_dynamic-update-slice_fusion.5
  45.1 0.7 constant_dynamic-update-slice_fusion.4
  45.8 0.6 constant_dynamic-update-slice_fusion.3
  46.4 8.0 %collective-permute-done.3 = bf16[4,2,136,128]{3,2,1,0:T(8,128)(2,1)S(1)} collective-permute-done((bf16[4,2,136,128]{3,2,1,0:T(8,128)(2,1)S(1)}, bf16[4,2,136,128]{3,2,1,0:T(8,128)(2,1)S(1)}, u32[]{:S(2)}, u32[]{:S(2)}) %collective-permute-start.3) | collective-permute-done | bytes 278560 | tf_op jit(solution)/shard_map/ppermute | solution.py:26
  54.4 0.8 constant_dynamic-update-slice_fusion.2
  55.2 6.6 %collective-permute-done.4 = bf16[4,2,136,128]{3,2,1,0:T(8,128)(2,1)S(1)} collective-permute-done((bf16[4,2,136,128]{3,2,1,0:T(8,128)(2,1)S(1)}, bf16[4,2,136,128]{3,2,1,0:T(8,128)(2,1)S(1)}, u32[]{:S(2)}, u32[]{:S(2)}) %collective-permute-start.4) | collective-permute-done | bytes 278560 | tf_op jit(solution)/shard_map/ppermute | solution.py:26
  61.8 0.8 constant_dynamic-update-slice_fusion.1
  62.6 0.0 copy-done.1
  62.6 0.0 copy-start.2
  62.6 2.8 %collective-permute-done.5 = bf16[4,2,136,128]{3,2,1,0:T(8,128)(2,1)S(1)} collective-permute-done((bf16[4,2,136,128]{3,2,1,0:T(8,128)(2,1)S(1)}, bf16[4,2,136,128]{3,2,1,0:T(8,128)(2,1)S(1)}, u32[]{:S(2)}, u32[]{:S(2)}) %collective-permute-start.5) | collective-permute-done | bytes 278560 | tf_op jit(solution)/shard_map/ppermute | solution.py:26
  65.4 0.0 copy-done.2
  65.4 0.7 constant_dynamic-update-slice_fusion
  66.1 2.7 %collective-permute-start.6 = (bf16[16,2,136,128]{3,2,1,0:T(8,128)(2,1)}, bf16[16,2,136,128]{3,2,1,0:T(8,128)(2,1)S(1)}, u32[]{:S(2)}, u32[]{:S(2)}) collective-permute-start(bf16[16,2,136,128]{3,2,1,0:T(8,128)(2,1)} %constant_dynamic-update-slice_fusion), channel_id=1, source_target_pairs={{0,128},{8,136},{16,144},{24,152},{32,160},{40,168},{48,176},{56,1... | collective-permute-start | bytes 3342344 | tf_op jit(solution)/shard_map/ppermute | solution.py:26
  68.9 1.2 gather_fusion
  70.1 0.6 fusion.1
  73.5 1.1 slice.68
  74.7 2.9 %collective-permute-start.7 = (bf16[9,2,136,128]{3,2,1,0:T(8,128)(2,1)S(1)}, bf16[9,2,136,128]{3,2,1,0:T(8,128)(2,1)S(1)}, u32[]{:S(2)}, u32[]{:S(2)}) collective-permute-start(bf16[9,2,136,128]{3,2,1,0:T(8,128)(2,1)S(1)} %slice.68), channel_id=1, source_target_pairs={{0,256},{8,264},{16,272},{24,280},{32,288},{40,296},{48,304},{56,3... | collective-permute-start | bytes 1880072 | tf_op jit(solution)/shard_map/ppermute | solution.py:26
  77.6 1.3 add_add_fusion.refs_0_
  78.9 0.1 pad.18.clone
  79.0 1.2 add_add_fusion.1.refs_0_
  80.2 1.3 add_add_fusion.2.refs_0_
  81.5 0.0 copy-done
  81.5 0.8 copy_bitcast_fusion
  82.3 0.7 broadcast_in_dim.26.refs_3_
  83.0 7.0 %shard_map.73 = (f32[8,128,128]{2,1,0:T(8,128)}, f32[8,128,128]{2,1,0:T(8,128)}, f32[8,128,128]{2,1,0:T(8,128)}) custom-call(s32[3]{0:T(128)} %add_add_fusion.2.refs_0_, bf16[1024,128]{1,0:T(8,128)(2,1)} %bitcast.48, bf16[4,2,136,128]{3,2,1,0:T(8,128)(2,1)} %copy-done.1, s32[128,128]{1,0:T(8,128)} %broadcast_in_dim.26.refs_3_, f32[1,128]{1,0:T(1,128)} %bitcast.57), custom_call_target="tpu_custom_call" | custom-call | tf_op jit(solution)/shard_map/pallas_call | solution.py:140
  90.0 1.1 pad_maximum_fusion.refs_2_
  91.1 15.8 %shard_map.74 = (f32[8,128,128]{2,1,0:T(8,128)}, f32[8,128,128]{2,1,0:T(8,128)}, f32[8,128,128]{2,1,0:T(8,128)}) custom-call(s32[3]{0:T(128)} %add_add_fusion.1.refs_0_, bf16[1024,128]{1,0:T(8,128)(2,1)} %bitcast.49, bf16[12,2,136,128]{3,2,1,0:T(8,128)(2,1)} %pad_maximum_fusion.refs_2_, s32[128,128]{1,0:T(8,128)} %broadcast_in_dim.26.refs_3_, ...), custom_call_target="tpu_custom_call" | custom-call | tf_op jit(solution)/shard_map/pallas_call | solution.py:140
  106.9 1.2 collective-permute-done.7
  108.0 0.0 collective-permute-done.6
  108.1 1.5 %maximum_maximum_fusion.refs_2_ = bf16[26,2,136,128]{3,2,1,0:T(8,128)(2,1)} fusion(bf16[9,2,136,128]{3,2,1,0:T(8,128)(2,1)S(1)} %collective-permute-done.7, bf16[16,2,136,128]{3,2,1,0:T(8,128)(2,1)S(1)} %collective-permute-done.6, bf16[26]{0:T(256)(128)(2,1)S(1)} %pad.18.clone), kind=kLoop, calls=%fused_computation.1 | loop fusion | flops 1810432 | bytes 3551284 | tf_op jit(solution)/shard_map/concatenate | solution.py:189
  109.5 25.9 %shard_map.75 = bf16[128,1024]{1,0:T(8,128)(2,1)} custom-call(s32[3]{0:T(128)} %add_add_fusion.refs_0_, bf16[1024,128]{1,0:T(8,128)(2,1)} %bitcast.50, bf16[26,2,136,128]{3,2,1,0:T(8,128)(2,1)} %maximum_maximum_fusion.refs_2_, s32[128,128]{1,0:T(8,128)} %broadcast_in_dim.26.refs_3_, f32[1,128]{1,0:T(1,128)} %bitcast.59, ...), custom_call_target="tpu_custom_call" | custom-call | tf_op jit(solution)/shard_map/pallas_call | solution.py:140
  (10 shorter events, 0.1 us)
Async XLA Ops:
  0.0 81.5 %copy-start = (bf16[128,1024]{1,0:T(8,128)(2,1)S(1)}, bf16[128,1024]{1,0:T(8,128)(2,1)}, u32[]{:S(2)}) copy-start(bf16[128,1024]{1,0:T(8,128)(2,1)} %param.11) | copy-start | bytes 786436
  2.2 15.3 %all-to-all-start = ((bf16[16,2,8,128]{3,0,1,2:T(8,128)(2,1)}), bf16[16,2,8,128]{3,0,1,2:T(8,128)(2,1)S(1)}, u32[]{:S(2)}, u32[]{:S(2)}) async-start(bf16[16,2,8,128]{3,0,1,2:T(8,128)(2,1)} %copy.29), calls=%async_computation | async-start | bytes 131072 | tf_op jit(solution)/shard_map/all_to_all | solution.py:157
  17.7 8.8 %collective-permute-start = (bf16[1,2,136,128]{3,2,1,0:T(8,128)(2,1)S(1)}, bf16[1,2,136,128]{3,2,1,0:T(8,128)(2,1)S(1)}, u32[]{:S(2)}, u32[]{:S(2)}) collective-permute-start(bf16[1,2,136,128]{3,2,1,0:T(8,128)(2,1)S(1)} %maximum_bitcast_fusion), channel_id=1, source_target_pairs={{0,8},{8,16},{16,24},{24,32},{32,40},{40,48},{48,56},{56,64},{64,7... | collective-permute-start | bytes 208904 | tf_op jit(solution)/shard_map/ppermute | solution.py:26
  20.6 6.2 %collective-permute-start.1 = (bf16[1,2,136,128]{3,2,1,0:T(8,128)(2,1)S(1)}, bf16[1,2,136,128]{3,2,1,0:T(8,128)(2,1)S(1)}, u32[]{:S(2)}, u32[]{:S(2)}) collective-permute-start(bf16[1,2,136,128]{3,2,1,0:T(8,128)(2,1)S(1)} %maximum_bitcast_fusion), channel_id=1, source_target_pairs={{0,16},{8,24},{16,32},{24,40},{32,48},{40,56},{48,64},{56,72},{64,... | collective-permute-start | bytes 208904 | tf_op jit(solution)/shard_map/ppermute | solution.py:26
  23.9 8.2 %collective-permute-start.2 = (bf16[1,2,136,128]{3,2,1,0:T(8,128)(2,1)S(1)}, bf16[1,2,136,128]{3,2,1,0:T(8,128)(2,1)S(1)}, u32[]{:S(2)}, u32[]{:S(2)}) collective-permute-start(bf16[1,2,136,128]{3,2,1,0:T(8,128)(2,1)S(1)} %maximum_bitcast_fusion), channel_id=1, source_target_pairs={{0,24},{8,32},{16,40},{24,48},{32,56},{40,64},{48,72},{56,80},{64,... | collective-permute-start | bytes 208904 | tf_op jit(solution)/shard_map/ppermute | solution.py:26
  32.2 30.4 %copy-start.1 = (bf16[4,2,136,128]{3,2,1,0:T(8,128)(2,1)}, bf16[4,2,136,128]{3,2,1,0:T(8,128)(2,1)S(1)}, u32[]{:S(2)}) copy-start(bf16[4,2,136,128]{3,2,1,0:T(8,128)(2,1)S(1)} %pad_maximum_fusion.1.refs_2_) | copy-start | bytes 835588
  32.2 22.2 %collective-permute-start.3 = (bf16[4,2,136,128]{3,2,1,0:T(8,128)(2,1)S(1)}, bf16[4,2,136,128]{3,2,1,0:T(8,128)(2,1)S(1)}, u32[]{:S(2)}, u32[]{:S(2)}) collective-permute-start(bf16[4,2,136,128]{3,2,1,0:T(8,128)(2,1)S(1)} %pad_maximum_fusion.1.refs_2_), channel_id=1, source_target_pairs={{0,32},{8,40},{16,48},{24,56},{32,64},{40,72},{48,80},{56,88},{64,... | collective-permute-start | bytes 835592 | tf_op jit(solution)/shard_map/ppermute | solution.py:26
  35.9 26.0 %collective-permute-start.4 = (bf16[4,2,136,128]{3,2,1,0:T(8,128)(2,1)S(1)}, bf16[4,2,136,128]{3,2,1,0:T(8,128)(2,1)S(1)}, u32[]{:S(2)}, u32[]{:S(2)}) collective-permute-start(bf16[4,2,136,128]{3,2,1,0:T(8,128)(2,1)S(1)} %pad_maximum_fusion.1.refs_2_), channel_id=1, source_target_pairs={{0,64},{8,72},{16,80},{24,88},{32,96},{40,104},{48,112},{56,120},{... | collective-permute-start | bytes 835592 | tf_op jit(solution)/shard_map/ppermute | solution.py:26
  42.5 22.9 %collective-permute-start.5 = (bf16[4,2,136,128]{3,2,1,0:T(8,128)(2,1)S(1)}, bf16[4,2,136,128]{3,2,1,0:T(8,128)(2,1)S(1)}, u32[]{:S(2)}, u32[]{:S(2)}) collective-permute-start(bf16[4,2,136,128]{3,2,1,0:T(8,128)(2,1)S(1)} %pad_maximum_fusion.1.refs_2_), channel_id=1, source_target_pairs={{0,96},{8,104},{16,112},{24,120},{32,128},{40,136},{48,144},{56,15... | collective-permute-start | bytes 835592 | tf_op jit(solution)/shard_map/ppermute | solution.py:26
  62.6 2.8 %copy-start.2 = (bf16[12,2,136,128]{3,2,1,0:T(8,128)(2,1)}, bf16[12,2,136,128]{3,2,1,0:T(8,128)(2,1)S(1)}, u32[]{:S(2)}) copy-start(bf16[12,2,136,128]{3,2,1,0:T(8,128)(2,1)S(1)} %get-tuple-element.42) | copy-start | bytes 2506756
  66.1 41.9 %collective-permute-start.6 = (bf16[16,2,136,128]{3,2,1,0:T(8,128)(2,1)}, bf16[16,2,136,128]{3,2,1,0:T(8,128)(2,1)S(1)}, u32[]{:S(2)}, u32[]{:S(2)}) collective-permute-start(bf16[16,2,136,128]{3,2,1,0:T(8,128)(2,1)} %constant_dynamic-update-slice_fusion), channel_id=1, source_target_pairs={{0,128},{8,136},{16,144},{24,152},{32,160},{40,168},{48,176},{56,1... | collective-permute-start | bytes 3342344 | tf_op jit(solution)/shard_map/ppermute | solution.py:26
  74.7 33.4 %collective-permute-start.7 = (bf16[9,2,136,128]{3,2,1,0:T(8,128)(2,1)S(1)}, bf16[9,2,136,128]{3,2,1,0:T(8,128)(2,1)S(1)}, u32[]{:S(2)}, u32[]{:S(2)}) collective-permute-start(bf16[9,2,136,128]{3,2,1,0:T(8,128)(2,1)S(1)} %slice.68), channel_id=1, source_target_pairs={{0,256},{8,264},{16,272},{24,280},{32,288},{40,296},{48,304},{56,3... | collective-permute-start | bytes 1880072 | tf_op jit(solution)/shard_map/ppermute | solution.py:26

commit v7 on v5

--- a/solution.py
+++ b/solution.py
@@ -71,6 +71,7 @@
     query_all = query_ref[...]
 
     low_top = info_ref[2]
+    ones = jnp.ones((rows, HD), jnp.bfloat16)
 
     def fold_pair(pair, masked):
         parts = []
@@ -92,20 +93,26 @@
         for scores, _, _, _ in parts:
             new_max = jnp.maximum(new_max, jnp.max(scores, axis=2, keepdims=True))
         factor = jnp.exp(run_max - new_max)
-        run_sum = sum_ref[...][:, :, :1] * factor
+        run_sum = sum_ref[...] * factor
         acc = acc_ref[...] * factor
         for scores, allowed, value_scale, slot in parts:
             weights = jnp.exp(scores - new_max)
             if masked:
                 weights = jnp.where(allowed, weights, 0.0)
-            run_sum = run_sum + jnp.sum(weights, axis=2, keepdims=True)
+            flat = weights.reshape(group_size * rows, rows)
+            high = flat.astype(jnp.bfloat16)
+            low_part = (flat - high.astype(jnp.float32)).astype(jnp.bfloat16)
+            row_sum = jnp.dot(high, ones, preferred_element_type=jnp.float32) + jnp.dot(
+                low_part, ones, preferred_element_type=jnp.float32
+            )
+            run_sum = run_sum + row_sum.reshape(group_size, rows, HD)
             scaled = (weights * value_scale).astype(jnp.bfloat16).reshape(group_size * rows, rows)
             value_tile = window_ref[slot, 1, :rows, :]
             mixed = jnp.dot(scaled, value_tile, preferred_element_type=jnp.float32)
             acc = acc + mixed.reshape(group_size, rows, HD)
         acc_ref[...] = acc
         max_ref[...] = jnp.broadcast_to(new_max, max_ref.shape)
-        sum_ref[...] = jnp.broadcast_to(run_sum, sum_ref.shape)
+        sum_ref[...] = run_sum
 
     def one_pair(pair, carry):
         nearest = offset + 2 * pair

time: 141 us -> 130 us (0.922)
  Pallas kernels: 43.4 us -> 30.1 us
  waiting for transfers between devices: 29.7 us -> 31.8 us
    pallas_call x3, Pallas kernels: 43.4 us -> 30.1 us  [attend_part(): pl.pallas_call(kernel, out_shape=out_shape, grid_spec=pltpu.PrefetchScala...]
    ppermute x8, waiting for transfers between devices: 25.1 us -> 27.2 us  [shift_from(): return lax.ppermute(x, 'seq', pairs)]
  transfers between devices with their start and end apart: 9 -> 9, of which waited for: 6 -> 6; matrix products, arithmetic and copies ran while one was open for 12% -> 13% of each run, Pallas kernels for 14% -> 13%
where the time goes in v7:
time: 130 us; the launch traced here: 129 us
  starting transfers between devices  42.5 us (33%)
  waiting for transfers between devices  31.8 us (24%)
  Pallas kernels  30.1 us (23%)
  local copies, waits for them, and re-layouts  12.2 us (9%)
  other arithmetic  9.59 us (7%)
  between operations  2.95 us (2%)
    ppermute x8, starting transfers between devices, shift_from(): return lax.ppermute(x, 'seq', pairs)  35.3 us
    pallas_call x3, Pallas kernels, attend_part(): pl.pallas_call(kernel, out_shape=out_shape, grid_spec=pltpu.PrefetchScala...  30.1 us
    ppermute x8, waiting for transfers between devices, shift_from(): return lax.ppermute(x, 'seq', pairs)  27.2 us
    all_to_all x1, starting transfers between devices, shards(): both = lax.all_to_all(both, 'head', split_axis=2, concat_axis=0, tiled=True)  7.1 us
    unnamed x13, local copies, waits for them, and re-layouts  5.08 us
    all_to_all x1, waiting for transfers between devices, shards(): both = lax.all_to_all(both, 'head', split_axis=2, concat_axis=0, tiled=True)  4.6 us
    another operation x3, other arithmetic, shards(): jnp.stack([seq_index.astype(jnp.int32), pairs, low[-1].astype(jnp.int32)])  3.85 us
  transfers between devices with their start and end apart: 9, of which 6 were waited for; matrix products, arithmetic and copies ran while one was open for 13% of the time, Pallas kernels for 13%

profile of v7, /device:TPU:134, one launch (start us, length us, event | category | flops | bytes accessed | tf_op | source)
XLA Modules:
  0.0 129.0 jit_solution(15208962550730238789)
XLA Ops:
  0.0 0.0 copy-start
  0.0 0.8 copy.34
  0.8 0.8 copy.33
  1.6 0.6 copy.29
  2.2 7.1 %all-to-all-start = ((bf16[16,2,8,128]{3,0,1,2:T(8,128)(2,1)}), bf16[16,2,8,128]{3,0,1,2:T(8,128)(2,1)S(1)}, u32[]{:S(2)}, u32[]{:S(2)}) async-start(bf16[16,2,8,128]{3,0,1,2:T(8,128)(2,1)} %copy.29), calls=%async_computation | async-start | bytes 131072 | tf_op jit(solution)/shard_map/all_to_all | solution.py:164
  9.3 0.7 copy.27
  10.1 0.1 reduce-window.9
  10.2 0.1 reduce.4
  10.3 0.7 sub.27
  11.0 0.8 reduce.5
  11.7 0.1 broadcast_in_dim.10
  11.8 0.1 reshape.146
  11.9 0.8 reduce.6
  12.7 0.1 broadcast_in_dim.11
  12.7 0.1 reshape.148
  12.9 0.1 convert_reduce_fusion
  13.0 4.6 %all-to-all-done = bf16[16,2,8,128]{3,0,1,2:T(8,128)(2,1)S(1)} async-done(((bf16[16,2,8,128]{3,0,1,2:T(8,128)(2,1)}), bf16[16,2,8,128]{3,0,1,2:T(8,128)(2,1)S(1)}, u32[]{:S(2)}, u32[]{:S(2)}) %all-to-all-start) | async-done | bytes 65568 | tf_op jit(solution)/shard_map/all_to_all | solution.py:164
  17.6 0.1 copy.31
  17.7 2.8 %collective-permute-start = (bf16[1,2,136,128]{3,2,1,0:T(8,128)(2,1)S(1)}, bf16[1,2,136,128]{3,2,1,0:T(8,128)(2,1)S(1)}, u32[]{:S(2)}, u32[]{:S(2)}) collective-permute-start(bf16[1,2,136,128]{3,2,1,0:T(8,128)(2,1)S(1)} %maximum_bitcast_fusion), channel_id=1, source_target_pairs={{0,8},{8,16},{16,24},{24,32},{32,40},{40,48},{48,56},{56,64},{64,7... | collective-permute-start | bytes 208904 | tf_op jit(solution)/shard_map/ppermute | solution.py:26
  20.6 4.3 %collective-permute-start.1 = (bf16[1,2,136,128]{3,2,1,0:T(8,128)(2,1)S(1)}, bf16[1,2,136,128]{3,2,1,0:T(8,128)(2,1)S(1)}, u32[]{:S(2)}, u32[]{:S(2)}) collective-permute-start(bf16[1,2,136,128]{3,2,1,0:T(8,128)(2,1)S(1)} %maximum_bitcast_fusion), channel_id=1, source_target_pairs={{0,16},{8,24},{16,32},{24,40},{32,48},{40,56},{48,64},{56,72},{64,... | collective-permute-start | bytes 208904 | tf_op jit(solution)/shard_map/ppermute | solution.py:26
  24.8 6.9 %collective-permute-start.2 = (bf16[1,2,136,128]{3,2,1,0:T(8,128)(2,1)S(1)}, bf16[1,2,136,128]{3,2,1,0:T(8,128)(2,1)S(1)}, u32[]{:S(2)}, u32[]{:S(2)}) collective-permute-start(bf16[1,2,136,128]{3,2,1,0:T(8,128)(2,1)S(1)} %maximum_bitcast_fusion), channel_id=1, source_target_pairs={{0,24},{8,32},{16,40},{24,48},{32,56},{40,64},{48,72},{56,80},{64,... | collective-permute-start | bytes 208904 | tf_op jit(solution)/shard_map/ppermute | solution.py:26
  31.8 0.7 constant_dynamic-update-slice_fusion.6
  32.4 0.0 collective-permute-done
  32.4 0.0 collective-permute-done.1
  32.4 1.3 collective-permute-done.2
  33.7 0.0 copy-start.1
  33.8 7.5 %collective-permute-start.3 = (bf16[4,2,136,128]{3,2,1,0:T(8,128)(2,1)S(1)}, bf16[4,2,136,128]{3,2,1,0:T(8,128)(2,1)S(1)}, u32[]{:S(2)}, u32[]{:S(2)}) collective-permute-start(bf16[4,2,136,128]{3,2,1,0:T(8,128)(2,1)S(1)} %pad_maximum_fusion.1.refs_2_), channel_id=1, source_target_pairs={{0,32},{8,40},{16,48},{24,56},{32,64},{40,72},{48,80},{56,88},{64,... | collective-permute-start | bytes 835592 | tf_op jit(solution)/shard_map/ppermute | solution.py:26
  41.3 4.9 %collective-permute-start.4 = (bf16[4,2,136,128]{3,2,1,0:T(8,128)(2,1)S(1)}, bf16[4,2,136,128]{3,2,1,0:T(8,128)(2,1)S(1)}, u32[]{:S(2)}, u32[]{:S(2)}) collective-permute-start(bf16[4,2,136,128]{3,2,1,0:T(8,128)(2,1)S(1)} %pad_maximum_fusion.1.refs_2_), channel_id=1, source_target_pairs={{0,64},{8,72},{16,80},{24,88},{32,96},{40,104},{48,112},{56,120},{... | collective-permute-start | bytes 835592 | tf_op jit(solution)/shard_map/ppermute | solution.py:26
  46.2 1.9 %collective-permute-start.5 = (bf16[4,2,136,128]{3,2,1,0:T(8,128)(2,1)S(1)}, bf16[4,2,136,128]{3,2,1,0:T(8,128)(2,1)S(1)}, u32[]{:S(2)}, u32[]{:S(2)}) collective-permute-start(bf16[4,2,136,128]{3,2,1,0:T(8,128)(2,1)S(1)} %pad_maximum_fusion.1.refs_2_), channel_id=1, source_target_pairs={{0,96},{8,104},{16,112},{24,120},{32,128},{40,136},{48,144},{56,15... | collective-permute-start | bytes 835592 | tf_op jit(solution)/shard_map/ppermute | solution.py:26
  48.1 0.7 constant_dynamic-update-slice_fusion.5
  48.8 0.7 constant_dynamic-update-slice_fusion.4
  49.4 0.6 constant_dynamic-update-slice_fusion.3
  50.1 8.1 %collective-permute-done.3 = bf16[4,2,136,128]{3,2,1,0:T(8,128)(2,1)S(1)} collective-permute-done((bf16[4,2,136,128]{3,2,1,0:T(8,128)(2,1)S(1)}, bf16[4,2,136,128]{3,2,1,0:T(8,128)(2,1)S(1)}, u32[]{:S(2)}, u32[]{:S(2)}) %collective-permute-start.3) | collective-permute-done | bytes 278560 | tf_op jit(solution)/shard_map/ppermute | solution.py:26
  58.2 0.8 constant_dynamic-update-slice_fusion.2
  59.0 8.4 %collective-permute-done.4 = bf16[4,2,136,128]{3,2,1,0:T(8,128)(2,1)S(1)} collective-permute-done((bf16[4,2,136,128]{3,2,1,0:T(8,128)(2,1)S(1)}, bf16[4,2,136,128]{3,2,1,0:T(8,128)(2,1)S(1)}, u32[]{:S(2)}, u32[]{:S(2)}) %collective-permute-start.4) | collective-permute-done | bytes 278560 | tf_op jit(solution)/shard_map/ppermute | solution.py:26
  67.4 0.8 constant_dynamic-update-slice_fusion.1
  68.2 0.0 copy-done.1
  68.2 0.0 copy-start.2
  68.2 3.4 %collective-permute-done.5 = bf16[4,2,136,128]{3,2,1,0:T(8,128)(2,1)S(1)} collective-permute-done((bf16[4,2,136,128]{3,2,1,0:T(8,128)(2,1)S(1)}, bf16[4,2,136,128]{3,2,1,0:T(8,128)(2,1)S(1)}, u32[]{:S(2)}, u32[]{:S(2)}) %collective-permute-start.5) | collective-permute-done | bytes 278560 | tf_op jit(solution)/shard_map/ppermute | solution.py:26
  71.6 0.0 copy-done.2
  71.6 0.7 constant_dynamic-update-slice_fusion
  72.3 5.0 %collective-permute-start.6 = (bf16[16,2,136,128]{3,2,1,0:T(8,128)(2,1)}, bf16[16,2,136,128]{3,2,1,0:T(8,128)(2,1)S(1)}, u32[]{:S(2)}, u32[]{:S(2)}) collective-permute-start(bf16[16,2,136,128]{3,2,1,0:T(8,128)(2,1)} %constant_dynamic-update-slice_fusion), channel_id=1, source_target_pairs={{0,128},{8,136},{16,144},{24,152},{32,160},{40,168},{48,176},{56,1... | collective-permute-start | bytes 3342344 | tf_op jit(solution)/shard_map/ppermute | solution.py:26
  77.4 1.2 gather_fusion
  78.6 0.6 fusion.1
  82.0 1.1 slice.68
  83.1 1.9 %collective-permute-start.7 = (bf16[9,2,136,128]{3,2,1,0:T(8,128)(2,1)S(1)}, bf16[9,2,136,128]{3,2,1,0:T(8,128)(2,1)S(1)}, u32[]{:S(2)}, u32[]{:S(2)}) collective-permute-start(bf16[9,2,136,128]{3,2,1,0:T(8,128)(2,1)S(1)} %slice.68), channel_id=1, source_target_pairs={{0,256},{8,264},{16,272},{24,280},{32,288},{40,296},{48,304},{56,3... | collective-permute-start | bytes 1880072 | tf_op jit(solution)/shard_map/ppermute | solution.py:26
  85.0 1.3 %add_add_fusion.refs_0_ = s32[3]{0:T(128)} fusion(s32[1]{0:T(128)} %bitcast.6, s32[1]{0:T(128)} %get-tuple-element.55, s32[1]{0:T(128)} %bitcast), kind=kLoop, calls=%fused_computation.26 | loop fusion | flops 6 | bytes 24 | tf_op jit(solution)/shard_map/stack | solution.py:198
  86.4 0.1 pad.18.clone
  86.4 1.2 add_add_fusion.1.refs_0_
  87.7 1.3 %add_add_fusion.2.refs_0_ = s32[3]{0:T(128)} fusion(s32[1]{0:T(128)} %bitcast.20, s32[1]{0:T(128)} %get-tuple-element.55, s32[1]{0:T(128)} %bitcast), kind=kLoop, calls=%fused_computation.28 | loop fusion | flops 6 | bytes 24 | tf_op jit(solution)/shard_map/stack | solution.py:198
  89.0 0.0 copy-done
  89.0 0.8 copy_bitcast_fusion
  89.7 0.7 broadcast_in_dim.26.refs_3_
  90.4 5.7 %shard_map.73 = (f32[8,128,128]{2,1,0:T(8,128)}, f32[8,128,128]{2,1,0:T(8,128)}, f32[8,128,128]{2,1,0:T(8,128)}) custom-call(s32[3]{0:T(128)} %add_add_fusion.2.refs_0_, bf16[1024,128]{1,0:T(8,128)(2,1)} %bitcast.48, bf16[4,2,136,128]{3,2,1,0:T(8,128)(2,1)} %copy-done.1, s32[128,128]{1,0:T(8,128)} %broadcast_in_dim.26.refs_3_, f32[1,128]{1,0:T(1,128)} %bitcast.57), custom_call_target="tpu_custom_call" | custom-call | tf_op jit(solution)/shard_map/pallas_call | solution.py:147
  96.1 1.1 pad_maximum_fusion.refs_2_
  97.2 11.6 %shard_map.74 = (f32[8,128,128]{2,1,0:T(8,128)}, f32[8,128,128]{2,1,0:T(8,128)}, f32[8,128,128]{2,1,0:T(8,128)}) custom-call(s32[3]{0:T(128)} %add_add_fusion.1.refs_0_, bf16[1024,128]{1,0:T(8,128)(2,1)} %bitcast.49, bf16[12,2,136,128]{3,2,1,0:T(8,128)(2,1)} %pad_maximum_fusion.refs_2_, s32[128,128]{1,0:T(8,128)} %broadcast_in_dim.26.refs_3_, ...), custom_call_target="tpu_custom_call" | custom-call | tf_op jit(solution)/shard_map/pallas_call | solution.py:147
  108.8 0.0 collective-permute-done.7
  108.8 6.0 %collective-permute-done.6 = bf16[16,2,136,128]{3,2,1,0:T(8,128)(2,1)S(1)} collective-permute-done((bf16[16,2,136,128]{3,2,1,0:T(8,128)(2,1)}, bf16[16,2,136,128]{3,2,1,0:T(8,128)(2,1)S(1)}, u32[]{:S(2)}, u32[]{:S(2)}) %collective-permute-start.6) | collective-permute-done | bytes 1114144 | tf_op jit(solution)/shard_map/ppermute | solution.py:26
  114.8 1.5 %maximum_maximum_fusion.refs_2_ = bf16[26,2,136,128]{3,2,1,0:T(8,128)(2,1)} fusion(bf16[9,2,136,128]{3,2,1,0:T(8,128)(2,1)S(1)} %collective-permute-done.7, bf16[16,2,136,128]{3,2,1,0:T(8,128)(2,1)S(1)} %collective-permute-done.6, bf16[26]{0:T(256)(128)(2,1)S(1)} %pad.18.clone), kind=kLoop, calls=%fused_computation.1 | loop fusion | flops 1810432 | bytes 3551284 | tf_op jit(solution)/shard_map/concatenate | solution.py:196
  116.2 12.8 %shard_map.75 = bf16[128,1024]{1,0:T(8,128)(2,1)} custom-call(s32[3]{0:T(128)} %add_add_fusion.refs_0_, bf16[1024,128]{1,0:T(8,128)(2,1)} %bitcast.50, bf16[26,2,136,128]{3,2,1,0:T(8,128)(2,1)} %maximum_maximum_fusion.refs_2_, s32[128,128]{1,0:T(8,128)} %broadcast_in_dim.26.refs_3_, f32[1,128]{1,0:T(1,128)} %bitcast.59, ...), custom_call_target="tpu_custom_call" | custom-call | tf_op jit(solution)/shard_map/pallas_call | solution.py:147
  (10 shorter events, 0.1 us)
Async XLA Ops:
  0.0 89.0 %copy-start = (bf16[128,1024]{1,0:T(8,128)(2,1)S(1)}, bf16[128,1024]{1,0:T(8,128)(2,1)}, u32[]{:S(2)}) copy-start(bf16[128,1024]{1,0:T(8,128)(2,1)} %param.11) | copy-start | bytes 786436
  2.2 15.3 %all-to-all-start = ((bf16[16,2,8,128]{3,0,1,2:T(8,128)(2,1)}), bf16[16,2,8,128]{3,0,1,2:T(8,128)(2,1)S(1)}, u32[]{:S(2)}, u32[]{:S(2)}) async-start(bf16[16,2,8,128]{3,0,1,2:T(8,128)(2,1)} %copy.29), calls=%async_computation | async-start | bytes 131072 | tf_op jit(solution)/shard_map/all_to_all | solution.py:164
  17.7 14.7 %collective-permute-start = (bf16[1,2,136,128]{3,2,1,0:T(8,128)(2,1)S(1)}, bf16[1,2,136,128]{3,2,1,0:T(8,128)(2,1)S(1)}, u32[]{:S(2)}, u32[]{:S(2)}) collective-permute-start(bf16[1,2,136,128]{3,2,1,0:T(8,128)(2,1)S(1)} %maximum_bitcast_fusion), channel_id=1, source_target_pairs={{0,8},{8,16},{16,24},{24,32},{32,40},{40,48},{48,56},{56,64},{64,7... | collective-permute-start | bytes 208904 | tf_op jit(solution)/shard_map/ppermute | solution.py:26
  20.6 11.9 %collective-permute-start.1 = (bf16[1,2,136,128]{3,2,1,0:T(8,128)(2,1)S(1)}, bf16[1,2,136,128]{3,2,1,0:T(8,128)(2,1)S(1)}, u32[]{:S(2)}, u32[]{:S(2)}) collective-permute-start(bf16[1,2,136,128]{3,2,1,0:T(8,128)(2,1)S(1)} %maximum_bitcast_fusion), channel_id=1, source_target_pairs={{0,16},{8,24},{16,32},{24,40},{32,48},{40,56},{48,64},{56,72},{64,... | collective-permute-start | bytes 208904 | tf_op jit(solution)/shard_map/ppermute | solution.py:26
  24.8 8.9 %collective-permute-start.2 = (bf16[1,2,136,128]{3,2,1,0:T(8,128)(2,1)S(1)}, bf16[1,2,136,128]{3,2,1,0:T(8,128)(2,1)S(1)}, u32[]{:S(2)}, u32[]{:S(2)}) collective-permute-start(bf16[1,2,136,128]{3,2,1,0:T(8,128)(2,1)S(1)} %maximum_bitcast_fusion), channel_id=1, source_target_pairs={{0,24},{8,32},{16,40},{24,48},{32,56},{40,64},{48,72},{56,80},{64,... | collective-permute-start | bytes 208904 | tf_op jit(solution)/shard_map/ppermute | solution.py:26
  33.7 34.4 %copy-start.1 = (bf16[4,2,136,128]{3,2,1,0:T(8,128)(2,1)}, bf16[4,2,136,128]{3,2,1,0:T(8,128)(2,1)S(1)}, u32[]{:S(2)}) copy-start(bf16[4,2,136,128]{3,2,1,0:T(8,128)(2,1)S(1)} %pad_maximum_fusion.1.refs_2_) | copy-start | bytes 835588
  33.8 24.4 %collective-permute-start.3 = (bf16[4,2,136,128]{3,2,1,0:T(8,128)(2,1)S(1)}, bf16[4,2,136,128]{3,2,1,0:T(8,128)(2,1)S(1)}, u32[]{:S(2)}, u32[]{:S(2)}) collective-permute-start(bf16[4,2,136,128]{3,2,1,0:T(8,128)(2,1)S(1)} %pad_maximum_fusion.1.refs_2_), channel_id=1, source_target_pairs={{0,32},{8,40},{16,48},{24,56},{32,64},{40,72},{48,80},{56,88},{64,... | collective-permute-start | bytes 835592 | tf_op jit(solution)/shard_map/ppermute | solution.py:26
  41.3 26.1 %collective-permute-start.4 = (bf16[4,2,136,128]{3,2,1,0:T(8,128)(2,1)S(1)}, bf16[4,2,136,128]{3,2,1,0:T(8,128)(2,1)S(1)}, u32[]{:S(2)}, u32[]{:S(2)}) collective-permute-start(bf16[4,2,136,128]{3,2,1,0:T(8,128)(2,1)S(1)} %pad_maximum_fusion.1.refs_2_), channel_id=1, source_target_pairs={{0,64},{8,72},{16,80},{24,88},{32,96},{40,104},{48,112},{56,120},{... | collective-permute-start | bytes 835592 | tf_op jit(solution)/shard_map/ppermute | solution.py:26
  46.2 25.4 %collective-permute-start.5 = (bf16[4,2,136,128]{3,2,1,0:T(8,128)(2,1)S(1)}, bf16[4,2,136,128]{3,2,1,0:T(8,128)(2,1)S(1)}, u32[]{:S(2)}, u32[]{:S(2)}) collective-permute-start(bf16[4,2,136,128]{3,2,1,0:T(8,128)(2,1)S(1)} %pad_maximum_fusion.1.refs_2_), channel_id=1, source_target_pairs={{0,96},{8,104},{16,112},{24,120},{32,128},{40,136},{48,144},{56,15... | collective-permute-start | bytes 835592 | tf_op jit(solution)/shard_map/ppermute | solution.py:26
  68.2 3.4 %copy-start.2 = (bf16[12,2,136,128]{3,2,1,0:T(8,128)(2,1)}, bf16[12,2,136,128]{3,2,1,0:T(8,128)(2,1)S(1)}, u32[]{:S(2)}) copy-start(bf16[12,2,136,128]{3,2,1,0:T(8,128)(2,1)S(1)} %get-tuple-element.42) | copy-start | bytes 2506756
  72.3 42.5 %collective-permute-start.6 = (bf16[16,2,136,128]{3,2,1,0:T(8,128)(2,1)}, bf16[16,2,136,128]{3,2,1,0:T(8,128)(2,1)S(1)}, u32[]{:S(2)}, u32[]{:S(2)}) collective-permute-start(bf16[16,2,136,128]{3,2,1,0:T(8,128)(2,1)} %constant_dynamic-update-slice_fusion), channel_id=1, source_target_pairs={{0,128},{8,136},{16,144},{24,152},{32,160},{40,168},{48,176},{56,1... | collective-permute-start | bytes 3342344 | tf_op jit(solution)/shard_map/ppermute | solution.py:26
  83.1 25.7 %collective-permute-start.7 = (bf16[9,2,136,128]{3,2,1,0:T(8,128)(2,1)S(1)}, bf16[9,2,136,128]{3,2,1,0:T(8,128)(2,1)S(1)}, u32[]{:S(2)}, u32[]{:S(2)}) collective-permute-start(bf16[9,2,136,128]{3,2,1,0:T(8,128)(2,1)S(1)} %slice.68), channel_id=1, source_target_pairs={{0,256},{8,264},{16,272},{24,280},{32,288},{40,296},{48,304},{56,3... | collective-permute-start | bytes 1880072 | tf_op jit(solution)/shard_map/ppermute | solution.py:26

commit v8 on v5

--- a/solution.py
+++ b/solution.py
@@ -26,21 +26,23 @@
     return lax.ppermute(x, "seq", pairs)
 
 
-def gather_stages(packet, count, depth):
-    held = packet[None]
-    stages = [held]
-    for width, shifts in ((1, (1, 2, 3)), (4, (4, 8, 12)), (16, (16, 32))):
-        parts = []
-        for offset in shifts:
-            need = min(width, depth - offset)
-            if need > 0:
-                parts.append(shift_from(held[:need], offset, count))
-        stages.append(parts)
-        held = jnp.concatenate([held] + parts, axis=0)
-    return stages
-
-
-def attention_kernel(first, last, offset, *refs):
+def gather_chunks(packet, count, depth):
+    first = jnp.concatenate(
+        [packet[None]] + [shift_from(packet[None], offset, count) for offset in (1, 2, 3)], axis=0
+    )
+    near = [shift_from(first, offset, count) for offset in (4, 8, 12)]
+    far = [shift_from(first, offset, count) for offset in (16, 32)]
+    block = jnp.concatenate([first] + near, axis=0)
+    last = [shift_from(block[4:], 16, count), shift_from(block[4:depth - 32], 32, count)]
+    pad = jnp.zeros((1,) + packet.shape, packet.dtype)
+    return [
+        (first, ((0, 0),)),
+        (jnp.concatenate(near + far, axis=0), ((0, 4), (16, 16))),
+        (jnp.concatenate(last + [pad], axis=0), ((0, 20), (12, 24))),
+    ]
+
+
+def attention_kernel(first, last, segments, *refs):
     info_ref, query_ref, window_ref, low_ref, mean_ref = refs[:5]
     rest = refs[5:]
     if not first:
@@ -56,7 +58,7 @@
     group_size, rows, _ = acc_ref.shape
     inv_scale = 1.0 / math.sqrt(HD)
     seq_index = info_ref[0]
-    pairs = info_ref[1]
+    used = info_ref[1]
     if first:
         max_ref[...] = jnp.full(max_ref.shape, NEG, jnp.float32)
         sum_ref[...] = jnp.zeros(sum_ref.shape, jnp.float32)
@@ -72,7 +74,7 @@
 
     low_top = info_ref[2]
 
-    def fold_pair(pair, masked):
+    def fold_pair(pair, shift, masked):
         parts = []
         for half in range(2):
             slot = 2 * pair + half
@@ -83,7 +85,7 @@
             scores = scores.reshape(group_size, rows, rows) * key_scale[None]
             allowed = None
             if masked:
-                key_pos = (seq_index - offset - slot) * rows + lane
+                key_pos = (seq_index - shift - slot) * rows + lane
                 allowed = ((key_pos <= query_pos) & (key_pos >= low))[None]
                 scores = jnp.where(allowed, scores, NEG)
             parts.append((scores, allowed, value_scale[None], slot))
@@ -108,12 +110,23 @@
         sum_ref[...] = jnp.broadcast_to(run_sum, sum_ref.shape)
 
     def one_pair(pair, carry):
-        nearest = offset + 2 * pair
+        shift = jnp.int32(segments[0][1])
+        for begin, moved in segments[1:]:
+            shift = jnp.where(2 * pair >= begin, jnp.int32(moved), shift)
+        nearest = shift + 2 * pair
         inside = (nearest >= 1) & ((seq_index - nearest - 1) * rows >= low_top)
-        lax.cond(inside, lambda: fold_pair(pair, False), lambda: fold_pair(pair, True))
+        branch = jnp.where(nearest >= used, 0, jnp.where(inside, 1, 2))
+        lax.switch(
+            branch,
+            [
+                lambda: None,
+                lambda: fold_pair(pair, shift, False),
+                lambda: fold_pair(pair, shift, True),
+            ],
+        )
         return carry
 
-    lax.fori_loop(0, pairs, one_pair, 0)
+    lax.fori_loop(0, window_ref.shape[0] // 2, one_pair, 0)
     if last:
         result = acc_ref[...] / sum_ref[...] + mean_ref[...][None]
         for g in range(group_size):
@@ -124,7 +137,7 @@
         acc_out[...] = acc_ref[...]
 
 
-def attend_part(info, query_all, window, low, mean, state, offset, last, width):
+def attend_part(info, query_all, window, low, mean, state, segments, last, width):
     group_size = query_all.shape[0] // HD
     rows = low.shape[0]
     full = lambda shape: pl.BlockSpec(shape, lambda i, info: (0,) * len(shape))
@@ -136,7 +149,7 @@
     else:
         out_shape = (state_shape,) * 3
         out_specs = (full(state_shape.shape),) * 3
-    kernel = functools.partial(attention_kernel, state is None, last, offset)
+    kernel = functools.partial(attention_kernel, state is None, last, segments)
     return pl.pallas_call(
         kernel,
         out_shape=out_shape,
@@ -169,31 +182,20 @@
     scale_rows = jnp.zeros((2, pad_rows, row_count), jnp.bfloat16)
     scale_rows = scale_rows.at[0, 0].set(key_scale_row).at[1, 0].set(value_scale_row)
     packet = jnp.concatenate([jnp.stack([local_keys.T, local_values]), scale_rows], axis=1)
-    stages = gather_stages(packet, seq_count, depth)
+    chunks = gather_chunks(packet, seq_count, depth)
     own_pos = seq_index * row_count + jnp.arange(row_count, dtype=jnp.int32)
     low = starts[doc_index(own_pos, starts)]
     used = jnp.clip(seq_index - low[0] // row_count + 1, 1, depth).astype(jnp.int32)
     low_tile = jnp.broadcast_to(low[:, None], (row_count, row_count)).astype(jnp.int32)
     mean = value_means.reshape(1, HD)
     query_all = queries.reshape(row_count, group_size, HD).transpose(1, 0, 2).reshape(-1, HD)
-    chunks = [
-        jnp.concatenate([stages[0]] + stages[1], axis=0),
-        jnp.concatenate(stages[2], axis=0),
-        jnp.concatenate(stages[3], axis=0),
-    ]
+    info = jnp.stack([seq_index.astype(jnp.int32), used, low[-1].astype(jnp.int32)])
     state = None
-    offset = 0
-    for index, chunk in enumerate(chunks):
-        slots = chunk.shape[0]
-        if slots % 2:
-            chunk = jnp.concatenate([chunk, jnp.zeros((1,) + chunk.shape[1:], chunk.dtype)])
-        pairs = jnp.clip((used - offset + 1) // 2, 0, chunk.shape[0] // 2).astype(jnp.int32)
-        info = jnp.stack([seq_index.astype(jnp.int32), pairs, low[-1].astype(jnp.int32)])
+    for index, (chunk, segments) in enumerate(chunks):
         last = index == len(chunks) - 1
         state = attend_part(
-            info, query_all, chunk, low_tile, mean, state, offset, last, queries.shape[1]
+            info, query_all, chunk, low_tile, mean, state, segments, last, queries.shape[1]
         )
-        offset += slots
     return state
 
 

time: 141 us -> 156 us (1.11)
  waiting for transfers between devices: 29.7 us -> 44.3 us
  starting transfers between devices: 42.5 us -> 49.8 us
  Pallas kernels: 43.4 us -> 41 us
  other arithmetic: 9.59 us -> 7.21 us
  local copies, waits for them, and re-layouts: 12.2 us -> 10 us
    ppermute x8 -> x10, waiting for transfers between devices: 25.1 us -> 39.7 us  [shift_from(): return lax.ppermute(x, 'seq', pairs)]
    ppermute x8 -> x10, starting transfers between devices: 35.3 us -> 42.7 us  [shift_from(): return lax.ppermute(x, 'seq', pairs)]
    another operation x5 -> x3, other arithmetic: 4.05 us -> 1.42 us  [the longest x1 1.22 us: shards(): jnp.stack([seq_index.astype(jnp.int32), used, low[-1].astype(jnp.int32)])]
    pallas_call x3, Pallas kernels: 43.4 us -> 41 us  [attend_part(): pl.pallas_call(kernel, out_shape=out_shape, grid_spec=pltpu.PrefetchScala...]
    unnamed x13 -> x12, local copies, waits for them, and re-layouts: 5.08 us -> 3.78 us
    concatenate x3 -> x4, other arithmetic: 2.54 us -> 3.44 us  [the longest x1 2.37 us: gather_chunks(): jnp.concatenate(last + [pad], axis=0)]
  transfers between devices with their start and end apart: 9 -> 11, of which waited for: 6 -> 6; matrix products, arithmetic and copies ran while one was open for 12% -> 7% of each run, Pallas kernels for 14% -> 17%
where the time goes in v8:
time: 156 us; the launch traced here: 155 us
  starting transfers between devices  49.8 us (32%)
  waiting for transfers between devices  44.3 us (28%)
  Pallas kernels  41 us (26%)
  local copies, waits for them, and re-layouts  10 us (6%)
  other arithmetic  7.21 us (5%)
  between operations  2.84 us (2%)
    ppermute x10, starting transfers between devices, shift_from(): return lax.ppermute(x, 'seq', pairs)  42.7 us
    pallas_call x3, Pallas kernels, attend_part(): pl.pallas_call(kernel, out_shape=out_shape, grid_spec=pltpu.PrefetchScala...  41 us
    ppermute x10, waiting for transfers between devices, shift_from(): return lax.ppermute(x, 'seq', pairs)  39.7 us
    all_to_all x1, starting transfers between devices, shards(): both = lax.all_to_all(both, 'head', split_axis=2, concat_axis=0, tiled=True)  7.1 us
    all_to_all x1, waiting for transfers between devices, shards(): both = lax.all_to_all(both, 'head', split_axis=2, concat_axis=0, tiled=True)  4.6 us
    unnamed x12, local copies, waits for them, and re-layouts  3.78 us
  transfers between devices with their start and end apart: 11, of which 6 were waited for; matrix products, arithmetic and copies ran while one was open for 7% of the time, Pallas kernels for 17%

profile of v8, /device:TPU:134, one launch (start us, length us, event | category | flops | bytes accessed | tf_op | source)
XLA Modules:
  0.0 155.1 jit_solution(3761791486226404621)
XLA Ops:
  0.0 0.0 copy-start
  0.0 0.8 copy.33
  0.8 0.8 copy.34
  1.6 0.6 copy.29
  2.2 7.1 %all-to-all-start = ((bf16[16,2,8,128]{3,0,1,2:T(8,128)(2,1)}), bf16[16,2,8,128]{3,0,1,2:T(8,128)(2,1)S(1)}, u32[]{:S(2)}, u32[]{:S(2)}) async-start(bf16[16,2,8,128]{3,0,1,2:T(8,128)(2,1)} %copy.29), calls=%async_computation | async-start | bytes 131072 | tf_op jit(solution)/shard_map/all_to_all | solution.py:170
  9.3 0.8 reduce.5
  10.1 0.1 broadcast_in_dim.10
  10.2 0.1 reshape.146
  10.3 0.8 reduce.6
  11.0 0.1 broadcast_in_dim.11
  11.1 0.1 reshape.148
  11.2 0.7 copy.27
  12.0 0.1 reduce-window.9
  12.1 0.1 reduce.4
  12.2 0.7 sub.16
  12.9 0.1 convert_reduce_fusion
  13.0 4.6 %all-to-all-done = bf16[16,2,8,128]{3,0,1,2:T(8,128)(2,1)S(1)} async-done(((bf16[16,2,8,128]{3,0,1,2:T(8,128)(2,1)}), bf16[16,2,8,128]{3,0,1,2:T(8,128)(2,1)S(1)}, u32[]{:S(2)}, u32[]{:S(2)}) %all-to-all-start) | async-done | bytes 65568 | tf_op jit(solution)/shard_map/all_to_all | solution.py:170
  17.6 0.1 copy.31
  17.7 2.8 %collective-permute-start = (bf16[1,2,136,128]{3,2,1,0:T(8,128)(2,1)S(1)}, bf16[1,2,136,128]{3,2,1,0:T(8,128)(2,1)S(1)}, u32[]{:S(2)}, u32[]{:S(2)}) collective-permute-start(bf16[1,2,136,128]{3,2,1,0:T(8,128)(2,1)S(1)} %maximum_bitcast_fusion), channel_id=1, source_target_pairs={{0,8},{8,16},{16,24},{24,32},{32,40},{40,48},{48,56},{56,64},{64,7... | collective-permute-start | bytes 208904 | tf_op jit(solution)/shard_map/ppermute | solution.py:26
  20.6 4.3 %collective-permute-start.1 = (bf16[1,2,136,128]{3,2,1,0:T(8,128)(2,1)S(1)}, bf16[1,2,136,128]{3,2,1,0:T(8,128)(2,1)S(1)}, u32[]{:S(2)}, u32[]{:S(2)}) collective-permute-start(bf16[1,2,136,128]{3,2,1,0:T(8,128)(2,1)S(1)} %maximum_bitcast_fusion), channel_id=1, source_target_pairs={{0,16},{8,24},{16,32},{24,40},{32,48},{40,56},{48,64},{56,72},{64,... | collective-permute-start | bytes 208904 | tf_op jit(solution)/shard_map/ppermute | solution.py:26
  24.8 6.9 %collective-permute-start.2 = (bf16[1,2,136,128]{3,2,1,0:T(8,128)(2,1)S(1)}, bf16[1,2,136,128]{3,2,1,0:T(8,128)(2,1)S(1)}, u32[]{:S(2)}, u32[]{:S(2)}) collective-permute-start(bf16[1,2,136,128]{3,2,1,0:T(8,128)(2,1)S(1)} %maximum_bitcast_fusion), channel_id=1, source_target_pairs={{0,24},{8,32},{16,40},{24,48},{32,56},{40,64},{48,72},{56,80},{64,... | collective-permute-start | bytes 208904 | tf_op jit(solution)/shard_map/ppermute | solution.py:26
  31.8 0.0 collective-permute-done
  31.8 0.0 collective-permute-done.1
  31.8 1.9 %collective-permute-done.2 = bf16[1,2,136,128]{3,2,1,0:T(8,128)(2,1)S(1)} collective-permute-done((bf16[1,2,136,128]{3,2,1,0:T(8,128)(2,1)S(1)}, bf16[1,2,136,128]{3,2,1,0:T(8,128)(2,1)S(1)}, u32[]{:S(2)}, u32[]{:S(2)}) %collective-permute-start.2) | collective-permute-done | bytes 69664 | tf_op jit(solution)/shard_map/ppermute | solution.py:26
  33.7 0.0 copy-start.2
  33.8 7.5 %collective-permute-start.3 = (bf16[4,2,136,128]{3,2,1,0:T(8,128)(2,1)S(1)}, bf16[4,2,136,128]{3,2,1,0:T(8,128)(2,1)S(1)}, u32[]{:S(2)}, u32[]{:S(2)}) collective-permute-start(bf16[4,2,136,128]{3,2,1,0:T(8,128)(2,1)S(1)} %pad_maximum_fusion.2.refs_2_), channel_id=1, source_target_pairs={{0,32},{8,40},{16,48},{24,56},{32,64},{40,72},{48,80},{56,88},{64,... | collective-permute-start | bytes 835592 | tf_op jit(solution)/shard_map/ppermute | solution.py:26
  41.3 4.9 %collective-permute-start.4 = (bf16[4,2,136,128]{3,2,1,0:T(8,128)(2,1)S(1)}, bf16[4,2,136,128]{3,2,1,0:T(8,128)(2,1)S(1)}, u32[]{:S(2)}, u32[]{:S(2)}) collective-permute-start(bf16[4,2,136,128]{3,2,1,0:T(8,128)(2,1)S(1)} %pad_maximum_fusion.2.refs_2_), channel_id=1, source_target_pairs={{0,64},{8,72},{16,80},{24,88},{32,96},{40,104},{48,112},{56,120},{... | collective-permute-start | bytes 835592 | tf_op jit(solution)/shard_map/ppermute | solution.py:26
  46.2 1.9 %collective-permute-start.5 = (bf16[4,2,136,128]{3,2,1,0:T(8,128)(2,1)S(1)}, bf16[4,2,136,128]{3,2,1,0:T(8,128)(2,1)S(1)}, u32[]{:S(2)}, u32[]{:S(2)}) collective-permute-start(bf16[4,2,136,128]{3,2,1,0:T(8,128)(2,1)S(1)} %pad_maximum_fusion.2.refs_2_), channel_id=1, source_target_pairs={{0,96},{8,104},{16,112},{24,120},{32,128},{40,136},{48,144},{56,15... | collective-permute-start | bytes 835592 | tf_op jit(solution)/shard_map/ppermute | solution.py:26
  48.1 1.2 gather_fusion
  49.4 0.0 copy-done
  49.4 0.8 copy_bitcast_fusion
  50.1 8.1 %collective-permute-done.3 = bf16[4,2,136,128]{3,2,1,0:T(8,128)(2,1)S(1)} collective-permute-done((bf16[4,2,136,128]{3,2,1,0:T(8,128)(2,1)S(1)}, bf16[4,2,136,128]{3,2,1,0:T(8,128)(2,1)S(1)}, u32[]{:S(2)}, u32[]{:S(2)}) %collective-permute-start.3) | collective-permute-done | bytes 278560 | tf_op jit(solution)/shard_map/ppermute | solution.py:26
  58.2 9.2 %collective-permute-done.4 = bf16[4,2,136,128]{3,2,1,0:T(8,128)(2,1)S(1)} collective-permute-done((bf16[4,2,136,128]{3,2,1,0:T(8,128)(2,1)S(1)}, bf16[4,2,136,128]{3,2,1,0:T(8,128)(2,1)S(1)}, u32[]{:S(2)}, u32[]{:S(2)}) %collective-permute-start.4) | collective-permute-done | bytes 278560 | tf_op jit(solution)/shard_map/ppermute | solution.py:26
  67.4 4.2 %collective-permute-done.5 = bf16[4,2,136,128]{3,2,1,0:T(8,128)(2,1)S(1)} collective-permute-done((bf16[4,2,136,128]{3,2,1,0:T(8,128)(2,1)S(1)}, bf16[4,2,136,128]{3,2,1,0:T(8,128)(2,1)S(1)}, u32[]{:S(2)}, u32[]{:S(2)}) %collective-permute-start.5) | collective-permute-done | bytes 278560 | tf_op jit(solution)/shard_map/ppermute | solution.py:26
  71.6 1.0 pad_maximum_fusion
  72.6 5.0 %collective-permute-start.6 = (bf16[12,2,136,128]{3,2,1,0:T(8,128)(2,1)}, bf16[12,2,136,128]{3,2,1,0:T(8,128)(2,1)}, u32[]{:S(2)}, u32[]{:S(2)}) collective-permute-start(bf16[12,2,136,128]{3,2,1,0:T(8,128)(2,1)} %pad_maximum_fusion), channel_id=1, source_target_pairs={{0,128},{8,136},{16,144},{24,152},{32,160},{40,168},{48,176},{56,1... | collective-permute-start | bytes 2506760 | tf_op jit(solution)/shard_map/ppermute | solution.py:26
  77.6 0.6 fusion.1
  80.9 0.1 pad.9.clone
  80.9 1.2 pad_add_fusion.refs_0_
  82.2 1.9 %collective-permute-start.8 = (bf16[4,2,136,128]{3,2,1,0:T(8,128)(2,1)S(1)}, bf16[4,2,136,128]{3,2,1,0:T(8,128)(2,1)}, u32[]{:S(2)}, u32[]{:S(2)}) collective-permute-start(bf16[4,2,136,128]{3,2,1,0:T(8,128)(2,1)S(1)} %pad_maximum_fusion.2.refs_2_), channel_id=1, source_target_pairs={{0,128},{8,136},{16,144},{24,152},{32,160},{40,168},{48,176},{56,1... | collective-permute-start | bytes 835592 | tf_op jit(solution)/shard_map/ppermute | solution.py:26
  84.1 2.9 %collective-permute-start.9 = (bf16[4,2,136,128]{3,2,1,0:T(8,128)(2,1)S(1)}, bf16[4,2,136,128]{3,2,1,0:T(8,128)(2,1)}, u32[]{:S(2)}, u32[]{:S(2)}) collective-permute-start(bf16[4,2,136,128]{3,2,1,0:T(8,128)(2,1)S(1)} %pad_maximum_fusion.2.refs_2_), channel_id=1, source_target_pairs={{0,256},{8,264},{16,272},{24,280},{32,288},{40,296},{48,304},{56,3... | collective-permute-start | bytes 835592 | tf_op jit(solution)/shard_map/ppermute | solution.py:26
  86.9 0.7 broadcast_in_dim.14.refs_3_
  87.6 0.0 copy-done.2
  87.6 6.3 %shard_map.73 = (f32[8,128,128]{2,1,0:T(8,128)}, f32[8,128,128]{2,1,0:T(8,128)}, f32[8,128,128]{2,1,0:T(8,128)}) custom-call(s32[3]{0:T(128)} %pad_add_fusion.refs_0_, bf16[1024,128]{1,0:T(8,128)(2,1)} %bitcast.42, bf16[4,2,136,128]{3,2,1,0:T(8,128)(2,1)} %copy-done.2, s32[128,128]{1,0:T(8,128)} %broadcast_in_dim.14.refs_3_, f32[1,128]{1,0:T(1,128)} %bitcast.51), custom_call_target="tpu_custom_call" | custom-call | tf_op jit(solution)/shard_map/pallas_call | solution.py:153
  93.9 4.5 %collective-permute-start.7 = (bf16[5,2,136,128]{3,2,1,0:T(8,128)(2,1)S(1)}, bf16[5,2,136,128]{3,2,1,0:T(8,128)(2,1)S(1)}, u32[]{:S(2)}, u32[]{:S(2)}) collective-permute-start(bf16[5,2,136,128]{3,2,1,0:T(8,128)(2,1)S(1)} %pad_maximum_fusion.1), channel_id=1, source_target_pairs={{0,256},{8,264},{16,272},{24,280},{32,288},{40,296},{48,304},{56,3... | collective-permute-start | bytes 1044488 | tf_op jit(solution)/shard_map/ppermute | solution.py:26
  98.5 16.4 %collective-permute-done.8 = bf16[4,2,136,128]{3,2,1,0:T(8,128)(2,1)} collective-permute-done((bf16[4,2,136,128]{3,2,1,0:T(8,128)(2,1)S(1)}, bf16[4,2,136,128]{3,2,1,0:T(8,128)(2,1)}, u32[]{:S(2)}, u32[]{:S(2)}) %collective-permute-start.8) | collective-permute-done | bytes 278560 | tf_op jit(solution)/shard_map/ppermute | solution.py:26
  114.9 1.0 constant_dynamic-update-slice_fusion.1
  115.9 0.0 collective-permute-done.9
  115.9 1.0 constant_dynamic-update-slice_fusion.refs_2_
  116.9 0.0 copy-start.1
  116.9 1.1 copy-done.1
  118.0 20.0 %shard_map.74 = (f32[8,128,128]{2,1,0:T(8,128)}, f32[8,128,128]{2,1,0:T(8,128)}, f32[8,128,128]{2,1,0:T(8,128)}) custom-call(s32[3]{0:T(128)} %pad_add_fusion.refs_0_, bf16[1024,128]{1,0:T(8,128)(2,1)} %bitcast.43, bf16[20,2,136,128]{3,2,1,0:T(8,128)(2,1)} %copy-done.1, s32[128,128]{1,0:T(8,128)} %broadcast_in_dim.14.refs_3_, f32[1,128]{1,0:T(1,128)} %bitcast.52, ...), custom_call_target="tpu_custom_call" | custom-call | tf_op jit(solution)/shard_map/pallas_call | solution.py:153
  138.0 0.0 collective-permute-done.7
  138.0 0.0 collective-permute-done.6
  138.0 2.4 %maximum_maximum_fusion.refs_2_ = bf16[18,2,136,128]{3,2,1,0:T(8,128)(2,1)} fusion(bf16[5,2,136,128]{3,2,1,0:T(8,128)(2,1)S(1)} %collective-permute-done.7, bf16[12,2,136,128]{3,2,1,0:T(8,128)(2,1)} %collective-permute-done.6, bf16[18]{0:T(256)(128)(2,1)S(1)} %pad.9.clone), kind=kLoop, calls=%fused_computation.1 | loop fusion | flops 1253376 | bytes 2437156 | tf_op jit(solution)/shard_map/concatenate | solution.py:41
  140.4 14.7 %shard_map.75 = bf16[128,1024]{1,0:T(8,128)(2,1)} custom-call(s32[3]{0:T(128)} %pad_add_fusion.refs_0_, bf16[1024,128]{1,0:T(8,128)(2,1)} %bitcast.44, bf16[18,2,136,128]{3,2,1,0:T(8,128)(2,1)} %maximum_maximum_fusion.refs_2_, s32[128,128]{1,0:T(8,128)} %broadcast_in_dim.14.refs_3_, f32[1,128]{1,0:T(1,128)} %bitcast.53, ...), custom_call_target="tpu_custom_call" | custom-call | tf_op jit(solution)/shard_map/pallas_call | solution.py:153
  (14 shorter events, 0.2 us)
Async XLA Ops:
  0.0 49.4 %copy-start = (bf16[128,1024]{1,0:T(8,128)(2,1)S(1)}, bf16[128,1024]{1,0:T(8,128)(2,1)}, u32[]{:S(2)}) copy-start(bf16[128,1024]{1,0:T(8,128)(2,1)} %param.11) | copy-start | bytes 786436
  2.2 15.3 %all-to-all-start = ((bf16[16,2,8,128]{3,0,1,2:T(8,128)(2,1)}), bf16[16,2,8,128]{3,0,1,2:T(8,128)(2,1)S(1)}, u32[]{:S(2)}, u32[]{:S(2)}) async-start(bf16[16,2,8,128]{3,0,1,2:T(8,128)(2,1)} %copy.29), calls=%async_computation | async-start | bytes 131072 | tf_op jit(solution)/shard_map/all_to_all | solution.py:170
  17.7 14.1 %collective-permute-start = (bf16[1,2,136,128]{3,2,1,0:T(8,128)(2,1)S(1)}, bf16[1,2,136,128]{3,2,1,0:T(8,128)(2,1)S(1)}, u32[]{:S(2)}, u32[]{:S(2)}) collective-permute-start(bf16[1,2,136,128]{3,2,1,0:T(8,128)(2,1)S(1)} %maximum_bitcast_fusion), channel_id=1, source_target_pairs={{0,8},{8,16},{16,24},{24,32},{32,40},{40,48},{48,56},{56,64},{64,7... | collective-permute-start | bytes 208904 | tf_op jit(solution)/shard_map/ppermute | solution.py:26
  20.6 11.2 %collective-permute-start.1 = (bf16[1,2,136,128]{3,2,1,0:T(8,128)(2,1)S(1)}, bf16[1,2,136,128]{3,2,1,0:T(8,128)(2,1)S(1)}, u32[]{:S(2)}, u32[]{:S(2)}) collective-permute-start(bf16[1,2,136,128]{3,2,1,0:T(8,128)(2,1)S(1)} %maximum_bitcast_fusion), channel_id=1, source_target_pairs={{0,16},{8,24},{16,32},{24,40},{32,48},{40,56},{48,64},{56,72},{64,... | collective-permute-start | bytes 208904 | tf_op jit(solution)/shard_map/ppermute | solution.py:26
  24.8 8.9 %collective-permute-start.2 = (bf16[1,2,136,128]{3,2,1,0:T(8,128)(2,1)S(1)}, bf16[1,2,136,128]{3,2,1,0:T(8,128)(2,1)S(1)}, u32[]{:S(2)}, u32[]{:S(2)}) collective-permute-start(bf16[1,2,136,128]{3,2,1,0:T(8,128)(2,1)S(1)} %maximum_bitcast_fusion), channel_id=1, source_target_pairs={{0,24},{8,32},{16,40},{24,48},{32,56},{40,64},{48,72},{56,80},{64,... | collective-permute-start | bytes 208904 | tf_op jit(solution)/shard_map/ppermute | solution.py:26
  33.7 53.9 %copy-start.2 = (bf16[4,2,136,128]{3,2,1,0:T(8,128)(2,1)}, bf16[4,2,136,128]{3,2,1,0:T(8,128)(2,1)S(1)}, u32[]{:S(2)}) copy-start(bf16[4,2,136,128]{3,2,1,0:T(8,128)(2,1)S(1)} %pad_maximum_fusion.2.refs_2_) | copy-start | bytes 835588
  33.8 24.4 %collective-permute-start.3 = (bf16[4,2,136,128]{3,2,1,0:T(8,128)(2,1)S(1)}, bf16[4,2,136,128]{3,2,1,0:T(8,128)(2,1)S(1)}, u32[]{:S(2)}, u32[]{:S(2)}) collective-permute-start(bf16[4,2,136,128]{3,2,1,0:T(8,128)(2,1)S(1)} %pad_maximum_fusion.2.refs_2_), channel_id=1, source_target_pairs={{0,32},{8,40},{16,48},{24,56},{32,64},{40,72},{48,80},{56,88},{64,... | collective-permute-start | bytes 835592 | tf_op jit(solution)/shard_map/ppermute | solution.py:26
  41.3 26.1 %collective-permute-start.4 = (bf16[4,2,136,128]{3,2,1,0:T(8,128)(2,1)S(1)}, bf16[4,2,136,128]{3,2,1,0:T(8,128)(2,1)S(1)}, u32[]{:S(2)}, u32[]{:S(2)}) collective-permute-start(bf16[4,2,136,128]{3,2,1,0:T(8,128)(2,1)S(1)} %pad_maximum_fusion.2.refs_2_), channel_id=1, source_target_pairs={{0,64},{8,72},{16,80},{24,88},{32,96},{40,104},{48,112},{56,120},{... | collective-permute-start | bytes 835592 | tf_op jit(solution)/shard_map/ppermute | solution.py:26
  46.2 25.4 %collective-permute-start.5 = (bf16[4,2,136,128]{3,2,1,0:T(8,128)(2,1)S(1)}, bf16[4,2,136,128]{3,2,1,0:T(8,128)(2,1)S(1)}, u32[]{:S(2)}, u32[]{:S(2)}) collective-permute-start(bf16[4,2,136,128]{3,2,1,0:T(8,128)(2,1)S(1)} %pad_maximum_fusion.2.refs_2_), channel_id=1, source_target_pairs={{0,96},{8,104},{16,112},{24,120},{32,128},{40,136},{48,144},{56,15... | collective-permute-start | bytes 835592 | tf_op jit(solution)/shard_map/ppermute | solution.py:26
  72.6 65.5 %collective-permute-start.6 = (bf16[12,2,136,128]{3,2,1,0:T(8,128)(2,1)}, bf16[12,2,136,128]{3,2,1,0:T(8,128)(2,1)}, u32[]{:S(2)}, u32[]{:S(2)}) collective-permute-start(bf16[12,2,136,128]{3,2,1,0:T(8,128)(2,1)} %pad_maximum_fusion), channel_id=1, source_target_pairs={{0,128},{8,136},{16,144},{24,152},{32,160},{40,168},{48,176},{56,1... | collective-permute-start | bytes 2506760 | tf_op jit(solution)/shard_map/ppermute | solution.py:26
  82.2 32.8 %collective-permute-start.8 = (bf16[4,2,136,128]{3,2,1,0:T(8,128)(2,1)S(1)}, bf16[4,2,136,128]{3,2,1,0:T(8,128)(2,1)}, u32[]{:S(2)}, u32[]{:S(2)}) collective-permute-start(bf16[4,2,136,128]{3,2,1,0:T(8,128)(2,1)S(1)} %pad_maximum_fusion.2.refs_2_), channel_id=1, source_target_pairs={{0,128},{8,136},{16,144},{24,152},{32,160},{40,168},{48,176},{56,1... | collective-permute-start | bytes 835592 | tf_op jit(solution)/shard_map/ppermute | solution.py:26
  84.1 31.9 %collective-permute-start.9 = (bf16[4,2,136,128]{3,2,1,0:T(8,128)(2,1)S(1)}, bf16[4,2,136,128]{3,2,1,0:T(8,128)(2,1)}, u32[]{:S(2)}, u32[]{:S(2)}) collective-permute-start(bf16[4,2,136,128]{3,2,1,0:T(8,128)(2,1)S(1)} %pad_maximum_fusion.2.refs_2_), channel_id=1, source_target_pairs={{0,256},{8,264},{16,272},{24,280},{32,288},{40,296},{48,304},{56,3... | collective-permute-start | bytes 835592 | tf_op jit(solution)/shard_map/ppermute | solution.py:26
  93.9 44.1 %collective-permute-start.7 = (bf16[5,2,136,128]{3,2,1,0:T(8,128)(2,1)S(1)}, bf16[5,2,136,128]{3,2,1,0:T(8,128)(2,1)S(1)}, u32[]{:S(2)}, u32[]{:S(2)}) collective-permute-start(bf16[5,2,136,128]{3,2,1,0:T(8,128)(2,1)S(1)} %pad_maximum_fusion.1), channel_id=1, source_target_pairs={{0,256},{8,264},{16,272},{24,280},{32,288},{40,296},{48,304},{56,3... | collective-permute-start | bytes 1044488 | tf_op jit(solution)/shard_map/ppermute | solution.py:26
  116.9 1.1 copy-start.1

commit v9 on v6

--- a/solution.py
+++ b/solution.py
@@ -53,10 +53,11 @@
         max_out, sum_out, acc_out = rest[:3]
         rest = rest[3:]
     max_ref, sum_ref, acc_ref = rest
-    group_size, rows, _ = acc_ref.shape
+    group_size, rows = max_ref.shape
     inv_scale = 1.0 / math.sqrt(HD)
     seq_index = info_ref[0]
     pairs = info_ref[1]
+    low_top = info_ref[2]
     if first:
         max_ref[...] = jnp.full(max_ref.shape, NEG, jnp.float32)
         sum_ref[...] = jnp.zeros(sum_ref.shape, jnp.float32)
@@ -65,47 +66,53 @@
         max_ref[...] = max_in[...]
         sum_ref[...] = sum_in[...]
         acc_ref[...] = acc_in[...]
-    query_pos = seq_index * rows + lax.broadcasted_iota(jnp.int32, (rows, rows), 0)
-    low = low_ref[...]
-    lane = lax.broadcasted_iota(jnp.int32, (rows, rows), 1)
-    query_all = query_ref[...]
-
-    low_top = info_ref[2]
+    query_pos = seq_index * rows + lax.broadcasted_iota(jnp.int32, (rows, rows), 1)
+    low = jnp.broadcast_to(low_ref[0:1, :], (rows, rows))
+    sub = lax.broadcasted_iota(jnp.int32, (rows, rows), 0)
+    query_t = query_ref[...]
+
+    def column(slot, part):
+        row = window_ref[slot, part, rows:rows + 1, :].astype(jnp.float32)
+        return jnp.transpose(jnp.broadcast_to(row, (rows, rows)))
 
     def fold_pair(pair, masked):
         parts = []
         for half in range(2):
             slot = 2 * pair + half
-            key_t = window_ref[slot, 0, :HD, :]
-            key_scale = window_ref[slot, 0, HD:HD + 1, :].astype(jnp.float32) * inv_scale
-            value_scale = window_ref[slot, 1, rows:rows + 1, :].astype(jnp.float32)
-            scores = jnp.dot(query_all, key_t, preferred_element_type=jnp.float32)
-            scores = scores.reshape(group_size, rows, rows) * key_scale[None]
+            key_tile = window_ref[slot, 0, :rows, :]
+            scores = jnp.dot(key_tile, query_t, preferred_element_type=jnp.float32)
+            key_scale = column(slot, 0) * inv_scale
+            value_scale = column(slot, 1)
             allowed = None
             if masked:
-                key_pos = (seq_index - offset - slot) * rows + lane
-                allowed = ((key_pos <= query_pos) & (key_pos >= low))[None]
-                scores = jnp.where(allowed, scores, NEG)
-            parts.append((scores, allowed, value_scale[None], slot))
-        run_max = max_ref[...][:, :, :1]
-        both_max = jnp.maximum(parts[0][0], parts[1][0])
-        new_max = jnp.maximum(run_max, jnp.max(both_max, axis=2, keepdims=True))
-        factor = jnp.exp(run_max - new_max)
-        acc = acc_ref[...] * factor
-        weight_sum = None
-        for scores, allowed, value_scale, slot in parts:
-            weights = jnp.exp(scores - new_max)
-            if masked:
-                weights = jnp.where(allowed, weights, 0.0)
-            weight_sum = weights if weight_sum is None else weight_sum + weights
-            scaled = (weights * value_scale).astype(jnp.bfloat16).reshape(group_size * rows, rows)
-            value_tile = window_ref[slot, 1, :rows, :]
-            mixed = jnp.dot(scaled, value_tile, preferred_element_type=jnp.float32)
-            acc = acc + mixed.reshape(group_size, rows, HD)
-        run_sum = sum_ref[...][:, :, :1] * factor + jnp.sum(weight_sum, axis=2, keepdims=True)
-        acc_ref[...] = acc
-        max_ref[...] = jnp.broadcast_to(new_max, max_ref.shape)
-        sum_ref[...] = jnp.broadcast_to(run_sum, sum_ref.shape)
+                key_pos = (seq_index - offset - slot) * rows + sub
+                allowed = (key_pos <= query_pos) & (key_pos >= low)
+            blocks = []
+            for g in range(group_size):
+                block = scores[:, g * rows:(g + 1) * rows] * key_scale
+                if masked:
+                    block = jnp.where(allowed, block, NEG)
+                blocks.append(block)
+            parts.append((blocks, allowed, value_scale, slot))
+        for g in range(group_size):
+            run_max = max_ref[g:g + 1, :]
+            new_max = run_max
+            for blocks, _, _, _ in parts:
+                new_max = jnp.maximum(new_max, jnp.max(blocks[g], axis=0, keepdims=True))
+            factor = jnp.exp(run_max - new_max)
+            run_sum = sum_ref[g:g + 1, :] * factor
+            acc = acc_ref[:, g * rows:(g + 1) * rows] * factor
+            for blocks, allowed, value_scale, slot in parts:
+                weights = jnp.exp(blocks[g] - new_max)
+                if masked:
+                    weights = jnp.where(allowed, weights, 0.0)
+                run_sum = run_sum + jnp.sum(weights, axis=0, keepdims=True)
+                scaled = (weights * value_scale).astype(jnp.bfloat16)
+                value_t = window_ref[slot, 1, :HD, :]
+                acc = acc + jnp.dot(value_t, scaled, preferred_element_type=jnp.float32)
+            acc_ref[:, g * rows:(g + 1) * rows] = acc
+            max_ref[g:g + 1, :] = new_max
+            sum_ref[g:g + 1, :] = run_sum
 
     def one_pair(pair, carry):
         nearest = offset + 2 * pair
@@ -115,27 +122,29 @@
 
     lax.fori_loop(0, pairs, one_pair, 0)
     if last:
-        result = acc_ref[...] / sum_ref[...] + mean_ref[...][None]
+        mean = mean_ref[...]
         for g in range(group_size):
-            out_ref[:, g * HD:(g + 1) * HD] = result[g].astype(jnp.bfloat16)
+            block = acc_ref[:, g * rows:(g + 1) * rows] / sum_ref[g:g + 1, :] + mean
+            out_ref[:, g * HD:(g + 1) * HD] = jnp.transpose(block).astype(jnp.bfloat16)
     else:
         max_out[...] = max_ref[...]
         sum_out[...] = sum_ref[...]
         acc_out[...] = acc_ref[...]
 
 
-def attend_part(info, query_all, window, low, mean, state, offset, last, width):
-    group_size = query_all.shape[0] // HD
-    rows = low.shape[0]
+def attend_part(info, query_t, window, low, mean, state, offset, last, width):
+    group_size = query_t.shape[1] // HD
+    rows = low.shape[1]
     full = lambda shape: pl.BlockSpec(shape, lambda i, info: (0,) * len(shape))
-    state_shape = jax.ShapeDtypeStruct((group_size, rows, HD), jnp.float32)
-    operands = [query_all, window, low, mean] + ([] if state is None else list(state))
+    row_shape = jax.ShapeDtypeStruct((group_size, rows), jnp.float32)
+    acc_shape = jax.ShapeDtypeStruct((HD, group_size * rows), jnp.float32)
+    operands = [query_t, window, low, mean] + ([] if state is None else list(state))
     if last:
         out_shape = jax.ShapeDtypeStruct((rows, width), jnp.bfloat16)
         out_specs = full((rows, width))
     else:
-        out_shape = (state_shape,) * 3
-        out_specs = (full(state_shape.shape),) * 3
+        out_shape = (row_shape, row_shape, acc_shape)
+        out_specs = (full(row_shape.shape), full(row_shape.shape), full(acc_shape.shape))
     kernel = functools.partial(attention_kernel, state is None, last, offset)
     return pl.pallas_call(
         kernel,
@@ -145,7 +154,11 @@
             grid=(1,),
             in_specs=[full(x.shape) for x in operands],
             out_specs=out_specs,
-            scratch_shapes=[pltpu.VMEM((group_size, rows, HD), jnp.float32)] * 3,
+            scratch_shapes=[
+                pltpu.VMEM(row_shape.shape, jnp.float32),
+                pltpu.VMEM(row_shape.shape, jnp.float32),
+                pltpu.VMEM(acc_shape.shape, jnp.float32),
+            ],
         ),
     )(info, *operands)
 
@@ -168,14 +181,14 @@
     value_scale_row = jnp.repeat(value_scales.reshape(-1), BLK)
     scale_rows = jnp.zeros((2, pad_rows, row_count), jnp.bfloat16)
     scale_rows = scale_rows.at[0, 0].set(key_scale_row).at[1, 0].set(value_scale_row)
-    packet = jnp.concatenate([jnp.stack([local_keys.T, local_values]), scale_rows], axis=1)
+    packet = jnp.concatenate([jnp.stack([local_keys, local_values.T]), scale_rows], axis=1)
     stages = gather_stages(packet, seq_count, depth)
     own_pos = seq_index * row_count + jnp.arange(row_count, dtype=jnp.int32)
     low = starts[doc_index(own_pos, starts)]
     used = jnp.clip(seq_index - low[0] // row_count + 1, 1, depth).astype(jnp.int32)
-    low_tile = jnp.broadcast_to(low[:, None], (row_count, row_count)).astype(jnp.int32)
-    mean = value_means.reshape(1, HD)
-    query_all = queries.reshape(row_count, group_size, HD).transpose(1, 0, 2).reshape(-1, HD)
+    low_tile = jnp.broadcast_to(low[None, :], (8, row_count)).astype(jnp.int32)
+    mean = jnp.broadcast_to(value_means.reshape(HD, 1), (HD, row_count))
+    query_all = queries.reshape(row_count, group_size, HD).transpose(2, 1, 0).reshape(HD, -1)
     chunks = [
         jnp.concatenate([stages[0]] + stages[1], axis=0),
         jnp.concatenate(stages[2], axis=0),

time: 136 us -> 130 us (0.956)
  the two profiles are of different devices: /device:TPU:388 before, /device:TPU:6 now
where the time goes in v9:
time: 130 us
  starting transfers between devices  43 us (33%)
  waiting for transfers between devices  36.3 us (28%)
  Pallas kernels  25.6 us (20%)
  local copies, waits for them, and re-layouts  12.7 us (10%)
  other arithmetic  9.53 us (7%)
  between operations  2.5 us (2%)
    ppermute x8, starting transfers between devices, shift_from(): return lax.ppermute(x, 'seq', pairs)  35.9 us
    ppermute x8, waiting for transfers between devices, shift_from(): return lax.ppermute(x, 'seq', pairs)  31.6 us
    pallas_call x3, Pallas kernels, attend_part(): pl.pallas_call(kernel, out_shape=out_shape, grid_spec=pltpu.PrefetchScala...  25.6 us
    all_to_all x1, starting transfers between devices, shards(): both = lax.all_to_all(both, 'head', split_axis=2, concat_axis=0, tiled=True)  7.1 us
    unnamed x16, local copies, waits for them, and re-layouts  5.92 us
    all_to_all x1, waiting for transfers between devices, shards(): both = lax.all_to_all(both, 'head', split_axis=2, concat_axis=0, tiled=True)  4.7 us
    another operation x3, other arithmetic, shards(): jnp.stack([seq_index.astype(jnp.int32), pairs, low[-1].astype(jnp.int32)])  3.79 us
  transfers between devices with their start and end apart: 9, of which 6 were waited for; matrix products, arithmetic and copies ran while one was open for 14% of the time, Pallas kernels for 9%

profile of v9, /device:TPU:6, one launch (start us, length us, event | category | flops | bytes accessed | tf_op | source)
XLA Modules:
  0.0 129.7 jit_solution(4363428146612500895)
XLA Ops:
  0.0 0.8 copy.38
  0.8 0.8 copy.37
  1.5 0.6 copy.30
  2.2 7.1 %all-to-all-start = ((bf16[16,2,8,128]{3,0,1,2:T(8,128)(2,1)}), bf16[16,2,8,128]{3,0,1,2:T(8,128)(2,1)S(1)}, u32[]{:S(2)}, u32[]{:S(2)}) async-start(bf16[16,2,8,128]{3,0,1,2:T(8,128)(2,1)} %copy.30), calls=%async_computation | async-start | bytes 131072 | tf_op jit(solution)/shard_map/all_to_all | solution.py:170
  9.3 0.7 copy.28
  10.0 0.1 reduce-window.9
  10.1 0.1 reduce.4
  10.2 0.7 sub.27
  10.9 0.8 reduce.5
  11.7 0.1 broadcast_in_dim.12
  11.8 0.1 reshape.145
  11.8 0.8 reduce.6
  12.6 0.1 broadcast_in_dim.13
  12.7 0.1 reshape.147
  12.8 4.7 %all-to-all-done = bf16[16,2,8,128]{3,0,1,2:T(8,128)(2,1)S(1)} async-done(((bf16[16,2,8,128]{3,0,1,2:T(8,128)(2,1)}), bf16[16,2,8,128]{3,0,1,2:T(8,128)(2,1)S(1)}, u32[]{:S(2)}, u32[]{:S(2)}) %all-to-all-start) | async-done | bytes 65568 | tf_op jit(solution)/shard_map/all_to_all | solution.py:170
  17.5 0.1 copy.34
  17.7 2.8 %collective-permute-start = (bf16[1,2,136,128]{3,2,1,0:T(8,128)(2,1)S(1)}, bf16[1,2,136,128]{3,2,1,0:T(8,128)(2,1)S(1)}, u32[]{:S(2)}, u32[]{:S(2)}) collective-permute-start(bf16[1,2,136,128]{3,2,1,0:T(8,128)(2,1)S(1)} %maximum_bitcast_fusion), channel_id=1, source_target_pairs={{0,8},{8,16},{16,24},{24,32},{32,40},{40,48},{48,56},{56,64},{64,7... | collective-permute-start | bytes 208904 | tf_op jit(solution)/shard_map/ppermute | solution.py:26
  20.5 4.3 %collective-permute-start.1 = (bf16[1,2,136,128]{3,2,1,0:T(8,128)(2,1)S(1)}, bf16[1,2,136,128]{3,2,1,0:T(8,128)(2,1)S(1)}, u32[]{:S(2)}, u32[]{:S(2)}) collective-permute-start(bf16[1,2,136,128]{3,2,1,0:T(8,128)(2,1)S(1)} %maximum_bitcast_fusion), channel_id=1, source_target_pairs={{0,16},{8,24},{16,32},{24,40},{32,48},{40,56},{48,64},{56,72},{64,... | collective-permute-start | bytes 208904 | tf_op jit(solution)/shard_map/ppermute | solution.py:26
  24.8 6.6 %collective-permute-start.2 = (bf16[1,2,136,128]{3,2,1,0:T(8,128)(2,1)S(1)}, bf16[1,2,136,128]{3,2,1,0:T(8,128)(2,1)S(1)}, u32[]{:S(2)}, u32[]{:S(2)}) collective-permute-start(bf16[1,2,136,128]{3,2,1,0:T(8,128)(2,1)S(1)} %maximum_bitcast_fusion), channel_id=1, source_target_pairs={{0,24},{8,32},{16,40},{24,48},{32,56},{40,64},{48,72},{56,80},{64,... | collective-permute-start | bytes 208904 | tf_op jit(solution)/shard_map/ppermute | solution.py:26
  31.4 0.6 constant_dynamic-update-slice_fusion.6
  32.1 0.0 collective-permute-done
  32.1 2.7 %collective-permute-done.1 = bf16[1,2,136,128]{3,2,1,0:T(8,128)(2,1)S(1)} collective-permute-done((bf16[1,2,136,128]{3,2,1,0:T(8,128)(2,1)S(1)}, bf16[1,2,136,128]{3,2,1,0:T(8,128)(2,1)S(1)}, u32[]{:S(2)}, u32[]{:S(2)}) %collective-permute-start.1) | collective-permute-done | bytes 69664 | tf_op jit(solution)/shard_map/ppermute | solution.py:26
  34.8 3.3 %collective-permute-done.2 = bf16[1,2,136,128]{3,2,1,0:T(8,128)(2,1)S(1)} collective-permute-done((bf16[1,2,136,128]{3,2,1,0:T(8,128)(2,1)S(1)}, bf16[1,2,136,128]{3,2,1,0:T(8,128)(2,1)S(1)}, u32[]{:S(2)}, u32[]{:S(2)}) %collective-permute-start.2) | collective-permute-done | bytes 69664 | tf_op jit(solution)/shard_map/ppermute | solution.py:26
  38.2 0.0 copy-start
  38.2 1.9 %collective-permute-start.3 = (bf16[4,2,136,128]{3,2,1,0:T(8,128)(2,1)S(1)}, bf16[4,2,136,128]{3,2,1,0:T(8,128)(2,1)S(1)}, u32[]{:S(2)}, u32[]{:S(2)}) collective-permute-start(bf16[4,2,136,128]{3,2,1,0:T(8,128)(2,1)S(1)} %pad_maximum_fusion.1.refs_2_), channel_id=1, source_target_pairs={{0,32},{8,40},{16,48},{24,56},{32,64},{40,72},{48,80},{56,88},{64,... | collective-permute-start | bytes 835592 | tf_op jit(solution)/shard_map/ppermute | solution.py:26
  40.1 7.3 %collective-permute-start.4 = (bf16[4,2,136,128]{3,2,1,0:T(8,128)(2,1)S(1)}, bf16[4,2,136,128]{3,2,1,0:T(8,128)(2,1)S(1)}, u32[]{:S(2)}, u32[]{:S(2)}) collective-permute-start(bf16[4,2,136,128]{3,2,1,0:T(8,128)(2,1)S(1)} %pad_maximum_fusion.1.refs_2_), channel_id=1, source_target_pairs={{0,64},{8,72},{16,80},{24,88},{32,96},{40,104},{48,112},{56,120},{... | collective-permute-start | bytes 835592 | tf_op jit(solution)/shard_map/ppermute | solution.py:26
  47.4 5.3 %collective-permute-start.5 = (bf16[4,2,136,128]{3,2,1,0:T(8,128)(2,1)S(1)}, bf16[4,2,136,128]{3,2,1,0:T(8,128)(2,1)S(1)}, u32[]{:S(2)}, u32[]{:S(2)}) collective-permute-start(bf16[4,2,136,128]{3,2,1,0:T(8,128)(2,1)S(1)} %pad_maximum_fusion.1.refs_2_), channel_id=1, source_target_pairs={{0,96},{8,104},{16,112},{24,120},{32,128},{40,136},{48,144},{56,15... | collective-permute-start | bytes 835592 | tf_op jit(solution)/shard_map/ppermute | solution.py:26
  52.7 0.6 constant_dynamic-update-slice_fusion.5
  53.4 0.6 constant_dynamic-update-slice_fusion.4
  54.0 0.6 constant_dynamic-update-slice_fusion.3
  54.7 9.5 %collective-permute-done.3 = bf16[4,2,136,128]{3,2,1,0:T(8,128)(2,1)S(1)} collective-permute-done((bf16[4,2,136,128]{3,2,1,0:T(8,128)(2,1)S(1)}, bf16[4,2,136,128]{3,2,1,0:T(8,128)(2,1)S(1)}, u32[]{:S(2)}, u32[]{:S(2)}) %collective-permute-start.3) | collective-permute-done | bytes 278560 | tf_op jit(solution)/shard_map/ppermute | solution.py:26
  64.1 0.8 constant_dynamic-update-slice_fusion.2
  64.9 0.0 collective-permute-done.4
  64.9 0.8 constant_dynamic-update-slice_fusion.1
  65.7 0.0 copy-done
  65.7 4.8 %collective-permute-done.5 = bf16[4,2,136,128]{3,2,1,0:T(8,128)(2,1)S(1)} collective-permute-done((bf16[4,2,136,128]{3,2,1,0:T(8,128)(2,1)S(1)}, bf16[4,2,136,128]{3,2,1,0:T(8,128)(2,1)S(1)}, u32[]{:S(2)}, u32[]{:S(2)}) %collective-permute-start.5) | collective-permute-done | bytes 278560 | tf_op jit(solution)/shard_map/ppermute | solution.py:26
  70.6 0.0 copy-start.1
  70.6 0.7 constant_dynamic-update-slice_fusion
  71.3 5.7 %collective-permute-start.6 = (bf16[16,2,136,128]{3,2,1,0:T(8,128)(2,1)}, bf16[16,2,136,128]{3,2,1,0:T(8,128)(2,1)S(1)}, u32[]{:S(2)}, u32[]{:S(2)}) collective-permute-start(bf16[16,2,136,128]{3,2,1,0:T(8,128)(2,1)} %constant_dynamic-update-slice_fusion), channel_id=1, source_target_pairs={{0,128},{8,136},{16,144},{24,152},{32,160},{40,168},{48,176},{56,1... | collective-permute-start | bytes 3342344 | tf_op jit(solution)/shard_map/ppermute | solution.py:26
  77.0 0.1 convert_reduce_fusion
  77.1 0.9 slice.68
  78.0 1.9 %collective-permute-start.7 = (bf16[9,2,136,128]{3,2,1,0:T(8,128)(2,1)}, bf16[9,2,136,128]{3,2,1,0:T(8,128)(2,1)S(1)}, u32[]{:S(2)}, u32[]{:S(2)}) collective-permute-start(bf16[9,2,136,128]{3,2,1,0:T(8,128)(2,1)} %slice.68), channel_id=1, source_target_pairs={{0,256},{8,264},{16,272},{24,280},{32,288},{40,296},{48,304},{56,3... | collective-permute-start | bytes 1880072 | tf_op jit(solution)/shard_map/ppermute | solution.py:26
  79.9 0.0 copy-start.2
  79.9 1.2 gather_fusion
  81.2 0.6 fusion.1
  84.1 0.0 copy-done.1
  84.1 0.2 copy.29
  84.4 0.7 copy.40
  85.1 0.1 pad.18.clone
  85.2 1.3 add_add_fusion.refs_0_
  86.5 1.2 add_add_fusion.1.refs_0_
  87.7 1.3 add_add_fusion.2.refs_0_
  89.0 0.6 broadcast_in_dim.31.refs_3_
  89.6 0.0 copy-done.2
  89.6 0.7 broadcast_in_dim.32.refs_4_
  90.3 4.2 %shard_map.73 = (f32[8,128]{1,0:T(8,128)}, f32[8,128]{1,0:T(8,128)}, f32[128,1024]{1,0:T(8,128)}) custom-call(s32[3]{0:T(128)} %add_add_fusion.2.refs_0_, bf16[128,1024]{1,0:T(8,128)(2,1)} %bitcast.48, bf16[4,2,136,128]{3,2,1,0:T(8,128)(2,1)} %copy-done, s32[8,128]{1,0:T(8,128)} %broadcast_in_dim.31.refs_3_, f32[128,128]{1,0:T(8,128)} %broadcast_in_dim.32.refs_4_), custom_call_target="tpu_custom_call" | custom-call | tf_op jit(solution)/shard_map/pallas_call | solution.py:149
  94.5 1.1 pad_maximum_fusion.refs_2_
  95.5 7.8 %shard_map.74 = (f32[8,128]{1,0:T(8,128)}, f32[8,128]{1,0:T(8,128)}, f32[128,1024]{1,0:T(8,128)}) custom-call(s32[3]{0:T(128)} %add_add_fusion.1.refs_0_, bf16[128,1024]{1,0:T(8,128)(2,1)} %bitcast.49, bf16[12,2,136,128]{3,2,1,0:T(8,128)(2,1)} %pad_maximum_fusion.refs_2_, s32[8,128]{1,0:T(8,128)} %broadcast_in_dim.31.refs_3_, ...), custom_call_target="tpu_custom_call" | custom-call | tf_op jit(solution)/shard_map/pallas_call | solution.py:149
  103.3 0.0 collective-permute-done.7
  103.3 11.3 %collective-permute-done.6 = bf16[16,2,136,128]{3,2,1,0:T(8,128)(2,1)S(1)} collective-permute-done((bf16[16,2,136,128]{3,2,1,0:T(8,128)(2,1)}, bf16[16,2,136,128]{3,2,1,0:T(8,128)(2,1)S(1)}, u32[]{:S(2)}, u32[]{:S(2)}) %collective-permute-start.6) | collective-permute-done | bytes 1114144 | tf_op jit(solution)/shard_map/ppermute | solution.py:26
  114.6 1.5 %maximum_maximum_fusion.refs_2_ = bf16[26,2,136,128]{3,2,1,0:T(8,128)(2,1)} fusion(bf16[9,2,136,128]{3,2,1,0:T(8,128)(2,1)S(1)} %collective-permute-done.7, bf16[16,2,136,128]{3,2,1,0:T(8,128)(2,1)S(1)} %collective-permute-done.6, bf16[26]{0:T(256)(128)(2,1)S(1)} %pad.18.clone), kind=kLoop, calls=%fused_computation.1 | loop fusion | flops 1810432 | bytes 3551284 | tf_op jit(solution)/shard_map/concatenate | solution.py:202
  116.0 13.6 %shard_map.75 = bf16[128,1024]{1,0:T(8,128)(2,1)} custom-call(s32[3]{0:T(128)} %add_add_fusion.refs_0_, bf16[128,1024]{1,0:T(8,128)(2,1)} %bitcast.50, bf16[26,2,136,128]{3,2,1,0:T(8,128)(2,1)} %maximum_maximum_fusion.refs_2_, s32[8,128]{1,0:T(8,128)} %broadcast_in_dim.31.refs_3_, f32[128,128]{1,0:T(8,128)} %broadcast_in_dim.32.refs_4_, ...), custom_call_target="tpu_custom_call" | custom-call | tf_op jit(solution)/shard_map/pallas_call | solution.py:149
  (12 shorter events, 0.2 us)
Async XLA Ops:
  2.2 15.3 %all-to-all-start = ((bf16[16,2,8,128]{3,0,1,2:T(8,128)(2,1)}), bf16[16,2,8,128]{3,0,1,2:T(8,128)(2,1)S(1)}, u32[]{:S(2)}, u32[]{:S(2)}) async-start(bf16[16,2,8,128]{3,0,1,2:T(8,128)(2,1)} %copy.30), calls=%async_computation | async-start | bytes 131072 | tf_op jit(solution)/shard_map/all_to_all | solution.py:170
  17.7 14.4 %collective-permute-start = (bf16[1,2,136,128]{3,2,1,0:T(8,128)(2,1)S(1)}, bf16[1,2,136,128]{3,2,1,0:T(8,128)(2,1)S(1)}, u32[]{:S(2)}, u32[]{:S(2)}) collective-permute-start(bf16[1,2,136,128]{3,2,1,0:T(8,128)(2,1)S(1)} %maximum_bitcast_fusion), channel_id=1, source_target_pairs={{0,8},{8,16},{16,24},{24,32},{32,40},{40,48},{48,56},{56,64},{64,7... | collective-permute-start | bytes 208904 | tf_op jit(solution)/shard_map/ppermute | solution.py:26
  20.5 14.2 %collective-permute-start.1 = (bf16[1,2,136,128]{3,2,1,0:T(8,128)(2,1)S(1)}, bf16[1,2,136,128]{3,2,1,0:T(8,128)(2,1)S(1)}, u32[]{:S(2)}, u32[]{:S(2)}) collective-permute-start(bf16[1,2,136,128]{3,2,1,0:T(8,128)(2,1)S(1)} %maximum_bitcast_fusion), channel_id=1, source_target_pairs={{0,16},{8,24},{16,32},{24,40},{32,48},{40,56},{48,64},{56,72},{64,... | collective-permute-start | bytes 208904 | tf_op jit(solution)/shard_map/ppermute | solution.py:26
  24.8 13.3 %collective-permute-start.2 = (bf16[1,2,136,128]{3,2,1,0:T(8,128)(2,1)S(1)}, bf16[1,2,136,128]{3,2,1,0:T(8,128)(2,1)S(1)}, u32[]{:S(2)}, u32[]{:S(2)}) collective-permute-start(bf16[1,2,136,128]{3,2,1,0:T(8,128)(2,1)S(1)} %maximum_bitcast_fusion), channel_id=1, source_target_pairs={{0,24},{8,32},{16,40},{24,48},{32,56},{40,64},{48,72},{56,80},{64,... | collective-permute-start | bytes 208904 | tf_op jit(solution)/shard_map/ppermute | solution.py:26
  38.2 27.6 %copy-start = (bf16[4,2,136,128]{3,2,1,0:T(8,128)(2,1)}, bf16[4,2,136,128]{3,2,1,0:T(8,128)(2,1)S(1)}, u32[]{:S(2)}) copy-start(bf16[4,2,136,128]{3,2,1,0:T(8,128)(2,1)S(1)} %pad_maximum_fusion.1.refs_2_) | copy-start | bytes 835588
  38.2 26.0 %collective-permute-start.3 = (bf16[4,2,136,128]{3,2,1,0:T(8,128)(2,1)S(1)}, bf16[4,2,136,128]{3,2,1,0:T(8,128)(2,1)S(1)}, u32[]{:S(2)}, u32[]{:S(2)}) collective-permute-start(bf16[4,2,136,128]{3,2,1,0:T(8,128)(2,1)S(1)} %pad_maximum_fusion.1.refs_2_), channel_id=1, source_target_pairs={{0,32},{8,40},{16,48},{24,56},{32,64},{40,72},{48,80},{56,88},{64,... | collective-permute-start | bytes 835592 | tf_op jit(solution)/shard_map/ppermute | solution.py:26
  40.1 24.8 %collective-permute-start.4 = (bf16[4,2,136,128]{3,2,1,0:T(8,128)(2,1)S(1)}, bf16[4,2,136,128]{3,2,1,0:T(8,128)(2,1)S(1)}, u32[]{:S(2)}, u32[]{:S(2)}) collective-permute-start(bf16[4,2,136,128]{3,2,1,0:T(8,128)(2,1)S(1)} %pad_maximum_fusion.1.refs_2_), channel_id=1, source_target_pairs={{0,64},{8,72},{16,80},{24,88},{32,96},{40,104},{48,112},{56,120},{... | collective-permute-start | bytes 835592 | tf_op jit(solution)/shard_map/ppermute | solution.py:26
  47.4 23.1 %collective-permute-start.5 = (bf16[4,2,136,128]{3,2,1,0:T(8,128)(2,1)S(1)}, bf16[4,2,136,128]{3,2,1,0:T(8,128)(2,1)S(1)}, u32[]{:S(2)}, u32[]{:S(2)}) collective-permute-start(bf16[4,2,136,128]{3,2,1,0:T(8,128)(2,1)S(1)} %pad_maximum_fusion.1.refs_2_), channel_id=1, source_target_pairs={{0,96},{8,104},{16,112},{24,120},{32,128},{40,136},{48,144},{56,15... | collective-permute-start | bytes 835592 | tf_op jit(solution)/shard_map/ppermute | solution.py:26
  70.6 13.5 %copy-start.1 = (bf16[128,1024]{1,0:T(8,128)(2,1)S(1)}, bf16[128,1024]{1,0:T(8,128)(2,1)}, u32[]{:S(2)}) copy-start(bf16[128,1024]{1,0:T(8,128)(2,1)} %param.11) | copy-start | bytes 786436
  71.3 43.3 %collective-permute-start.6 = (bf16[16,2,136,128]{3,2,1,0:T(8,128)(2,1)}, bf16[16,2,136,128]{3,2,1,0:T(8,128)(2,1)S(1)}, u32[]{:S(2)}, u32[]{:S(2)}) collective-permute-start(bf16[16,2,136,128]{3,2,1,0:T(8,128)(2,1)} %constant_dynamic-update-slice_fusion), channel_id=1, source_target_pairs={{0,128},{8,136},{16,144},{24,152},{32,160},{40,168},{48,176},{56,1... | collective-permute-start | bytes 3342344 | tf_op jit(solution)/shard_map/ppermute | solution.py:26
  78.0 25.3 %collective-permute-start.7 = (bf16[9,2,136,128]{3,2,1,0:T(8,128)(2,1)}, bf16[9,2,136,128]{3,2,1,0:T(8,128)(2,1)S(1)}, u32[]{:S(2)}, u32[]{:S(2)}) collective-permute-start(bf16[9,2,136,128]{3,2,1,0:T(8,128)(2,1)} %slice.68), channel_id=1, source_target_pairs={{0,256},{8,264},{16,272},{24,280},{32,288},{40,296},{48,304},{56,3... | collective-permute-start | bytes 1880072 | tf_op jit(solution)/shard_map/ppermute | solution.py:26
  79.9 9.7 %copy-start.2 = (f32[128]{0:T(128)S(1)}, f32[128]{0:T(128)}, u32[]{:S(2)}) copy-start(f32[128]{0:T(128)} %param.16) | copy-start | bytes 1540

commit v10 on v9

--- a/solution.py
+++ b/solution.py
@@ -27,17 +27,12 @@
 
 
 def gather_stages(packet, count, depth):
-    held = packet[None]
-    stages = [held]
-    for width, shifts in ((1, (1, 2, 3)), (4, (4, 8, 12)), (16, (16, 32))):
-        parts = []
-        for offset in shifts:
-            need = min(width, depth - offset)
-            if need > 0:
-                parts.append(shift_from(held[:need], offset, count))
-        stages.append(parts)
-        held = jnp.concatenate([held] + parts, axis=0)
-    return stages
+    first = [packet[None]] + [shift_from(packet[None], offset, count) for offset in (1, 2, 3)]
+    block = jnp.concatenate(first, axis=0)
+    middle = [shift_from(block, offset, count) for offset in (4, 8, 12, 16)]
+    block = jnp.concatenate([block] + middle, axis=0)
+    last = [shift_from(block[4:], 16, count), shift_from(block[4:depth - 32], 32, count)]
+    return [first, middle, last]
 
 
 def attention_kernel(first, last, offset, *refs):
@@ -189,11 +184,7 @@
     low_tile = jnp.broadcast_to(low[None, :], (8, row_count)).astype(jnp.int32)
     mean = jnp.broadcast_to(value_means.reshape(HD, 1), (HD, row_count))
     query_all = queries.reshape(row_count, group_size, HD).transpose(2, 1, 0).reshape(HD, -1)
-    chunks = [
-        jnp.concatenate([stages[0]] + stages[1], axis=0),
-        jnp.concatenate(stages[2], axis=0),
-        jnp.concatenate(stages[3], axis=0),
-    ]
+    chunks = [jnp.concatenate(stage, axis=0) for stage in stages]
     state = None
     offset = 0
     for index, chunk in enumerate(chunks):

time: 130 us -> 122 us (0.938)
  the two profiles are of different devices: /device:TPU:6 before, /device:TPU:134 now
where the time goes in v10:
time: 122 us; the launch traced here: 121 us
  starting transfers between devices  45.8 us (38%)
  waiting for transfers between devices  31.9 us (26%)
  Pallas kernels  25.5 us (21%)
  local copies, waits for them, and re-layouts  8.15 us (7%)
  other arithmetic  7 us (6%)
  between operations  2.79 us (2%)
    ppermute x9, starting transfers between devices, shift_from(): return lax.ppermute(x, 'seq', pairs)  38.7 us
    ppermute x9, waiting for transfers between devices, shift_from(): return lax.ppermute(x, 'seq', pairs)  25.6 us
    pallas_call x3, Pallas kernels, attend_part(): pl.pallas_call(kernel, out_shape=out_shape, grid_spec=pltpu.PrefetchScala...  25.5 us
    all_to_all x1, starting transfers between devices, shards(): both = lax.all_to_all(both, 'head', split_axis=2, concat_axis=0, tiled=True)  7.1 us
    all_to_all x1, waiting for transfers between devices, shards(): both = lax.all_to_all(both, 'head', split_axis=2, concat_axis=0, tiled=True)  6.32 us
    another operation x3, other arithmetic, shards(): jnp.stack([seq_index.astype(jnp.int32), pairs, low[-1].astype(jnp.int32)])  3.7 us
    unnamed x16, local copies, waits for them, and re-layouts  3.52 us
  transfers between devices with their start and end apart: 10, of which 6 were waited for; matrix products, arithmetic and copies ran while one was open for 9% of the time, Pallas kernels for 11%

profile of v10, /device:TPU:134, one launch (start us, length us, event | category | flops | bytes accessed | tf_op | source)
XLA Modules:
  0.0 121.1 jit_solution(360870638210881674)
XLA Ops:
  0.0 0.0 copy-start.2
  0.0 0.8 copy.37
  0.8 0.8 copy.38
  1.6 0.6 copy.30
  2.2 7.1 %all-to-all-start = ((bf16[16,2,8,128]{3,0,1,2:T(8,128)(2,1)}), bf16[16,2,8,128]{3,0,1,2:T(8,128)(2,1)S(1)}, u32[]{:S(2)}, u32[]{:S(2)}) async-start(bf16[16,2,8,128]{3,0,1,2:T(8,128)(2,1)} %copy.30), calls=%async_computation | async-start | bytes 131072 | tf_op jit(solution)/shard_map/all_to_all | solution.py:165
  9.3 0.8 reduce.5
  10.1 0.1 broadcast_in_dim.12
  10.1 0.1 reshape.145
  10.2 0.8 reduce.6
  11.0 0.1 broadcast_in_dim.13
  11.1 0.1 reshape.147
  11.2 6.3 %all-to-all-done = bf16[16,2,8,128]{3,0,1,2:T(8,128)(2,1)S(1)} async-done(((bf16[16,2,8,128]{3,0,1,2:T(8,128)(2,1)}), bf16[16,2,8,128]{3,0,1,2:T(8,128)(2,1)S(1)}, u32[]{:S(2)}, u32[]{:S(2)}) %all-to-all-start) | async-done | bytes 65568 | tf_op jit(solution)/shard_map/all_to_all | solution.py:165
  17.5 0.1 copy.34
  17.7 2.8 %collective-permute-start = (bf16[1,2,136,128]{3,2,1,0:T(8,128)(2,1)S(1)}, bf16[1,2,136,128]{3,2,1,0:T(8,128)(2,1)S(1)}, u32[]{:S(2)}, u32[]{:S(2)}) collective-permute-start(bf16[1,2,136,128]{3,2,1,0:T(8,128)(2,1)S(1)} %maximum_bitcast_fusion), channel_id=1, source_target_pairs={{0,8},{8,16},{16,24},{24,32},{32,40},{40,48},{48,56},{56,64},{64,7... | collective-permute-start | bytes 208904 | tf_op jit(solution)/shard_map/ppermute | solution.py:26
  20.5 4.3 %collective-permute-start.1 = (bf16[1,2,136,128]{3,2,1,0:T(8,128)(2,1)S(1)}, bf16[1,2,136,128]{3,2,1,0:T(8,128)(2,1)S(1)}, u32[]{:S(2)}, u32[]{:S(2)}) collective-permute-start(bf16[1,2,136,128]{3,2,1,0:T(8,128)(2,1)S(1)} %maximum_bitcast_fusion), channel_id=1, source_target_pairs={{0,16},{8,24},{16,32},{24,40},{32,48},{40,56},{48,64},{56,72},{64,... | collective-permute-start | bytes 208904 | tf_op jit(solution)/shard_map/ppermute | solution.py:26
  24.8 6.9 %collective-permute-start.2 = (bf16[1,2,136,128]{3,2,1,0:T(8,128)(2,1)S(1)}, bf16[1,2,136,128]{3,2,1,0:T(8,128)(2,1)S(1)}, u32[]{:S(2)}, u32[]{:S(2)}) collective-permute-start(bf16[1,2,136,128]{3,2,1,0:T(8,128)(2,1)S(1)} %maximum_bitcast_fusion), channel_id=1, source_target_pairs={{0,24},{8,32},{16,40},{24,48},{32,56},{40,64},{48,72},{56,80},{64,... | collective-permute-start | bytes 208904 | tf_op jit(solution)/shard_map/ppermute | solution.py:26
  31.8 0.0 collective-permute-done
  31.8 0.0 collective-permute-done.1
  31.8 1.9 %collective-permute-done.2 = bf16[1,2,136,128]{3,2,1,0:T(8,128)(2,1)S(1)} collective-permute-done((bf16[1,2,136,128]{3,2,1,0:T(8,128)(2,1)S(1)}, bf16[1,2,136,128]{3,2,1,0:T(8,128)(2,1)S(1)}, u32[]{:S(2)}, u32[]{:S(2)}) %collective-permute-start.2) | collective-permute-done | bytes 69664 | tf_op jit(solution)/shard_map/ppermute | solution.py:26
  33.7 0.0 copy-start.1
  33.7 7.5 %collective-permute-start.3 = (bf16[4,2,136,128]{3,2,1,0:T(8,128)(2,1)S(1)}, bf16[4,2,136,128]{3,2,1,0:T(8,128)(2,1)S(1)}, u32[]{:S(2)}, u32[]{:S(2)}) collective-permute-start(bf16[4,2,136,128]{3,2,1,0:T(8,128)(2,1)S(1)} %pad_maximum_fusion.1.refs_2_), channel_id=1, source_target_pairs={{0,32},{8,40},{16,48},{24,56},{32,64},{40,72},{48,80},{56,88},{64,... | collective-permute-start | bytes 835592 | tf_op jit(solution)/shard_map/ppermute | solution.py:26
  41.2 4.9 %collective-permute-start.4 = (bf16[4,2,136,128]{3,2,1,0:T(8,128)(2,1)S(1)}, bf16[4,2,136,128]{3,2,1,0:T(8,128)(2,1)S(1)}, u32[]{:S(2)}, u32[]{:S(2)}) collective-permute-start(bf16[4,2,136,128]{3,2,1,0:T(8,128)(2,1)S(1)} %pad_maximum_fusion.1.refs_2_), channel_id=1, source_target_pairs={{0,64},{8,72},{16,80},{24,88},{32,96},{40,104},{48,112},{56,120},{... | collective-permute-start | bytes 835592 | tf_op jit(solution)/shard_map/ppermute | solution.py:26
  46.2 1.9 %collective-permute-start.5 = (bf16[4,2,136,128]{3,2,1,0:T(8,128)(2,1)S(1)}, bf16[4,2,136,128]{3,2,1,0:T(8,128)(2,1)S(1)}, u32[]{:S(2)}, u32[]{:S(2)}) collective-permute-start(bf16[4,2,136,128]{3,2,1,0:T(8,128)(2,1)S(1)} %pad_maximum_fusion.1.refs_2_), channel_id=1, source_target_pairs={{0,96},{8,104},{16,112},{24,120},{32,128},{40,136},{48,144},{56,15... | collective-permute-start | bytes 835592 | tf_op jit(solution)/shard_map/ppermute | solution.py:26
  48.1 0.0 copy-done.2
  48.1 0.1 copy.28
  48.2 0.1 reduce-window.9
  48.3 0.1 reduce.4
  48.4 3.3 %collective-permute-start.6 = (bf16[4,2,136,128]{3,2,1,0:T(8,128)(2,1)S(1)}, bf16[4,2,136,128]{3,2,1,0:T(8,128)(2,1)S(1)}, u32[]{:S(2)}, u32[]{:S(2)}) collective-permute-start(bf16[4,2,136,128]{3,2,1,0:T(8,128)(2,1)S(1)} %pad_maximum_fusion.1.refs_2_), channel_id=1, source_target_pairs={{0,128},{8,136},{16,144},{24,152},{32,160},{40,168},{48,176},{56,1... | collective-permute-start | bytes 835592 | tf_op jit(solution)/shard_map/ppermute | solution.py:26
  51.7 6.4 %collective-permute-done.3 = bf16[4,2,136,128]{3,2,1,0:T(8,128)(2,1)S(1)} collective-permute-done((bf16[4,2,136,128]{3,2,1,0:T(8,128)(2,1)S(1)}, bf16[4,2,136,128]{3,2,1,0:T(8,128)(2,1)S(1)}, u32[]{:S(2)}, u32[]{:S(2)}) %collective-permute-start.3) | collective-permute-done | bytes 278560 | tf_op jit(solution)/shard_map/ppermute | solution.py:26
  58.2 9.2 %collective-permute-done.4 = bf16[4,2,136,128]{3,2,1,0:T(8,128)(2,1)S(1)} collective-permute-done((bf16[4,2,136,128]{3,2,1,0:T(8,128)(2,1)S(1)}, bf16[4,2,136,128]{3,2,1,0:T(8,128)(2,1)S(1)}, u32[]{:S(2)}, u32[]{:S(2)}) %collective-permute-start.4) | collective-permute-done | bytes 278560 | tf_op jit(solution)/shard_map/ppermute | solution.py:26
  67.4 4.1 %collective-permute-done.5 = bf16[4,2,136,128]{3,2,1,0:T(8,128)(2,1)S(1)} collective-permute-done((bf16[4,2,136,128]{3,2,1,0:T(8,128)(2,1)S(1)}, bf16[4,2,136,128]{3,2,1,0:T(8,128)(2,1)S(1)}, u32[]{:S(2)}, u32[]{:S(2)}) %collective-permute-start.5) | collective-permute-done | bytes 278560 | tf_op jit(solution)/shard_map/ppermute | solution.py:26
  71.6 0.0 collective-permute-done.6
  71.6 0.0 copy-done.1
  71.6 0.0 copy-start
  71.7 5.0 %collective-permute-start.7 = (bf16[16,2,136,128]{3,2,1,0:T(8,128)(2,1)S(1)}, bf16[16,2,136,128]{3,2,1,0:T(8,128)(2,1)S(1)}, u32[]{:S(2)}, u32[]{:S(2)}) collective-permute-start(bf16[16,2,136,128]{3,2,1,0:T(8,128)(2,1)S(1)} %constant_dynamic-update-slice_fusion.refs_2_), channel_id=1, source_target_pairs={{0,128},{8,136},{16,144},{24,152},{32,160},{40,168},{48,176},{56,1... | collective-permute-start | bytes 3342344 | tf_op jit(solution)/shard_map/ppermute | solution.py:26
  76.7 0.1 convert_reduce_fusion
  76.8 1.2 %gather_fusion = s32[128]{0:T(128)S(1)} fusion(s32[64]{0:T(128)S(1)} %sub.27, s32[1024]{0:T(1024)S(1)} %pad_clamp_fusion), kind=kCustom, calls=%fused_computation | custom fusion | bytes 1536 | tf_op jit(solution)/shard_map/gather | solution.py:182
  78.1 0.0 copy-start.3
  78.1 1.9 %collective-permute-start.8 = (bf16[5,2,136,128]{3,2,1,0:T(8,128)(2,1)S(1)}, bf16[5,2,136,128]{3,2,1,0:T(8,128)(2,1)S(1)}, u32[]{:S(2)}, u32[]{:S(2)}) collective-permute-start(bf16[5,2,136,128]{3,2,1,0:T(8,128)(2,1)S(1)} %pad_maximum_fusion), channel_id=1, source_target_pairs={{0,256},{8,264},{16,272},{24,280},{32,288},{40,296},{48,304},{56,3... | collective-permute-start | bytes 1044488 | tf_op jit(solution)/shard_map/ppermute | solution.py:26
  80.1 0.6 fusion.1
  83.2 1.0 copy.35
  84.2 0.2 copy.29
  84.5 0.0 copy-done
  84.5 0.8 copy.40
  85.2 0.1 pad.15.clone
  85.3 1.2 %add_add_fusion.2.refs_0_ = s32[3]{0:T(128)} fusion(s32[1]{0:T(128)} %bitcast.20, s32[1]{0:T(128)} %get-tuple-element.41, s32[1]{0:T(128)} %bitcast), kind=kLoop, calls=%fused_computation.18 | loop fusion | flops 6 | bytes 24 | tf_op jit(solution)/shard_map/stack | solution.py:195
  86.6 1.2 %add_add_fusion.1.refs_0_ = s32[3]{0:T(128)} fusion(s32[1]{0:T(128)} %bitcast.19, s32[1]{0:T(128)} %get-tuple-element.41, s32[1]{0:T(128)} %bitcast), kind=kLoop, calls=%fused_computation.17 | loop fusion | flops 6 | bytes 24 | tf_op jit(solution)/shard_map/stack | solution.py:195
  87.8 1.2 %add_add_fusion.refs_0_ = s32[3]{0:T(128)} fusion(s32[1]{0:T(128)} %bitcast.6, s32[1]{0:T(128)} %get-tuple-element.41, s32[1]{0:T(128)} %bitcast), kind=kLoop, calls=%fused_computation.16 | loop fusion | flops 6 | bytes 24 | tf_op jit(solution)/shard_map/stack | solution.py:195
  89.0 0.6 broadcast_in_dim.16.refs_3_
  89.6 0.0 copy-done.3
  89.6 0.7 broadcast_in_dim.17.refs_4_
  90.3 4.2 %shard_map.73 = (f32[8,128]{1,0:T(8,128)}, f32[8,128]{1,0:T(8,128)}, f32[128,1024]{1,0:T(8,128)}) custom-call(s32[3]{0:T(128)} %add_add_fusion.2.refs_0_, bf16[128,1024]{1,0:T(8,128)(2,1)} %bitcast.44, bf16[4,2,136,128]{3,2,1,0:T(8,128)(2,1)} %copy-done.1, s32[8,128]{1,0:T(8,128)} %broadcast_in_dim.16.refs_3_, f32[128,128]{1,0:T(8,128)} %broadcast_in_dim.17.refs_4_), custom_call_target="tpu_custom_call" | custom-call | tf_op jit(solution)/shard_map/pallas_call | solution.py:144
  94.5 9.4 %shard_map.74 = (f32[8,128]{1,0:T(8,128)}, f32[8,128]{1,0:T(8,128)}, f32[128,1024]{1,0:T(8,128)}) custom-call(s32[3]{0:T(128)} %add_add_fusion.1.refs_0_, bf16[128,1024]{1,0:T(8,128)(2,1)} %bitcast.45, bf16[16,2,136,128]{3,2,1,0:T(8,128)(2,1)} %copy-done, s32[8,128]{1,0:T(8,128)} %broadcast_in_dim.16.refs_3_, f32[128,128]{1,0:T(8,128)} %broadcast_in_dim.17.refs_4_, ...), custom_call_target="tpu_custom_call" | custom-call | tf_op jit(solution)/shard_map/pallas_call | solution.py:144
  103.9 0.0 collective-permute-done.8
  103.9 3.9 %collective-permute-done.7 = bf16[16,2,136,128]{3,2,1,0:T(8,128)(2,1)S(1)} collective-permute-done((bf16[16,2,136,128]{3,2,1,0:T(8,128)(2,1)S(1)}, bf16[16,2,136,128]{3,2,1,0:T(8,128)(2,1)S(1)}, u32[]{:S(2)}, u32[]{:S(2)}) %collective-permute-start.7) | collective-permute-done | bytes 1114144 | tf_op jit(solution)/shard_map/ppermute | solution.py:26
  107.9 1.3 %maximum_maximum_fusion.refs_2_ = bf16[22,2,136,128]{3,2,1,0:T(8,128)(2,1)} fusion(bf16[5,2,136,128]{3,2,1,0:T(8,128)(2,1)S(1)} %collective-permute-done.8, bf16[16,2,136,128]{3,2,1,0:T(8,128)(2,1)S(1)} %collective-permute-done.7, bf16[22]{0:T(256)(128)(2,1)S(1)} %pad.15.clone), kind=kLoop, calls=%fused_computation.1 | loop fusion | flops 1531904 | bytes 2994220 | tf_op jit(solution)/shard_map/concatenate | solution.py:193
  109.2 11.9 %shard_map.75 = bf16[128,1024]{1,0:T(8,128)(2,1)} custom-call(s32[3]{0:T(128)} %add_add_fusion.refs_0_, bf16[128,1024]{1,0:T(8,128)(2,1)} %bitcast.46, bf16[22,2,136,128]{3,2,1,0:T(8,128)(2,1)} %maximum_maximum_fusion.refs_2_, s32[8,128]{1,0:T(8,128)} %broadcast_in_dim.16.refs_3_, f32[128,128]{1,0:T(8,128)} %broadcast_in_dim.17.refs_4_, ...), custom_call_target="tpu_custom_call" | custom-call | tf_op jit(solution)/shard_map/pallas_call | solution.py:144
  (17 shorter events, 0.3 us)
Async XLA Ops:
  0.0 48.1 %copy-start.2 = (s32[64]{0:T(128)S(1)}, s32[64]{0:T(128)}, u32[]{:S(2)}) copy-start(s32[64]{0:T(128)} %param.17) | copy-start | bytes 772
  2.2 15.3 %all-to-all-start = ((bf16[16,2,8,128]{3,0,1,2:T(8,128)(2,1)}), bf16[16,2,8,128]{3,0,1,2:T(8,128)(2,1)S(1)}, u32[]{:S(2)}, u32[]{:S(2)}) async-start(bf16[16,2,8,128]{3,0,1,2:T(8,128)(2,1)} %copy.30), calls=%async_computation | async-start | bytes 131072 | tf_op jit(solution)/shard_map/all_to_all | solution.py:165
  17.7 14.1 %collective-permute-start = (bf16[1,2,136,128]{3,2,1,0:T(8,128)(2,1)S(1)}, bf16[1,2,136,128]{3,2,1,0:T(8,128)(2,1)S(1)}, u32[]{:S(2)}, u32[]{:S(2)}) collective-permute-start(bf16[1,2,136,128]{3,2,1,0:T(8,128)(2,1)S(1)} %maximum_bitcast_fusion), channel_id=1, source_target_pairs={{0,8},{8,16},{16,24},{24,32},{32,40},{40,48},{48,56},{56,64},{64,7... | collective-permute-start | bytes 208904 | tf_op jit(solution)/shard_map/ppermute | solution.py:26
  20.5 11.2 %collective-permute-start.1 = (bf16[1,2,136,128]{3,2,1,0:T(8,128)(2,1)S(1)}, bf16[1,2,136,128]{3,2,1,0:T(8,128)(2,1)S(1)}, u32[]{:S(2)}, u32[]{:S(2)}) collective-permute-start(bf16[1,2,136,128]{3,2,1,0:T(8,128)(2,1)S(1)} %maximum_bitcast_fusion), channel_id=1, source_target_pairs={{0,16},{8,24},{16,32},{24,40},{32,48},{40,56},{48,64},{56,72},{64,... | collective-permute-start | bytes 208904 | tf_op jit(solution)/shard_map/ppermute | solution.py:26
  24.8 8.9 %collective-permute-start.2 = (bf16[1,2,136,128]{3,2,1,0:T(8,128)(2,1)S(1)}, bf16[1,2,136,128]{3,2,1,0:T(8,128)(2,1)S(1)}, u32[]{:S(2)}, u32[]{:S(2)}) collective-permute-start(bf16[1,2,136,128]{3,2,1,0:T(8,128)(2,1)S(1)} %maximum_bitcast_fusion), channel_id=1, source_target_pairs={{0,24},{8,32},{16,40},{24,48},{32,56},{40,64},{48,72},{56,80},{64,... | collective-permute-start | bytes 208904 | tf_op jit(solution)/shard_map/ppermute | solution.py:26
  33.7 37.9 %copy-start.1 = (bf16[4,2,136,128]{3,2,1,0:T(8,128)(2,1)}, bf16[4,2,136,128]{3,2,1,0:T(8,128)(2,1)S(1)}, u32[]{:S(2)}) copy-start(bf16[4,2,136,128]{3,2,1,0:T(8,128)(2,1)S(1)} %pad_maximum_fusion.1.refs_2_) | copy-start | bytes 835588
  33.7 24.4 %collective-permute-start.3 = (bf16[4,2,136,128]{3,2,1,0:T(8,128)(2,1)S(1)}, bf16[4,2,136,128]{3,2,1,0:T(8,128)(2,1)S(1)}, u32[]{:S(2)}, u32[]{:S(2)}) collective-permute-start(bf16[4,2,136,128]{3,2,1,0:T(8,128)(2,1)S(1)} %pad_maximum_fusion.1.refs_2_), channel_id=1, source_target_pairs={{0,32},{8,40},{16,48},{24,56},{32,64},{40,72},{48,80},{56,88},{64,... | collective-permute-start | bytes 835592 | tf_op jit(solution)/shard_map/ppermute | solution.py:26
  41.2 26.1 %collective-permute-start.4 = (bf16[4,2,136,128]{3,2,1,0:T(8,128)(2,1)S(1)}, bf16[4,2,136,128]{3,2,1,0:T(8,128)(2,1)S(1)}, u32[]{:S(2)}, u32[]{:S(2)}) collective-permute-start(bf16[4,2,136,128]{3,2,1,0:T(8,128)(2,1)S(1)} %pad_maximum_fusion.1.refs_2_), channel_id=1, source_target_pairs={{0,64},{8,72},{16,80},{24,88},{32,96},{40,104},{48,112},{56,120},{... | collective-permute-start | bytes 835592 | tf_op jit(solution)/shard_map/ppermute | solution.py:26
  46.2 25.4 %collective-permute-start.5 = (bf16[4,2,136,128]{3,2,1,0:T(8,128)(2,1)S(1)}, bf16[4,2,136,128]{3,2,1,0:T(8,128)(2,1)S(1)}, u32[]{:S(2)}, u32[]{:S(2)}) collective-permute-start(bf16[4,2,136,128]{3,2,1,0:T(8,128)(2,1)S(1)} %pad_maximum_fusion.1.refs_2_), channel_id=1, source_target_pairs={{0,96},{8,104},{16,112},{24,120},{32,128},{40,136},{48,144},{56,15... | collective-permute-start | bytes 835592 | tf_op jit(solution)/shard_map/ppermute | solution.py:26
  48.4 23.1 %collective-permute-start.6 = (bf16[4,2,136,128]{3,2,1,0:T(8,128)(2,1)S(1)}, bf16[4,2,136,128]{3,2,1,0:T(8,128)(2,1)S(1)}, u32[]{:S(2)}, u32[]{:S(2)}) collective-permute-start(bf16[4,2,136,128]{3,2,1,0:T(8,128)(2,1)S(1)} %pad_maximum_fusion.1.refs_2_), channel_id=1, source_target_pairs={{0,128},{8,136},{16,144},{24,152},{32,160},{40,168},{48,176},{56,1... | collective-permute-start | bytes 835592 | tf_op jit(solution)/shard_map/ppermute | solution.py:26
  71.6 12.8 %copy-start = (bf16[16,2,136,128]{3,2,1,0:T(8,128)(2,1)}, bf16[16,2,136,128]{3,2,1,0:T(8,128)(2,1)S(1)}, u32[]{:S(2)}) copy-start(bf16[16,2,136,128]{3,2,1,0:T(8,128)(2,1)S(1)} %constant_dynamic-update-slice_fusion.refs_2_) | copy-start | bytes 3342340
  71.7 36.2 %collective-permute-start.7 = (bf16[16,2,136,128]{3,2,1,0:T(8,128)(2,1)S(1)}, bf16[16,2,136,128]{3,2,1,0:T(8,128)(2,1)S(1)}, u32[]{:S(2)}, u32[]{:S(2)}) collective-permute-start(bf16[16,2,136,128]{3,2,1,0:T(8,128)(2,1)S(1)} %constant_dynamic-update-slice_fusion.refs_2_), channel_id=1, source_target_pairs={{0,128},{8,136},{16,144},{24,152},{32,160},{40,168},{48,176},{56,1... | collective-permute-start | bytes 3342344 | tf_op jit(solution)/shard_map/ppermute | solution.py:26
  78.1 11.5 %copy-start.3 = (f32[128]{0:T(128)S(1)}, f32[128]{0:T(128)}, u32[]{:S(2)}) copy-start(f32[128]{0:T(128)} %param.16) | copy-start | bytes 1540
  78.1 25.8 %collective-permute-start.8 = (bf16[5,2,136,128]{3,2,1,0:T(8,128)(2,1)S(1)}, bf16[5,2,136,128]{3,2,1,0:T(8,128)(2,1)S(1)}, u32[]{:S(2)}, u32[]{:S(2)}) collective-permute-start(bf16[5,2,136,128]{3,2,1,0:T(8,128)(2,1)S(1)} %pad_maximum_fusion), channel_id=1, source_target_pairs={{0,256},{8,264},{16,272},{24,280},{32,288},{40,296},{48,304},{56,3... | collective-permute-start | bytes 1044488 | tf_op jit(solution)/shard_map/ppermute | solution.py:26

commit v11 on v10

--- a/solution.py
+++ b/solution.py
@@ -26,16 +26,22 @@
     return lax.ppermute(x, "seq", pairs)
 
 
-def gather_stages(packet, count, depth):
+def gather_chunks(packet, count, depth):
     first = [packet[None]] + [shift_from(packet[None], offset, count) for offset in (1, 2, 3)]
     block = jnp.concatenate(first, axis=0)
-    middle = [shift_from(block, offset, count) for offset in (4, 8, 12, 16)]
-    block = jnp.concatenate([block] + middle, axis=0)
-    last = [shift_from(block[4:], 16, count), shift_from(block[4:depth - 32], 32, count)]
-    return [first, middle, last]
-
-
-def attention_kernel(first, last, offset, *refs):
+    middle = [shift_from(block, offset, count) for offset in (4, 8, 12, 16, 32)]
+    near = jnp.concatenate([block] + middle[:3], axis=0)
+    near, *middle[3:] = lax.optimization_barrier([near] + middle[3:])
+    last = [shift_from(near[4:], 16, count), shift_from(near[4:depth - 32], 32, count)]
+    pad = jnp.zeros((1,) + packet.shape, packet.dtype)
+    return [
+        (block, ((0, 0),)),
+        (jnp.concatenate(middle, axis=0), ((0, 4), (16, 16))),
+        (jnp.concatenate(last + [pad], axis=0), ((0, 20), (12, 24))),
+    ]
+
+
+def attention_kernel(first, last, segments, *refs):
     info_ref, query_ref, window_ref, low_ref, mean_ref = refs[:5]
     rest = refs[5:]
     if not first:
@@ -51,7 +57,7 @@
     group_size, rows = max_ref.shape
     inv_scale = 1.0 / math.sqrt(HD)
     seq_index = info_ref[0]
-    pairs = info_ref[1]
+    used = info_ref[1]
     low_top = info_ref[2]
     if first:
         max_ref[...] = jnp.full(max_ref.shape, NEG, jnp.float32)
@@ -70,7 +76,7 @@
         row = window_ref[slot, part, rows:rows + 1, :].astype(jnp.float32)
         return jnp.transpose(jnp.broadcast_to(row, (rows, rows)))
 
-    def fold_pair(pair, masked):
+    def fold_pair(pair, shift, masked):
         parts = []
         for half in range(2):
             slot = 2 * pair + half
@@ -80,7 +86,7 @@
             value_scale = column(slot, 1)
             allowed = None
             if masked:
-                key_pos = (seq_index - offset - slot) * rows + sub
+                key_pos = (seq_index - shift - slot) * rows + sub
                 allowed = (key_pos <= query_pos) & (key_pos >= low)
             blocks = []
             for g in range(group_size):
@@ -110,12 +116,23 @@
             sum_ref[g:g + 1, :] = run_sum
 
     def one_pair(pair, carry):
-        nearest = offset + 2 * pair
+        shift = jnp.int32(segments[0][1])
+        for begin, moved in segments[1:]:
+            shift = jnp.where(2 * pair >= begin, jnp.int32(moved), shift)
+        nearest = shift + 2 * pair
         inside = (nearest >= 1) & ((seq_index - nearest - 1) * rows >= low_top)
-        lax.cond(inside, lambda: fold_pair(pair, False), lambda: fold_pair(pair, True))
+        branch = jnp.where(nearest >= used, 0, jnp.where(inside, 1, 2))
+        lax.switch(
+            branch,
+            [
+                lambda: None,
+                lambda: fold_pair(pair, shift, False),
+                lambda: fold_pair(pair, shift, True),
+            ],
+        )
         return carry
 
-    lax.fori_loop(0, pairs, one_pair, 0)
+    lax.fori_loop(0, window_ref.shape[0] // 2, one_pair, 0)
     if last:
         mean = mean_ref[...]
         for g in range(group_size):
@@ -127,7 +144,7 @@
         acc_out[...] = acc_ref[...]
 
 
-def attend_part(info, query_t, window, low, mean, state, offset, last, width):
+def attend_part(info, query_t, window, low, mean, state, segments, last, width):
     group_size = query_t.shape[1] // HD
     rows = low.shape[1]
     full = lambda shape: pl.BlockSpec(shape, lambda i, info: (0,) * len(shape))
@@ -140,7 +157,7 @@
     else:
         out_shape = (row_shape, row_shape, acc_shape)
         out_specs = (full(row_shape.shape), full(row_shape.shape), full(acc_shape.shape))
-    kernel = functools.partial(attention_kernel, state is None, last, offset)
+    kernel = functools.partial(attention_kernel, state is None, last, segments)
     return pl.pallas_call(
         kernel,
         out_shape=out_shape,
@@ -177,27 +194,20 @@
     scale_rows = jnp.zeros((2, pad_rows, row_count), jnp.bfloat16)
     scale_rows = scale_rows.at[0, 0].set(key_scale_row).at[1, 0].set(value_scale_row)
     packet = jnp.concatenate([jnp.stack([local_keys, local_values.T]), scale_rows], axis=1)
-    stages = gather_stages(packet, seq_count, depth)
+    chunks = gather_chunks(packet, seq_count, depth)
     own_pos = seq_index * row_count + jnp.arange(row_count, dtype=jnp.int32)
     low = starts[doc_index(own_pos, starts)]
     used = jnp.clip(seq_index - low[0] // row_count + 1, 1, depth).astype(jnp.int32)
     low_tile = jnp.broadcast_to(low[None, :], (8, row_count)).astype(jnp.int32)
     mean = jnp.broadcast_to(value_means.reshape(HD, 1), (HD, row_count))
     query_all = queries.reshape(row_count, group_size, HD).transpose(2, 1, 0).reshape(HD, -1)
-    chunks = [jnp.concatenate(stage, axis=0) for stage in stages]
+    info = jnp.stack([seq_index.astype(jnp.int32), used, low[-1].astype(jnp.int32)])
     state = None
-    offset = 0
-    for index, chunk in enumerate(chunks):
-        slots = chunk.shape[0]
-        if slots % 2:
-            chunk = jnp.concatenate([chunk, jnp.zeros((1,) + chunk.shape[1:], chunk.dtype)])
-        pairs = jnp.clip((used - offset + 1) // 2, 0, chunk.shape[0] // 2).astype(jnp.int32)
-        info = jnp.stack([seq_index.astype(jnp.int32), pairs, low[-1].astype(jnp.int32)])
+    for index, (chunk, segments) in enumerate(chunks):
         last = index == len(chunks) - 1
         state = attend_part(
-            info, query_all, chunk, low_tile, mean, state, offset, last, queries.shape[1]
+            info, query_all, chunk, low_tile, mean, state, segments, last, queries.shape[1]
         )
-        offset += slots
     return state
 
 

time: 122 us -> 121 us (level)
  the two profiles are of different devices: /device:TPU:134 before, /device:TPU:4 now
where the time goes in v11:
time: 121 us
  starting transfers between devices  48.7 us (40%)
  waiting for transfers between devices  30 us (25%)
  Pallas kernels  20.8 us (17%)
  local copies, waits for them, and re-layouts  11.9 us (10%)
  other arithmetic  6.25 us (5%)
  between operations  2.89 us (2%)
    ppermute x10, starting transfers between devices, shift_from(): return lax.ppermute(x, 'seq', pairs)  41.6 us
    ppermute x10, waiting for transfers between devices, shift_from(): return lax.ppermute(x, 'seq', pairs)  25.3 us
    pallas_call x3, Pallas kernels, attend_part(): pl.pallas_call(kernel, out_shape=out_shape, grid_spec=pltpu.PrefetchScala...  20.8 us
    all_to_all x1, starting transfers between devices, shards(): both = lax.all_to_all(both, 'head', split_axis=2, concat_axis=0, tiled=True)  7.1 us
    unnamed x22, local copies, waits for them, and re-layouts  5.59 us
    all_to_all x1, waiting for transfers between devices, shards(): both = lax.all_to_all(both, 'head', split_axis=2, concat_axis=0, tiled=True)  4.7 us
  transfers between devices with their start and end apart: 11, of which 6 were waited for; matrix products, arithmetic and copies ran while one was open for 9% of the time, Pallas kernels for 11%

profile of v11, /device:TPU:4, one launch (start us, length us, event | category | flops | bytes accessed | tf_op | source)
XLA Modules:
  0.0 120.6 jit_solution(5249646730827784541)
XLA Ops:
  0.0 0.8 copy.37
  0.8 0.8 copy.38
  1.5 0.6 copy.30
  2.2 7.1 %all-to-all-start = ((bf16[16,2,8,128]{3,0,1,2:T(8,128)(2,1)}), bf16[16,2,8,128]{3,0,1,2:T(8,128)(2,1)S(1)}, u32[]{:S(2)}, u32[]{:S(2)}) async-start(bf16[16,2,8,128]{3,0,1,2:T(8,128)(2,1)} %copy.30), calls=%async_computation | async-start | bytes 131072 | tf_op jit(solution)/shard_map/all_to_all | solution.py:182
  9.3 0.8 reduce.5
  10.1 0.1 broadcast_in_dim.12
  10.1 0.1 reshape.145
  10.2 0.8 reduce.6
  11.0 0.1 broadcast_in_dim.13
  11.1 0.1 reshape.147
  11.2 0.7 copy.28
  11.9 0.1 reduce-window.9
  12.0 0.1 reduce.4
  12.1 0.7 sub.16
  12.8 4.7 %all-to-all-done = bf16[16,2,8,128]{3,0,1,2:T(8,128)(2,1)S(1)} async-done(((bf16[16,2,8,128]{3,0,1,2:T(8,128)(2,1)}), bf16[16,2,8,128]{3,0,1,2:T(8,128)(2,1)S(1)}, u32[]{:S(2)}, u32[]{:S(2)}) %all-to-all-start) | async-done | bytes 65568 | tf_op jit(solution)/shard_map/all_to_all | solution.py:182
  17.5 0.1 copy.34
  17.7 2.8 %collective-permute-start = (bf16[1,2,136,128]{3,2,1,0:T(8,128)(2,1)S(1)}, bf16[1,2,136,128]{3,2,1,0:T(8,128)(2,1)S(1)}, u32[]{:S(2)}, u32[]{:S(2)}) collective-permute-start(bf16[1,2,136,128]{3,2,1,0:T(8,128)(2,1)S(1)} %maximum_bitcast_fusion), channel_id=1, source_target_pairs={{0,8},{8,16},{16,24},{24,32},{32,40},{40,48},{48,56},{56,64},{64,7... | collective-permute-start | bytes 208904 | tf_op jit(solution)/shard_map/ppermute | solution.py:26
  20.5 4.3 %collective-permute-start.1 = (bf16[1,2,136,128]{3,2,1,0:T(8,128)(2,1)S(1)}, bf16[1,2,136,128]{3,2,1,0:T(8,128)(2,1)S(1)}, u32[]{:S(2)}, u32[]{:S(2)}) collective-permute-start(bf16[1,2,136,128]{3,2,1,0:T(8,128)(2,1)S(1)} %maximum_bitcast_fusion), channel_id=1, source_target_pairs={{0,16},{8,24},{16,32},{24,40},{32,48},{40,56},{48,64},{56,72},{64,... | collective-permute-start | bytes 208904 | tf_op jit(solution)/shard_map/ppermute | solution.py:26
  24.8 6.6 %collective-permute-start.2 = (bf16[1,2,136,128]{3,2,1,0:T(8,128)(2,1)S(1)}, bf16[1,2,136,128]{3,2,1,0:T(8,128)(2,1)S(1)}, u32[]{:S(2)}, u32[]{:S(2)}) collective-permute-start(bf16[1,2,136,128]{3,2,1,0:T(8,128)(2,1)S(1)} %maximum_bitcast_fusion), channel_id=1, source_target_pairs={{0,24},{8,32},{16,40},{24,48},{32,56},{40,64},{48,72},{56,80},{64,... | collective-permute-start | bytes 208904 | tf_op jit(solution)/shard_map/ppermute | solution.py:26
  31.4 0.0 collective-permute-done
  31.5 3.0 %collective-permute-done.1 = bf16[1,2,136,128]{3,2,1,0:T(8,128)(2,1)S(1)} collective-permute-done((bf16[1,2,136,128]{3,2,1,0:T(8,128)(2,1)S(1)}, bf16[1,2,136,128]{3,2,1,0:T(8,128)(2,1)S(1)}, u32[]{:S(2)}, u32[]{:S(2)}) %collective-permute-start.1) | collective-permute-done | bytes 69664 | tf_op jit(solution)/shard_map/ppermute | solution.py:26
  34.5 3.3 %collective-permute-done.2 = bf16[1,2,136,128]{3,2,1,0:T(8,128)(2,1)S(1)} collective-permute-done((bf16[1,2,136,128]{3,2,1,0:T(8,128)(2,1)S(1)}, bf16[1,2,136,128]{3,2,1,0:T(8,128)(2,1)S(1)}, u32[]{:S(2)}, u32[]{:S(2)}) %collective-permute-start.2) | collective-permute-done | bytes 69664 | tf_op jit(solution)/shard_map/ppermute | solution.py:26
  37.9 0.0 copy-start.1
  37.9 1.9 %collective-permute-start.3 = (bf16[4,2,136,128]{3,2,1,0:T(8,128)(2,1)S(1)}, bf16[4,2,136,128]{3,2,1,0:T(8,128)(2,1)S(1)}, u32[]{:S(2)}, u32[]{:S(2)}) collective-permute-start(bf16[4,2,136,128]{3,2,1,0:T(8,128)(2,1)S(1)} %pad_maximum_fusion.refs_2_), channel_id=1, source_target_pairs={{0,32},{8,40},{16,48},{24,56},{32,64},{40,72},{48,80},{56,88},{64,... | collective-permute-start | bytes 835592 | tf_op jit(solution)/shard_map/ppermute | solution.py:26
  39.8 7.6 %collective-permute-start.4 = (bf16[4,2,136,128]{3,2,1,0:T(8,128)(2,1)S(1)}, bf16[4,2,136,128]{3,2,1,0:T(8,128)(2,1)S(1)}, u32[]{:S(2)}, u32[]{:S(2)}) collective-permute-start(bf16[4,2,136,128]{3,2,1,0:T(8,128)(2,1)S(1)} %pad_maximum_fusion.refs_2_), channel_id=1, source_target_pairs={{0,64},{8,72},{16,80},{24,88},{32,96},{40,104},{48,112},{56,120},{... | collective-permute-start | bytes 835592 | tf_op jit(solution)/shard_map/ppermute | solution.py:26
  47.4 6.0 %collective-permute-start.5 = (bf16[4,2,136,128]{3,2,1,0:T(8,128)(2,1)S(1)}, bf16[4,2,136,128]{3,2,1,0:T(8,128)(2,1)S(1)}, u32[]{:S(2)}, u32[]{:S(2)}) collective-permute-start(bf16[4,2,136,128]{3,2,1,0:T(8,128)(2,1)S(1)} %pad_maximum_fusion.refs_2_), channel_id=1, source_target_pairs={{0,96},{8,104},{16,112},{24,120},{32,128},{40,136},{48,144},{56,15... | collective-permute-start | bytes 835592 | tf_op jit(solution)/shard_map/ppermute | solution.py:26
  53.4 2.4 %collective-permute-start.6 = (bf16[4,2,136,128]{3,2,1,0:T(8,128)(2,1)S(1)}, bf16[4,2,136,128]{3,2,1,0:T(8,128)(2,1)S(1)}, u32[]{:S(2)}, u32[]{:S(2)}) collective-permute-start(bf16[4,2,136,128]{3,2,1,0:T(8,128)(2,1)S(1)} %pad_maximum_fusion.refs_2_), channel_id=1, source_target_pairs={{0,128},{8,136},{16,144},{24,152},{32,160},{40,168},{48,176},{56,1... | collective-permute-start | bytes 835592 | tf_op jit(solution)/shard_map/ppermute | solution.py:26
  55.8 3.7 %collective-permute-start.7 = (bf16[4,2,136,128]{3,2,1,0:T(8,128)(2,1)S(1)}, bf16[4,2,136,128]{3,2,1,0:T(8,128)(2,1)S(1)}, u32[]{:S(2)}, u32[]{:S(2)}) collective-permute-start(bf16[4,2,136,128]{3,2,1,0:T(8,128)(2,1)S(1)} %pad_maximum_fusion.refs_2_), channel_id=1, source_target_pairs={{0,256},{8,264},{16,272},{24,280},{32,288},{40,296},{48,304},{56,3... | collective-permute-start | bytes 835592 | tf_op jit(solution)/shard_map/ppermute | solution.py:26
  59.6 4.2 %collective-permute-done.3 = bf16[4,2,136,128]{3,2,1,0:T(8,128)(2,1)S(1)} collective-permute-done((bf16[4,2,136,128]{3,2,1,0:T(8,128)(2,1)S(1)}, bf16[4,2,136,128]{3,2,1,0:T(8,128)(2,1)S(1)}, u32[]{:S(2)}, u32[]{:S(2)}) %collective-permute-start.3) | collective-permute-done | bytes 278560 | tf_op jit(solution)/shard_map/ppermute | solution.py:26
  63.8 0.1 constant_dynamic-update-slice_fusion.11
  63.9 0.0 collective-permute-done.4
  64.0 0.1 constant_dynamic-update-slice_fusion.10
  64.1 6.5 %collective-permute-done.5 = bf16[4,2,136,128]{3,2,1,0:T(8,128)(2,1)S(1)} collective-permute-done((bf16[4,2,136,128]{3,2,1,0:T(8,128)(2,1)S(1)}, bf16[4,2,136,128]{3,2,1,0:T(8,128)(2,1)S(1)}, u32[]{:S(2)}, u32[]{:S(2)}) %collective-permute-start.5) | collective-permute-done | bytes 278560 | tf_op jit(solution)/shard_map/ppermute | solution.py:26
  70.6 0.1 constant_dynamic-update-slice_fusion.9
  70.7 0.0 copy-done.1
  70.7 8.2 %collective-permute-done.6 = bf16[4,2,136,128]{3,2,1,0:T(8,128)(2,1)S(1)} collective-permute-done((bf16[4,2,136,128]{3,2,1,0:T(8,128)(2,1)S(1)}, bf16[4,2,136,128]{3,2,1,0:T(8,128)(2,1)S(1)}, u32[]{:S(2)}, u32[]{:S(2)}) %collective-permute-start.6) | collective-permute-done | bytes 278560 | tf_op jit(solution)/shard_map/ppermute | solution.py:26
  78.9 0.0 collective-permute-done.7
  78.9 0.0 copy-start.2
  78.9 0.7 copy-done.2
  79.6 1.0 slice.63
  80.6 1.9 %collective-permute-start.8 = (bf16[12,2,136,128]{3,2,1,0:T(8,128)(2,1)}, bf16[12,2,136,128]{3,2,1,0:T(8,128)(2,1)}, u32[]{:S(2)}, u32[]{:S(2)}) collective-permute-start(bf16[12,2,136,128]{3,2,1,0:T(8,128)(2,1)} %slice.63), channel_id=1, source_target_pairs={{0,128},{8,136},{16,144},{24,152},{32,160},{40,168},{48,176},{56,1... | collective-permute-start | bytes 2506760 | tf_op jit(solution)/shard_map/ppermute | solution.py:26
  82.5 0.1 convert_reduce_fusion
  82.6 1.2 %gather_fusion = s32[128]{0:T(128)S(1)} fusion(s32[64]{0:T(128)S(1)} %sub.16, s32[1024]{0:T(1024)S(1)} %pad_clamp_fusion), kind=kCustom, calls=%fused_computation | custom fusion | bytes 1536 | tf_op jit(solution)/shard_map/gather | solution.py:199
  83.8 0.0 copy-start.4
  83.9 0.6 fusion.1
  87.1 1.0 copy.35
  88.1 0.2 copy.29
  88.4 0.7 copy.40
  89.1 0.1 pad.9.clone
  89.2 0.0 copy-start.3
  89.2 4.3 %collective-permute-start.9 = (bf16[5,2,136,128]{3,2,1,0:T(8,128)(2,1)S(1)}, bf16[5,2,136,128]{3,2,1,0:T(8,128)(2,1)S(1)}, u32[]{:S(2)}, u32[]{:S(2)}) collective-permute-start(bf16[5,2,136,128]{3,2,1,0:T(8,128)(2,1)S(1)} %slice.64), channel_id=1, source_target_pairs={{0,256},{8,264},{16,272},{24,280},{32,288},{40,296},{48,304},{56,3... | collective-permute-start | bytes 1044488 | tf_op jit(solution)/shard_map/ppermute | solution.py:26
  93.6 1.3 %pad_add_fusion.refs_0_ = s32[3]{0:T(128)} fusion(s32[1]{0:T(128)} %get-tuple-element.54, s32[1]{0:T(128)} %bitcast.6, s32[1]{0:T(128)} %bitcast), kind=kLoop, calls=%fused_computation.23 | loop fusion | flops 6 | bytes 24 | tf_op jit(solution)/shard_map/stack | solution.py:204
  94.9 0.6 broadcast_in_dim.16.refs_3_
  95.4 0.0 copy-done.4
  95.5 0.7 broadcast_in_dim.17.refs_4_
  96.2 4.2 %shard_map.73 = (f32[8,128]{1,0:T(8,128)}, f32[8,128]{1,0:T(8,128)}, f32[128,1024]{1,0:T(8,128)}) custom-call(s32[3]{0:T(128)} %pad_add_fusion.refs_0_, bf16[128,1024]{1,0:T(8,128)(2,1)} %bitcast.44, bf16[4,2,136,128]{3,2,1,0:T(8,128)(2,1)} %copy-done.1, s32[8,128]{1,0:T(8,128)} %broadcast_in_dim.16.refs_3_, f32[128,128]{1,0:T(8,128)} %broadcast_in_dim.17.refs_4_), custom_call_target="tpu_custom_call" | custom-call | tf_op jit(solution)/shard_map/pallas_call | solution.py:161
  100.4 0.0 copy-done.3
  100.4 0.0 copy-start
  100.4 1.1 copy-done
  101.5 9.5 %shard_map.74 = (f32[8,128]{1,0:T(8,128)}, f32[8,128]{1,0:T(8,128)}, f32[128,1024]{1,0:T(8,128)}) custom-call(s32[3]{0:T(128)} %pad_add_fusion.refs_0_, bf16[128,1024]{1,0:T(8,128)(2,1)} %bitcast.45, bf16[20,2,136,128]{3,2,1,0:T(8,128)(2,1)} %copy-done, s32[8,128]{1,0:T(8,128)} %broadcast_in_dim.16.refs_3_, f32[128,128]{1,0:T(8,128)} %broadcast_in_dim.17.refs_4_, ...), custom_call_target="tpu_custom_call" | custom-call | tf_op jit(solution)/shard_map/pallas_call | solution.py:161
  111.1 0.0 collective-permute-done.9
  111.1 0.0 collective-permute-done.8
  111.1 2.4 %maximum_maximum_fusion.refs_2_ = bf16[18,2,136,128]{3,2,1,0:T(8,128)(2,1)} fusion(bf16[5,2,136,128]{3,2,1,0:T(8,128)(2,1)S(1)} %collective-permute-done.9, bf16[12,2,136,128]{3,2,1,0:T(8,128)(2,1)} %collective-permute-done.8, bf16[18]{0:T(256)(128)(2,1)S(1)} %pad.9.clone), kind=kLoop, calls=%fused_computation.1 | loop fusion | flops 1253376 | bytes 2437156 | tf_op jit(solution)/shard_map/concatenate | solution.py:40
  113.4 7.1 %shard_map.75 = bf16[128,1024]{1,0:T(8,128)(2,1)} custom-call(s32[3]{0:T(128)} %pad_add_fusion.refs_0_, bf16[128,1024]{1,0:T(8,128)(2,1)} %bitcast.46, bf16[18,2,136,128]{3,2,1,0:T(8,128)(2,1)} %maximum_maximum_fusion.refs_2_, s32[8,128]{1,0:T(8,128)} %broadcast_in_dim.16.refs_3_, f32[128,128]{1,0:T(8,128)} %broadcast_in_dim.17.refs_4_, ...), custom_call_target="tpu_custom_call" | custom-call | tf_op jit(solution)/shard_map/pallas_call | solution.py:161
  (18 shorter events, 0.3 us)
Async XLA Ops:
  2.2 15.3 %all-to-all-start = ((bf16[16,2,8,128]{3,0,1,2:T(8,128)(2,1)}), bf16[16,2,8,128]{3,0,1,2:T(8,128)(2,1)S(1)}, u32[]{:S(2)}, u32[]{:S(2)}) async-start(bf16[16,2,8,128]{3,0,1,2:T(8,128)(2,1)} %copy.30), calls=%async_computation | async-start | bytes 131072 | tf_op jit(solution)/shard_map/all_to_all | solution.py:182
  17.7 13.8 %collective-permute-start = (bf16[1,2,136,128]{3,2,1,0:T(8,128)(2,1)S(1)}, bf16[1,2,136,128]{3,2,1,0:T(8,128)(2,1)S(1)}, u32[]{:S(2)}, u32[]{:S(2)}) collective-permute-start(bf16[1,2,136,128]{3,2,1,0:T(8,128)(2,1)S(1)} %maximum_bitcast_fusion), channel_id=1, source_target_pairs={{0,8},{8,16},{16,24},{24,32},{32,40},{40,48},{48,56},{56,64},{64,7... | collective-permute-start | bytes 208904 | tf_op jit(solution)/shard_map/ppermute | solution.py:26
  20.5 13.9 %collective-permute-start.1 = (bf16[1,2,136,128]{3,2,1,0:T(8,128)(2,1)S(1)}, bf16[1,2,136,128]{3,2,1,0:T(8,128)(2,1)S(1)}, u32[]{:S(2)}, u32[]{:S(2)}) collective-permute-start(bf16[1,2,136,128]{3,2,1,0:T(8,128)(2,1)S(1)} %maximum_bitcast_fusion), channel_id=1, source_target_pairs={{0,16},{8,24},{16,32},{24,40},{32,48},{40,56},{48,64},{56,72},{64,... | collective-permute-start | bytes 208904 | tf_op jit(solution)/shard_map/ppermute | solution.py:26
  24.8 13.0 %collective-permute-start.2 = (bf16[1,2,136,128]{3,2,1,0:T(8,128)(2,1)S(1)}, bf16[1,2,136,128]{3,2,1,0:T(8,128)(2,1)S(1)}, u32[]{:S(2)}, u32[]{:S(2)}) collective-permute-start(bf16[1,2,136,128]{3,2,1,0:T(8,128)(2,1)S(1)} %maximum_bitcast_fusion), channel_id=1, source_target_pairs={{0,24},{8,32},{16,40},{24,48},{32,56},{40,64},{48,72},{56,80},{64,... | collective-permute-start | bytes 208904 | tf_op jit(solution)/shard_map/ppermute | solution.py:26
  37.9 32.8 %copy-start.1 = (bf16[4,2,136,128]{3,2,1,0:T(8,128)(2,1)}, bf16[4,2,136,128]{3,2,1,0:T(8,128)(2,1)S(1)}, u32[]{:S(2)}) copy-start(bf16[4,2,136,128]{3,2,1,0:T(8,128)(2,1)S(1)} %pad_maximum_fusion.refs_2_) | copy-start | bytes 835588
  37.9 26.0 %collective-permute-start.3 = (bf16[4,2,136,128]{3,2,1,0:T(8,128)(2,1)S(1)}, bf16[4,2,136,128]{3,2,1,0:T(8,128)(2,1)S(1)}, u32[]{:S(2)}, u32[]{:S(2)}) collective-permute-start(bf16[4,2,136,128]{3,2,1,0:T(8,128)(2,1)S(1)} %pad_maximum_fusion.refs_2_), channel_id=1, source_target_pairs={{0,32},{8,40},{16,48},{24,56},{32,64},{40,72},{48,80},{56,88},{64,... | collective-permute-start | bytes 835592 | tf_op jit(solution)/shard_map/ppermute | solution.py:26
  39.8 24.1 %collective-permute-start.4 = (bf16[4,2,136,128]{3,2,1,0:T(8,128)(2,1)S(1)}, bf16[4,2,136,128]{3,2,1,0:T(8,128)(2,1)S(1)}, u32[]{:S(2)}, u32[]{:S(2)}) collective-permute-start(bf16[4,2,136,128]{3,2,1,0:T(8,128)(2,1)S(1)} %pad_maximum_fusion.refs_2_), channel_id=1, source_target_pairs={{0,64},{8,72},{16,80},{24,88},{32,96},{40,104},{48,112},{56,120},{... | collective-permute-start | bytes 835592 | tf_op jit(solution)/shard_map/ppermute | solution.py:26
  47.4 23.1 %collective-permute-start.5 = (bf16[4,2,136,128]{3,2,1,0:T(8,128)(2,1)S(1)}, bf16[4,2,136,128]{3,2,1,0:T(8,128)(2,1)S(1)}, u32[]{:S(2)}, u32[]{:S(2)}) collective-permute-start(bf16[4,2,136,128]{3,2,1,0:T(8,128)(2,1)S(1)} %pad_maximum_fusion.refs_2_), channel_id=1, source_target_pairs={{0,96},{8,104},{16,112},{24,120},{32,128},{40,136},{48,144},{56,15... | collective-permute-start | bytes 835592 | tf_op jit(solution)/shard_map/ppermute | solution.py:26
  53.4 25.5 %collective-permute-start.6 = (bf16[4,2,136,128]{3,2,1,0:T(8,128)(2,1)S(1)}, bf16[4,2,136,128]{3,2,1,0:T(8,128)(2,1)S(1)}, u32[]{:S(2)}, u32[]{:S(2)}) collective-permute-start(bf16[4,2,136,128]{3,2,1,0:T(8,128)(2,1)S(1)} %pad_maximum_fusion.refs_2_), channel_id=1, source_target_pairs={{0,128},{8,136},{16,144},{24,152},{32,160},{40,168},{48,176},{56,1... | collective-permute-start | bytes 835592 | tf_op jit(solution)/shard_map/ppermute | solution.py:26
  55.8 23.1 %collective-permute-start.7 = (bf16[4,2,136,128]{3,2,1,0:T(8,128)(2,1)S(1)}, bf16[4,2,136,128]{3,2,1,0:T(8,128)(2,1)S(1)}, u32[]{:S(2)}, u32[]{:S(2)}) collective-permute-start(bf16[4,2,136,128]{3,2,1,0:T(8,128)(2,1)S(1)} %pad_maximum_fusion.refs_2_), channel_id=1, source_target_pairs={{0,256},{8,264},{16,272},{24,280},{32,288},{40,296},{48,304},{56,3... | collective-permute-start | bytes 835592 | tf_op jit(solution)/shard_map/ppermute | solution.py:26
  78.9 0.7 copy-start.2
  80.6 30.5 %collective-permute-start.8 = (bf16[12,2,136,128]{3,2,1,0:T(8,128)(2,1)}, bf16[12,2,136,128]{3,2,1,0:T(8,128)(2,1)}, u32[]{:S(2)}, u32[]{:S(2)}) collective-permute-start(bf16[12,2,136,128]{3,2,1,0:T(8,128)(2,1)} %slice.63), channel_id=1, source_target_pairs={{0,128},{8,136},{16,144},{24,152},{32,160},{40,168},{48,176},{56,1... | collective-permute-start | bytes 2506760 | tf_op jit(solution)/shard_map/ppermute | solution.py:26
  83.8 11.6 %copy-start.4 = (f32[128]{0:T(128)S(1)}, f32[128]{0:T(128)}, u32[]{:S(2)}) copy-start(f32[128]{0:T(128)} %param.16) | copy-start | bytes 1540
  89.2 11.2 %copy-start.3 = (bf16[4,2,136,128]{3,2,1,0:T(8,128)(2,1)S(1)}, bf16[4,2,136,128]{3,2,1,0:T(8,128)(2,1)}, u32[]{:S(2)}) copy-start(bf16[4,2,136,128]{3,2,1,0:T(8,128)(2,1)} %copy-done.2) | copy-start | bytes 835588
  89.2 21.8 %collective-permute-start.9 = (bf16[5,2,136,128]{3,2,1,0:T(8,128)(2,1)S(1)}, bf16[5,2,136,128]{3,2,1,0:T(8,128)(2,1)S(1)}, u32[]{:S(2)}, u32[]{:S(2)}) collective-permute-start(bf16[5,2,136,128]{3,2,1,0:T(8,128)(2,1)S(1)} %slice.64), channel_id=1, source_target_pairs={{0,256},{8,264},{16,272},{24,280},{32,288},{40,296},{48,304},{56,3... | collective-permute-start | bytes 1044488 | tf_op jit(solution)/shard_map/ppermute | solution.py:26
  100.4 1.1 copy-start

commit v12 on v10

--- a/solution.py
+++ b/solution.py
@@ -160,11 +160,12 @@
 
 def shards(queries, key_tokens, value_tokens, key_scales, value_scales, value_means, doc_lengths):
     heads = lax.axis_size("head")
-    both = jnp.stack([key_tokens, value_tokens], axis=1)
-    both = both.reshape(both.shape[0], 2, heads, -1)
-    both = lax.all_to_all(both, "head", split_axis=2, concat_axis=0, tiled=True)
-    local_keys = both[:, 0, 0]
-    local_values = both[:, 1, 0]
+    rows_in = key_tokens.shape[0]
+    both = jnp.concatenate([key_tokens, value_tokens], axis=0)
+    both = lax.all_to_all(both, "head", split_axis=1, concat_axis=0, tiled=True)
+    both = both.reshape(heads, 2, rows_in, HD)
+    local_keys = both[:, 0].reshape(heads * rows_in, HD)
+    local_values = both[:, 1].reshape(heads * rows_in, HD)
     row_count = local_keys.shape[0]
     group_size = QH // KVH
     seq_count = lax.axis_size("seq")

time: 122 us -> 120 us (0.984)
  the two profiles are of different devices: /device:TPU:134 before, /device:TPU:6 now
where the time goes in v12:
time: 120 us; the launch traced here: 119 us
  starting transfers between devices  46.1 us (38%)
  waiting for transfers between devices  31.5 us (26%)
  Pallas kernels  24.6 us (20%)
  other arithmetic  8.46 us (7%)
  local copies, waits for them, and re-layouts  5.91 us (5%)
  between operations  2.76 us (2%)
    ppermute x9, starting transfers between devices, shift_from(): return lax.ppermute(x, 'seq', pairs)  39 us
    ppermute x9, waiting for transfers between devices, shift_from(): return lax.ppermute(x, 'seq', pairs)  25.2 us
    pallas_call x3, Pallas kernels, attend_part(): pl.pallas_call(kernel, out_shape=out_shape, grid_spec=pltpu.PrefetchScala...  24.6 us
    all_to_all x1, starting transfers between devices, shards(): both = lax.all_to_all(both, 'head', split_axis=1, concat_axis=0, tiled=True)  7.1 us
    all_to_all x1, waiting for transfers between devices, shards(): both = lax.all_to_all(both, 'head', split_axis=1, concat_axis=0, tiled=True)  6.32 us
    another operation x3, other arithmetic, shards(): jnp.stack([seq_index.astype(jnp.int32), pairs, low[-1].astype(jnp.int32)])  3.72 us
  transfers between devices with their start and end apart: 10, of which 8 were waited for; matrix products, arithmetic and copies ran while one was open for 10% of the time, Pallas kernels for 11%

profile of v12, /device:TPU:6, one launch (start us, length us, event | category | flops | bytes accessed | tf_op | source)
XLA Modules:
  0.0 119.3 jit_solution(16549910476410538030)
XLA Ops:
  0.0 0.0 copy-start.2
  0.0 1.4 %copy_bitcast_fusion.1 = bf16[32,8,128]{2,0,1:T(8,128)(2,1)} fusion(bf16[16,1024]{1,0:T(8,128)(2,1)} %param.13, bf16[16,1024]{1,0:T(8,128)(2,1)} %param.12), kind=kLoop, calls=%fused_computation.6 | loop fusion | flops 131072 | bytes 131072 | tf_op jit(solution)/shard_map/all_to_all | solution.py:165
  1.4 7.1 %all-to-all-start = ((bf16[32,8,128]{2,0,1:T(8,128)(2,1)}), bf16[32,8,128]{2,0,1:T(8,128)(2,1)S(1)}, u32[]{:S(2)}, u32[]{:S(2)}) async-start(bf16[32,8,128]{2,0,1:T(8,128)(2,1)} %copy_bitcast_fusion.1), calls=%async_computation | async-start | bytes 131072 | tf_op jit(solution)/shard_map/all_to_all | solution.py:165
  8.5 0.8 reduce.5
  9.3 0.1 broadcast_in_dim.12
  9.4 0.1 reshape.148
  9.5 0.8 reduce.6
  10.2 0.1 broadcast_in_dim.13
  10.3 0.1 reshape.150
  10.4 6.3 %all-to-all-done = bf16[32,8,128]{2,0,1:T(8,128)(2,1)S(1)} async-done(((bf16[32,8,128]{2,0,1:T(8,128)(2,1)}), bf16[32,8,128]{2,0,1:T(8,128)(2,1)S(1)}, u32[]{:S(2)}, u32[]{:S(2)}) %all-to-all-start) | async-done | bytes 65568 | tf_op jit(solution)/shard_map/all_to_all | solution.py:165
  16.8 0.1 copy.25
  16.9 2.8 %collective-permute-start = (bf16[1,2,136,128]{3,2,1,0:T(8,128)(2,1)S(1)}, bf16[1,2,136,128]{3,2,1,0:T(8,128)(2,1)S(1)}, u32[]{:S(2)}, u32[]{:S(2)}) collective-permute-start(bf16[1,2,136,128]{3,2,1,0:T(8,128)(2,1)S(1)} %maximum_bitcast_fusion), channel_id=1, source_target_pairs={{0,8},{8,16},{16,24},{24,32},{32,40},{40,48},{48,56},{56,64},{64,7... | collective-permute-start | bytes 208904 | tf_op jit(solution)/shard_map/ppermute | solution.py:26
  19.8 4.3 %collective-permute-start.1 = (bf16[1,2,136,128]{3,2,1,0:T(8,128)(2,1)S(1)}, bf16[1,2,136,128]{3,2,1,0:T(8,128)(2,1)S(1)}, u32[]{:S(2)}, u32[]{:S(2)}) collective-permute-start(bf16[1,2,136,128]{3,2,1,0:T(8,128)(2,1)S(1)} %maximum_bitcast_fusion), channel_id=1, source_target_pairs={{0,16},{8,24},{16,32},{24,40},{32,48},{40,56},{48,64},{56,72},{64,... | collective-permute-start | bytes 208904 | tf_op jit(solution)/shard_map/ppermute | solution.py:26
  24.0 6.6 %collective-permute-start.2 = (bf16[1,2,136,128]{3,2,1,0:T(8,128)(2,1)S(1)}, bf16[1,2,136,128]{3,2,1,0:T(8,128)(2,1)S(1)}, u32[]{:S(2)}, u32[]{:S(2)}) collective-permute-start(bf16[1,2,136,128]{3,2,1,0:T(8,128)(2,1)S(1)} %maximum_bitcast_fusion), channel_id=1, source_target_pairs={{0,24},{8,32},{16,40},{24,48},{32,56},{40,64},{48,72},{56,80},{64,... | collective-permute-start | bytes 208904 | tf_op jit(solution)/shard_map/ppermute | solution.py:26
  30.7 0.1 collective-permute-done
  30.8 3.2 %collective-permute-done.1 = bf16[1,2,136,128]{3,2,1,0:T(8,128)(2,1)S(1)} collective-permute-done((bf16[1,2,136,128]{3,2,1,0:T(8,128)(2,1)S(1)}, bf16[1,2,136,128]{3,2,1,0:T(8,128)(2,1)S(1)}, u32[]{:S(2)}, u32[]{:S(2)}) %collective-permute-start.1) | collective-permute-done | bytes 69664 | tf_op jit(solution)/shard_map/ppermute | solution.py:26
  34.0 3.3 %collective-permute-done.2 = bf16[1,2,136,128]{3,2,1,0:T(8,128)(2,1)S(1)} collective-permute-done((bf16[1,2,136,128]{3,2,1,0:T(8,128)(2,1)S(1)}, bf16[1,2,136,128]{3,2,1,0:T(8,128)(2,1)S(1)}, u32[]{:S(2)}, u32[]{:S(2)}) %collective-permute-start.2) | collective-permute-done | bytes 69664 | tf_op jit(solution)/shard_map/ppermute | solution.py:26
  37.4 0.0 copy-start.1
  37.4 1.9 %collective-permute-start.3 = (bf16[4,2,136,128]{3,2,1,0:T(8,128)(2,1)S(1)}, bf16[4,2,136,128]{3,2,1,0:T(8,128)(2,1)S(1)}, u32[]{:S(2)}, u32[]{:S(2)}) collective-permute-start(bf16[4,2,136,128]{3,2,1,0:T(8,128)(2,1)S(1)} %pad_maximum_fusion.1.refs_2_), channel_id=1, source_target_pairs={{0,32},{8,40},{16,48},{24,56},{32,64},{40,72},{48,80},{56,88},{64,... | collective-permute-start | bytes 835592 | tf_op jit(solution)/shard_map/ppermute | solution.py:26
  39.3 7.3 %collective-permute-start.4 = (bf16[4,2,136,128]{3,2,1,0:T(8,128)(2,1)S(1)}, bf16[4,2,136,128]{3,2,1,0:T(8,128)(2,1)S(1)}, u32[]{:S(2)}, u32[]{:S(2)}) collective-permute-start(bf16[4,2,136,128]{3,2,1,0:T(8,128)(2,1)S(1)} %pad_maximum_fusion.1.refs_2_), channel_id=1, source_target_pairs={{0,64},{8,72},{16,80},{24,88},{32,96},{40,104},{48,112},{56,120},{... | collective-permute-start | bytes 835592 | tf_op jit(solution)/shard_map/ppermute | solution.py:26
  46.6 5.3 %collective-permute-start.5 = (bf16[4,2,136,128]{3,2,1,0:T(8,128)(2,1)S(1)}, bf16[4,2,136,128]{3,2,1,0:T(8,128)(2,1)S(1)}, u32[]{:S(2)}, u32[]{:S(2)}) collective-permute-start(bf16[4,2,136,128]{3,2,1,0:T(8,128)(2,1)S(1)} %pad_maximum_fusion.1.refs_2_), channel_id=1, source_target_pairs={{0,96},{8,104},{16,112},{24,120},{32,128},{40,136},{48,144},{56,15... | collective-permute-start | bytes 835592 | tf_op jit(solution)/shard_map/ppermute | solution.py:26
  52.0 0.0 copy-done.2
  52.0 0.1 copy.22
  52.1 0.1 reduce-window.9
  52.2 0.1 reduce.4
  52.3 3.4 %collective-permute-start.6 = (bf16[4,2,136,128]{3,2,1,0:T(8,128)(2,1)S(1)}, bf16[4,2,136,128]{3,2,1,0:T(8,128)(2,1)S(1)}, u32[]{:S(2)}, u32[]{:S(2)}) collective-permute-start(bf16[4,2,136,128]{3,2,1,0:T(8,128)(2,1)S(1)} %pad_maximum_fusion.1.refs_2_), channel_id=1, source_target_pairs={{0,128},{8,136},{16,144},{24,152},{32,160},{40,168},{48,176},{56,1... | collective-permute-start | bytes 835592 | tf_op jit(solution)/shard_map/ppermute | solution.py:26
  55.7 7.7 %collective-permute-done.3 = bf16[4,2,136,128]{3,2,1,0:T(8,128)(2,1)S(1)} collective-permute-done((bf16[4,2,136,128]{3,2,1,0:T(8,128)(2,1)S(1)}, bf16[4,2,136,128]{3,2,1,0:T(8,128)(2,1)S(1)}, u32[]{:S(2)}, u32[]{:S(2)}) %collective-permute-start.3) | collective-permute-done | bytes 278560 | tf_op jit(solution)/shard_map/ppermute | solution.py:26
  63.4 0.0 collective-permute-done.4
  63.5 6.4 %collective-permute-done.5 = bf16[4,2,136,128]{3,2,1,0:T(8,128)(2,1)S(1)} collective-permute-done((bf16[4,2,136,128]{3,2,1,0:T(8,128)(2,1)S(1)}, bf16[4,2,136,128]{3,2,1,0:T(8,128)(2,1)S(1)}, u32[]{:S(2)}, u32[]{:S(2)}) %collective-permute-start.5) | collective-permute-done | bytes 278560 | tf_op jit(solution)/shard_map/ppermute | solution.py:26
  69.9 1.7 %collective-permute-done.6 = bf16[4,2,136,128]{3,2,1,0:T(8,128)(2,1)S(1)} collective-permute-done((bf16[4,2,136,128]{3,2,1,0:T(8,128)(2,1)S(1)}, bf16[4,2,136,128]{3,2,1,0:T(8,128)(2,1)S(1)}, u32[]{:S(2)}, u32[]{:S(2)}) %collective-permute-start.6) | collective-permute-done | bytes 278560 | tf_op jit(solution)/shard_map/ppermute | solution.py:26
  71.7 0.0 copy-done.1
  71.7 0.0 copy-start
  71.7 4.9 %collective-permute-start.7 = (bf16[16,2,136,128]{3,2,1,0:T(8,128)(2,1)S(1)}, bf16[16,2,136,128]{3,2,1,0:T(8,128)(2,1)S(1)}, u32[]{:S(2)}, u32[]{:S(2)}) collective-permute-start(bf16[16,2,136,128]{3,2,1,0:T(8,128)(2,1)S(1)} %constant_dynamic-update-slice_fusion.refs_2_), channel_id=1, source_target_pairs={{0,128},{8,136},{16,144},{24,152},{32,160},{40,168},{48,176},{56,1... | collective-permute-start | bytes 3342344 | tf_op jit(solution)/shard_map/ppermute | solution.py:26
  76.6 0.1 convert_reduce_fusion
  76.7 1.2 %gather_fusion = s32[128]{0:T(128)S(1)} fusion(s32[64]{0:T(128)S(1)} %sub.27, s32[1024]{0:T(1024)S(1)} %pad_clamp_fusion), kind=kCustom, calls=%fused_computation | custom fusion | bytes 1536 | tf_op jit(solution)/shard_map/gather | solution.py:183
  78.0 0.0 copy-start.3
  78.0 2.4 %collective-permute-start.8 = (bf16[5,2,136,128]{3,2,1,0:T(8,128)(2,1)S(1)}, bf16[5,2,136,128]{3,2,1,0:T(8,128)(2,1)S(1)}, u32[]{:S(2)}, u32[]{:S(2)}) collective-permute-start(bf16[5,2,136,128]{3,2,1,0:T(8,128)(2,1)S(1)} %pad_maximum_fusion), channel_id=1, source_target_pairs={{0,256},{8,264},{16,272},{24,280},{32,288},{40,296},{48,304},{56,3... | collective-permute-start | bytes 1044488 | tf_op jit(solution)/shard_map/ppermute | solution.py:26
  80.5 0.6 fusion.2
  83.6 1.0 copy.27
  84.6 0.2 copy.23
  84.8 0.0 copy-done
  84.8 0.8 copy.31
  85.6 0.1 pad.15.clone
  85.7 1.3 %add_add_fusion.2.refs_0_ = s32[3]{0:T(128)} fusion(s32[1]{0:T(128)} %bitcast.17, s32[1]{0:T(128)} %get-tuple-element.43, s32[1]{0:T(128)} %bitcast), kind=kLoop, calls=%fused_computation.18 | loop fusion | flops 6 | bytes 24 | tf_op jit(solution)/shard_map/stack | solution.py:196
  86.9 1.3 %add_add_fusion.1.refs_0_ = s32[3]{0:T(128)} fusion(s32[1]{0:T(128)} %bitcast.16, s32[1]{0:T(128)} %get-tuple-element.43, s32[1]{0:T(128)} %bitcast), kind=kLoop, calls=%fused_computation.17 | loop fusion | flops 6 | bytes 24 | tf_op jit(solution)/shard_map/stack | solution.py:196
  88.2 1.2 %add_add_fusion.refs_0_ = s32[3]{0:T(128)} fusion(s32[1]{0:T(128)} %bitcast.6, s32[1]{0:T(128)} %get-tuple-element.43, s32[1]{0:T(128)} %bitcast), kind=kLoop, calls=%fused_computation.16 | loop fusion | flops 6 | bytes 24 | tf_op jit(solution)/shard_map/stack | solution.py:196
  89.4 0.6 broadcast_in_dim.16.refs_3_
  90.0 0.0 copy-done.3
  90.0 0.7 broadcast_in_dim.17.refs_4_
  90.7 4.2 %shard_map.73 = (f32[8,128]{1,0:T(8,128)}, f32[8,128]{1,0:T(8,128)}, f32[128,1024]{1,0:T(8,128)}) custom-call(s32[3]{0:T(128)} %add_add_fusion.2.refs_0_, bf16[128,1024]{1,0:T(8,128)(2,1)} %bitcast.35, bf16[4,2,136,128]{3,2,1,0:T(8,128)(2,1)} %copy-done.1, s32[8,128]{1,0:T(8,128)} %broadcast_in_dim.16.refs_3_, f32[128,128]{1,0:T(8,128)} %broadcast_in_dim.17.refs_4_), custom_call_target="tpu_custom_call" | custom-call | tf_op jit(solution)/shard_map/pallas_call | solution.py:144
  94.8 9.3 %shard_map.74 = (f32[8,128]{1,0:T(8,128)}, f32[8,128]{1,0:T(8,128)}, f32[128,1024]{1,0:T(8,128)}) custom-call(s32[3]{0:T(128)} %add_add_fusion.1.refs_0_, bf16[128,1024]{1,0:T(8,128)(2,1)} %bitcast.36, bf16[16,2,136,128]{3,2,1,0:T(8,128)(2,1)} %copy-done, s32[8,128]{1,0:T(8,128)} %broadcast_in_dim.16.refs_3_, f32[128,128]{1,0:T(8,128)} %broadcast_in_dim.17.refs_4_, ...), custom_call_target="tpu_custom_call" | custom-call | tf_op jit(solution)/shard_map/pallas_call | solution.py:144
  104.2 0.0 collective-permute-done.8
  104.2 2.7 %collective-permute-done.7 = bf16[16,2,136,128]{3,2,1,0:T(8,128)(2,1)S(1)} collective-permute-done((bf16[16,2,136,128]{3,2,1,0:T(8,128)(2,1)S(1)}, bf16[16,2,136,128]{3,2,1,0:T(8,128)(2,1)S(1)}, u32[]{:S(2)}, u32[]{:S(2)}) %collective-permute-start.7) | collective-permute-done | bytes 1114144 | tf_op jit(solution)/shard_map/ppermute | solution.py:26
  106.9 1.4 %maximum_maximum_fusion.refs_2_ = bf16[22,2,136,128]{3,2,1,0:T(8,128)(2,1)} fusion(bf16[5,2,136,128]{3,2,1,0:T(8,128)(2,1)S(1)} %collective-permute-done.8, bf16[16,2,136,128]{3,2,1,0:T(8,128)(2,1)S(1)} %collective-permute-done.7, bf16[22]{0:T(256)(128)(2,1)S(1)} %pad.15.clone), kind=kLoop, calls=%fused_computation.1 | loop fusion | flops 1531904 | bytes 2994220 | tf_op jit(solution)/shard_map/concatenate | solution.py:194
  108.3 11.1 %shard_map.75 = bf16[128,1024]{1,0:T(8,128)(2,1)} custom-call(s32[3]{0:T(128)} %add_add_fusion.refs_0_, bf16[128,1024]{1,0:T(8,128)(2,1)} %bitcast.37, bf16[22,2,136,128]{3,2,1,0:T(8,128)(2,1)} %maximum_maximum_fusion.refs_2_, s32[8,128]{1,0:T(8,128)} %broadcast_in_dim.16.refs_3_, f32[128,128]{1,0:T(8,128)} %broadcast_in_dim.17.refs_4_, ...), custom_call_target="tpu_custom_call" | custom-call | tf_op jit(solution)/shard_map/pallas_call | solution.py:144
  (14 shorter events, 0.3 us)
Async XLA Ops:
  0.0 52.0 %copy-start.2 = (s32[64]{0:T(128)S(1)}, s32[64]{0:T(128)}, u32[]{:S(2)}) copy-start(s32[64]{0:T(128)} %param.17) | copy-start | bytes 772
  1.4 15.3 %all-to-all-start = ((bf16[32,8,128]{2,0,1:T(8,128)(2,1)}), bf16[32,8,128]{2,0,1:T(8,128)(2,1)S(1)}, u32[]{:S(2)}, u32[]{:S(2)}) async-start(bf16[32,8,128]{2,0,1:T(8,128)(2,1)} %copy_bitcast_fusion.1), calls=%async_computation | async-start | bytes 131072 | tf_op jit(solution)/shard_map/all_to_all | solution.py:165
  16.9 13.9 %collective-permute-start = (bf16[1,2,136,128]{3,2,1,0:T(8,128)(2,1)S(1)}, bf16[1,2,136,128]{3,2,1,0:T(8,128)(2,1)S(1)}, u32[]{:S(2)}, u32[]{:S(2)}) collective-permute-start(bf16[1,2,136,128]{3,2,1,0:T(8,128)(2,1)S(1)} %maximum_bitcast_fusion), channel_id=1, source_target_pairs={{0,8},{8,16},{16,24},{24,32},{32,40},{40,48},{48,56},{56,64},{64,7... | collective-permute-start | bytes 208904 | tf_op jit(solution)/shard_map/ppermute | solution.py:26
  19.8 14.2 %collective-permute-start.1 = (bf16[1,2,136,128]{3,2,1,0:T(8,128)(2,1)S(1)}, bf16[1,2,136,128]{3,2,1,0:T(8,128)(2,1)S(1)}, u32[]{:S(2)}, u32[]{:S(2)}) collective-permute-start(bf16[1,2,136,128]{3,2,1,0:T(8,128)(2,1)S(1)} %maximum_bitcast_fusion), channel_id=1, source_target_pairs={{0,16},{8,24},{16,32},{24,40},{32,48},{40,56},{48,64},{56,72},{64,... | collective-permute-start | bytes 208904 | tf_op jit(solution)/shard_map/ppermute | solution.py:26
  24.0 13.3 %collective-permute-start.2 = (bf16[1,2,136,128]{3,2,1,0:T(8,128)(2,1)S(1)}, bf16[1,2,136,128]{3,2,1,0:T(8,128)(2,1)S(1)}, u32[]{:S(2)}, u32[]{:S(2)}) collective-permute-start(bf16[1,2,136,128]{3,2,1,0:T(8,128)(2,1)S(1)} %maximum_bitcast_fusion), channel_id=1, source_target_pairs={{0,24},{8,32},{16,40},{24,48},{32,56},{40,64},{48,72},{56,80},{64,... | collective-permute-start | bytes 208904 | tf_op jit(solution)/shard_map/ppermute | solution.py:26
  37.4 34.3 %copy-start.1 = (bf16[4,2,136,128]{3,2,1,0:T(8,128)(2,1)}, bf16[4,2,136,128]{3,2,1,0:T(8,128)(2,1)S(1)}, u32[]{:S(2)}) copy-start(bf16[4,2,136,128]{3,2,1,0:T(8,128)(2,1)S(1)} %pad_maximum_fusion.1.refs_2_) | copy-start | bytes 835588
  37.4 26.0 %collective-permute-start.3 = (bf16[4,2,136,128]{3,2,1,0:T(8,128)(2,1)S(1)}, bf16[4,2,136,128]{3,2,1,0:T(8,128)(2,1)S(1)}, u32[]{:S(2)}, u32[]{:S(2)}) collective-permute-start(bf16[4,2,136,128]{3,2,1,0:T(8,128)(2,1)S(1)} %pad_maximum_fusion.1.refs_2_), channel_id=1, source_target_pairs={{0,32},{8,40},{16,48},{24,56},{32,64},{40,72},{48,80},{56,88},{64,... | collective-permute-start | bytes 835592 | tf_op jit(solution)/shard_map/ppermute | solution.py:26
  39.3 24.1 %collective-permute-start.4 = (bf16[4,2,136,128]{3,2,1,0:T(8,128)(2,1)S(1)}, bf16[4,2,136,128]{3,2,1,0:T(8,128)(2,1)S(1)}, u32[]{:S(2)}, u32[]{:S(2)}) collective-permute-start(bf16[4,2,136,128]{3,2,1,0:T(8,128)(2,1)S(1)} %pad_maximum_fusion.1.refs_2_), channel_id=1, source_target_pairs={{0,64},{8,72},{16,80},{24,88},{32,96},{40,104},{48,112},{56,120},{... | collective-permute-start | bytes 835592 | tf_op jit(solution)/shard_map/ppermute | solution.py:26
  46.6 23.2 %collective-permute-start.5 = (bf16[4,2,136,128]{3,2,1,0:T(8,128)(2,1)S(1)}, bf16[4,2,136,128]{3,2,1,0:T(8,128)(2,1)S(1)}, u32[]{:S(2)}, u32[]{:S(2)}) collective-permute-start(bf16[4,2,136,128]{3,2,1,0:T(8,128)(2,1)S(1)} %pad_maximum_fusion.1.refs_2_), channel_id=1, source_target_pairs={{0,96},{8,104},{16,112},{24,120},{32,128},{40,136},{48,144},{56,15... | collective-permute-start | bytes 835592 | tf_op jit(solution)/shard_map/ppermute | solution.py:26
  52.3 19.3 %collective-permute-start.6 = (bf16[4,2,136,128]{3,2,1,0:T(8,128)(2,1)S(1)}, bf16[4,2,136,128]{3,2,1,0:T(8,128)(2,1)S(1)}, u32[]{:S(2)}, u32[]{:S(2)}) collective-permute-start(bf16[4,2,136,128]{3,2,1,0:T(8,128)(2,1)S(1)} %pad_maximum_fusion.1.refs_2_), channel_id=1, source_target_pairs={{0,128},{8,136},{16,144},{24,152},{32,160},{40,168},{48,176},{56,1... | collective-permute-start | bytes 835592 | tf_op jit(solution)/shard_map/ppermute | solution.py:26
  71.7 13.2 %copy-start = (bf16[16,2,136,128]{3,2,1,0:T(8,128)(2,1)}, bf16[16,2,136,128]{3,2,1,0:T(8,128)(2,1)S(1)}, u32[]{:S(2)}) copy-start(bf16[16,2,136,128]{3,2,1,0:T(8,128)(2,1)S(1)} %constant_dynamic-update-slice_fusion.refs_2_) | copy-start | bytes 3342340
  71.7 35.2 %collective-permute-start.7 = (bf16[16,2,136,128]{3,2,1,0:T(8,128)(2,1)S(1)}, bf16[16,2,136,128]{3,2,1,0:T(8,128)(2,1)S(1)}, u32[]{:S(2)}, u32[]{:S(2)}) collective-permute-start(bf16[16,2,136,128]{3,2,1,0:T(8,128)(2,1)S(1)} %constant_dynamic-update-slice_fusion.refs_2_), channel_id=1, source_target_pairs={{0,128},{8,136},{16,144},{24,152},{32,160},{40,168},{48,176},{56,1... | collective-permute-start | bytes 3342344 | tf_op jit(solution)/shard_map/ppermute | solution.py:26
  78.0 12.0 %copy-start.3 = (f32[128]{0:T(128)S(1)}, f32[128]{0:T(128)}, u32[]{:S(2)}) copy-start(f32[128]{0:T(128)} %param.16) | copy-start | bytes 1540
  78.0 26.2 %collective-permute-start.8 = (bf16[5,2,136,128]{3,2,1,0:T(8,128)(2,1)S(1)}, bf16[5,2,136,128]{3,2,1,0:T(8,128)(2,1)S(1)}, u32[]{:S(2)}, u32[]{:S(2)}) collective-permute-start(bf16[5,2,136,128]{3,2,1,0:T(8,128)(2,1)S(1)} %pad_maximum_fusion), channel_id=1, source_target_pairs={{0,256},{8,264},{16,272},{24,280},{32,288},{40,296},{48,304},{56,3... | collective-permute-start | bytes 1044488 | tf_op jit(solution)/shard_map/ppermute | solution.py:26

commit v13 on v12

--- a/solution.py
+++ b/solution.py
@@ -15,6 +15,7 @@
 MOST = 5120
 
 NEG = -1e30
+STEP = 4
 
 
 def doc_index(positions, starts):
@@ -72,8 +73,8 @@
 
     def fold_pair(pair, masked):
         parts = []
-        for half in range(2):
-            slot = 2 * pair + half
+        for half in range(STEP):
+            slot = STEP * pair + half
             key_tile = window_ref[slot, 0, :rows, :]
             scores = jnp.dot(key_tile, query_t, preferred_element_type=jnp.float32)
             key_scale = column(slot, 0) * inv_scale
@@ -110,8 +111,8 @@
             sum_ref[g:g + 1, :] = run_sum
 
     def one_pair(pair, carry):
-        nearest = offset + 2 * pair
-        inside = (nearest >= 1) & ((seq_index - nearest - 1) * rows >= low_top)
+        nearest = offset + STEP * pair
+        inside = (nearest >= 1) & ((seq_index - nearest - STEP + 1) * rows >= low_top)
         lax.cond(inside, lambda: fold_pair(pair, False), lambda: fold_pair(pair, True))
         return carry
 
@@ -190,9 +191,11 @@
     offset = 0
     for index, chunk in enumerate(chunks):
         slots = chunk.shape[0]
-        if slots % 2:
-            chunk = jnp.concatenate([chunk, jnp.zeros((1,) + chunk.shape[1:], chunk.dtype)])
-        pairs = jnp.clip((used - offset + 1) // 2, 0, chunk.shape[0] // 2).astype(jnp.int32)
+        if slots % STEP:
+            fill = STEP - slots % STEP
+            chunk = jnp.concatenate([chunk, jnp.zeros((fill,) + chunk.shape[1:], chunk.dtype)])
+        pairs = jnp.clip((used - offset + STEP - 1) // STEP, 0, chunk.shape[0] // STEP)
+        pairs = pairs.astype(jnp.int32)
         info = jnp.stack([seq_index.astype(jnp.int32), pairs, low[-1].astype(jnp.int32)])
         last = index == len(chunks) - 1
         state = attend_part(

time: 120 us -> 119 us (level); the launches traced: 119 us -> 116 us
  Pallas kernels: 24.6 us -> 19.4 us
  waiting for transfers between devices: 31.5 us -> 33.6 us
    pallas_call x3, Pallas kernels: 24.6 us -> 19.4 us  [attend_part(): pl.pallas_call(kernel, out_shape=out_shape, grid_spec=pltpu.PrefetchScala...]
    ppermute x9, waiting for transfers between devices: 25.2 us -> 27.3 us  [shift_from(): return lax.ppermute(x, 'seq', pairs)]
  transfers between devices with their start and end apart: 10 -> 10, of which waited for: 8 -> 8; matrix products, arithmetic and copies ran while one was open for 10% -> 9% of each run, Pallas kernels for 11% -> 10%
where the time goes in v13:
time: 119 us; the launch traced here: 116 us
  starting transfers between devices  46.1 us (39%)
  waiting for transfers between devices  33.6 us (28%)
  Pallas kernels  19.4 us (16%)
  other arithmetic  9.45 us (8%)
  local copies, waits for them, and re-layouts  5.01 us (4%)
  between operations  2.84 us (2%)
    ppermute x9, starting transfers between devices, shift_from(): return lax.ppermute(x, 'seq', pairs)  39 us
    ppermute x9, waiting for transfers between devices, shift_from(): return lax.ppermute(x, 'seq', pairs)  27.3 us
    pallas_call x3, Pallas kernels, attend_part(): pl.pallas_call(kernel, out_shape=out_shape, grid_spec=pltpu.PrefetchScala...  19.4 us
    all_to_all x1, starting transfers between devices, shards(): both = lax.all_to_all(both, 'head', split_axis=1, concat_axis=0, tiled=True)  7.1 us
    all_to_all x1, waiting for transfers between devices, shards(): both = lax.all_to_all(both, 'head', split_axis=1, concat_axis=0, tiled=True)  6.32 us
    another operation x3, other arithmetic, shards(): jnp.stack([seq_index.astype(jnp.int32), pairs, low[-1].astype(jnp.int32)])  3.7 us
  transfers between devices with their start and end apart: 10, of which 8 were waited for; matrix products, arithmetic and copies ran while one was open for 9% of the time, Pallas kernels for 10%

profile of v13, /device:TPU:6, one launch (start us, length us, event | category | flops | bytes accessed | tf_op | source)
XLA Modules:
  0.0 116.5 jit_solution(14034037859455640725)
XLA Ops:
  0.0 0.0 copy-start.3
  0.0 1.4 %copy_bitcast_fusion.1 = bf16[32,8,128]{2,0,1:T(8,128)(2,1)} fusion(bf16[16,1024]{1,0:T(8,128)(2,1)} %param.13, bf16[16,1024]{1,0:T(8,128)(2,1)} %param.12), kind=kLoop, calls=%fused_computation.6 | loop fusion | flops 131072 | bytes 131072 | tf_op jit(solution)/shard_map/all_to_all | solution.py:166
  1.4 7.1 %all-to-all-start = ((bf16[32,8,128]{2,0,1:T(8,128)(2,1)}), bf16[32,8,128]{2,0,1:T(8,128)(2,1)S(1)}, u32[]{:S(2)}, u32[]{:S(2)}) async-start(bf16[32,8,128]{2,0,1:T(8,128)(2,1)} %copy_bitcast_fusion.1), calls=%async_computation | async-start | bytes 131072 | tf_op jit(solution)/shard_map/all_to_all | solution.py:166
  8.5 0.8 reduce.5
  9.3 0.1 broadcast_in_dim.12
  9.4 0.1 reshape.148
  9.5 0.8 reduce.6
  10.2 0.1 broadcast_in_dim.13
  10.3 0.1 reshape.150
  10.4 6.3 %all-to-all-done = bf16[32,8,128]{2,0,1:T(8,128)(2,1)S(1)} async-done(((bf16[32,8,128]{2,0,1:T(8,128)(2,1)}), bf16[32,8,128]{2,0,1:T(8,128)(2,1)S(1)}, u32[]{:S(2)}, u32[]{:S(2)}) %all-to-all-start) | async-done | bytes 65568 | tf_op jit(solution)/shard_map/all_to_all | solution.py:166
  16.8 0.1 copy.25
  16.9 2.8 %collective-permute-start = (bf16[1,2,136,128]{3,2,1,0:T(8,128)(2,1)S(1)}, bf16[1,2,136,128]{3,2,1,0:T(8,128)(2,1)S(1)}, u32[]{:S(2)}, u32[]{:S(2)}) collective-permute-start(bf16[1,2,136,128]{3,2,1,0:T(8,128)(2,1)S(1)} %maximum_bitcast_fusion), channel_id=1, source_target_pairs={{0,8},{8,16},{16,24},{24,32},{32,40},{40,48},{48,56},{56,64},{64,7... | collective-permute-start | bytes 208904 | tf_op jit(solution)/shard_map/ppermute | solution.py:27
  19.8 4.3 %collective-permute-start.1 = (bf16[1,2,136,128]{3,2,1,0:T(8,128)(2,1)S(1)}, bf16[1,2,136,128]{3,2,1,0:T(8,128)(2,1)S(1)}, u32[]{:S(2)}, u32[]{:S(2)}) collective-permute-start(bf16[1,2,136,128]{3,2,1,0:T(8,128)(2,1)S(1)} %maximum_bitcast_fusion), channel_id=1, source_target_pairs={{0,16},{8,24},{16,32},{24,40},{32,48},{40,56},{48,64},{56,72},{64,... | collective-permute-start | bytes 208904 | tf_op jit(solution)/shard_map/ppermute | solution.py:27
  24.0 6.6 %collective-permute-start.2 = (bf16[1,2,136,128]{3,2,1,0:T(8,128)(2,1)S(1)}, bf16[1,2,136,128]{3,2,1,0:T(8,128)(2,1)S(1)}, u32[]{:S(2)}, u32[]{:S(2)}) collective-permute-start(bf16[1,2,136,128]{3,2,1,0:T(8,128)(2,1)S(1)} %maximum_bitcast_fusion), channel_id=1, source_target_pairs={{0,24},{8,32},{16,40},{24,48},{32,56},{40,64},{48,72},{56,80},{64,... | collective-permute-start | bytes 208904 | tf_op jit(solution)/shard_map/ppermute | solution.py:27
  30.7 0.1 collective-permute-done
  30.8 3.2 %collective-permute-done.1 = bf16[1,2,136,128]{3,2,1,0:T(8,128)(2,1)S(1)} collective-permute-done((bf16[1,2,136,128]{3,2,1,0:T(8,128)(2,1)S(1)}, bf16[1,2,136,128]{3,2,1,0:T(8,128)(2,1)S(1)}, u32[]{:S(2)}, u32[]{:S(2)}) %collective-permute-start.1) | collective-permute-done | bytes 69664 | tf_op jit(solution)/shard_map/ppermute | solution.py:27
  34.0 3.3 %collective-permute-done.2 = bf16[1,2,136,128]{3,2,1,0:T(8,128)(2,1)S(1)} collective-permute-done((bf16[1,2,136,128]{3,2,1,0:T(8,128)(2,1)S(1)}, bf16[1,2,136,128]{3,2,1,0:T(8,128)(2,1)S(1)}, u32[]{:S(2)}, u32[]{:S(2)}) %collective-permute-start.2) | collective-permute-done | bytes 69664 | tf_op jit(solution)/shard_map/ppermute | solution.py:27
  37.4 0.0 copy-start.1
  37.4 1.9 %collective-permute-start.3 = (bf16[4,2,136,128]{3,2,1,0:T(8,128)(2,1)S(1)}, bf16[4,2,136,128]{3,2,1,0:T(8,128)(2,1)S(1)}, u32[]{:S(2)}, u32[]{:S(2)}) collective-permute-start(bf16[4,2,136,128]{3,2,1,0:T(8,128)(2,1)S(1)} %pad_maximum_fusion.1.refs_2_), channel_id=1, source_target_pairs={{0,32},{8,40},{16,48},{24,56},{32,64},{40,72},{48,80},{56,88},{64,... | collective-permute-start | bytes 835592 | tf_op jit(solution)/shard_map/ppermute | solution.py:27
  39.3 7.3 %collective-permute-start.4 = (bf16[4,2,136,128]{3,2,1,0:T(8,128)(2,1)S(1)}, bf16[4,2,136,128]{3,2,1,0:T(8,128)(2,1)S(1)}, u32[]{:S(2)}, u32[]{:S(2)}) collective-permute-start(bf16[4,2,136,128]{3,2,1,0:T(8,128)(2,1)S(1)} %pad_maximum_fusion.1.refs_2_), channel_id=1, source_target_pairs={{0,64},{8,72},{16,80},{24,88},{32,96},{40,104},{48,112},{56,120},{... | collective-permute-start | bytes 835592 | tf_op jit(solution)/shard_map/ppermute | solution.py:27
  46.6 5.3 %collective-permute-start.5 = (bf16[4,2,136,128]{3,2,1,0:T(8,128)(2,1)S(1)}, bf16[4,2,136,128]{3,2,1,0:T(8,128)(2,1)S(1)}, u32[]{:S(2)}, u32[]{:S(2)}) collective-permute-start(bf16[4,2,136,128]{3,2,1,0:T(8,128)(2,1)S(1)} %pad_maximum_fusion.1.refs_2_), channel_id=1, source_target_pairs={{0,96},{8,104},{16,112},{24,120},{32,128},{40,136},{48,144},{56,15... | collective-permute-start | bytes 835592 | tf_op jit(solution)/shard_map/ppermute | solution.py:27
  52.0 0.0 copy-done.3
  52.0 0.1 copy.22
  52.1 0.1 reduce-window.9
  52.2 0.1 reduce.4
  52.3 3.4 %collective-permute-start.6 = (bf16[4,2,136,128]{3,2,1,0:T(8,128)(2,1)S(1)}, bf16[4,2,136,128]{3,2,1,0:T(8,128)(2,1)S(1)}, u32[]{:S(2)}, u32[]{:S(2)}) collective-permute-start(bf16[4,2,136,128]{3,2,1,0:T(8,128)(2,1)S(1)} %pad_maximum_fusion.1.refs_2_), channel_id=1, source_target_pairs={{0,128},{8,136},{16,144},{24,152},{32,160},{40,168},{48,176},{56,1... | collective-permute-start | bytes 835592 | tf_op jit(solution)/shard_map/ppermute | solution.py:27
  55.7 7.7 %collective-permute-done.3 = bf16[4,2,136,128]{3,2,1,0:T(8,128)(2,1)S(1)} collective-permute-done((bf16[4,2,136,128]{3,2,1,0:T(8,128)(2,1)S(1)}, bf16[4,2,136,128]{3,2,1,0:T(8,128)(2,1)S(1)}, u32[]{:S(2)}, u32[]{:S(2)}) %collective-permute-start.3) | collective-permute-done | bytes 278560 | tf_op jit(solution)/shard_map/ppermute | solution.py:27
  63.4 0.0 collective-permute-done.4
  63.5 6.4 %collective-permute-done.5 = bf16[4,2,136,128]{3,2,1,0:T(8,128)(2,1)S(1)} collective-permute-done((bf16[4,2,136,128]{3,2,1,0:T(8,128)(2,1)S(1)}, bf16[4,2,136,128]{3,2,1,0:T(8,128)(2,1)S(1)}, u32[]{:S(2)}, u32[]{:S(2)}) %collective-permute-start.5) | collective-permute-done | bytes 278560 | tf_op jit(solution)/shard_map/ppermute | solution.py:27
  69.9 0.0 copy-start.2
  69.9 1.7 %collective-permute-done.6 = bf16[4,2,136,128]{3,2,1,0:T(8,128)(2,1)S(1)} collective-permute-done((bf16[4,2,136,128]{3,2,1,0:T(8,128)(2,1)S(1)}, bf16[4,2,136,128]{3,2,1,0:T(8,128)(2,1)S(1)}, u32[]{:S(2)}, u32[]{:S(2)}) %collective-permute-start.6) | collective-permute-done | bytes 278560 | tf_op jit(solution)/shard_map/ppermute | solution.py:27
  71.7 0.0 copy-done.1
  71.7 0.0 copy-start
  71.7 4.9 %collective-permute-start.7 = (bf16[16,2,136,128]{3,2,1,0:T(8,128)(2,1)S(1)}, bf16[16,2,136,128]{3,2,1,0:T(8,128)(2,1)S(1)}, u32[]{:S(2)}, u32[]{:S(2)}) collective-permute-start(bf16[16,2,136,128]{3,2,1,0:T(8,128)(2,1)S(1)} %constant_dynamic-update-slice_fusion.refs_2_), channel_id=1, source_target_pairs={{0,128},{8,136},{16,144},{24,152},{32,160},{40,168},{48,176},{56,1... | collective-permute-start | bytes 3342344 | tf_op jit(solution)/shard_map/ppermute | solution.py:27
  76.6 0.1 convert_reduce_fusion
  76.7 1.2 %gather_fusion = s32[128]{0:T(128)S(1)} fusion(s32[64]{0:T(128)S(1)} %sub.36, s32[1024]{0:T(1024)S(1)} %pad_clamp_fusion), kind=kCustom, calls=%fused_computation | custom fusion | bytes 1536 | tf_op jit(solution)/shard_map/gather | solution.py:184
  78.0 0.0 copy-start.4
  78.0 2.4 %collective-permute-start.8 = (bf16[5,2,136,128]{3,2,1,0:T(8,128)(2,1)S(1)}, bf16[5,2,136,128]{3,2,1,0:T(8,128)(2,1)}, u32[]{:S(2)}, u32[]{:S(2)}) collective-permute-start(bf16[5,2,136,128]{3,2,1,0:T(8,128)(2,1)S(1)} %pad_maximum_fusion), channel_id=1, source_target_pairs={{0,256},{8,264},{16,272},{24,280},{32,288},{40,296},{48,304},{56,3... | collective-permute-start | bytes 1044488 | tf_op jit(solution)/shard_map/ppermute | solution.py:27
  80.5 0.6 fusion.2
  83.7 0.0 copy-done.2
  83.7 0.2 copy.23
  84.0 0.0 copy-done
  84.0 0.8 copy.31
  84.8 0.1 pad.15.clone
  84.8 1.2 %add_add_fusion.2.refs_0_ = s32[3]{0:T(128)} fusion(s32[1]{0:T(128)} %bitcast.17, s32[1]{0:T(128)} %get-tuple-element.43, s32[1]{0:T(128)} %bitcast), kind=kLoop, calls=%fused_computation.18 | loop fusion | flops 6 | bytes 24 | tf_op jit(solution)/shard_map/stack | solution.py:199
  86.1 1.3 %add_add_fusion.1.refs_0_ = s32[3]{0:T(128)} fusion(s32[1]{0:T(128)} %bitcast.16, s32[1]{0:T(128)} %get-tuple-element.43, s32[1]{0:T(128)} %bitcast), kind=kLoop, calls=%fused_computation.17 | loop fusion | flops 6 | bytes 24 | tf_op jit(solution)/shard_map/stack | solution.py:199
  87.3 1.2 %add_add_fusion.refs_0_ = s32[3]{0:T(128)} fusion(s32[1]{0:T(128)} %bitcast.6, s32[1]{0:T(128)} %get-tuple-element.43, s32[1]{0:T(128)} %bitcast), kind=kLoop, calls=%fused_computation.16 | loop fusion | flops 6 | bytes 24 | tf_op jit(solution)/shard_map/stack | solution.py:199
  88.5 0.6 broadcast_in_dim.16.refs_3_
  89.1 0.0 copy-done.4
  89.1 0.7 broadcast_in_dim.17.refs_4_
  89.8 4.0 %shard_map.73 = (f32[8,128]{1,0:T(8,128)}, f32[8,128]{1,0:T(8,128)}, f32[128,1024]{1,0:T(8,128)}) custom-call(s32[3]{0:T(128)} %add_add_fusion.2.refs_0_, bf16[128,1024]{1,0:T(8,128)(2,1)} %bitcast.34, bf16[4,2,136,128]{3,2,1,0:T(8,128)(2,1)} %copy-done.1, s32[8,128]{1,0:T(8,128)} %broadcast_in_dim.16.refs_3_, f32[128,128]{1,0:T(8,128)} %broadcast_in_dim.17.refs_4_), custom_call_target="tpu_custom_call" | custom-call | tf_op jit(solution)/shard_map/pallas_call | solution.py:145
  93.8 8.2 %shard_map.74 = (f32[8,128]{1,0:T(8,128)}, f32[8,128]{1,0:T(8,128)}, f32[128,1024]{1,0:T(8,128)}) custom-call(s32[3]{0:T(128)} %add_add_fusion.1.refs_0_, bf16[128,1024]{1,0:T(8,128)(2,1)} %bitcast.35, bf16[16,2,136,128]{3,2,1,0:T(8,128)(2,1)} %copy-done, s32[8,128]{1,0:T(8,128)} %broadcast_in_dim.16.refs_3_, f32[128,128]{1,0:T(8,128)} %broadcast_in_dim.17.refs_4_, ...), custom_call_target="tpu_custom_call" | custom-call | tf_op jit(solution)/shard_map/pallas_call | solution.py:145
  102.1 0.0 collective-permute-done.8
  102.1 4.9 %collective-permute-done.7 = bf16[16,2,136,128]{3,2,1,0:T(8,128)(2,1)S(1)} collective-permute-done((bf16[16,2,136,128]{3,2,1,0:T(8,128)(2,1)S(1)}, bf16[16,2,136,128]{3,2,1,0:T(8,128)(2,1)S(1)}, u32[]{:S(2)}, u32[]{:S(2)}) %collective-permute-start.7) | collective-permute-done | bytes 1114144 | tf_op jit(solution)/shard_map/ppermute | solution.py:27
  106.9 2.4 %maximum_maximum_fusion.refs_2_ = bf16[24,2,136,128]{3,2,1,0:T(8,128)(2,1)} fusion(bf16[5,2,136,128]{3,2,1,0:T(8,128)(2,1)} %collective-permute-done.8, bf16[16,2,136,128]{3,2,1,0:T(8,128)(2,1)S(1)} %collective-permute-done.7, bf16[24]{0:T(256)(128)(2,1)S(1)} %pad.15.clone), kind=kLoop, calls=%fused_computation.1 | loop fusion | flops 1671168 | bytes 3133488 | tf_op jit(solution)/shard_map/concatenate | solution.py:196
  109.3 7.2 %shard_map.75 = bf16[128,1024]{1,0:T(8,128)(2,1)} custom-call(s32[3]{0:T(128)} %add_add_fusion.refs_0_, bf16[128,1024]{1,0:T(8,128)(2,1)} %bitcast.36, bf16[24,2,136,128]{3,2,1,0:T(8,128)(2,1)} %maximum_maximum_fusion.refs_2_, s32[8,128]{1,0:T(8,128)} %broadcast_in_dim.16.refs_3_, f32[128,128]{1,0:T(8,128)} %broadcast_in_dim.17.refs_4_, ...), custom_call_target="tpu_custom_call" | custom-call | tf_op jit(solution)/shard_map/pallas_call | solution.py:145
  (16 shorter events, 0.3 us)
Async XLA Ops:
  0.0 52.0 %copy-start.3 = (s32[64]{0:T(128)S(1)}, s32[64]{0:T(128)}, u32[]{:S(2)}) copy-start(s32[64]{0:T(128)} %param.17) | copy-start | bytes 772
  1.4 15.3 %all-to-all-start = ((bf16[32,8,128]{2,0,1:T(8,128)(2,1)}), bf16[32,8,128]{2,0,1:T(8,128)(2,1)S(1)}, u32[]{:S(2)}, u32[]{:S(2)}) async-start(bf16[32,8,128]{2,0,1:T(8,128)(2,1)} %copy_bitcast_fusion.1), calls=%async_computation | async-start | bytes 131072 | tf_op jit(solution)/shard_map/all_to_all | solution.py:166
  16.9 13.9 %collective-permute-start = (bf16[1,2,136,128]{3,2,1,0:T(8,128)(2,1)S(1)}, bf16[1,2,136,128]{3,2,1,0:T(8,128)(2,1)S(1)}, u32[]{:S(2)}, u32[]{:S(2)}) collective-permute-start(bf16[1,2,136,128]{3,2,1,0:T(8,128)(2,1)S(1)} %maximum_bitcast_fusion), channel_id=1, source_target_pairs={{0,8},{8,16},{16,24},{24,32},{32,40},{40,48},{48,56},{56,64},{64,7... | collective-permute-start | bytes 208904 | tf_op jit(solution)/shard_map/ppermute | solution.py:27
  19.8 14.2 %collective-permute-start.1 = (bf16[1,2,136,128]{3,2,1,0:T(8,128)(2,1)S(1)}, bf16[1,2,136,128]{3,2,1,0:T(8,128)(2,1)S(1)}, u32[]{:S(2)}, u32[]{:S(2)}) collective-permute-start(bf16[1,2,136,128]{3,2,1,0:T(8,128)(2,1)S(1)} %maximum_bitcast_fusion), channel_id=1, source_target_pairs={{0,16},{8,24},{16,32},{24,40},{32,48},{40,56},{48,64},{56,72},{64,... | collective-permute-start | bytes 208904 | tf_op jit(solution)/shard_map/ppermute | solution.py:27
  24.0 13.3 %collective-permute-start.2 = (bf16[1,2,136,128]{3,2,1,0:T(8,128)(2,1)S(1)}, bf16[1,2,136,128]{3,2,1,0:T(8,128)(2,1)S(1)}, u32[]{:S(2)}, u32[]{:S(2)}) collective-permute-start(bf16[1,2,136,128]{3,2,1,0:T(8,128)(2,1)S(1)} %maximum_bitcast_fusion), channel_id=1, source_target_pairs={{0,24},{8,32},{16,40},{24,48},{32,56},{40,64},{48,72},{56,80},{64,... | collective-permute-start | bytes 208904 | tf_op jit(solution)/shard_map/ppermute | solution.py:27
  37.4 34.3 %copy-start.1 = (bf16[4,2,136,128]{3,2,1,0:T(8,128)(2,1)}, bf16[4,2,136,128]{3,2,1,0:T(8,128)(2,1)S(1)}, u32[]{:S(2)}) copy-start(bf16[4,2,136,128]{3,2,1,0:T(8,128)(2,1)S(1)} %pad_maximum_fusion.1.refs_2_) | copy-start | bytes 835588
  37.4 26.0 %collective-permute-start.3 = (bf16[4,2,136,128]{3,2,1,0:T(8,128)(2,1)S(1)}, bf16[4,2,136,128]{3,2,1,0:T(8,128)(2,1)S(1)}, u32[]{:S(2)}, u32[]{:S(2)}) collective-permute-start(bf16[4,2,136,128]{3,2,1,0:T(8,128)(2,1)S(1)} %pad_maximum_fusion.1.refs_2_), channel_id=1, source_target_pairs={{0,32},{8,40},{16,48},{24,56},{32,64},{40,72},{48,80},{56,88},{64,... | collective-permute-start | bytes 835592 | tf_op jit(solution)/shard_map/ppermute | solution.py:27
  39.3 24.1 %collective-permute-start.4 = (bf16[4,2,136,128]{3,2,1,0:T(8,128)(2,1)S(1)}, bf16[4,2,136,128]{3,2,1,0:T(8,128)(2,1)S(1)}, u32[]{:S(2)}, u32[]{:S(2)}) collective-permute-start(bf16[4,2,136,128]{3,2,1,0:T(8,128)(2,1)S(1)} %pad_maximum_fusion.1.refs_2_), channel_id=1, source_target_pairs={{0,64},{8,72},{16,80},{24,88},{32,96},{40,104},{48,112},{56,120},{... | collective-permute-start | bytes 835592 | tf_op jit(solution)/shard_map/ppermute | solution.py:27
  46.6 23.2 %collective-permute-start.5 = (bf16[4,2,136,128]{3,2,1,0:T(8,128)(2,1)S(1)}, bf16[4,2,136,128]{3,2,1,0:T(8,128)(2,1)S(1)}, u32[]{:S(2)}, u32[]{:S(2)}) collective-permute-start(bf16[4,2,136,128]{3,2,1,0:T(8,128)(2,1)S(1)} %pad_maximum_fusion.1.refs_2_), channel_id=1, source_target_pairs={{0,96},{8,104},{16,112},{24,120},{32,128},{40,136},{48,144},{56,15... | collective-permute-start | bytes 835592 | tf_op jit(solution)/shard_map/ppermute | solution.py:27
  52.3 19.3 %collective-permute-start.6 = (bf16[4,2,136,128]{3,2,1,0:T(8,128)(2,1)S(1)}, bf16[4,2,136,128]{3,2,1,0:T(8,128)(2,1)S(1)}, u32[]{:S(2)}, u32[]{:S(2)}) collective-permute-start(bf16[4,2,136,128]{3,2,1,0:T(8,128)(2,1)S(1)} %pad_maximum_fusion.1.refs_2_), channel_id=1, source_target_pairs={{0,128},{8,136},{16,144},{24,152},{32,160},{40,168},{48,176},{56,1... | collective-permute-start | bytes 835592 | tf_op jit(solution)/shard_map/ppermute | solution.py:27
  69.9 13.7 %copy-start.2 = (bf16[128,1024]{1,0:T(8,128)(2,1)S(1)}, bf16[128,1024]{1,0:T(8,128)(2,1)}, u32[]{:S(2)}) copy-start(bf16[128,1024]{1,0:T(8,128)(2,1)} %param.11) | copy-start | bytes 786436
  71.7 12.3 %copy-start = (bf16[16,2,136,128]{3,2,1,0:T(8,128)(2,1)}, bf16[16,2,136,128]{3,2,1,0:T(8,128)(2,1)S(1)}, u32[]{:S(2)}) copy-start(bf16[16,2,136,128]{3,2,1,0:T(8,128)(2,1)S(1)} %constant_dynamic-update-slice_fusion.refs_2_) | copy-start | bytes 3342340
  71.7 35.2 %collective-permute-start.7 = (bf16[16,2,136,128]{3,2,1,0:T(8,128)(2,1)S(1)}, bf16[16,2,136,128]{3,2,1,0:T(8,128)(2,1)S(1)}, u32[]{:S(2)}, u32[]{:S(2)}) collective-permute-start(bf16[16,2,136,128]{3,2,1,0:T(8,128)(2,1)S(1)} %constant_dynamic-update-slice_fusion.refs_2_), channel_id=1, source_target_pairs={{0,128},{8,136},{16,144},{24,152},{32,160},{40,168},{48,176},{56,1... | collective-permute-start | bytes 3342344 | tf_op jit(solution)/shard_map/ppermute | solution.py:27
  78.0 11.2 %copy-start.4 = (f32[128]{0:T(128)S(1)}, f32[128]{0:T(128)}, u32[]{:S(2)}) copy-start(f32[128]{0:T(128)} %param.16) | copy-start | bytes 1540
  78.0 24.0 %collective-permute-start.8 = (bf16[5,2,136,128]{3,2,1,0:T(8,128)(2,1)S(1)}, bf16[5,2,136,128]{3,2,1,0:T(8,128)(2,1)}, u32[]{:S(2)}, u32[]{:S(2)}) collective-permute-start(bf16[5,2,136,128]{3,2,1,0:T(8,128)(2,1)S(1)} %pad_maximum_fusion), channel_id=1, source_target_pairs={{0,256},{8,264},{16,272},{24,280},{32,288},{40,296},{48,304},{56,3... | collective-permute-start | bytes 1044488 | tf_op jit(solution)/shard_map/ppermute | solution.py:27

commit v14 on v12

--- a/solution.py
+++ b/solution.py
@@ -29,7 +29,13 @@
 def gather_stages(packet, count, depth):
     first = [packet[None]] + [shift_from(packet[None], offset, count) for offset in (1, 2, 3)]
     block = jnp.concatenate(first, axis=0)
-    middle = [shift_from(block, offset, count) for offset in (4, 8, 12, 16)]
+    middle = [
+        shift_from(block, 4, count),
+        shift_from(block[:2], 8, count),
+        shift_from(block[:2], 10, count),
+        shift_from(block, 12, count),
+        shift_from(block, 16, count),
+    ]
     block = jnp.concatenate([block] + middle, axis=0)
     last = [shift_from(block[4:], 16, count), shift_from(block[4:depth - 32], 32, count)]
     return [first, middle, last]

time: 120 us -> 118 us (0.983)
  the two profiles are of different devices: /device:TPU:6 before, /device:TPU:132 now
where the time goes in v14:
time: 118 us
  starting transfers between devices  49.6 us (42%)
  waiting for transfers between devices  30.2 us (26%)
  Pallas kernels  20.6 us (17%)
  other arithmetic  8.51 us (7%)
  local copies, waits for them, and re-layouts  5.94 us (5%)
  between operations  2.81 us (2%)
    ppermute x10, starting transfers between devices, shift_from(): return lax.ppermute(x, 'seq', pairs)  42.5 us
    ppermute x10, waiting for transfers between devices, shift_from(): return lax.ppermute(x, 'seq', pairs)  23.9 us
    pallas_call x3, Pallas kernels, attend_part(): pl.pallas_call(kernel, out_shape=out_shape, grid_spec=pltpu.PrefetchScala...  20.6 us
    all_to_all x1, starting transfers between devices, shards(): both = lax.all_to_all(both, 'head', split_axis=1, concat_axis=0, tiled=True)  7.1 us
    all_to_all x1, waiting for transfers between devices, shards(): both = lax.all_to_all(both, 'head', split_axis=1, concat_axis=0, tiled=True)  6.32 us
    another operation x3, other arithmetic, shards(): jnp.stack([seq_index.astype(jnp.int32), pairs, low[-1].astype(jnp.int32)])  3.76 us
  transfers between devices with their start and end apart: 11, of which 6 were waited for; matrix products, arithmetic and copies ran while one was open for 10% of the time, Pallas kernels for 11%

profile of v14, /device:TPU:132, one launch (start us, length us, event | category | flops | bytes accessed | tf_op | source)
XLA Modules:
  0.0 117.7 jit_solution(187791453679284784)
XLA Ops:
  0.0 0.0 copy-start.2
  0.0 1.4 %copy_bitcast_fusion.1 = bf16[32,8,128]{2,0,1:T(8,128)(2,1)} fusion(bf16[16,1024]{1,0:T(8,128)(2,1)} %param.13, bf16[16,1024]{1,0:T(8,128)(2,1)} %param.12), kind=kLoop, calls=%fused_computation.7 | loop fusion | flops 131072 | bytes 131072 | tf_op jit(solution)/shard_map/all_to_all | solution.py:171
  1.4 7.1 %all-to-all-start = ((bf16[32,8,128]{2,0,1:T(8,128)(2,1)}), bf16[32,8,128]{2,0,1:T(8,128)(2,1)S(1)}, u32[]{:S(2)}, u32[]{:S(2)}) async-start(bf16[32,8,128]{2,0,1:T(8,128)(2,1)} %copy_bitcast_fusion.1), calls=%async_computation | async-start | bytes 131072 | tf_op jit(solution)/shard_map/all_to_all | solution.py:171
  8.5 0.8 reduce.5
  9.3 0.1 broadcast_in_dim.12
  9.4 0.1 reshape.148
  9.5 0.8 reduce.6
  10.2 0.1 broadcast_in_dim.13
  10.3 0.1 reshape.150
  10.4 6.3 %all-to-all-done = bf16[32,8,128]{2,0,1:T(8,128)(2,1)S(1)} async-done(((bf16[32,8,128]{2,0,1:T(8,128)(2,1)}), bf16[32,8,128]{2,0,1:T(8,128)(2,1)S(1)}, u32[]{:S(2)}, u32[]{:S(2)}) %all-to-all-start) | async-done | bytes 65568 | tf_op jit(solution)/shard_map/all_to_all | solution.py:171
  16.8 0.1 copy.25
  16.9 2.8 %collective-permute-start = (bf16[1,2,136,128]{3,2,1,0:T(8,128)(2,1)S(1)}, bf16[1,2,136,128]{3,2,1,0:T(8,128)(2,1)S(1)}, u32[]{:S(2)}, u32[]{:S(2)}) collective-permute-start(bf16[1,2,136,128]{3,2,1,0:T(8,128)(2,1)S(1)} %maximum_bitcast_fusion), channel_id=1, source_target_pairs={{0,8},{8,16},{16,24},{24,32},{32,40},{40,48},{48,56},{56,64},{64,7... | collective-permute-start | bytes 208904 | tf_op jit(solution)/shard_map/ppermute | solution.py:26
  19.8 4.3 %collective-permute-start.1 = (bf16[1,2,136,128]{3,2,1,0:T(8,128)(2,1)S(1)}, bf16[1,2,136,128]{3,2,1,0:T(8,128)(2,1)S(1)}, u32[]{:S(2)}, u32[]{:S(2)}) collective-permute-start(bf16[1,2,136,128]{3,2,1,0:T(8,128)(2,1)S(1)} %maximum_bitcast_fusion), channel_id=1, source_target_pairs={{0,16},{8,24},{16,32},{24,40},{32,48},{40,56},{48,64},{56,72},{64,... | collective-permute-start | bytes 208904 | tf_op jit(solution)/shard_map/ppermute | solution.py:26
  24.0 6.9 %collective-permute-start.2 = (bf16[1,2,136,128]{3,2,1,0:T(8,128)(2,1)S(1)}, bf16[1,2,136,128]{3,2,1,0:T(8,128)(2,1)S(1)}, u32[]{:S(2)}, u32[]{:S(2)}) collective-permute-start(bf16[1,2,136,128]{3,2,1,0:T(8,128)(2,1)S(1)} %maximum_bitcast_fusion), channel_id=1, source_target_pairs={{0,24},{8,32},{16,40},{24,48},{32,56},{40,64},{48,72},{56,80},{64,... | collective-permute-start | bytes 208904 | tf_op jit(solution)/shard_map/ppermute | solution.py:26
  31.0 0.0 collective-permute-done
  31.0 0.0 collective-permute-done.1
  31.0 1.9 %collective-permute-done.2 = bf16[1,2,136,128]{3,2,1,0:T(8,128)(2,1)S(1)} collective-permute-done((bf16[1,2,136,128]{3,2,1,0:T(8,128)(2,1)S(1)}, bf16[1,2,136,128]{3,2,1,0:T(8,128)(2,1)S(1)}, u32[]{:S(2)}, u32[]{:S(2)}) %collective-permute-start.2) | collective-permute-done | bytes 69664 | tf_op jit(solution)/shard_map/ppermute | solution.py:26
  32.9 0.0 copy-start.1
  32.9 7.5 %collective-permute-start.3 = (bf16[4,2,136,128]{3,2,1,0:T(8,128)(2,1)S(1)}, bf16[4,2,136,128]{3,2,1,0:T(8,128)(2,1)S(1)}, u32[]{:S(2)}, u32[]{:S(2)}) collective-permute-start(bf16[4,2,136,128]{3,2,1,0:T(8,128)(2,1)S(1)} %pad_maximum_fusion.1.refs_2_), channel_id=1, source_target_pairs={{0,32},{8,40},{16,48},{24,56},{32,64},{40,72},{48,80},{56,88},{64,... | collective-permute-start | bytes 835592 | tf_op jit(solution)/shard_map/ppermute | solution.py:26
  40.5 3.7 %collective-permute-start.4 = (bf16[2,2,136,128]{3,2,1,0:T(8,128)(2,1)S(1)}, bf16[2,2,136,128]{3,2,1,0:T(8,128)(2,1)S(1)}, u32[]{:S(2)}, u32[]{:S(2)}) collective-permute-start(bf16[2,2,136,128]{3,2,1,0:T(8,128)(2,1)S(1)} %pad_maximum_fusion.2), channel_id=1, source_target_pairs={{0,64},{8,72},{16,80},{24,88},{32,96},{40,104},{48,112},{56,120},{... | collective-permute-start | bytes 417800 | tf_op jit(solution)/shard_map/ppermute | solution.py:26
  44.2 0.0 copy-done.2
  44.2 0.1 copy.22
  44.3 0.1 reduce-window.9
  44.4 0.1 reduce.4
  44.5 6.4 %collective-permute-start.5 = (bf16[2,2,136,128]{3,2,1,0:T(8,128)(2,1)S(1)}, bf16[2,2,136,128]{3,2,1,0:T(8,128)(2,1)S(1)}, u32[]{:S(2)}, u32[]{:S(2)}) collective-permute-start(bf16[2,2,136,128]{3,2,1,0:T(8,128)(2,1)S(1)} %pad_maximum_fusion.2), channel_id=1, source_target_pairs={{0,80},{8,88},{16,96},{24,104},{32,112},{40,120},{48,128},{56,136}... | collective-permute-start | bytes 417800 | tf_op jit(solution)/shard_map/ppermute | solution.py:26
  51.0 1.9 %collective-permute-start.6 = (bf16[4,2,136,128]{3,2,1,0:T(8,128)(2,1)S(1)}, bf16[4,2,136,128]{3,2,1,0:T(8,128)(2,1)S(1)}, u32[]{:S(2)}, u32[]{:S(2)}) collective-permute-start(bf16[4,2,136,128]{3,2,1,0:T(8,128)(2,1)S(1)} %pad_maximum_fusion.1.refs_2_), channel_id=1, source_target_pairs={{0,96},{8,104},{16,112},{24,120},{32,128},{40,136},{48,144},{56,15... | collective-permute-start | bytes 835592 | tf_op jit(solution)/shard_map/ppermute | solution.py:26
  52.9 2.9 %collective-permute-start.7 = (bf16[4,2,136,128]{3,2,1,0:T(8,128)(2,1)S(1)}, bf16[4,2,136,128]{3,2,1,0:T(8,128)(2,1)S(1)}, u32[]{:S(2)}, u32[]{:S(2)}) collective-permute-start(bf16[4,2,136,128]{3,2,1,0:T(8,128)(2,1)S(1)} %pad_maximum_fusion.1.refs_2_), channel_id=1, source_target_pairs={{0,128},{8,136},{16,144},{24,152},{32,160},{40,168},{48,176},{56,1... | collective-permute-start | bytes 835592 | tf_op jit(solution)/shard_map/ppermute | solution.py:26
  55.8 0.0 collective-permute-done.3
  55.8 3.4 %collective-permute-done.4 = bf16[2,2,136,128]{3,2,1,0:T(8,128)(2,1)S(1)} collective-permute-done((bf16[2,2,136,128]{3,2,1,0:T(8,128)(2,1)S(1)}, bf16[2,2,136,128]{3,2,1,0:T(8,128)(2,1)S(1)}, u32[]{:S(2)}, u32[]{:S(2)}) %collective-permute-start.4) | collective-permute-done | bytes 139296 | tf_op jit(solution)/shard_map/ppermute | solution.py:26
  59.3 5.3 %collective-permute-done.5 = bf16[2,2,136,128]{3,2,1,0:T(8,128)(2,1)S(1)} collective-permute-done((bf16[2,2,136,128]{3,2,1,0:T(8,128)(2,1)S(1)}, bf16[2,2,136,128]{3,2,1,0:T(8,128)(2,1)S(1)}, u32[]{:S(2)}, u32[]{:S(2)}) %collective-permute-start.5) | collective-permute-done | bytes 139296 | tf_op jit(solution)/shard_map/ppermute | solution.py:26
  64.6 8.9 %collective-permute-done.6 = bf16[4,2,136,128]{3,2,1,0:T(8,128)(2,1)S(1)} collective-permute-done((bf16[4,2,136,128]{3,2,1,0:T(8,128)(2,1)S(1)}, bf16[4,2,136,128]{3,2,1,0:T(8,128)(2,1)S(1)}, u32[]{:S(2)}, u32[]{:S(2)}) %collective-permute-start.6) | collective-permute-done | bytes 278560 | tf_op jit(solution)/shard_map/ppermute | solution.py:26
  73.5 0.0 collective-permute-done.7
  73.5 0.0 copy-done.1
  73.5 0.0 copy-start
  73.5 2.7 %collective-permute-start.8 = (bf16[16,2,136,128]{3,2,1,0:T(8,128)(2,1)S(1)}, bf16[16,2,136,128]{3,2,1,0:T(8,128)(2,1)S(1)}, u32[]{:S(2)}, u32[]{:S(2)}) collective-permute-start(bf16[16,2,136,128]{3,2,1,0:T(8,128)(2,1)S(1)} %constant_dynamic-update-slice_fusion.refs_2_), channel_id=1, source_target_pairs={{0,128},{8,136},{16,144},{24,152},{32,160},{40,168},{48,176},{56,1... | collective-permute-start | bytes 3342344 | tf_op jit(solution)/shard_map/ppermute | solution.py:26
  76.3 0.1 convert_reduce_fusion
  76.4 1.2 %gather_fusion = s32[128]{0:T(128)S(1)} fusion(s32[64]{0:T(128)S(1)} %sub.27, s32[1024]{0:T(1024)S(1)} %pad_clamp_fusion), kind=kCustom, calls=%fused_computation | custom fusion | bytes 1536 | tf_op jit(solution)/shard_map/gather | solution.py:189
  77.6 0.0 copy-start.3
  77.7 3.3 %collective-permute-start.9 = (bf16[5,2,136,128]{3,2,1,0:T(8,128)(2,1)S(1)}, bf16[5,2,136,128]{3,2,1,0:T(8,128)(2,1)S(1)}, u32[]{:S(2)}, u32[]{:S(2)}) collective-permute-start(bf16[5,2,136,128]{3,2,1,0:T(8,128)(2,1)S(1)} %pad_maximum_fusion), channel_id=1, source_target_pairs={{0,256},{8,264},{16,272},{24,280},{32,288},{40,296},{48,304},{56,3... | collective-permute-start | bytes 1044488 | tf_op jit(solution)/shard_map/ppermute | solution.py:26
  81.0 0.6 fusion.2
  84.2 1.0 copy.27
  85.2 0.2 copy.23
  85.4 0.0 copy-done
  85.4 0.7 copy.31
  86.2 0.1 pad.15.clone
  86.3 1.2 %add_add_fusion.2.refs_0_ = s32[3]{0:T(128)} fusion(s32[1]{0:T(128)} %bitcast.17, s32[1]{0:T(128)} %get-tuple-element.43, s32[1]{0:T(128)} %bitcast), kind=kLoop, calls=%fused_computation.20 | loop fusion | flops 6 | bytes 24 | tf_op jit(solution)/shard_map/stack | solution.py:202
  87.5 1.3 %add_add_fusion.1.refs_0_ = s32[3]{0:T(128)} fusion(s32[1]{0:T(128)} %bitcast.16, s32[1]{0:T(128)} %get-tuple-element.43, s32[1]{0:T(128)} %bitcast), kind=kLoop, calls=%fused_computation.19 | loop fusion | flops 6 | bytes 24 | tf_op jit(solution)/shard_map/stack | solution.py:202
  88.8 1.3 %add_add_fusion.refs_0_ = s32[3]{0:T(128)} fusion(s32[1]{0:T(128)} %bitcast.6, s32[1]{0:T(128)} %get-tuple-element.43, s32[1]{0:T(128)} %bitcast), kind=kLoop, calls=%fused_computation.18 | loop fusion | flops 6 | bytes 24 | tf_op jit(solution)/shard_map/stack | solution.py:202
  90.0 0.6 broadcast_in_dim.16.refs_3_
  90.6 0.0 copy-done.3
  90.6 0.7 broadcast_in_dim.17.refs_4_
  91.3 4.2 %shard_map.73 = (f32[8,128]{1,0:T(8,128)}, f32[8,128]{1,0:T(8,128)}, f32[128,1024]{1,0:T(8,128)}) custom-call(s32[3]{0:T(128)} %add_add_fusion.2.refs_0_, bf16[128,1024]{1,0:T(8,128)(2,1)} %bitcast.35, bf16[4,2,136,128]{3,2,1,0:T(8,128)(2,1)} %copy-done.1, s32[8,128]{1,0:T(8,128)} %broadcast_in_dim.16.refs_3_, f32[128,128]{1,0:T(8,128)} %broadcast_in_dim.17.refs_4_), custom_call_target="tpu_custom_call" | custom-call | tf_op jit(solution)/shard_map/pallas_call | solution.py:150
  95.5 9.3 %shard_map.74 = (f32[8,128]{1,0:T(8,128)}, f32[8,128]{1,0:T(8,128)}, f32[128,1024]{1,0:T(8,128)}) custom-call(s32[3]{0:T(128)} %add_add_fusion.1.refs_0_, bf16[128,1024]{1,0:T(8,128)(2,1)} %bitcast.36, bf16[16,2,136,128]{3,2,1,0:T(8,128)(2,1)} %copy-done, s32[8,128]{1,0:T(8,128)} %broadcast_in_dim.16.refs_3_, f32[128,128]{1,0:T(8,128)} %broadcast_in_dim.17.refs_4_, ...), custom_call_target="tpu_custom_call" | custom-call | tf_op jit(solution)/shard_map/pallas_call | solution.py:150
  104.8 4.4 %collective-permute-done.9 = bf16[5,2,136,128]{3,2,1,0:T(8,128)(2,1)S(1)} collective-permute-done((bf16[5,2,136,128]{3,2,1,0:T(8,128)(2,1)S(1)}, bf16[5,2,136,128]{3,2,1,0:T(8,128)(2,1)S(1)}, u32[]{:S(2)}, u32[]{:S(2)}) %collective-permute-start.9) | collective-permute-done | bytes 348192 | tf_op jit(solution)/shard_map/ppermute | solution.py:26
  109.2 0.0 collective-permute-done.8
  109.2 1.3 %maximum_maximum_fusion.refs_2_ = bf16[22,2,136,128]{3,2,1,0:T(8,128)(2,1)} fusion(bf16[5,2,136,128]{3,2,1,0:T(8,128)(2,1)S(1)} %collective-permute-done.9, bf16[16,2,136,128]{3,2,1,0:T(8,128)(2,1)S(1)} %collective-permute-done.8, bf16[22]{0:T(256)(128)(2,1)S(1)} %pad.15.clone), kind=kLoop, calls=%fused_computation.1 | loop fusion | flops 1531904 | bytes 2994220 | tf_op jit(solution)/shard_map/concatenate | solution.py:200
  110.6 7.1 %shard_map.75 = bf16[128,1024]{1,0:T(8,128)(2,1)} custom-call(s32[3]{0:T(128)} %add_add_fusion.refs_0_, bf16[128,1024]{1,0:T(8,128)(2,1)} %bitcast.37, bf16[22,2,136,128]{3,2,1,0:T(8,128)(2,1)} %maximum_maximum_fusion.refs_2_, s32[8,128]{1,0:T(8,128)} %broadcast_in_dim.16.refs_3_, f32[128,128]{1,0:T(8,128)} %broadcast_in_dim.17.refs_4_, ...), custom_call_target="tpu_custom_call" | custom-call | tf_op jit(solution)/shard_map/pallas_call | solution.py:150
  (16 shorter events, 0.3 us)
Async XLA Ops:
  0.0 44.2 %copy-start.2 = (s32[64]{0:T(128)S(1)}, s32[64]{0:T(128)}, u32[]{:S(2)}) copy-start(s32[64]{0:T(128)} %param.17) | copy-start | bytes 772
  1.4 15.3 %all-to-all-start = ((bf16[32,8,128]{2,0,1:T(8,128)(2,1)}), bf16[32,8,128]{2,0,1:T(8,128)(2,1)S(1)}, u32[]{:S(2)}, u32[]{:S(2)}) async-start(bf16[32,8,128]{2,0,1:T(8,128)(2,1)} %copy_bitcast_fusion.1), calls=%async_computation | async-start | bytes 131072 | tf_op jit(solution)/shard_map/all_to_all | solution.py:171
  16.9 14.1 %collective-permute-start = (bf16[1,2,136,128]{3,2,1,0:T(8,128)(2,1)S(1)}, bf16[1,2,136,128]{3,2,1,0:T(8,128)(2,1)S(1)}, u32[]{:S(2)}, u32[]{:S(2)}) collective-permute-start(bf16[1,2,136,128]{3,2,1,0:T(8,128)(2,1)S(1)} %maximum_bitcast_fusion), channel_id=1, source_target_pairs={{0,8},{8,16},{16,24},{24,32},{32,40},{40,48},{48,56},{56,64},{64,7... | collective-permute-start | bytes 208904 | tf_op jit(solution)/shard_map/ppermute | solution.py:26
  19.8 11.2 %collective-permute-start.1 = (bf16[1,2,136,128]{3,2,1,0:T(8,128)(2,1)S(1)}, bf16[1,2,136,128]{3,2,1,0:T(8,128)(2,1)S(1)}, u32[]{:S(2)}, u32[]{:S(2)}) collective-permute-start(bf16[1,2,136,128]{3,2,1,0:T(8,128)(2,1)S(1)} %maximum_bitcast_fusion), channel_id=1, source_target_pairs={{0,16},{8,24},{16,32},{24,40},{32,48},{40,56},{48,64},{56,72},{64,... | collective-permute-start | bytes 208904 | tf_op jit(solution)/shard_map/ppermute | solution.py:26
  24.0 8.9 %collective-permute-start.2 = (bf16[1,2,136,128]{3,2,1,0:T(8,128)(2,1)S(1)}, bf16[1,2,136,128]{3,2,1,0:T(8,128)(2,1)S(1)}, u32[]{:S(2)}, u32[]{:S(2)}) collective-permute-start(bf16[1,2,136,128]{3,2,1,0:T(8,128)(2,1)S(1)} %maximum_bitcast_fusion), channel_id=1, source_target_pairs={{0,24},{8,32},{16,40},{24,48},{32,56},{40,64},{48,72},{56,80},{64,... | collective-permute-start | bytes 208904 | tf_op jit(solution)/shard_map/ppermute | solution.py:26
  32.9 40.6 %copy-start.1 = (bf16[4,2,136,128]{3,2,1,0:T(8,128)(2,1)}, bf16[4,2,136,128]{3,2,1,0:T(8,128)(2,1)S(1)}, u32[]{:S(2)}) copy-start(bf16[4,2,136,128]{3,2,1,0:T(8,128)(2,1)S(1)} %pad_maximum_fusion.1.refs_2_) | copy-start | bytes 835588
  32.9 22.8 %collective-permute-start.3 = (bf16[4,2,136,128]{3,2,1,0:T(8,128)(2,1)S(1)}, bf16[4,2,136,128]{3,2,1,0:T(8,128)(2,1)S(1)}, u32[]{:S(2)}, u32[]{:S(2)}) collective-permute-start(bf16[4,2,136,128]{3,2,1,0:T(8,128)(2,1)S(1)} %pad_maximum_fusion.1.refs_2_), channel_id=1, source_target_pairs={{0,32},{8,40},{16,48},{24,56},{32,64},{40,72},{48,80},{56,88},{64,... | collective-permute-start | bytes 835592 | tf_op jit(solution)/shard_map/ppermute | solution.py:26
  40.5 18.7 %collective-permute-start.4 = (bf16[2,2,136,128]{3,2,1,0:T(8,128)(2,1)S(1)}, bf16[2,2,136,128]{3,2,1,0:T(8,128)(2,1)S(1)}, u32[]{:S(2)}, u32[]{:S(2)}) collective-permute-start(bf16[2,2,136,128]{3,2,1,0:T(8,128)(2,1)S(1)} %pad_maximum_fusion.2), channel_id=1, source_target_pairs={{0,64},{8,72},{16,80},{24,88},{32,96},{40,104},{48,112},{56,120},{... | collective-permute-start | bytes 417800 | tf_op jit(solution)/shard_map/ppermute | solution.py:26
  44.5 20.0 %collective-permute-start.5 = (bf16[2,2,136,128]{3,2,1,0:T(8,128)(2,1)S(1)}, bf16[2,2,136,128]{3,2,1,0:T(8,128)(2,1)S(1)}, u32[]{:S(2)}, u32[]{:S(2)}) collective-permute-start(bf16[2,2,136,128]{3,2,1,0:T(8,128)(2,1)S(1)} %pad_maximum_fusion.2), channel_id=1, source_target_pairs={{0,80},{8,88},{16,96},{24,104},{32,112},{40,120},{48,128},{56,136}... | collective-permute-start | bytes 417800 | tf_op jit(solution)/shard_map/ppermute | solution.py:26
  51.0 22.5 %collective-permute-start.6 = (bf16[4,2,136,128]{3,2,1,0:T(8,128)(2,1)S(1)}, bf16[4,2,136,128]{3,2,1,0:T(8,128)(2,1)S(1)}, u32[]{:S(2)}, u32[]{:S(2)}) collective-permute-start(bf16[4,2,136,128]{3,2,1,0:T(8,128)(2,1)S(1)} %pad_maximum_fusion.1.refs_2_), channel_id=1, source_target_pairs={{0,96},{8,104},{16,112},{24,120},{32,128},{40,136},{48,144},{56,15... | collective-permute-start | bytes 835592 | tf_op jit(solution)/shard_map/ppermute | solution.py:26
  52.9 20.6 %collective-permute-start.7 = (bf16[4,2,136,128]{3,2,1,0:T(8,128)(2,1)S(1)}, bf16[4,2,136,128]{3,2,1,0:T(8,128)(2,1)S(1)}, u32[]{:S(2)}, u32[]{:S(2)}) collective-permute-start(bf16[4,2,136,128]{3,2,1,0:T(8,128)(2,1)S(1)} %pad_maximum_fusion.1.refs_2_), channel_id=1, source_target_pairs={{0,128},{8,136},{16,144},{24,152},{32,160},{40,168},{48,176},{56,1... | collective-permute-start | bytes 835592 | tf_op jit(solution)/shard_map/ppermute | solution.py:26
  73.5 11.9 %copy-start = (bf16[16,2,136,128]{3,2,1,0:T(8,128)(2,1)}, bf16[16,2,136,128]{3,2,1,0:T(8,128)(2,1)S(1)}, u32[]{:S(2)}) copy-start(bf16[16,2,136,128]{3,2,1,0:T(8,128)(2,1)S(1)} %constant_dynamic-update-slice_fusion.refs_2_) | copy-start | bytes 3342340
  73.5 35.7 %collective-permute-start.8 = (bf16[16,2,136,128]{3,2,1,0:T(8,128)(2,1)S(1)}, bf16[16,2,136,128]{3,2,1,0:T(8,128)(2,1)S(1)}, u32[]{:S(2)}, u32[]{:S(2)}) collective-permute-start(bf16[16,2,136,128]{3,2,1,0:T(8,128)(2,1)S(1)} %constant_dynamic-update-slice_fusion.refs_2_), channel_id=1, source_target_pairs={{0,128},{8,136},{16,144},{24,152},{32,160},{40,168},{48,176},{56,1... | collective-permute-start | bytes 3342344 | tf_op jit(solution)/shard_map/ppermute | solution.py:26
  77.6 13.0 %copy-start.3 = (f32[128]{0:T(128)S(1)}, f32[128]{0:T(128)}, u32[]{:S(2)}) copy-start(f32[128]{0:T(128)} %param.16) | copy-start | bytes 1540
  77.7 31.6 %collective-permute-start.9 = (bf16[5,2,136,128]{3,2,1,0:T(8,128)(2,1)S(1)}, bf16[5,2,136,128]{3,2,1,0:T(8,128)(2,1)S(1)}, u32[]{:S(2)}, u32[]{:S(2)}) collective-permute-start(bf16[5,2,136,128]{3,2,1,0:T(8,128)(2,1)S(1)} %pad_maximum_fusion), channel_id=1, source_target_pairs={{0,256},{8,264},{16,272},{24,280},{32,288},{40,296},{48,304},{56,3... | collective-permute-start | bytes 1044488 | tf_op jit(solution)/shard_map/ppermute | solution.py:26

commit v15 on v12

--- a/solution.py
+++ b/solution.py
@@ -35,9 +35,12 @@
     return [first, middle, last]
 
 
-def attention_kernel(first, last, offset, *refs):
-    info_ref, query_ref, window_ref, low_ref, mean_ref = refs[:5]
-    rest = refs[5:]
+def attention_kernel(first, last, layout, *refs):
+    count = len(layout)
+    info_ref, query_ref = refs[:2]
+    windows = refs[2:2 + count]
+    low_ref, mean_ref = refs[2 + count:4 + count]
+    rest = refs[4 + count:]
     if not first:
         max_in, sum_in, acc_in = rest[:3]
         rest = rest[3:]
@@ -51,7 +54,7 @@
     group_size, rows = max_ref.shape
     inv_scale = 1.0 / math.sqrt(HD)
     seq_index = info_ref[0]
-    pairs = info_ref[1]
+    used = info_ref[1]
     low_top = info_ref[2]
     if first:
         max_ref[...] = jnp.full(max_ref.shape, NEG, jnp.float32)
@@ -66,18 +69,18 @@
     sub = lax.broadcasted_iota(jnp.int32, (rows, rows), 0)
     query_t = query_ref[...]
 
-    def column(slot, part):
+    def column(window_ref, slot, part):
         row = window_ref[slot, part, rows:rows + 1, :].astype(jnp.float32)
         return jnp.transpose(jnp.broadcast_to(row, (rows, rows)))
 
-    def fold_pair(pair, masked):
+    def fold_pair(window_ref, offset, step, pair, masked):
         parts = []
-        for half in range(2):
-            slot = 2 * pair + half
+        for half in range(step):
+            slot = step * pair + half
             key_tile = window_ref[slot, 0, :rows, :]
             scores = jnp.dot(key_tile, query_t, preferred_element_type=jnp.float32)
-            key_scale = column(slot, 0) * inv_scale
-            value_scale = column(slot, 1)
+            key_scale = column(window_ref, slot, 0) * inv_scale
+            value_scale = column(window_ref, slot, 1)
             allowed = None
             if masked:
                 key_pos = (seq_index - offset - slot) * rows + sub
@@ -109,13 +112,20 @@
             max_ref[g:g + 1, :] = new_max
             sum_ref[g:g + 1, :] = run_sum
 
-    def one_pair(pair, carry):
-        nearest = offset + 2 * pair
-        inside = (nearest >= 1) & ((seq_index - nearest - 1) * rows >= low_top)
-        lax.cond(inside, lambda: fold_pair(pair, False), lambda: fold_pair(pair, True))
-        return carry
-
-    lax.fori_loop(0, pairs, one_pair, 0)
+    for window_ref, (offset, step) in zip(windows, layout):
+
+        def one_step(pair, carry, window_ref=window_ref, offset=offset, step=step):
+            nearest = offset + step * pair
+            inside = (nearest >= 1) & ((seq_index - nearest - step + 1) * rows >= low_top)
+            lax.cond(
+                inside,
+                lambda: fold_pair(window_ref, offset, step, pair, False),
+                lambda: fold_pair(window_ref, offset, step, pair, True),
+            )
+            return carry
+
+        reach = jnp.minimum(jnp.maximum(used - offset, 0), window_ref.shape[0])
+        lax.fori_loop(0, (reach + step - 1) // step, one_step, 0)
     if last:
         mean = mean_ref[...]
         for g in range(group_size):
@@ -127,20 +137,20 @@
         acc_out[...] = acc_ref[...]
 
 
-def attend_part(info, query_t, window, low, mean, state, offset, last, width):
+def attend_part(info, query_t, windows, layout, low, mean, state, last, width):
     group_size = query_t.shape[1] // HD
     rows = low.shape[1]
     full = lambda shape: pl.BlockSpec(shape, lambda i, info: (0,) * len(shape))
     row_shape = jax.ShapeDtypeStruct((group_size, rows), jnp.float32)
     acc_shape = jax.ShapeDtypeStruct((HD, group_size * rows), jnp.float32)
-    operands = [query_t, window, low, mean] + ([] if state is None else list(state))
+    operands = [query_t] + list(windows) + [low, mean] + ([] if state is None else list(state))
     if last:
         out_shape = jax.ShapeDtypeStruct((rows, width), jnp.bfloat16)
         out_specs = full((rows, width))
     else:
         out_shape = (row_shape, row_shape, acc_shape)
         out_specs = (full(row_shape.shape), full(row_shape.shape), full(acc_shape.shape))
-    kernel = functools.partial(attention_kernel, state is None, last, offset)
+    kernel = functools.partial(attention_kernel, state is None, last, layout)
     return pl.pallas_call(
         kernel,
         out_shape=out_shape,
@@ -185,20 +195,20 @@
     low_tile = jnp.broadcast_to(low[None, :], (8, row_count)).astype(jnp.int32)
     mean = jnp.broadcast_to(value_means.reshape(HD, 1), (HD, row_count))
     query_all = queries.reshape(row_count, group_size, HD).transpose(2, 1, 0).reshape(HD, -1)
-    chunks = [jnp.concatenate(stage, axis=0) for stage in stages]
+    info = jnp.stack([seq_index.astype(jnp.int32), used, low[-1].astype(jnp.int32)])
+    first, middle, final = stages
+    near, far = final
+    parts = [
+        ([jnp.concatenate(first, axis=0)], ((0, 2),)),
+        ([jnp.concatenate(middle, axis=0)], ((4, 2),)),
+        ([near, far], ((20, 2), (20 + near.shape[0], 1))),
+    ]
     state = None
-    offset = 0
-    for index, chunk in enumerate(chunks):
-        slots = chunk.shape[0]
-        if slots % 2:
-            chunk = jnp.concatenate([chunk, jnp.zeros((1,) + chunk.shape[1:], chunk.dtype)])
-        pairs = jnp.clip((used - offset + 1) // 2, 0, chunk.shape[0] // 2).astype(jnp.int32)
-        info = jnp.stack([seq_index.astype(jnp.int32), pairs, low[-1].astype(jnp.int32)])
-        last = index == len(chunks) - 1
+    for index, (windows, layout) in enumerate(parts):
+        last = index == len(parts) - 1
         state = attend_part(
-            info, query_all, chunk, low_tile, mean, state, offset, last, queries.shape[1]
+            info, query_all, windows, layout, low_tile, mean, state, last, queries.shape[1]
         )
-        offset += slots
     return state
 
 

time: 120 us -> 119 us (level)
  other arithmetic: 8.46 us -> 4.51 us
  waiting for transfers between devices: 31.5 us -> 33.3 us
    another operation x5 -> x3, other arithmetic: 3.93 us -> 1.36 us  [the longest x1 1.15 us: shards(): jnp.stack([seq_index.astype(jnp.int32), used, low[-1].astype(jnp.int32)])]
    ppermute x9, waiting for transfers between devices: 25.2 us -> 26.9 us  [shift_from(): return lax.ppermute(x, 'seq', pairs)]
    concatenate x1 -> x0, other arithmetic: 1.35 us -> none  [shards(): jnp.concatenate([chunk, jnp.zeros((1,) + chunk.shape[1:], chunk.dtype)])]
  transfers between devices with their start and end apart: 10 -> 10, of which waited for: 8 -> 9; matrix products, arithmetic and copies ran while one was open for 10% -> 7% of each run, Pallas kernels for 11% -> 11%
where the time goes in v15:
time: 119 us
  starting transfers between devices  47.3 us (40%)
  waiting for transfers between devices  33.3 us (28%)
  Pallas kernels  25.1 us (21%)
  local copies, waits for them, and re-layouts  5.87 us (5%)
  other arithmetic  4.51 us (4%)
  between operations  2.82 us (2%)
    ppermute x9, starting transfers between devices, shift_from(): return lax.ppermute(x, 'seq', pairs)  40.2 us
    ppermute x9, waiting for transfers between devices, shift_from(): return lax.ppermute(x, 'seq', pairs)  26.9 us
    pallas_call x3, Pallas kernels, attend_part(): pl.pallas_call(kernel, out_shape=out_shape, grid_spec=pltpu.PrefetchScala...  25.1 us
    all_to_all x1, starting transfers between devices, shards(): both = lax.all_to_all(both, 'head', split_axis=1, concat_axis=0, tiled=True)  7.1 us
    all_to_all x1, waiting for transfers between devices, shards(): both = lax.all_to_all(both, 'head', split_axis=1, concat_axis=0, tiled=True)  6.32 us
  transfers between devices with their start and end apart: 10, of which 9 were waited for; matrix products, arithmetic and copies ran while one was open for 7% of the time, Pallas kernels for 11%

profile of v15, /device:TPU:6, one launch (start us, length us, event | category | flops | bytes accessed | tf_op | source)
XLA Modules:
  0.0 118.9 jit_solution(14094938140015521596)
XLA Ops:
  0.0 1.4 %copy_bitcast_fusion.1 = bf16[32,8,128]{2,0,1:T(8,128)(2,1)} fusion(bf16[16,1024]{1,0:T(8,128)(2,1)} %param.13, bf16[16,1024]{1,0:T(8,128)(2,1)} %param.12), kind=kLoop, calls=%fused_computation.5 | loop fusion | flops 131072 | bytes 131072 | tf_op jit(solution)/shard_map/all_to_all | solution.py:175
  1.4 7.1 %all-to-all-start = ((bf16[32,8,128]{2,0,1:T(8,128)(2,1)}), bf16[32,8,128]{2,0,1:T(8,128)(2,1)S(1)}, u32[]{:S(2)}, u32[]{:S(2)}) async-start(bf16[32,8,128]{2,0,1:T(8,128)(2,1)} %copy_bitcast_fusion.1), calls=%async_computation | async-start | bytes 131072 | tf_op jit(solution)/shard_map/all_to_all | solution.py:175
  8.5 0.8 reduce.5
  9.3 0.1 broadcast_in_dim.10
  9.4 0.1 reshape.148
  9.5 0.8 reduce.6
  10.2 0.1 broadcast_in_dim.11
  10.3 0.1 reshape.150
  10.4 6.3 %all-to-all-done = bf16[32,8,128]{2,0,1:T(8,128)(2,1)S(1)} async-done(((bf16[32,8,128]{2,0,1:T(8,128)(2,1)}), bf16[32,8,128]{2,0,1:T(8,128)(2,1)S(1)}, u32[]{:S(2)}, u32[]{:S(2)}) %all-to-all-start) | async-done | bytes 65568 | tf_op jit(solution)/shard_map/all_to_all | solution.py:175
  16.8 0.1 copy.25
  16.9 4.7 %collective-permute-start.2 = (bf16[1,2,136,128]{3,2,1,0:T(8,128)(2,1)S(1)}, bf16[1,2,136,128]{3,2,1,0:T(8,128)(2,1)S(1)}, u32[]{:S(2)}, u32[]{:S(2)}) collective-permute-start(bf16[1,2,136,128]{3,2,1,0:T(8,128)(2,1)S(1)} %maximum_bitcast_fusion), channel_id=1, source_target_pairs={{0,24},{8,32},{16,40},{24,48},{32,56},{40,64},{48,72},{56,80},{64,... | collective-permute-start | bytes 208904 | tf_op jit(solution)/shard_map/ppermute | solution.py:26
  21.5 4.3 %collective-permute-start.1 = (bf16[1,2,136,128]{3,2,1,0:T(8,128)(2,1)S(1)}, bf16[1,2,136,128]{3,2,1,0:T(8,128)(2,1)S(1)}, u32[]{:S(2)}, u32[]{:S(2)}) collective-permute-start(bf16[1,2,136,128]{3,2,1,0:T(8,128)(2,1)S(1)} %maximum_bitcast_fusion), channel_id=1, source_target_pairs={{0,16},{8,24},{16,32},{24,40},{32,48},{40,56},{48,64},{56,72},{64,... | collective-permute-start | bytes 208904 | tf_op jit(solution)/shard_map/ppermute | solution.py:26
  25.8 4.8 %collective-permute-start = (bf16[1,2,136,128]{3,2,1,0:T(8,128)(2,1)S(1)}, bf16[1,2,136,128]{3,2,1,0:T(8,128)(2,1)S(1)}, u32[]{:S(2)}, u32[]{:S(2)}) collective-permute-start(bf16[1,2,136,128]{3,2,1,0:T(8,128)(2,1)S(1)} %maximum_bitcast_fusion), channel_id=1, source_target_pairs={{0,8},{8,16},{16,24},{24,32},{32,40},{40,48},{48,56},{56,64},{64,7... | collective-permute-start | bytes 208904 | tf_op jit(solution)/shard_map/ppermute | solution.py:26
  30.7 1.2 collective-permute-done.2
  31.8 2.1 %collective-permute-done.1 = bf16[1,2,136,128]{3,2,1,0:T(8,128)(2,1)S(1)} collective-permute-done((bf16[1,2,136,128]{3,2,1,0:T(8,128)(2,1)S(1)}, bf16[1,2,136,128]{3,2,1,0:T(8,128)(2,1)S(1)}, u32[]{:S(2)}, u32[]{:S(2)}) %collective-permute-start.1) | collective-permute-done | bytes 69664 | tf_op jit(solution)/shard_map/ppermute | solution.py:26
  34.0 1.1 collective-permute-done
  35.1 0.0 copy-start.2
  35.1 0.0 copy-start.4
  35.1 5.3 %collective-permute-start.3 = (bf16[4,2,136,128]{3,2,1,0:T(8,128)(2,1)S(1)}, bf16[4,2,136,128]{3,2,1,0:T(8,128)(2,1)S(1)}, u32[]{:S(2)}, u32[]{:S(2)}) collective-permute-start(bf16[4,2,136,128]{3,2,1,0:T(8,128)(2,1)S(1)} %pad_maximum_fusion.1.refs_2_), channel_id=1, source_target_pairs={{0,32},{8,40},{16,48},{24,56},{32,64},{40,72},{48,80},{56,88},{64,... | collective-permute-start | bytes 835592 | tf_op jit(solution)/shard_map/ppermute | solution.py:26
  40.4 5.0 %collective-permute-start.4 = (bf16[4,2,136,128]{3,2,1,0:T(8,128)(2,1)S(1)}, bf16[4,2,136,128]{3,2,1,0:T(8,128)(2,1)S(1)}, u32[]{:S(2)}, u32[]{:S(2)}) collective-permute-start(bf16[4,2,136,128]{3,2,1,0:T(8,128)(2,1)S(1)} %pad_maximum_fusion.1.refs_2_), channel_id=1, source_target_pairs={{0,64},{8,72},{16,80},{24,88},{32,96},{40,104},{48,112},{56,120},{... | collective-permute-start | bytes 835592 | tf_op jit(solution)/shard_map/ppermute | solution.py:26
  45.4 5.9 %collective-permute-start.5 = (bf16[4,2,136,128]{3,2,1,0:T(8,128)(2,1)S(1)}, bf16[4,2,136,128]{3,2,1,0:T(8,128)(2,1)S(1)}, u32[]{:S(2)}, u32[]{:S(2)}) collective-permute-start(bf16[4,2,136,128]{3,2,1,0:T(8,128)(2,1)S(1)} %pad_maximum_fusion.1.refs_2_), channel_id=1, source_target_pairs={{0,96},{8,104},{16,112},{24,120},{32,128},{40,136},{48,144},{56,15... | collective-permute-start | bytes 835592 | tf_op jit(solution)/shard_map/ppermute | solution.py:26
  51.4 3.4 %collective-permute-start.6 = (bf16[4,2,136,128]{3,2,1,0:T(8,128)(2,1)S(1)}, bf16[4,2,136,128]{3,2,1,0:T(8,128)(2,1)S(1)}, u32[]{:S(2)}, u32[]{:S(2)}) collective-permute-start(bf16[4,2,136,128]{3,2,1,0:T(8,128)(2,1)S(1)} %pad_maximum_fusion.1.refs_2_), channel_id=1, source_target_pairs={{0,128},{8,136},{16,144},{24,152},{32,160},{40,168},{48,176},{56,1... | collective-permute-start | bytes 835592 | tf_op jit(solution)/shard_map/ppermute | solution.py:26
  54.8 2.6 %collective-permute-done.3 = bf16[4,2,136,128]{3,2,1,0:T(8,128)(2,1)S(1)} collective-permute-done((bf16[4,2,136,128]{3,2,1,0:T(8,128)(2,1)S(1)}, bf16[4,2,136,128]{3,2,1,0:T(8,128)(2,1)S(1)}, u32[]{:S(2)}, u32[]{:S(2)}) %collective-permute-start.3) | collective-permute-done | bytes 278560 | tf_op jit(solution)/shard_map/ppermute | solution.py:26
  57.4 3.6 %collective-permute-done.4 = bf16[4,2,136,128]{3,2,1,0:T(8,128)(2,1)S(1)} collective-permute-done((bf16[4,2,136,128]{3,2,1,0:T(8,128)(2,1)S(1)}, bf16[4,2,136,128]{3,2,1,0:T(8,128)(2,1)S(1)}, u32[]{:S(2)}, u32[]{:S(2)}) %collective-permute-start.4) | collective-permute-done | bytes 278560 | tf_op jit(solution)/shard_map/ppermute | solution.py:26
  61.1 8.5 %collective-permute-done.5 = bf16[4,2,136,128]{3,2,1,0:T(8,128)(2,1)S(1)} collective-permute-done((bf16[4,2,136,128]{3,2,1,0:T(8,128)(2,1)S(1)}, bf16[4,2,136,128]{3,2,1,0:T(8,128)(2,1)S(1)}, u32[]{:S(2)}, u32[]{:S(2)}) %collective-permute-start.5) | collective-permute-done | bytes 278560 | tf_op jit(solution)/shard_map/ppermute | solution.py:26
  69.7 0.0 copy-start.3
  69.7 1.3 %collective-permute-done.6 = bf16[4,2,136,128]{3,2,1,0:T(8,128)(2,1)S(1)} collective-permute-done((bf16[4,2,136,128]{3,2,1,0:T(8,128)(2,1)S(1)}, bf16[4,2,136,128]{3,2,1,0:T(8,128)(2,1)S(1)}, u32[]{:S(2)}, u32[]{:S(2)}) %collective-permute-start.6) | collective-permute-done | bytes 278560 | tf_op jit(solution)/shard_map/ppermute | solution.py:26
  71.0 0.0 copy-start
  71.0 4.8 %collective-permute-start.7 = (bf16[16,2,136,128]{3,2,1,0:T(8,128)(2,1)S(1)}, bf16[16,2,136,128]{3,2,1,0:T(8,128)(2,1)S(1)}, u32[]{:S(2)}, u32[]{:S(2)}) collective-permute-start(bf16[16,2,136,128]{3,2,1,0:T(8,128)(2,1)S(1)} %constant_dynamic-update-slice_fusion.refs_2_), channel_id=1, source_target_pairs={{0,128},{8,136},{16,144},{24,152},{32,160},{40,168},{48,176},{56,1... | collective-permute-start | bytes 3342344 | tf_op jit(solution)/shard_map/ppermute | solution.py:26
  75.9 0.0 copy-done.2
  75.9 0.0 copy-done.4
  75.9 0.1 copy.22
  76.0 0.1 reduce-window.9
  76.1 0.1 reduce.4
  76.2 0.1 convert_reduce_fusion
  76.3 0.0 copy-start.5
  76.4 2.0 %collective-permute-start.8 = (bf16[5,2,136,128]{3,2,1,0:T(8,128)(2,1)S(1)}, bf16[5,2,136,128]{3,2,1,0:T(8,128)(2,1)}, u32[]{:S(2)}, u32[]{:S(2)}) collective-permute-start(bf16[5,2,136,128]{3,2,1,0:T(8,128)(2,1)S(1)} %pad_maximum_fusion), channel_id=1, source_target_pairs={{0,256},{8,264},{16,272},{24,280},{32,288},{40,296},{48,304},{56,3... | collective-permute-start | bytes 1044488 | tf_op jit(solution)/shard_map/ppermute | solution.py:26
  78.4 1.2 %gather_fusion = s32[128]{0:T(128)S(1)} fusion(s32[64]{0:T(128)S(1)} %sub.16, s32[1024]{0:T(1024)S(1)} %pad_clamp_fusion), kind=kCustom, calls=%fused_computation | custom fusion | bytes 1536 | tf_op jit(solution)/shard_map/gather | solution.py:193
  79.6 0.6 fusion.2
  82.8 0.0 copy-done.3
  82.9 0.2 copy.23
  83.1 0.0 copy-done
  83.1 0.8 copy.31
  83.9 1.2 pad_add_fusion.refs_0_
  85.0 0.6 broadcast_in_dim.13.refs_3_.refs_4_
  85.6 0.0 copy-done.5
  85.6 0.7 broadcast_in_dim.14.refs_4_.refs_5_
  86.3 4.2 %shard_map.73 = (f32[8,128]{1,0:T(8,128)}, f32[8,128]{1,0:T(8,128)}, f32[128,1024]{1,0:T(8,128)}) custom-call(s32[3]{0:T(128)} %pad_add_fusion.refs_0_, bf16[128,1024]{1,0:T(8,128)(2,1)} %bitcast.32, bf16[4,2,136,128]{3,2,1,0:T(8,128)(2,1)} %copy-done.2, s32[8,128]{1,0:T(8,128)} %broadcast_in_dim.13.refs_3_.refs_4_, f32[128,128]{1,0:T(8,128)} %broadcast_in_dim.14.refs_4_.refs_5_), custom_call_target="tpu_custom_call" | custom-call | tf_op jit(solution)/shard_map/pallas_call | solution.py:154
  90.5 9.4 %shard_map.74 = (f32[8,128]{1,0:T(8,128)}, f32[8,128]{1,0:T(8,128)}, f32[128,1024]{1,0:T(8,128)}) custom-call(s32[3]{0:T(128)} %pad_add_fusion.refs_0_, bf16[128,1024]{1,0:T(8,128)(2,1)} %bitcast.33, bf16[16,2,136,128]{3,2,1,0:T(8,128)(2,1)} %copy-done, s32[8,128]{1,0:T(8,128)} %broadcast_in_dim.13.refs_3_.refs_4_, ...), custom_call_target="tpu_custom_call" | custom-call | tf_op jit(solution)/shard_map/pallas_call | solution.py:154
  99.9 0.0 collective-permute-done.8.refs_3_
  99.9 6.4 %collective-permute-done.7.refs_2_ = bf16[16,2,136,128]{3,2,1,0:T(8,128)(2,1)S(1)} collective-permute-done((bf16[16,2,136,128]{3,2,1,0:T(8,128)(2,1)S(1)}, bf16[16,2,136,128]{3,2,1,0:T(8,128)(2,1)S(1)}, u32[]{:S(2)}, u32[]{:S(2)}) %collective-permute-start.7) | collective-permute-done | bytes 1114144 | tf_op jit(solution)/shard_map/ppermute | solution.py:26
  106.3 0.0 copy-start.1
  106.3 1.0 copy-done.1
  107.3 11.6 %shard_map.75 = bf16[128,1024]{1,0:T(8,128)(2,1)} custom-call(s32[3]{0:T(128)} %pad_add_fusion.refs_0_, bf16[128,1024]{1,0:T(8,128)(2,1)} %bitcast.34, bf16[16,2,136,128]{3,2,1,0:T(8,128)(2,1)} %copy-done.1, bf16[5,2,136,128]{3,2,1,0:T(8,128)(2,1)} %collective-permute-done.8.refs_3_, s32[8,128]{1,0:T(8,128)} %broadcast_in_dim.13.refs_3_.refs_4_, ...), custom_call_target="tpu_custom_call" | custom-call | tf_op jit(solution)/shard_map/pallas_call | solution.py:154
  (15 shorter events, 0.3 us)
Async XLA Ops:
  1.4 15.3 %all-to-all-start = ((bf16[32,8,128]{2,0,1:T(8,128)(2,1)}), bf16[32,8,128]{2,0,1:T(8,128)(2,1)S(1)}, u32[]{:S(2)}, u32[]{:S(2)}) async-start(bf16[32,8,128]{2,0,1:T(8,128)(2,1)} %copy_bitcast_fusion.1), calls=%async_computation | async-start | bytes 131072 | tf_op jit(solution)/shard_map/all_to_all | solution.py:175
  16.9 14.9 %collective-permute-start.2 = (bf16[1,2,136,128]{3,2,1,0:T(8,128)(2,1)S(1)}, bf16[1,2,136,128]{3,2,1,0:T(8,128)(2,1)S(1)}, u32[]{:S(2)}, u32[]{:S(2)}) collective-permute-start(bf16[1,2,136,128]{3,2,1,0:T(8,128)(2,1)S(1)} %maximum_bitcast_fusion), channel_id=1, source_target_pairs={{0,24},{8,32},{16,40},{24,48},{32,56},{40,64},{48,72},{56,80},{64,... | collective-permute-start | bytes 208904 | tf_op jit(solution)/shard_map/ppermute | solution.py:26
  21.5 12.4 %collective-permute-start.1 = (bf16[1,2,136,128]{3,2,1,0:T(8,128)(2,1)S(1)}, bf16[1,2,136,128]{3,2,1,0:T(8,128)(2,1)S(1)}, u32[]{:S(2)}, u32[]{:S(2)}) collective-permute-start(bf16[1,2,136,128]{3,2,1,0:T(8,128)(2,1)S(1)} %maximum_bitcast_fusion), channel_id=1, source_target_pairs={{0,16},{8,24},{16,32},{24,40},{32,48},{40,56},{48,64},{56,72},{64,... | collective-permute-start | bytes 208904 | tf_op jit(solution)/shard_map/ppermute | solution.py:26
  25.8 9.2 %collective-permute-start = (bf16[1,2,136,128]{3,2,1,0:T(8,128)(2,1)S(1)}, bf16[1,2,136,128]{3,2,1,0:T(8,128)(2,1)S(1)}, u32[]{:S(2)}, u32[]{:S(2)}) collective-permute-start(bf16[1,2,136,128]{3,2,1,0:T(8,128)(2,1)S(1)} %maximum_bitcast_fusion), channel_id=1, source_target_pairs={{0,8},{8,16},{16,24},{24,32},{32,40},{40,48},{48,56},{56,64},{64,7... | collective-permute-start | bytes 208904 | tf_op jit(solution)/shard_map/ppermute | solution.py:26
  35.1 40.8 %copy-start.2 = (bf16[4,2,136,128]{3,2,1,0:T(8,128)(2,1)}, bf16[4,2,136,128]{3,2,1,0:T(8,128)(2,1)S(1)}, u32[]{:S(2)}) copy-start(bf16[4,2,136,128]{3,2,1,0:T(8,128)(2,1)S(1)} %pad_maximum_fusion.1.refs_2_) | copy-start | bytes 835588
  35.1 40.8 %copy-start.4 = (s32[64]{0:T(128)S(1)}, s32[64]{0:T(128)}, u32[]{:S(2)}) copy-start(s32[64]{0:T(128)} %param.17) | copy-start | bytes 772
  35.1 22.3 %collective-permute-start.3 = (bf16[4,2,136,128]{3,2,1,0:T(8,128)(2,1)S(1)}, bf16[4,2,136,128]{3,2,1,0:T(8,128)(2,1)S(1)}, u32[]{:S(2)}, u32[]{:S(2)}) collective-permute-start(bf16[4,2,136,128]{3,2,1,0:T(8,128)(2,1)S(1)} %pad_maximum_fusion.1.refs_2_), channel_id=1, source_target_pairs={{0,32},{8,40},{16,48},{24,56},{32,64},{40,72},{48,80},{56,88},{64,... | collective-permute-start | bytes 835592 | tf_op jit(solution)/shard_map/ppermute | solution.py:26
  40.4 20.6 %collective-permute-start.4 = (bf16[4,2,136,128]{3,2,1,0:T(8,128)(2,1)S(1)}, bf16[4,2,136,128]{3,2,1,0:T(8,128)(2,1)S(1)}, u32[]{:S(2)}, u32[]{:S(2)}) collective-permute-start(bf16[4,2,136,128]{3,2,1,0:T(8,128)(2,1)S(1)} %pad_maximum_fusion.1.refs_2_), channel_id=1, source_target_pairs={{0,64},{8,72},{16,80},{24,88},{32,96},{40,104},{48,112},{56,120},{... | collective-permute-start | bytes 835592 | tf_op jit(solution)/shard_map/ppermute | solution.py:26
  45.4 24.2 %collective-permute-start.5 = (bf16[4,2,136,128]{3,2,1,0:T(8,128)(2,1)S(1)}, bf16[4,2,136,128]{3,2,1,0:T(8,128)(2,1)S(1)}, u32[]{:S(2)}, u32[]{:S(2)}) collective-permute-start(bf16[4,2,136,128]{3,2,1,0:T(8,128)(2,1)S(1)} %pad_maximum_fusion.1.refs_2_), channel_id=1, source_target_pairs={{0,96},{8,104},{16,112},{24,120},{32,128},{40,136},{48,144},{56,15... | collective-permute-start | bytes 835592 | tf_op jit(solution)/shard_map/ppermute | solution.py:26
  51.4 19.6 %collective-permute-start.6 = (bf16[4,2,136,128]{3,2,1,0:T(8,128)(2,1)S(1)}, bf16[4,2,136,128]{3,2,1,0:T(8,128)(2,1)S(1)}, u32[]{:S(2)}, u32[]{:S(2)}) collective-permute-start(bf16[4,2,136,128]{3,2,1,0:T(8,128)(2,1)S(1)} %pad_maximum_fusion.1.refs_2_), channel_id=1, source_target_pairs={{0,128},{8,136},{16,144},{24,152},{32,160},{40,168},{48,176},{56,1... | collective-permute-start | bytes 835592 | tf_op jit(solution)/shard_map/ppermute | solution.py:26
  69.7 13.1 %copy-start.3 = (bf16[128,1024]{1,0:T(8,128)(2,1)S(1)}, bf16[128,1024]{1,0:T(8,128)(2,1)}, u32[]{:S(2)}) copy-start(bf16[128,1024]{1,0:T(8,128)(2,1)} %param.11) | copy-start | bytes 786436
  71.0 12.1 %copy-start = (bf16[16,2,136,128]{3,2,1,0:T(8,128)(2,1)}, bf16[16,2,136,128]{3,2,1,0:T(8,128)(2,1)S(1)}, u32[]{:S(2)}) copy-start(bf16[16,2,136,128]{3,2,1,0:T(8,128)(2,1)S(1)} %constant_dynamic-update-slice_fusion.refs_2_) | copy-start | bytes 3342340
  71.0 35.3 %collective-permute-start.7 = (bf16[16,2,136,128]{3,2,1,0:T(8,128)(2,1)S(1)}, bf16[16,2,136,128]{3,2,1,0:T(8,128)(2,1)S(1)}, u32[]{:S(2)}, u32[]{:S(2)}) collective-permute-start(bf16[16,2,136,128]{3,2,1,0:T(8,128)(2,1)S(1)} %constant_dynamic-update-slice_fusion.refs_2_), channel_id=1, source_target_pairs={{0,128},{8,136},{16,144},{24,152},{32,160},{40,168},{48,176},{56,1... | collective-permute-start | bytes 3342344 | tf_op jit(solution)/shard_map/ppermute | solution.py:26
  76.3 9.3 %copy-start.5 = (f32[128]{0:T(128)S(1)}, f32[128]{0:T(128)}, u32[]{:S(2)}) copy-start(f32[128]{0:T(128)} %param.16) | copy-start | bytes 1540
  76.4 23.5 %collective-permute-start.8 = (bf16[5,2,136,128]{3,2,1,0:T(8,128)(2,1)S(1)}, bf16[5,2,136,128]{3,2,1,0:T(8,128)(2,1)}, u32[]{:S(2)}, u32[]{:S(2)}) collective-permute-start(bf16[5,2,136,128]{3,2,1,0:T(8,128)(2,1)S(1)} %pad_maximum_fusion), channel_id=1, source_target_pairs={{0,256},{8,264},{16,272},{24,280},{32,288},{40,296},{48,304},{56,3... | collective-permute-start | bytes 1044488 | tf_op jit(solution)/shard_map/ppermute | solution.py:26
  106.3 1.0 copy-start.1

commit v16 on v15

--- a/solution.py
+++ b/solution.py
@@ -32,7 +32,7 @@
     middle = [shift_from(block, offset, count) for offset in (4, 8, 12, 16)]
     block = jnp.concatenate([block] + middle, axis=0)
     last = [shift_from(block[4:], 16, count), shift_from(block[4:depth - 32], 32, count)]
-    return [first, middle, last]
+    return block, last
 
 
 def attention_kernel(first, last, layout, *refs):
@@ -196,12 +196,10 @@
     mean = jnp.broadcast_to(value_means.reshape(HD, 1), (HD, row_count))
     query_all = queries.reshape(row_count, group_size, HD).transpose(2, 1, 0).reshape(HD, -1)
     info = jnp.stack([seq_index.astype(jnp.int32), used, low[-1].astype(jnp.int32)])
-    first, middle, final = stages
-    near, far = final
+    block, (near, far) = stages
     parts = [
-        ([jnp.concatenate(first, axis=0)], ((0, 2),)),
-        ([jnp.concatenate(middle, axis=0)], ((4, 2),)),
-        ([near, far], ((20, 2), (20 + near.shape[0], 1))),
+        ([block], ((0, 2),)),
+        ([near, far], ((block.shape[0], 2), (block.shape[0] + near.shape[0], 1))),
     ]
     state = None
     for index, (windows, layout) in enumerate(parts):

time: 119 us -> 116 us (0.975)
  the two profiles are of different devices: /device:TPU:6 before, /device:TPU:134 now
where the time goes in v16:
time: 116 us
  starting transfers between devices  45.8 us (39%)
  waiting for transfers between devices  37 us (32%)
  Pallas kernels  17.9 us (15%)
  other arithmetic  6.43 us (6%)
  local copies, waits for them, and re-layouts  5.65 us (5%)
  between operations  2.84 us (2%)
    ppermute x9, starting transfers between devices, shift_from(): return lax.ppermute(x, 'seq', pairs)  38.7 us
    ppermute x9, waiting for transfers between devices, shift_from(): return lax.ppermute(x, 'seq', pairs)  32.3 us
    pallas_call x2, Pallas kernels, attend_part(): pl.pallas_call(kernel, out_shape=out_shape, grid_spec=pltpu.PrefetchScala...  17.9 us
    all_to_all x1, starting transfers between devices, shards(): both = lax.all_to_all(both, 'head', split_axis=1, concat_axis=0, tiled=True)  7.1 us
    all_to_all x1, waiting for transfers between devices, shards(): both = lax.all_to_all(both, 'head', split_axis=1, concat_axis=0, tiled=True)  4.7 us
  transfers between devices with their start and end apart: 10, of which 6 were waited for; matrix products, arithmetic and copies ran while one was open for 8% of the time, Pallas kernels for 9%

profile of v16, /device:TPU:134, one launch (start us, length us, event | category | flops | bytes accessed | tf_op | source)
XLA Modules:
  0.0 115.5 jit_solution(7994454164001907517)
XLA Ops:
  0.0 0.0 copy-start.2
  0.0 1.5 %copy_bitcast_fusion.1 = bf16[32,8,128]{2,0,1:T(8,128)(2,1)} fusion(bf16[16,1024]{1,0:T(8,128)(2,1)} %param.13, bf16[16,1024]{1,0:T(8,128)(2,1)} %param.12), kind=kLoop, calls=%fused_computation.6 | loop fusion | flops 131072 | bytes 131072 | tf_op jit(solution)/shard_map/all_to_all | solution.py:175
  1.5 7.1 %all-to-all-start = ((bf16[32,8,128]{2,0,1:T(8,128)(2,1)}), bf16[32,8,128]{2,0,1:T(8,128)(2,1)S(1)}, u32[]{:S(2)}, u32[]{:S(2)}) async-start(bf16[32,8,128]{2,0,1:T(8,128)(2,1)} %copy_bitcast_fusion.1), calls=%async_computation | async-start | bytes 131072 | tf_op jit(solution)/shard_map/all_to_all | solution.py:175
  8.6 0.8 reduce.5
  9.3 0.1 broadcast_in_dim.10
  9.4 0.1 reshape.148
  9.5 0.8 reduce.6
  10.3 0.1 broadcast_in_dim.11
  10.4 0.1 reshape.150
  10.4 0.7 copy.22
  11.2 0.1 reduce-window.9
  11.3 0.1 reduce.4
  11.4 0.7 sub.16
  12.1 4.7 %all-to-all-done = bf16[32,8,128]{2,0,1:T(8,128)(2,1)S(1)} async-done(((bf16[32,8,128]{2,0,1:T(8,128)(2,1)}), bf16[32,8,128]{2,0,1:T(8,128)(2,1)S(1)}, u32[]{:S(2)}, u32[]{:S(2)}) %all-to-all-start) | async-done | bytes 65568 | tf_op jit(solution)/shard_map/all_to_all | solution.py:175
  16.8 0.1 copy.25
  16.9 2.8 %collective-permute-start = (bf16[1,2,136,128]{3,2,1,0:T(8,128)(2,1)S(1)}, bf16[1,2,136,128]{3,2,1,0:T(8,128)(2,1)S(1)}, u32[]{:S(2)}, u32[]{:S(2)}) collective-permute-start(bf16[1,2,136,128]{3,2,1,0:T(8,128)(2,1)S(1)} %maximum_bitcast_fusion), channel_id=1, source_target_pairs={{0,8},{8,16},{16,24},{24,32},{32,40},{40,48},{48,56},{56,64},{64,7... | collective-permute-start | bytes 208904 | tf_op jit(solution)/shard_map/ppermute | solution.py:26
  19.8 4.3 %collective-permute-start.1 = (bf16[1,2,136,128]{3,2,1,0:T(8,128)(2,1)S(1)}, bf16[1,2,136,128]{3,2,1,0:T(8,128)(2,1)S(1)}, u32[]{:S(2)}, u32[]{:S(2)}) collective-permute-start(bf16[1,2,136,128]{3,2,1,0:T(8,128)(2,1)S(1)} %maximum_bitcast_fusion), channel_id=1, source_target_pairs={{0,16},{8,24},{16,32},{24,40},{32,48},{40,56},{48,64},{56,72},{64,... | collective-permute-start | bytes 208904 | tf_op jit(solution)/shard_map/ppermute | solution.py:26
  24.1 6.9 %collective-permute-start.2 = (bf16[1,2,136,128]{3,2,1,0:T(8,128)(2,1)S(1)}, bf16[1,2,136,128]{3,2,1,0:T(8,128)(2,1)S(1)}, u32[]{:S(2)}, u32[]{:S(2)}) collective-permute-start(bf16[1,2,136,128]{3,2,1,0:T(8,128)(2,1)S(1)} %maximum_bitcast_fusion), channel_id=1, source_target_pairs={{0,24},{8,32},{16,40},{24,48},{32,56},{40,64},{48,72},{56,80},{64,... | collective-permute-start | bytes 208904 | tf_op jit(solution)/shard_map/ppermute | solution.py:26
  31.0 0.1 convert_reduce_fusion
  31.1 0.0 collective-permute-done
  31.1 0.0 collective-permute-done.1
  31.1 1.8 %collective-permute-done.2 = bf16[1,2,136,128]{3,2,1,0:T(8,128)(2,1)S(1)} collective-permute-done((bf16[1,2,136,128]{3,2,1,0:T(8,128)(2,1)S(1)}, bf16[1,2,136,128]{3,2,1,0:T(8,128)(2,1)S(1)}, u32[]{:S(2)}, u32[]{:S(2)}) %collective-permute-start.2) | collective-permute-done | bytes 69664 | tf_op jit(solution)/shard_map/ppermute | solution.py:26
  33.0 7.5 %collective-permute-start.3 = (bf16[4,2,136,128]{3,2,1,0:T(8,128)(2,1)S(1)}, bf16[4,2,136,128]{3,2,1,0:T(8,128)(2,1)S(1)}, u32[]{:S(2)}, u32[]{:S(2)}) collective-permute-start(bf16[4,2,136,128]{3,2,1,0:T(8,128)(2,1)S(1)} %pad_maximum_fusion.2), channel_id=1, source_target_pairs={{0,32},{8,40},{16,48},{24,56},{32,64},{40,72},{48,80},{56,88},{64,... | collective-permute-start | bytes 835592 | tf_op jit(solution)/shard_map/ppermute | solution.py:26
  40.5 4.9 %collective-permute-start.4 = (bf16[4,2,136,128]{3,2,1,0:T(8,128)(2,1)S(1)}, bf16[4,2,136,128]{3,2,1,0:T(8,128)(2,1)S(1)}, u32[]{:S(2)}, u32[]{:S(2)}) collective-permute-start(bf16[4,2,136,128]{3,2,1,0:T(8,128)(2,1)S(1)} %pad_maximum_fusion.2), channel_id=1, source_target_pairs={{0,64},{8,72},{16,80},{24,88},{32,96},{40,104},{48,112},{56,120},{... | collective-permute-start | bytes 835592 | tf_op jit(solution)/shard_map/ppermute | solution.py:26
  45.4 1.9 %collective-permute-start.5 = (bf16[4,2,136,128]{3,2,1,0:T(8,128)(2,1)S(1)}, bf16[4,2,136,128]{3,2,1,0:T(8,128)(2,1)S(1)}, u32[]{:S(2)}, u32[]{:S(2)}) collective-permute-start(bf16[4,2,136,128]{3,2,1,0:T(8,128)(2,1)S(1)} %pad_maximum_fusion.2), channel_id=1, source_target_pairs={{0,96},{8,104},{16,112},{24,120},{32,128},{40,136},{48,144},{56,15... | collective-permute-start | bytes 835592 | tf_op jit(solution)/shard_map/ppermute | solution.py:26
  47.3 3.3 %collective-permute-start.6 = (bf16[4,2,136,128]{3,2,1,0:T(8,128)(2,1)S(1)}, bf16[4,2,136,128]{3,2,1,0:T(8,128)(2,1)S(1)}, u32[]{:S(2)}, u32[]{:S(2)}) collective-permute-start(bf16[4,2,136,128]{3,2,1,0:T(8,128)(2,1)S(1)} %pad_maximum_fusion.2), channel_id=1, source_target_pairs={{0,128},{8,136},{16,144},{24,152},{32,160},{40,168},{48,176},{56,1... | collective-permute-start | bytes 835592 | tf_op jit(solution)/shard_map/ppermute | solution.py:26
  50.7 1.2 %gather_fusion = s32[128]{0:T(128)S(1)} fusion(s32[64]{0:T(128)S(1)} %sub.16, s32[1024]{0:T(1024)S(1)} %pad_clamp_fusion), kind=kCustom, calls=%fused_computation | custom fusion | bytes 1536 | tf_op jit(solution)/shard_map/gather | solution.py:193
  51.9 0.6 fusion.2
  55.1 0.0 copy-done.2
  55.2 0.2 copy.23
  55.4 0.7 copy.31
  56.2 1.2 %collective-permute-done.3 = bf16[4,2,136,128]{3,2,1,0:T(8,128)(2,1)S(1)} collective-permute-done((bf16[4,2,136,128]{3,2,1,0:T(8,128)(2,1)S(1)}, bf16[4,2,136,128]{3,2,1,0:T(8,128)(2,1)S(1)}, u32[]{:S(2)}, u32[]{:S(2)}) %collective-permute-start.3) | collective-permute-done | bytes 278560 | tf_op jit(solution)/shard_map/ppermute | solution.py:26
  57.4 9.2 %collective-permute-done.4 = bf16[4,2,136,128]{3,2,1,0:T(8,128)(2,1)S(1)} collective-permute-done((bf16[4,2,136,128]{3,2,1,0:T(8,128)(2,1)S(1)}, bf16[4,2,136,128]{3,2,1,0:T(8,128)(2,1)S(1)}, u32[]{:S(2)}, u32[]{:S(2)}) %collective-permute-start.4) | collective-permute-done | bytes 278560 | tf_op jit(solution)/shard_map/ppermute | solution.py:26
  66.6 4.2 %collective-permute-done.5 = bf16[4,2,136,128]{3,2,1,0:T(8,128)(2,1)S(1)} collective-permute-done((bf16[4,2,136,128]{3,2,1,0:T(8,128)(2,1)S(1)}, bf16[4,2,136,128]{3,2,1,0:T(8,128)(2,1)S(1)}, u32[]{:S(2)}, u32[]{:S(2)}) %collective-permute-start.5) | collective-permute-done | bytes 278560 | tf_op jit(solution)/shard_map/ppermute | solution.py:26
  70.8 0.0 collective-permute-done.6
  70.8 1.1 pad_maximum_fusion
  71.9 5.0 %collective-permute-start.7 = (bf16[16,2,136,128]{3,2,1,0:T(8,128)(2,1)}, bf16[16,2,136,128]{3,2,1,0:T(8,128)(2,1)}, u32[]{:S(2)}, u32[]{:S(2)}) collective-permute-start(bf16[16,2,136,128]{3,2,1,0:T(8,128)(2,1)} %pad_maximum_fusion), channel_id=1, source_target_pairs={{0,128},{8,136},{16,144},{24,152},{32,160},{40,168},{48,176},{56,1... | collective-permute-start | bytes 3342344 | tf_op jit(solution)/shard_map/ppermute | solution.py:26
  77.0 1.2 %pad_add_fusion.refs_0_ = s32[3]{0:T(128)} fusion(s32[1]{0:T(128)} %get-tuple-element.38, s32[1]{0:T(128)} %bitcast.6, s32[1]{0:T(128)} %bitcast), kind=kLoop, calls=%fused_computation.20 | loop fusion | flops 6 | bytes 24 | tf_op jit(solution)/shard_map/stack | solution.py:198
  78.2 0.0 copy-start.3
  78.3 1.9 %collective-permute-start.8 = (bf16[5,2,136,128]{3,2,1,0:T(8,128)(2,1)S(1)}, bf16[5,2,136,128]{3,2,1,0:T(8,128)(2,1)S(1)}, u32[]{:S(2)}, u32[]{:S(2)}) collective-permute-start(bf16[5,2,136,128]{3,2,1,0:T(8,128)(2,1)S(1)} %pad_maximum_fusion.1), channel_id=1, source_target_pairs={{0,256},{8,264},{16,272},{24,280},{32,288},{40,296},{48,304},{56,3... | collective-permute-start | bytes 1044488 | tf_op jit(solution)/shard_map/ppermute | solution.py:26
  80.4 0.0 copy-start
  80.4 0.6 broadcast_in_dim.13.refs_3_.refs_4_
  81.1 0.0 copy-done.3
  81.1 0.7 broadcast_in_dim.14.refs_4_.refs_5_
  81.8 0.0 copy-done
  81.8 10.8 %shard_map.73 = (f32[8,128]{1,0:T(8,128)}, f32[8,128]{1,0:T(8,128)}, f32[128,1024]{1,0:T(8,128)}) custom-call(s32[3]{0:T(128)} %pad_add_fusion.refs_0_, bf16[128,1024]{1,0:T(8,128)(2,1)} %bitcast.34, bf16[20,2,136,128]{3,2,1,0:T(8,128)(2,1)} %copy-done, s32[8,128]{1,0:T(8,128)} %broadcast_in_dim.13.refs_3_.refs_4_, f32[128,128]{1,0:T(8,128)} %broadcast_in_dim.14.refs_4_.refs_5_), custom_call_target="tpu_custom_call" | custom-call | tf_op jit(solution)/shard_map/pallas_call | solution.py:154
  92.6 0.0 collective-permute-done.8.refs_3_
  92.6 0.0 copy-start.1
  92.6 15.9 %collective-permute-done.7.refs_2_ = bf16[16,2,136,128]{3,2,1,0:T(8,128)(2,1)} collective-permute-done((bf16[16,2,136,128]{3,2,1,0:T(8,128)(2,1)}, bf16[16,2,136,128]{3,2,1,0:T(8,128)(2,1)}, u32[]{:S(2)}, u32[]{:S(2)}) %collective-permute-start.7) | collective-permute-done | bytes 1114144 | tf_op jit(solution)/shard_map/ppermute | solution.py:26
  108.4 0.0 copy-done.1
  108.4 7.1 %shard_map.74 = bf16[128,1024]{1,0:T(8,128)(2,1)} custom-call(s32[3]{0:T(128)} %pad_add_fusion.refs_0_, bf16[128,1024]{1,0:T(8,128)(2,1)} %bitcast.35, bf16[16,2,136,128]{3,2,1,0:T(8,128)(2,1)} %collective-permute-done.7.refs_2_, bf16[5,2,136,128]{3,2,1,0:T(8,128)(2,1)} %copy-done.1, s32[8,128]{1,0:T(8,128)} %broadcast_in_dim.13.refs_3_.refs_4_, ...), custom_call_target="tpu_custom_call" | custom-call | tf_op jit(solution)/shard_map/pallas_call | solution.py:154
  (18 shorter events, 0.4 us)
Async XLA Ops:
  0.0 55.1 %copy-start.2 = (bf16[128,1024]{1,0:T(8,128)(2,1)S(1)}, bf16[128,1024]{1,0:T(8,128)(2,1)}, u32[]{:S(2)}) copy-start(bf16[128,1024]{1,0:T(8,128)(2,1)} %param.11) | copy-start | bytes 786436
  1.5 15.3 %all-to-all-start = ((bf16[32,8,128]{2,0,1:T(8,128)(2,1)}), bf16[32,8,128]{2,0,1:T(8,128)(2,1)S(1)}, u32[]{:S(2)}, u32[]{:S(2)}) async-start(bf16[32,8,128]{2,0,1:T(8,128)(2,1)} %copy_bitcast_fusion.1), calls=%async_computation | async-start | bytes 131072 | tf_op jit(solution)/shard_map/all_to_all | solution.py:175
  16.9 14.2 %collective-permute-start = (bf16[1,2,136,128]{3,2,1,0:T(8,128)(2,1)S(1)}, bf16[1,2,136,128]{3,2,1,0:T(8,128)(2,1)S(1)}, u32[]{:S(2)}, u32[]{:S(2)}) collective-permute-start(bf16[1,2,136,128]{3,2,1,0:T(8,128)(2,1)S(1)} %maximum_bitcast_fusion), channel_id=1, source_target_pairs={{0,8},{8,16},{16,24},{24,32},{32,40},{40,48},{48,56},{56,64},{64,7... | collective-permute-start | bytes 208904 | tf_op jit(solution)/shard_map/ppermute | solution.py:26
  19.8 11.3 %collective-permute-start.1 = (bf16[1,2,136,128]{3,2,1,0:T(8,128)(2,1)S(1)}, bf16[1,2,136,128]{3,2,1,0:T(8,128)(2,1)S(1)}, u32[]{:S(2)}, u32[]{:S(2)}) collective-permute-start(bf16[1,2,136,128]{3,2,1,0:T(8,128)(2,1)S(1)} %maximum_bitcast_fusion), channel_id=1, source_target_pairs={{0,16},{8,24},{16,32},{24,40},{32,48},{40,56},{48,64},{56,72},{64,... | collective-permute-start | bytes 208904 | tf_op jit(solution)/shard_map/ppermute | solution.py:26
  24.1 8.9 %collective-permute-start.2 = (bf16[1,2,136,128]{3,2,1,0:T(8,128)(2,1)S(1)}, bf16[1,2,136,128]{3,2,1,0:T(8,128)(2,1)S(1)}, u32[]{:S(2)}, u32[]{:S(2)}) collective-permute-start(bf16[1,2,136,128]{3,2,1,0:T(8,128)(2,1)S(1)} %maximum_bitcast_fusion), channel_id=1, source_target_pairs={{0,24},{8,32},{16,40},{24,48},{32,56},{40,64},{48,72},{56,80},{64,... | collective-permute-start | bytes 208904 | tf_op jit(solution)/shard_map/ppermute | solution.py:26
  33.0 24.4 %collective-permute-start.3 = (bf16[4,2,136,128]{3,2,1,0:T(8,128)(2,1)S(1)}, bf16[4,2,136,128]{3,2,1,0:T(8,128)(2,1)S(1)}, u32[]{:S(2)}, u32[]{:S(2)}) collective-permute-start(bf16[4,2,136,128]{3,2,1,0:T(8,128)(2,1)S(1)} %pad_maximum_fusion.2), channel_id=1, source_target_pairs={{0,32},{8,40},{16,48},{24,56},{32,64},{40,72},{48,80},{56,88},{64,... | collective-permute-start | bytes 835592 | tf_op jit(solution)/shard_map/ppermute | solution.py:26
  40.5 26.1 %collective-permute-start.4 = (bf16[4,2,136,128]{3,2,1,0:T(8,128)(2,1)S(1)}, bf16[4,2,136,128]{3,2,1,0:T(8,128)(2,1)S(1)}, u32[]{:S(2)}, u32[]{:S(2)}) collective-permute-start(bf16[4,2,136,128]{3,2,1,0:T(8,128)(2,1)S(1)} %pad_maximum_fusion.2), channel_id=1, source_target_pairs={{0,64},{8,72},{16,80},{24,88},{32,96},{40,104},{48,112},{56,120},{... | collective-permute-start | bytes 835592 | tf_op jit(solution)/shard_map/ppermute | solution.py:26
  45.4 25.4 %collective-permute-start.5 = (bf16[4,2,136,128]{3,2,1,0:T(8,128)(2,1)S(1)}, bf16[4,2,136,128]{3,2,1,0:T(8,128)(2,1)S(1)}, u32[]{:S(2)}, u32[]{:S(2)}) collective-permute-start(bf16[4,2,136,128]{3,2,1,0:T(8,128)(2,1)S(1)} %pad_maximum_fusion.2), channel_id=1, source_target_pairs={{0,96},{8,104},{16,112},{24,120},{32,128},{40,136},{48,144},{56,15... | collective-permute-start | bytes 835592 | tf_op jit(solution)/shard_map/ppermute | solution.py:26
  47.3 23.4 %collective-permute-start.6 = (bf16[4,2,136,128]{3,2,1,0:T(8,128)(2,1)S(1)}, bf16[4,2,136,128]{3,2,1,0:T(8,128)(2,1)S(1)}, u32[]{:S(2)}, u32[]{:S(2)}) collective-permute-start(bf16[4,2,136,128]{3,2,1,0:T(8,128)(2,1)S(1)} %pad_maximum_fusion.2), channel_id=1, source_target_pairs={{0,128},{8,136},{16,144},{24,152},{32,160},{40,168},{48,176},{56,1... | collective-permute-start | bytes 835592 | tf_op jit(solution)/shard_map/ppermute | solution.py:26
  71.9 36.5 %collective-permute-start.7 = (bf16[16,2,136,128]{3,2,1,0:T(8,128)(2,1)}, bf16[16,2,136,128]{3,2,1,0:T(8,128)(2,1)}, u32[]{:S(2)}, u32[]{:S(2)}) collective-permute-start(bf16[16,2,136,128]{3,2,1,0:T(8,128)(2,1)} %pad_maximum_fusion), channel_id=1, source_target_pairs={{0,128},{8,136},{16,144},{24,152},{32,160},{40,168},{48,176},{56,1... | collective-permute-start | bytes 3342344 | tf_op jit(solution)/shard_map/ppermute | solution.py:26
  78.2 2.8 %copy-start.3 = (f32[128]{0:T(128)S(1)}, f32[128]{0:T(128)}, u32[]{:S(2)}) copy-start(f32[128]{0:T(128)} %param.16) | copy-start | bytes 1540
  78.3 14.3 %collective-permute-start.8 = (bf16[5,2,136,128]{3,2,1,0:T(8,128)(2,1)S(1)}, bf16[5,2,136,128]{3,2,1,0:T(8,128)(2,1)S(1)}, u32[]{:S(2)}, u32[]{:S(2)}) collective-permute-start(bf16[5,2,136,128]{3,2,1,0:T(8,128)(2,1)S(1)} %pad_maximum_fusion.1), channel_id=1, source_target_pairs={{0,256},{8,264},{16,272},{24,280},{32,288},{40,296},{48,304},{56,3... | collective-permute-start | bytes 1044488 | tf_op jit(solution)/shard_map/ppermute | solution.py:26
  80.4 1.4 %copy-start = (bf16[20,2,136,128]{3,2,1,0:T(8,128)(2,1)}, bf16[20,2,136,128]{3,2,1,0:T(8,128)(2,1)S(1)}, u32[]{:S(2)}) copy-start(bf16[20,2,136,128]{3,2,1,0:T(8,128)(2,1)S(1)} %constant_dynamic-update-slice_fusion.refs_2_) | copy-start | bytes 4177924
  92.6 15.9 %copy-start.1 = (bf16[5,2,136,128]{3,2,1,0:T(8,128)(2,1)}, bf16[5,2,136,128]{3,2,1,0:T(8,128)(2,1)S(1)}, u32[]{:S(2)}) copy-start(bf16[5,2,136,128]{3,2,1,0:T(8,128)(2,1)S(1)} %collective-permute-done.8.refs_3_) | copy-start | bytes 1044484

commit v17 on v15

--- a/solution.py
+++ b/solution.py
@@ -200,7 +200,7 @@
     near, far = final
     parts = [
         ([jnp.concatenate(first, axis=0)], ((0, 2),)),
-        ([jnp.concatenate(middle, axis=0)], ((4, 2),)),
+        (middle, tuple((4 * (index + 1), 2) for index in range(len(middle)))),
         ([near, far], ((20, 2), (20 + near.shape[0], 1))),
     ]
     state = None

time: 119 us -> 117 us (0.983)
  the two profiles are of different devices: /device:TPU:6 before, /device:TPU:64 now
where the time goes in v17:
time: 117 us; the launch traced here: 116 us
  starting transfers between devices  48.1 us (41%)
  waiting for transfers between devices  44.4 us (38%)
  Pallas kernels  9.63 us (8%)
  local copies, waits for them, and re-layouts  6.81 us (6%)
  other arithmetic  4.65 us (4%)
  between operations  2.52 us (2%)
    ppermute x9, starting transfers between devices, shift_from(): return lax.ppermute(x, 'seq', pairs)  41 us
    ppermute x9, waiting for transfers between devices, shift_from(): return lax.ppermute(x, 'seq', pairs)  38 us
    pallas_call x3, Pallas kernels, attend_part(): pl.pallas_call(kernel, out_shape=out_shape, grid_spec=pltpu.PrefetchScala...  9.63 us
    all_to_all x1, starting transfers between devices, shards(): both = lax.all_to_all(both, 'head', split_axis=1, concat_axis=0, tiled=True)  7.1 us
    all_to_all x1, waiting for transfers between devices, shards(): both = lax.all_to_all(both, 'head', split_axis=1, concat_axis=0, tiled=True)  6.32 us
    unnamed x20, local copies, waits for them, and re-layouts  2.89 us
  transfers between devices with their start and end apart: 10, of which 7 were waited for; matrix products, arithmetic and copies ran while one was open for 7% of the time, Pallas kernels for 6%

profile of v17, /device:TPU:64, one launch (start us, length us, event | category | flops | bytes accessed | tf_op | source)
XLA Modules:
  0.0 116.1 jit_solution(14166988498529341597)
XLA Ops:
  0.0 1.4 %copy_bitcast_fusion.1 = bf16[32,8,128]{2,0,1:T(8,128)(2,1)} fusion(bf16[16,1024]{1,0:T(8,128)(2,1)} %param.13, bf16[16,1024]{1,0:T(8,128)(2,1)} %param.12), kind=kLoop, calls=%fused_computation.6 | loop fusion | flops 131072 | bytes 131072 | tf_op jit(solution)/shard_map/all_to_all | solution.py:175
  1.4 7.1 %all-to-all-start = ((bf16[32,8,128]{2,0,1:T(8,128)(2,1)}), bf16[32,8,128]{2,0,1:T(8,128)(2,1)S(1)}, u32[]{:S(2)}, u32[]{:S(2)}) async-start(bf16[32,8,128]{2,0,1:T(8,128)(2,1)} %copy_bitcast_fusion.1), calls=%async_computation | async-start | bytes 131072 | tf_op jit(solution)/shard_map/all_to_all | solution.py:175
  8.5 0.8 reduce.5
  9.3 0.1 broadcast_in_dim.10
  9.4 0.1 reshape.148
  9.5 0.8 reduce.6
  10.2 0.1 broadcast_in_dim.11
  10.3 0.1 reshape.150
  10.4 6.3 %all-to-all-done = bf16[32,8,128]{2,0,1:T(8,128)(2,1)S(1)} async-done(((bf16[32,8,128]{2,0,1:T(8,128)(2,1)}), bf16[32,8,128]{2,0,1:T(8,128)(2,1)S(1)}, u32[]{:S(2)}, u32[]{:S(2)}) %all-to-all-start) | async-done | bytes 65568 | tf_op jit(solution)/shard_map/all_to_all | solution.py:175
  16.8 0.1 copy.25
  16.9 4.7 %collective-permute-start.2 = (bf16[1,2,136,128]{3,2,1,0:T(8,128)(2,1)S(1)}, bf16[1,2,136,128]{3,2,1,0:T(8,128)(2,1)S(1)}, u32[]{:S(2)}, u32[]{:S(2)}) collective-permute-start(bf16[1,2,136,128]{3,2,1,0:T(8,128)(2,1)S(1)} %maximum_bitcast_fusion), channel_id=1, source_target_pairs={{0,24},{8,32},{16,40},{24,48},{32,56},{40,64},{48,72},{56,80},{64,... | collective-permute-start | bytes 208904 | tf_op jit(solution)/shard_map/ppermute | solution.py:26
  21.5 4.3 %collective-permute-start.1 = (bf16[1,2,136,128]{3,2,1,0:T(8,128)(2,1)S(1)}, bf16[1,2,136,128]{3,2,1,0:T(8,128)(2,1)S(1)}, u32[]{:S(2)}, u32[]{:S(2)}) collective-permute-start(bf16[1,2,136,128]{3,2,1,0:T(8,128)(2,1)S(1)} %maximum_bitcast_fusion), channel_id=1, source_target_pairs={{0,16},{8,24},{16,32},{24,40},{32,48},{40,56},{48,64},{56,72},{64,... | collective-permute-start | bytes 208904 | tf_op jit(solution)/shard_map/ppermute | solution.py:26
  25.8 6.0 %collective-permute-start = (bf16[1,2,136,128]{3,2,1,0:T(8,128)(2,1)S(1)}, bf16[1,2,136,128]{3,2,1,0:T(8,128)(2,1)S(1)}, u32[]{:S(2)}, u32[]{:S(2)}) collective-permute-start(bf16[1,2,136,128]{3,2,1,0:T(8,128)(2,1)S(1)} %maximum_bitcast_fusion), channel_id=1, source_target_pairs={{0,8},{8,16},{16,24},{24,32},{32,40},{40,48},{48,56},{56,64},{64,7... | collective-permute-start | bytes 208904 | tf_op jit(solution)/shard_map/ppermute | solution.py:26
  31.9 1.0 collective-permute-done.2
  32.8 0.0 collective-permute-done.1
  32.8 0.9 collective-permute-done
  33.8 0.0 copy-start.3
  33.8 0.0 copy-start.7
  33.8 3.5 %collective-permute-start.6 = (bf16[4,2,136,128]{3,2,1,0:T(8,128)(2,1)S(1)}, bf16[4,2,136,128]{3,2,1,0:T(8,128)(2,1)S(1)}, u32[]{:S(2)}, u32[]{:S(2)}) collective-permute-start(bf16[4,2,136,128]{3,2,1,0:T(8,128)(2,1)S(1)} %pad_maximum_fusion.2.refs_2_), channel_id=1, source_target_pairs={{0,128},{8,136},{16,144},{24,152},{32,160},{40,168},{48,176},{56,1... | collective-permute-start | bytes 835592 | tf_op jit(solution)/shard_map/ppermute | solution.py:26
  37.4 4.1 %collective-permute-start.5 = (bf16[4,2,136,128]{3,2,1,0:T(8,128)(2,1)S(1)}, bf16[4,2,136,128]{3,2,1,0:T(8,128)(2,1)S(1)}, u32[]{:S(2)}, u32[]{:S(2)}) collective-permute-start(bf16[4,2,136,128]{3,2,1,0:T(8,128)(2,1)S(1)} %pad_maximum_fusion.2.refs_2_), channel_id=1, source_target_pairs={{0,96},{8,104},{16,112},{24,120},{32,128},{40,136},{48,144},{56,15... | collective-permute-start | bytes 835592 | tf_op jit(solution)/shard_map/ppermute | solution.py:26
  41.5 7.9 %collective-permute-start.4 = (bf16[4,2,136,128]{3,2,1,0:T(8,128)(2,1)S(1)}, bf16[4,2,136,128]{3,2,1,0:T(8,128)(2,1)S(1)}, u32[]{:S(2)}, u32[]{:S(2)}) collective-permute-start(bf16[4,2,136,128]{3,2,1,0:T(8,128)(2,1)S(1)} %pad_maximum_fusion.2.refs_2_), channel_id=1, source_target_pairs={{0,64},{8,72},{16,80},{24,88},{32,96},{40,104},{48,112},{56,120},{... | collective-permute-start | bytes 835592 | tf_op jit(solution)/shard_map/ppermute | solution.py:26
  49.4 3.1 %collective-permute-start.3 = (bf16[4,2,136,128]{3,2,1,0:T(8,128)(2,1)S(1)}, bf16[4,2,136,128]{3,2,1,0:T(8,128)(2,1)S(1)}, u32[]{:S(2)}, u32[]{:S(2)}) collective-permute-start(bf16[4,2,136,128]{3,2,1,0:T(8,128)(2,1)S(1)} %pad_maximum_fusion.2.refs_2_), channel_id=1, source_target_pairs={{0,32},{8,40},{16,48},{24,56},{32,64},{40,72},{48,80},{56,88},{64,... | collective-permute-start | bytes 835592 | tf_op jit(solution)/shard_map/ppermute | solution.py:26
  52.5 0.0 collective-permute-done.6.refs_5_
  52.5 0.0 copy-start.4
  52.5 0.4 collective-permute-done.5.refs_4_
  52.9 0.0 copy-start.5
  52.9 17.4 %collective-permute-done.4.refs_3_ = bf16[4,2,136,128]{3,2,1,0:T(8,128)(2,1)S(1)} collective-permute-done((bf16[4,2,136,128]{3,2,1,0:T(8,128)(2,1)S(1)}, bf16[4,2,136,128]{3,2,1,0:T(8,128)(2,1)S(1)}, u32[]{:S(2)}, u32[]{:S(2)}) %collective-permute-start.4) | collective-permute-done | bytes 278560 | tf_op jit(solution)/shard_map/ppermute | solution.py:26
  70.3 0.0 copy-start
  70.3 4.1 %collective-permute-done.3.refs_2_ = bf16[4,2,136,128]{3,2,1,0:T(8,128)(2,1)S(1)} collective-permute-done((bf16[4,2,136,128]{3,2,1,0:T(8,128)(2,1)S(1)}, bf16[4,2,136,128]{3,2,1,0:T(8,128)(2,1)S(1)}, u32[]{:S(2)}, u32[]{:S(2)}) %collective-permute-start.3) | collective-permute-done | bytes 278560 | tf_op jit(solution)/shard_map/ppermute | solution.py:26
  74.3 0.0 copy-done.5
  74.3 0.0 copy-start.1
  74.3 0.1 pad_maximum_fusion
  74.5 0.0 copy-done.3
  74.5 0.0 copy-done.4
  74.5 2.0 %collective-permute-start.7 = (bf16[16,2,136,128]{3,2,1,0:T(8,128)(2,1)S(1)}, bf16[16,2,136,128]{3,2,1,0:T(8,128)(2,1)S(1)}, u32[]{:S(2)}, u32[]{:S(2)}) collective-permute-start(bf16[16,2,136,128]{3,2,1,0:T(8,128)(2,1)S(1)} %pad_maximum_fusion), channel_id=1, source_target_pairs={{0,128},{8,136},{16,144},{24,152},{32,160},{40,168},{48,176},{56,1... | collective-permute-start | bytes 3342344 | tf_op jit(solution)/shard_map/ppermute | solution.py:26
  76.5 0.0 copy-done.7
  76.5 0.1 copy.22
  76.6 0.1 reduce-window.9
  76.7 0.1 reduce.4
  76.8 0.1 convert_reduce_fusion
  76.9 0.0 copy-done
  76.9 0.0 copy-done.1
  77.0 0.0 copy-start.8
  77.0 5.5 %collective-permute-start.8 = (bf16[5,2,136,128]{3,2,1,0:T(8,128)(2,1)S(1)}, bf16[5,2,136,128]{3,2,1,0:T(8,128)(2,1)S(1)}, u32[]{:S(2)}, u32[]{:S(2)}) collective-permute-start(bf16[5,2,136,128]{3,2,1,0:T(8,128)(2,1)S(1)} %pad_maximum_fusion.1), channel_id=1, source_target_pairs={{0,256},{8,264},{16,272},{24,280},{32,288},{40,296},{48,304},{56,3... | collective-permute-start | bytes 1044488 | tf_op jit(solution)/shard_map/ppermute | solution.py:26
  82.5 1.2 %gather_fusion = s32[128]{0:T(128)S(1)} fusion(s32[64]{0:T(128)S(1)} %sub.16, s32[1024]{0:T(1024)S(1)} %pad_clamp_fusion), kind=kCustom, calls=%fused_computation | custom fusion | bytes 1536 | tf_op jit(solution)/shard_map/gather | solution.py:193
  83.7 0.6 fusion.2
  86.6 1.0 copy.27
  87.6 0.2 copy.23
  87.8 0.7 copy.31
  88.6 1.1 pad_add_fusion.refs_0_
  89.7 0.6 broadcast_in_dim.13.refs_3_.refs_6_.refs_4_
  90.3 0.0 copy-done.8
  90.3 0.7 broadcast_in_dim.14.refs_4_.refs_7_.refs_5_
  91.0 3.4 %shard_map.73 = (f32[8,128]{1,0:T(8,128)}, f32[8,128]{1,0:T(8,128)}, f32[128,1024]{1,0:T(8,128)}) custom-call(s32[3]{0:T(128)} %pad_add_fusion.refs_0_, bf16[128,1024]{1,0:T(8,128)(2,1)} %bitcast.32, bf16[4,2,136,128]{3,2,1,0:T(8,128)(2,1)} %copy-done.3, s32[8,128]{1,0:T(8,128)} %broadcast_in_dim.13.refs_3_.refs_6_.refs_4_, ...), custom_call_target="tpu_custom_call" | custom-call | tf_op jit(solution)/shard_map/pallas_call | solution.py:154
  94.4 3.1 %shard_map.74 = (f32[8,128]{1,0:T(8,128)}, f32[8,128]{1,0:T(8,128)}, f32[128,1024]{1,0:T(8,128)}) custom-call(s32[3]{0:T(128)} %pad_add_fusion.refs_0_, bf16[128,1024]{1,0:T(8,128)(2,1)} %bitcast.33, bf16[4,2,136,128]{3,2,1,0:T(8,128)(2,1)} %copy-done.1, bf16[4,2,136,128]{3,2,1,0:T(8,128)(2,1)} %copy-done, bf16[4,2,136,128]{3,2,1,0:T(8,128)(2,1)} %copy-done.5, ...), custom_call_target="tpu_custom_call" | custom-call | tf_op jit(solution)/shard_map/pallas_call | solution.py:154
  97.5 14.3 %collective-permute-done.8.refs_3_ = bf16[5,2,136,128]{3,2,1,0:T(8,128)(2,1)S(1)} collective-permute-done((bf16[5,2,136,128]{3,2,1,0:T(8,128)(2,1)S(1)}, bf16[5,2,136,128]{3,2,1,0:T(8,128)(2,1)S(1)}, u32[]{:S(2)}, u32[]{:S(2)}) %collective-permute-start.8) | collective-permute-done | bytes 348192 | tf_op jit(solution)/shard_map/ppermute | solution.py:26
  111.8 0.0 copy-start.6
  111.8 0.0 collective-permute-done.7.refs_2_
  111.8 0.0 copy-start.2
  111.8 0.7 copy-done.6
  112.5 0.4 copy-done.2
  112.9 3.2 %shard_map.75 = bf16[128,1024]{1,0:T(8,128)(2,1)} custom-call(s32[3]{0:T(128)} %pad_add_fusion.refs_0_, bf16[128,1024]{1,0:T(8,128)(2,1)} %bitcast.34, bf16[16,2,136,128]{3,2,1,0:T(8,128)(2,1)} %copy-done.2, bf16[5,2,136,128]{3,2,1,0:T(8,128)(2,1)} %copy-done.6, s32[8,128]{1,0:T(8,128)} %broadcast_in_dim.13.refs_3_.refs_6_.refs_4_, ...), custom_call_target="tpu_custom_call" | custom-call | tf_op jit(solution)/shard_map/pallas_call | solution.py:154
  (10 shorter events, 0.1 us)
Async XLA Ops:
  1.4 15.3 %all-to-all-start = ((bf16[32,8,128]{2,0,1:T(8,128)(2,1)}), bf16[32,8,128]{2,0,1:T(8,128)(2,1)S(1)}, u32[]{:S(2)}, u32[]{:S(2)}) async-start(bf16[32,8,128]{2,0,1:T(8,128)(2,1)} %copy_bitcast_fusion.1), calls=%async_computation | async-start | bytes 131072 | tf_op jit(solution)/shard_map/all_to_all | solution.py:175
  16.9 16.0 %collective-permute-start.2 = (bf16[1,2,136,128]{3,2,1,0:T(8,128)(2,1)S(1)}, bf16[1,2,136,128]{3,2,1,0:T(8,128)(2,1)S(1)}, u32[]{:S(2)}, u32[]{:S(2)}) collective-permute-start(bf16[1,2,136,128]{3,2,1,0:T(8,128)(2,1)S(1)} %maximum_bitcast_fusion), channel_id=1, source_target_pairs={{0,24},{8,32},{16,40},{24,48},{32,56},{40,64},{48,72},{56,80},{64,... | collective-permute-start | bytes 208904 | tf_op jit(solution)/shard_map/ppermute | solution.py:26
  21.5 11.3 %collective-permute-start.1 = (bf16[1,2,136,128]{3,2,1,0:T(8,128)(2,1)S(1)}, bf16[1,2,136,128]{3,2,1,0:T(8,128)(2,1)S(1)}, u32[]{:S(2)}, u32[]{:S(2)}) collective-permute-start(bf16[1,2,136,128]{3,2,1,0:T(8,128)(2,1)S(1)} %maximum_bitcast_fusion), channel_id=1, source_target_pairs={{0,16},{8,24},{16,32},{24,40},{32,48},{40,56},{48,64},{56,72},{64,... | collective-permute-start | bytes 208904 | tf_op jit(solution)/shard_map/ppermute | solution.py:26
  25.8 7.9 %collective-permute-start = (bf16[1,2,136,128]{3,2,1,0:T(8,128)(2,1)S(1)}, bf16[1,2,136,128]{3,2,1,0:T(8,128)(2,1)S(1)}, u32[]{:S(2)}, u32[]{:S(2)}) collective-permute-start(bf16[1,2,136,128]{3,2,1,0:T(8,128)(2,1)S(1)} %maximum_bitcast_fusion), channel_id=1, source_target_pairs={{0,8},{8,16},{16,24},{24,32},{32,40},{40,48},{48,56},{56,64},{64,7... | collective-permute-start | bytes 208904 | tf_op jit(solution)/shard_map/ppermute | solution.py:26
  33.8 40.6 %copy-start.3 = (bf16[4,2,136,128]{3,2,1,0:T(8,128)(2,1)}, bf16[4,2,136,128]{3,2,1,0:T(8,128)(2,1)S(1)}, u32[]{:S(2)}) copy-start(bf16[4,2,136,128]{3,2,1,0:T(8,128)(2,1)S(1)} %pad_maximum_fusion.2.refs_2_) | copy-start | bytes 835588
  33.8 42.7 %copy-start.7 = (s32[64]{0:T(128)S(1)}, s32[64]{0:T(128)}, u32[]{:S(2)}) copy-start(s32[64]{0:T(128)} %param.17) | copy-start | bytes 772
  33.8 18.6 %collective-permute-start.6 = (bf16[4,2,136,128]{3,2,1,0:T(8,128)(2,1)S(1)}, bf16[4,2,136,128]{3,2,1,0:T(8,128)(2,1)S(1)}, u32[]{:S(2)}, u32[]{:S(2)}) collective-permute-start(bf16[4,2,136,128]{3,2,1,0:T(8,128)(2,1)S(1)} %pad_maximum_fusion.2.refs_2_), channel_id=1, source_target_pairs={{0,128},{8,136},{16,144},{24,152},{32,160},{40,168},{48,176},{56,1... | collective-permute-start | bytes 835592 | tf_op jit(solution)/shard_map/ppermute | solution.py:26
  37.4 15.5 %collective-permute-start.5 = (bf16[4,2,136,128]{3,2,1,0:T(8,128)(2,1)S(1)}, bf16[4,2,136,128]{3,2,1,0:T(8,128)(2,1)S(1)}, u32[]{:S(2)}, u32[]{:S(2)}) collective-permute-start(bf16[4,2,136,128]{3,2,1,0:T(8,128)(2,1)S(1)} %pad_maximum_fusion.2.refs_2_), channel_id=1, source_target_pairs={{0,96},{8,104},{16,112},{24,120},{32,128},{40,136},{48,144},{56,15... | collective-permute-start | bytes 835592 | tf_op jit(solution)/shard_map/ppermute | solution.py:26
  41.5 28.8 %collective-permute-start.4 = (bf16[4,2,136,128]{3,2,1,0:T(8,128)(2,1)S(1)}, bf16[4,2,136,128]{3,2,1,0:T(8,128)(2,1)S(1)}, u32[]{:S(2)}, u32[]{:S(2)}) collective-permute-start(bf16[4,2,136,128]{3,2,1,0:T(8,128)(2,1)S(1)} %pad_maximum_fusion.2.refs_2_), channel_id=1, source_target_pairs={{0,64},{8,72},{16,80},{24,88},{32,96},{40,104},{48,112},{56,120},{... | collective-permute-start | bytes 835592 | tf_op jit(solution)/shard_map/ppermute | solution.py:26
  49.4 25.0 %collective-permute-start.3 = (bf16[4,2,136,128]{3,2,1,0:T(8,128)(2,1)S(1)}, bf16[4,2,136,128]{3,2,1,0:T(8,128)(2,1)S(1)}, u32[]{:S(2)}, u32[]{:S(2)}) collective-permute-start(bf16[4,2,136,128]{3,2,1,0:T(8,128)(2,1)S(1)} %pad_maximum_fusion.2.refs_2_), channel_id=1, source_target_pairs={{0,32},{8,40},{16,48},{24,56},{32,64},{40,72},{48,80},{56,88},{64,... | collective-permute-start | bytes 835592 | tf_op jit(solution)/shard_map/ppermute | solution.py:26
  52.5 22.0 %copy-start.4 = (bf16[4,2,136,128]{3,2,1,0:T(8,128)(2,1)}, bf16[4,2,136,128]{3,2,1,0:T(8,128)(2,1)S(1)}, u32[]{:S(2)}) copy-start(bf16[4,2,136,128]{3,2,1,0:T(8,128)(2,1)S(1)} %collective-permute-done.6.refs_5_) | copy-start | bytes 835588
  52.9 21.4 %copy-start.5 = (bf16[4,2,136,128]{3,2,1,0:T(8,128)(2,1)}, bf16[4,2,136,128]{3,2,1,0:T(8,128)(2,1)S(1)}, u32[]{:S(2)}) copy-start(bf16[4,2,136,128]{3,2,1,0:T(8,128)(2,1)S(1)} %collective-permute-done.5.refs_4_) | copy-start | bytes 835588
  70.3 6.7 %copy-start = (bf16[4,2,136,128]{3,2,1,0:T(8,128)(2,1)}, bf16[4,2,136,128]{3,2,1,0:T(8,128)(2,1)S(1)}, u32[]{:S(2)}) copy-start(bf16[4,2,136,128]{3,2,1,0:T(8,128)(2,1)S(1)} %collective-permute-done.4.refs_3_) | copy-start | bytes 835588
  74.3 2.6 %copy-start.1 = (bf16[4,2,136,128]{3,2,1,0:T(8,128)(2,1)}, bf16[4,2,136,128]{3,2,1,0:T(8,128)(2,1)S(1)}, u32[]{:S(2)}) copy-start(bf16[4,2,136,128]{3,2,1,0:T(8,128)(2,1)S(1)} %collective-permute-done.3.refs_2_) | copy-start | bytes 835588
  74.5 37.3 %collective-permute-start.7 = (bf16[16,2,136,128]{3,2,1,0:T(8,128)(2,1)S(1)}, bf16[16,2,136,128]{3,2,1,0:T(8,128)(2,1)S(1)}, u32[]{:S(2)}, u32[]{:S(2)}) collective-permute-start(bf16[16,2,136,128]{3,2,1,0:T(8,128)(2,1)S(1)} %pad_maximum_fusion), channel_id=1, source_target_pairs={{0,128},{8,136},{16,144},{24,152},{32,160},{40,168},{48,176},{56,1... | collective-permute-start | bytes 3342344 | tf_op jit(solution)/shard_map/ppermute | solution.py:26
  77.0 13.3 %copy-start.8 = (f32[128]{0:T(128)S(1)}, f32[128]{0:T(128)}, u32[]{:S(2)}) copy-start(f32[128]{0:T(128)} %param.16) | copy-start | bytes 1540
  77.0 34.8 %collective-permute-start.8 = (bf16[5,2,136,128]{3,2,1,0:T(8,128)(2,1)S(1)}, bf16[5,2,136,128]{3,2,1,0:T(8,128)(2,1)S(1)}, u32[]{:S(2)}, u32[]{:S(2)}) collective-permute-start(bf16[5,2,136,128]{3,2,1,0:T(8,128)(2,1)S(1)} %pad_maximum_fusion.1), channel_id=1, source_target_pairs={{0,256},{8,264},{16,272},{24,280},{32,288},{40,296},{48,304},{56,3... | collective-permute-start | bytes 1044488 | tf_op jit(solution)/shard_map/ppermute | solution.py:26
  111.8 0.7 copy-start.6
  111.8 1.1 copy-start.2
